TPU v7x, 128 devices: a whole 4x4x4 slice. The times are simulated.
128 devices in a mesh: tile: 64 (over z_hi, y, x, core), head: 2 (over z_lo).
Axes of the slice: x: 4, y: 4, z: 4 (z_hi: 2, z_lo: 2; z = z_hi * 2 + z_lo), core: 2. Of those that a mesh axis runs over, the one named last changes fastest.
Arguments:
- traces: bfloat16 [4096, 128, 128], P('tile'), may hold values from -6 to 6
- trace_mask: int32 [4096, 128], P('tile'), may hold values 0 or 1
- embed_voxel: bfloat16 [4096, 768], P(None, 'head'), may hold values from -0.125 to 0.125
- embed_mask: bfloat16 [256, 768], P(None, 'head'), may hold values from -0.5 to 0.5
- position: bfloat16 [512, 768], P(None, 'head'), may hold values from -3 to 3
- norm_gain: float32 [3, 768], replicated, may hold values from 0.5 to 1.5
- norm_bias: float32 [3, 768], replicated, may hold values from -2 to 2
- w_qkv: bfloat16 [1, 3, 768, 768], P(None, None, None, 'head'), may hold values from -8 to 8
- w_out: bfloat16 [1, 768, 768], P(None, 'head'), may hold values from -0.21875 to 0.21875
- w_up: bfloat16 [1, 768, 3072], P(None, None, 'head'), may hold values from -0.21875 to 0.21875
- w_down: bfloat16 [1, 3072, 768], P(None, 'head'), may hold values from -0.109375 to 0.109375
- w_decode: bfloat16 [768, 4096], P(None, 'head'), may hold values from -0.21875 to 0.21875
Outputs:
- reconstruction: bfloat16 [4096, 128, 128], P('tile')
Inputs may be any that keep to these rules, and one draw needn't show every extreme that they name: `trace_mask`: 1 marks a recorded trace, 0 a missing one.
All inputs are finite; a program needn't handle non-finite values. No bound on the sum of `trace_mask` on one device may be relied on, other than what follows from the above.
Results may differ from a plain program's by a relative error of at most 0.019.
Values may be sent and summed in bfloat16 or wider, within the bound.
No kernel may reach another device: no remote copies, remote signals or barrier semaphores. Data moves between devices by JAX's collectives and lax.ppermute only.
A program may use at most 256 MiB of HBM per device.

v0:
```python
import jax
import jax.numpy as jnp
from jax import lax
from jax.sharding import PartitionSpec as P

PATCH = 16
LAYERS = 1
WIN = 128
HEAD_DIM = 64
HALF = 64


EPSILON = 1e-06


def from_behind(block, axis, distance):
    devices = range(lax.axis_size(axis))
    route = [(i - distance, i) for i in devices if i - distance in devices]
    return lax.ppermute(block, axis, route)


def layer_norm(values, gain, bias):
    average = jnp.mean(values, axis=-1, keepdims=True)
    centered = values - average
    variance = jnp.mean(centered * centered, axis=-1, keepdims=True)
    return centered * lax.rsqrt(variance + EPSILON) * gain + bias


def blend_profile(offset, inner_rows):
    side = WIN // PATCH
    blocks = jnp.arange(side, dtype=jnp.float32)[:, None] * PATCH
    inner = jnp.arange(inner_rows, dtype=jnp.float32)[None, :]
    places = blocks + offset + inner
    return jnp.exp(-0.5 * ((places - (WIN - 1) / 2) / (WIN / 4)) ** 2)


def embed_planes(amplitudes, live, embed_voxel, embed_mask):
    side = WIN // PATCH
    depth_side = amplitudes.shape[0] // PATCH
    rows = depth_side * side * side
    masked = amplitudes * live[:, :, None]
    voxels = (
        masked.reshape(depth_side, PATCH, side, PATCH, side, PATCH)
        .transpose(0, 2, 4, 1, 3, 5)
        .reshape(rows, PATCH**3)
    )
    mask_patches = (
        live.reshape(depth_side, PATCH, side, PATCH)
        .transpose(0, 2, 1, 3)
        .reshape(depth_side * side, PATCH * PATCH)
    )
    embedded = jnp.dot(voxels, embed_voxel, preferred_element_type=jnp.float32)
    mask_terms = jnp.dot(mask_patches, embed_mask, preferred_element_type=jnp.float32)
    local_width = mask_terms.shape[1]
    return embedded + jnp.broadcast_to(
        mask_terms[:, None, :], (depth_side * side, side, local_width)
    ).reshape(rows, local_width)


def body(
    traces,
    trace_mask,
    embed_voxel,
    embed_mask,
    position,
    norm_gain,
    norm_bias,
    w_qkv,
    w_out,
    w_up,
    w_down,
    w_decode,
):
    side = WIN // PATCH
    tokens = side**3
    tile_index = lax.axis_index("tile")
    own_live = trace_mask.astype(jnp.bfloat16)
    own_embedded = embed_planes(traces, own_live, embed_voxel, embed_mask)
    next_traces, next_live = from_behind((traces, own_live), "tile", -1)
    arrived_rows = embed_planes(next_traces, next_live, embed_voxel, embed_mask)
    embedded = jnp.concatenate([own_embedded, arrived_rows], 0)
    embedded = embedded + position.astype(jnp.float32)
    stream = lax.all_gather(embedded.astype(jnp.bfloat16), "head", axis=1, tiled=True).astype(
        embedded.dtype
    )
    local_heads = w_qkv.shape[3] // HEAD_DIM
    normed = layer_norm(stream, norm_gain[0], norm_bias[0]).astype(jnp.bfloat16)
    projected = jnp.einsum(
        "td,sde->ste", normed, w_qkv[0], preferred_element_type=jnp.float32
    ).astype(jnp.bfloat16)
    query = projected[0].reshape(tokens, local_heads, HEAD_DIM)
    keys = projected[1].reshape(tokens, local_heads, HEAD_DIM)
    values = projected[2].reshape(tokens, local_heads, HEAD_DIM)
    scores = jnp.einsum(
        "thd,shd->hts", query, keys, preferred_element_type=jnp.float32
    ) * HEAD_DIM ** (-0.5)
    weights = jax.nn.softmax(scores, axis=-1).astype(jnp.bfloat16)
    attended = jnp.einsum(
        "hts,shd->thd", weights, values, preferred_element_type=jnp.float32
    ).astype(jnp.bfloat16)
    attended = attended.reshape(tokens, local_heads * HEAD_DIM)
    partial_attention = jnp.dot(attended, w_out[0], preferred_element_type=jnp.float32)
    stream = stream + lax.psum(partial_attention.astype(jnp.bfloat16), "head").astype(jnp.float32)
    normed = layer_norm(stream, norm_gain[1], norm_bias[1]).astype(jnp.bfloat16)
    hidden = jax.nn.gelu(
        jnp.dot(normed, w_up[0], preferred_element_type=jnp.float32), approximate=True
    ).astype(jnp.bfloat16)
    partial_forward = jnp.dot(hidden, w_down[0], preferred_element_type=jnp.float32)
    stream = stream + lax.psum(partial_forward.astype(jnp.bfloat16), "head").astype(jnp.float32)
    latent = layer_norm(stream, norm_gain[2 * LAYERS], norm_bias[2 * LAYERS]).astype(jnp.bfloat16)
    half_side = side // 2
    decoded = jnp.dot(latent, w_decode, preferred_element_type=jnp.float32).astype(jnp.bfloat16)
    decoded = lax.all_gather(decoded, "head", axis=1, tiled=True)
    inner_rows = PATCH
    offset = 0
    cells = decoded.reshape(side, side * side, inner_rows, PATCH * PATCH)
    profile = blend_profile(offset, inner_rows)
    upper_part = from_behind(cells[half_side:], "tile", 1)
    numerator = (
        cells[:half_side].astype(jnp.float32) * profile[:half_side, None, :, None]
        + upper_part.astype(jnp.float32) * profile[half_side:, None, :, None]
    )
    later = (tile_index > 0).astype(jnp.float32)
    denominator = profile[:half_side] + later * profile[half_side:]
    blended = (numerator / denominator[:, None, :, None]).astype(jnp.bfloat16)
    arranged = blended.reshape(half_side, side, side, PATCH, PATCH, PATCH).transpose(
        0, 3, 1, 4, 2, 5
    )
    return arranged.reshape(HALF, WIN, WIN)


def solution(mesh):
    return jax.shard_map(
        body,
        mesh=mesh,
        in_specs=(
            P("tile", None, None),
            P("tile", None),
            P(None, "head"),
            P(None, "head"),
            P(None, "head"),
            P(),
            P(),
            P(None, None, None, "head"),
            P(None, "head", None),
            P(None, None, "head"),
            P(None, "head", None),
            P(None, "head"),
        ),
        out_specs=P("tile", None, None),
        check_vma=False,
    )
```

profile of v0, /device:TPU:31, one launch (start us, length us, event | category | flops | bytes accessed | tf_op | source)
XLA Modules:
  0.0 455.8 jit_solution(2542849643086816779)
XLA Ops:
  6.5 2.8 collective-permute-start
  9.4 0.8 convert_element_type.69
  10.1 2.2 collective-permute-start.1
  12.3 0.1 reshape.96
  12.5 3.4 broadcast_multiply_fusion.1
  15.9 17.6 %reshape.94 = bf16[4,16,8,16,8,16]{5,4,3,2,1,0:T(8,128)(2,1)} reshape(bf16[64,128,128]{2,1,0:T(8,128)(2,1)} %broadcast_multiply_fusion.1) | data formatting | bytes 4194304 | tf_op jit(solution)/shard_map/reshape | solution.py:43
  33.5 15.1 %copy.34 = bf16[4,16,8,16,8,16]{5,3,1,4,2,0:T(8,128)(2,1)} copy(bf16[4,16,8,16,8,16]{5,4,3,2,1,0:T(8,128)(2,1)} %reshape.94) | data formatting | bytes 4194304 | tf_op jit(solution)/shard_map/reshape | solution.py:43
  48.6 29.8 %reshape.95 = bf16[256,4096]{1,0:T(8,128)(2,1)} reshape(bf16[4,8,8,16,16,16]{5,4,3,2,1,0:T(8,128)(2,1)} %bitcast.93) | data formatting | bytes 4194304 | tf_op jit(solution)/shard_map/reshape | solution.py:45
  78.4 0.7 copy.36
  79.0 1.1 reshape.97
  80.1 0.1 fusion.76
  80.3 4.6 convolution_add_fusion.1
  84.9 0.8 reshape.101
  85.7 0.9 copy.35
  86.6 0.2 reshape.102
  86.8 0.1 fusion.77
  86.9 3.4 broadcast_multiply_fusion
  90.4 17.6 %reshape.99 = bf16[4,16,8,16,8,16]{5,4,3,2,1,0:T(8,128)(2,1)} reshape(bf16[64,128,128]{2,1,0:T(8,128)(2,1)} %broadcast_multiply_fusion) | data formatting | bytes 4194304 | tf_op jit(solution)/shard_map/reshape | solution.py:43
  108.0 15.1 %copy.33 = bf16[4,16,8,16,8,16]{5,3,1,4,2,0:T(8,128)(2,1)} copy(bf16[4,16,8,16,8,16]{5,4,3,2,1,0:T(8,128)(2,1)} %reshape.99) | data formatting | bytes 4194304 | tf_op jit(solution)/shard_map/reshape | solution.py:43
  123.1 29.7 %reshape.100 = bf16[256,4096]{1,0:T(8,128)(2,1)} reshape(bf16[4,8,8,16,16,16]{5,4,3,2,1,0:T(8,128)(2,1)} %bitcast.94) | data formatting | bytes 4194304 | tf_op jit(solution)/shard_map/reshape | solution.py:45
  152.8 3.9 convolution_add_fusion
  156.8 11.4 %all_gather.6 = bf16[512,768]{1,0:T(8,128)(2,1)S(1)} all-gather(bf16[512,384]{1,0:T(8,128)(2,1)S(1)} %fusion.46), channel_id=1, replica_groups=mesh['tile'=64,'head'=2] {'head'}, dimensions={1}, use_global_device_ids=true | all-gather | bytes 1179648 | tf_op jit(solution)/shard_map/all_gather | solution.py:83
  168.2 0.2 convert_reduce_fusion
  168.4 0.4 fusion.27
  168.8 1.3 fusion.34
  170.1 1.0 fusion.73
  171.1 6.5 %fusion.75 = (f32[6,512]{1,0:T(8,128)}, f32[6,512,512]{1,2,0:T(8,128)}) fusion(bf16[512,6,64]{0,2,1:T(8,128)(2,1)} %bitcast.103, bf16[512,6,64]{0,2,1:T(8,128)(2,1)} %bitcast.102), kind=kOutput, calls=%fused_computation.98 | convolution fusion | flops 206045696 | bytes 7090176 | tf_op jit(solution)/shard_map/sub | solution.py:97
  177.6 3.5 fusion.41
  181.1 1.5 convolution_convert_fusion.1
  182.7 43.5 %all-reduce.3.cloned.1.call-done = bf16[512,768]{1,0:T(8,128)(2,1)} async-done(((bf16[512,768]{1,0:T(8,128)(2,1)}), bf16[512,768]{1,0:T(8,128)(2,1)}) %all-reduce.3.cloned.1.call-update) | async-done | bytes 786448 | tf_op jit(solution)/shard_map/psum | solution.py:103
  226.2 1.8 fusion.40
  228.0 0.4 multiply_reduce_fusion.2
  228.5 6.6 %fusion.37 = bf16[512,768]{1,0:T(8,128)(2,1)} fusion(bf16[1,1536,768]{2,1,0:T(8,128)(2,1)} %param.22, bf16[1,768,1536]{2,1,0:T(8,128)(2,1)} %param.21, bf16[512,768]{1,0:T(8,128)(2,1)} %all-reduce.3.cloned.1.call-done, bf16[512,768]{1,0:T(8,128)(2,1)} %copy-done.1, f32[768]{0:T(1024)S(1)} %get-tuple-element.8, f32[768]{0:T(1024)S(1)} %get-tuple-element.23, ...), kind=kOutput, calls=%fused_computation.47 | convolution fusion | flops 2426535936 | bytes 7088128 | tf_op jit(solution)/shard_map/dot_general | solution.py:108
  235.2 42.2 %all-reduce.5.cloned.1.call-done = bf16[512,768]{1,0:T(8,128)(2,1)} async-done(((bf16[512,768]{1,0:T(8,128)(2,1)}), bf16[512,768]{1,0:T(8,128)(2,1)}) %all-reduce.5.cloned.1.call-update) | async-done | bytes 786448 | tf_op jit(solution)/shard_map/psum | solution.py:109
  277.4 2.1 fusion.66
  279.5 0.1 copy-done.6
  279.7 0.5 multiply_reduce_fusion.1
  280.2 3.4 convolution_convert_fusion
  283.6 60.4 %all-gather.2.cloned.1.call-done = bf16[512,4096]{1,0:T(8,128)(2,1)} async-done(((bf16[512,2048]{1,0:T(8,128)(2,1)}), bf16[512,4096]{1,0:T(8,128)(2,1)}) %all-gather.2.cloned.1.call-update) | async-done | bytes 4194320 | tf_op jit(solution)/shard_map/all_gather | solution.py:113
  344.0 4.8 %fusion.72 = (bf16[256,4096]{1,0:T(8,128)(2,1)S(1)}, f32[256,4096]{1,0:T(8,128)}) fusion(bf16[512,4096]{1,0:T(8,128)(2,1)} %all-gather.2.cloned.1.call-done), kind=kLoop, calls=%fused_computation.95 | loop fusion | flops 1048576 | bytes 10485760 | tf_op jit(solution)/shard_map/slice | solution.py:118
  348.8 2.0 copy.26
  350.7 5.3 %collective-permute-start.2 = (bf16[4,64,16,256]{3,2,1,0:T(8,128)(2,1)}, bf16[4,64,16,256]{3,2,1,0:T(8,128)(2,1)}, u32[]{:S(2)}, u32[]{:S(2)}) collective-permute-start(bf16[4,64,16,256]{3,2,1,0:T(8,128)(2,1)} %bitcast.28), channel_id=1, source_target_pairs={{0,2},{2,4},{4,6},{6,8},{8,10},{10,12},{12,14},{14,16},{16,18},{18... | collective-permute-start | bytes 6291464 | tf_op jit(solution)/shard_map/ppermute | solution.py:19
  356.2 3.9 copy.25
  360.1 19.0 %collective-permute-done.2 = bf16[4,64,16,256]{3,2,1,0:T(8,128)(2,1)} collective-permute-done((bf16[4,64,16,256]{3,2,1,0:T(8,128)(2,1)}, bf16[4,64,16,256]{3,2,1,0:T(8,128)(2,1)}, u32[]{:S(2)}, u32[]{:S(2)}) %collective-permute-start.2) | collective-permute-done | bytes 2097184 | tf_op jit(solution)/shard_map/ppermute | solution.py:19
  379.1 3.9 fusion.6
  383.1 17.4 %reshape.105 = bf16[4,8,8,16,16,16]{5,4,3,2,1,0:T(8,128)(2,1)} reshape(bf16[4,64,16,256]{3,2,1,0:T(8,128)(2,1)} %fusion.6) | data formatting | bytes 4194304 | tf_op jit(solution)/shard_map/reshape | solution.py:126
  400.4 30.1 %copy.32 = bf16[4,8,8,16,16,16]{5,2,4,1,3,0:T(8,128)(2,1)} copy(bf16[4,8,8,16,16,16]{5,4,3,2,1,0:T(8,128)(2,1)} %reshape.105) | data formatting | bytes 4194304 | tf_op jit(solution)/shard_map/reshape | solution.py:126
  430.5 18.8 %reshape.106 = bf16[64,128,128]{2,1,0:T(8,128)(2,1)} reshape(bf16[4,16,8,16,8,16]{5,4,3,2,1,0:T(8,128)(2,1)} %bitcast.95) | data formatting | bytes 4194304 | tf_op jit(solution)/shard_map/reshape | solution.py:129
  (46 shorter events, 0.5 us)
Async XLA Ops:
  6.5 273.6 %copy-start = (bf16[768,2048]{1,0:T(8,128)(2,1)S(1)}, bf16[768,2048]{1,0:T(8,128)(2,1)}, u32[]{:S(2)}) copy-start(bf16[768,2048]{1,0:T(8,128)(2,1)} %param.23) | copy-start | bytes 9437188
  6.5 219.7 %all-reduce.3.cloned.1.call-start = ((), (), s32[]{:S(2)}) async-start(), calls=%async_computation | async-start | bytes 1572864 | tf_op jit(solution)/shard_map/psum | solution.py:103
  6.5 80.4 %collective-permute-start = (bf16[64,128,128]{2,1,0:T(8,128)(2,1)}, bf16[64,128,128]{2,1,0:T(8,128)(2,1)}, u32[]{:S(2)}, u32[]{:S(2)}) collective-permute-start(bf16[64,128,128]{2,1,0:T(8,128)(2,1)} %param.12), channel_id=1, source_target_pairs={{2,0},{4,2},{6,4},{8,6},{10,8},{12,10},{14,12},{16,14},{18,16},{20... | collective-permute-start | bytes 6291464 | tf_op jit(solution)/shard_map/ppermute | solution.py:19
  10.1 74.7 %collective-permute-start.1 = (bf16[64,128]{1,0:T(8,128)(2,1)S(1)}, bf16[64,128]{1,0:T(8,128)(2,1)S(1)}, u32[]{:S(2)}, u32[]{:S(2)}) collective-permute-start(bf16[64,128]{1,0:T(8,128)(2,1)S(1)} %convert_element_type.69), channel_id=1, source_target_pairs={{2,0},{4,2},{6,4},{8,6},{10,8},{12,10},{14,12},{16,14},{18,16},{20... | collective-permute-start | bytes 49160 | tf_op jit(solution)/shard_map/ppermute | solution.py:19
  48.6 31.5 %copy-start.7 = (bf16[256,384]{1,0:T(8,128)(2,1)S(1)}, bf16[256,384]{1,0:T(8,128)(2,1)}, u32[]{:S(2)}) copy-start(bf16[256,384]{1,0:T(8,128)(2,1)} %param.15) | copy-start | bytes 589828
  80.3 4.6 %copy-start.11 = (f32[3,768]{1,0:T(4,128)S(1)}, f32[3,768]{1,0:T(4,128)}, u32[]{:S(2)}) copy-start(f32[3,768]{1,0:T(4,128)} %param.18) | copy-start | bytes 27652
  80.3 4.6 %copy-start.12 = (f32[3,768]{1,0:T(4,128)S(1)}, f32[3,768]{1,0:T(4,128)}, u32[]{:S(2)}) copy-start(f32[3,768]{1,0:T(4,128)} %param.17) | copy-start | bytes 27652
  152.8 3.9 copy-start.9
  152.8 3.9 copy-start.10
  156.7 12.0 %copy-start.13 = (bf16[1,3,768,384]{3,2,1,0:T(8,128)(2,1)S(1)}, bf16[1,3,768,384]{3,2,1,0:T(8,128)(2,1)}, u32[]{:S(2)}) copy-start(bf16[1,3,768,384]{3,2,1,0:T(8,128)(2,1)} %param.19) | copy-start | bytes 5308420
  168.2 1.9 copy-start.1
  177.6 3.5 copy-start.8
  182.6 94.7 %all-reduce.5.cloned.1.call-start = ((), (), s32[]{:S(2)}) async-start(), calls=%async_computation.1 | async-start | bytes 1572864 | tf_op jit(solution)/shard_map/psum | solution.py:109
  226.2 1.8 copy-start.2
  226.2 1.8 copy-start.4
  235.1 108.9 %all-gather.2.cloned.1.call-start = ((), (), s32[]{:S(2)}) async-start(), calls=%async_computation.2 | async-start | bytes 6291456 | tf_op jit(solution)/shard_map/all_gather | solution.py:113
  277.3 2.2 copy-start.3
  277.3 2.2 copy-start.5
  277.3 2.3 copy-start.6
  350.7 28.4 %collective-permute-start.2 = (bf16[4,64,16,256]{3,2,1,0:T(8,128)(2,1)}, bf16[4,64,16,256]{3,2,1,0:T(8,128)(2,1)}, u32[]{:S(2)}, u32[]{:S(2)}) collective-permute-start(bf16[4,64,16,256]{3,2,1,0:T(8,128)(2,1)} %bitcast.28), channel_id=1, source_target_pairs={{0,2},{2,4},{4,6},{6,8},{8,10},{10,12},{12,14},{14,16},{16,18},{18... | collective-permute-start | bytes 6291464 | tf_op jit(solution)/shard_map/ppermute | solution.py:19
Sparse Core Ops, SparseCore 0:
  182.8 43.3 all-reduce.2
  235.2 42.0 all-reduce.4
  283.7 60.2 all-gather.1
where the time goes:
time: 463 us; the launch traced here: 456 us
  local copies, waits for them, and re-layouts  202 us (44%)
  waiting for transfers between devices  165 us (36%)
  matrix products  31.6 us (7%)
  other arithmetic  21.9 us (5%)
  between operations  13.4 us (3%)
  blocking collectives  11.4 us (2%)
  starting transfers between devices  10.4 us (2%)
    reshape x4, local copies, waits for them, and re-layouts, embed_planes(): masked.reshape(depth_side, PATCH, side, PATCH, side, PATCH)  65.4 us
    all_gather x1, waiting for transfers between devices, body(): decoded = lax.all_gather(decoded, 'head', axis=1, tiled=True)  60.4 us
    reshape x2, local copies, waits for them, and re-layouts, embed_planes(): voxels = masked.reshape(depth_side, PATCH, side, PATCH, side, PATCH).tran...  59.5 us
    reshape x2, local copies, waits for them, and re-layouts, body(): blended.reshape(half_side, side, side, PATCH, PATCH, PATCH)  47.5 us
    psum x1, waiting for transfers between devices, body(): lax.psum(partial_attention.astype(jnp.bfloat16), 'head').astype(jnp.float32)  43.5 us
    psum x1, waiting for transfers between devices, body(): lax.psum(partial_forward.astype(jnp.bfloat16), 'head').astype(jnp.float32)  42.2 us
    ppermute x3, waiting for transfers between devices, from_behind(): return lax.ppermute(block, axis, route)  19 us
    reshape x1, local copies, waits for them, and re-layouts, body(): return arranged.reshape(HALF, WIN, WIN)  18.8 us
  transfers between devices with their start and end apart: 6, of which 4 were waited for; matrix products, arithmetic and copies ran while one was open for 17% of the time, Pallas kernels for 0%

commit v1 on v0

v1 whole, which is shorter than its diff:
```python
import jax
import jax.numpy as jnp
from jax import lax
from jax.sharding import PartitionSpec as P

PATCH = 16
LAYERS = 1
WIN = 128
HEAD_DIM = 64
HALF = 64


EPSILON = 1e-06


def from_behind(block, axis, distance):
    devices = range(lax.axis_size(axis))
    route = [(i - distance, i) for i in devices if i - distance in devices]
    return lax.ppermute(block, axis, route)


def partner_sum(term):
    rounded = term.astype(jnp.bfloat16)
    other = lax.ppermute(rounded, "head", [(0, 1), (1, 0)])
    return rounded.astype(jnp.float32) + other.astype(jnp.float32)


def layer_norm(values, gain, bias):
    average = jnp.mean(values, axis=-1, keepdims=True)
    centered = values - average
    variance = jnp.mean(centered * centered, axis=-1, keepdims=True)
    return centered * lax.rsqrt(variance + EPSILON) * gain + bias


def profile_of(places):
    return jnp.exp(-0.5 * ((places - (WIN - 1) / 2) / (WIN / 4)) ** 2)


def embed_planes(amplitudes, live, embed_by_depth, embed_mask):
    side = WIN // PATCH
    depth_side = amplitudes.shape[0] // PATCH
    rows = depth_side * side * side
    masked = amplitudes * live[:, :, None]
    grouped = masked.reshape(depth_side, PATCH, side, PATCH, WIN).transpose(0, 2, 1, 3, 4)
    grouped = grouped.reshape(depth_side * side, PATCH * PATCH, WIN)
    voxels = jnp.swapaxes(grouped, 1, 2).reshape(rows, PATCH, PATCH * PATCH)
    embedded = lax.dot_general(
        voxels, embed_by_depth, (((1, 2), (0, 1)), ((), ())),
        preferred_element_type=jnp.float32,
    )
    mask_patches = (
        live.reshape(depth_side, PATCH, side, PATCH)
        .transpose(0, 2, 1, 3)
        .reshape(depth_side * side, PATCH * PATCH)
    )
    mask_terms = jnp.dot(mask_patches, embed_mask, preferred_element_type=jnp.float32)
    local_width = mask_terms.shape[1]
    return embedded + jnp.broadcast_to(
        mask_terms[:, None, :], (depth_side * side, side, local_width)
    ).reshape(rows, local_width)


def body(
    traces,
    trace_mask,
    embed_voxel,
    embed_mask,
    position,
    norm_gain,
    norm_bias,
    w_qkv,
    w_out,
    w_up,
    w_down,
    w_decode,
):
    side = WIN // PATCH
    tokens = side**3
    half_tokens = tokens // 2
    tile_index = lax.axis_index("tile")
    head_index = lax.axis_index("head")
    own_live = trace_mask.astype(jnp.bfloat16)
    next_traces, next_live = from_behind((traces, own_live), "tile", -1)
    local_width = embed_voxel.shape[1]
    embed_by_depth = embed_voxel.reshape(PATCH * PATCH, PATCH, local_width).transpose(1, 0, 2)
    own_embedded = embed_planes(traces, own_live, embed_by_depth, embed_mask)
    arrived_rows = embed_planes(next_traces, next_live, embed_by_depth, embed_mask)
    embedded = jnp.concatenate([own_embedded, arrived_rows], 0)
    embedded = (embedded + position.astype(jnp.float32)).astype(jnp.bfloat16)
    other_columns = lax.ppermute(embedded, "head", [(0, 1), (1, 0)])
    stream = jnp.where(
        head_index == 0,
        jnp.concatenate([embedded, other_columns], 1),
        jnp.concatenate([other_columns, embedded], 1),
    ).astype(jnp.float32)
    local_heads = w_qkv.shape[3] // HEAD_DIM
    normed = layer_norm(stream, norm_gain[0], norm_bias[0]).astype(jnp.bfloat16)
    projected = jnp.einsum(
        "td,sde->ste", normed, w_qkv[0], preferred_element_type=jnp.float32
    ).astype(jnp.bfloat16)
    query = projected[0].reshape(tokens, local_heads, HEAD_DIM)
    keys = projected[1].reshape(tokens, local_heads, HEAD_DIM)
    values = projected[2].reshape(tokens, local_heads, HEAD_DIM)
    scores = jnp.einsum(
        "thd,shd->hts", query, keys, preferred_element_type=jnp.float32
    ) * HEAD_DIM ** (-0.5)
    weights = jax.nn.softmax(scores, axis=-1).astype(jnp.bfloat16)
    attended = jnp.einsum(
        "hts,shd->thd", weights, values, preferred_element_type=jnp.float32
    ).astype(jnp.bfloat16)
    attended = attended.reshape(tokens, local_heads * HEAD_DIM)
    partial_attention = jnp.dot(attended, w_out[0], preferred_element_type=jnp.float32)
    stream = stream + partner_sum(partial_attention)
    normed = layer_norm(stream, norm_gain[1], norm_bias[1]).astype(jnp.bfloat16)
    hidden = jax.nn.gelu(
        jnp.dot(normed, w_up[0], preferred_element_type=jnp.float32), approximate=True
    ).astype(jnp.bfloat16)
    partial_forward = jnp.dot(hidden, w_down[0], preferred_element_type=jnp.float32)
    stream = stream + partner_sum(partial_forward)
    latent = layer_norm(stream, norm_gain[2 * LAYERS], norm_bias[2 * LAYERS]).astype(jnp.bfloat16)
    inner_rows = w_decode.shape[1] // (PATCH * PATCH)
    cell_cols = inner_rows * PATCH
    decode_by_depth = (
        w_decode.T.reshape(inner_rows, PATCH, PATCH, -1)
        .transpose(2, 0, 1, 3)
        .reshape(PATCH, cell_cols, -1)
    )
    decoded = lax.dot_general(
        latent, decode_by_depth, (((1,), (2,)), ((), ())),
        preferred_element_type=jnp.float32,
    ).astype(jnp.bfloat16)
    upper_part = from_behind(decoded[half_tokens:], "tile", 1)
    lower_part = decoded[:half_tokens]
    shape = lower_part.shape
    token_a = lax.broadcasted_iota(jnp.int32, shape, 0) // (side * side)
    inner = lax.broadcasted_iota(jnp.int32, shape, 2) // PATCH
    places = (token_a * PATCH + head_index * inner_rows + inner).astype(jnp.float32)
    lower_profile = profile_of(places)
    upper_profile = profile_of(places + HALF)
    later = (tile_index > 0).astype(jnp.float32)
    numerator = (
        lower_part.astype(jnp.float32) * lower_profile
        + upper_part.astype(jnp.float32) * upper_profile
    )
    denominator = lower_profile + later * upper_profile
    blended = (numerator / denominator).astype(jnp.bfloat16)
    half_side = side // 2
    arranged = blended.reshape(half_side * side, WIN, cell_cols)
    arranged = jnp.swapaxes(arranged, 1, 2).reshape(half_side, side, inner_rows, PATCH, WIN)
    arranged = arranged.transpose(0, 2, 1, 3, 4)
    other_rows = lax.ppermute(arranged, "head", [(0, 1), (1, 0)])
    whole = jnp.where(
        head_index == 0,
        jnp.concatenate([arranged, other_rows], 1),
        jnp.concatenate([other_rows, arranged], 1),
    )
    return whole.reshape(HALF, WIN, WIN)


def solution(mesh):
    return jax.shard_map(
        body,
        mesh=mesh,
        in_specs=(
            P("tile", None, None),
            P("tile", None),
            P(None, "head"),
            P(None, "head"),
            P(None, "head"),
            P(),
            P(),
            P(None, None, None, "head"),
            P(None, "head", None),
            P(None, None, "head"),
            P(None, "head", None),
            P(None, "head"),
        ),
        out_specs=P("tile", None, None),
        check_vma=False,
    )
```

time: 463 us -> 187 us (0.40)
  the two profiles are of different devices: /device:TPU:31 before, /device:TPU:8 now
where the time goes in v1:
time: 187 us; the launch traced here: 186 us
  waiting for transfers between devices  78.2 us (42%)
  local copies, waits for them, and re-layouts  40.8 us (22%)
  matrix products  31.2 us (17%)
  other arithmetic  20.1 us (11%)
  starting transfers between devices  15.5 us (8%)
    ppermute x2, waiting for transfers between devices, partner_sum(): other = lax.ppermute(rounded, 'head', [(0, 1), (1, 0)])  28.4 us
    ppermute x1, waiting for transfers between devices, body(): other_rows = lax.ppermute(arranged, 'head', [(0, 1), (1, 0)])  22.9 us
    ppermute x3, waiting for transfers between devices, from_behind(): return lax.ppermute(block, axis, route)  19.4 us
    reshape x2, local copies, waits for them, and re-layouts, embed_planes(): voxels = jnp.swapaxes(grouped, 1, 2).reshape(rows, PATCH, PATCH * PATCH)  9.68 us
    ppermute x3, starting transfers between devices, from_behind(): return lax.ppermute(block, axis, route)  8.61 us
    transpose x2, local copies, waits for them, and re-layouts, embed_planes(): voxels = jnp.swapaxes(grouped, 1, 2).reshape(rows, PATCH, PATCH * PATCH)  8.18 us
    ppermute x1, waiting for transfers between devices, body(): other_columns = lax.ppermute(embedded, 'head', [(0, 1), (1, 0)])  7.58 us
    dot_general x1, matrix products, body(): jnp.dot(hidden, w_down[0], preferred_element_type=jnp.float32)  7.23 us
  transfers between devices with their start and end apart: 7, of which 6 were waited for; matrix products, arithmetic and copies ran while one was open for 15% of the time, Pallas kernels for 0%

profile of v1, /device:TPU:8, one launch (start us, length us, event | category | flops | bytes accessed | tf_op | source)
XLA Modules:
  0.0 186.1 jit_solution(7818209192748534463)
XLA Ops:
  0.0 0.9 convert_element_type.75
  0.9 4.1 %collective-permute-start.1 = (bf16[64,128]{1,0:T(8,128)(2,1)S(1)}, bf16[64,128]{1,0:T(8,128)(2,1)S(1)}, u32[]{:S(2)}, u32[]{:S(2)}) collective-permute-start(bf16[64,128]{1,0:T(8,128)(2,1)S(1)} %convert_element_type.75), channel_id=1, source_target_pairs={{2,0},{4,2},{6,4},{8,6},{10,8},{12,10},{14,12},{16,14},{18,16},{20... | collective-permute-start | bytes 49160 | tf_op jit(solution)/shard_map/ppermute | solution.py:19
  5.0 2.6 %collective-permute-start = (bf16[64,128,128]{2,1,0:T(8,128)(2,1)}, bf16[64,128,128]{2,1,0:T(8,128)(2,1)}, u32[]{:S(2)}, u32[]{:S(2)}) collective-permute-start(bf16[64,128,128]{2,1,0:T(8,128)(2,1)} %param.12), channel_id=1, source_target_pairs={{2,0},{4,2},{6,4},{8,6},{10,8},{12,10},{14,12},{16,14},{18,16},{20... | collective-permute-start | bytes 6291464 | tf_op jit(solution)/shard_map/ppermute | solution.py:19
  7.8 2.5 %broadcast_multiply_fusion.1 = bf16[64,128,128]{2,1,0:T(8,128)(2,1)S(1)} fusion(bf16[64,128,128]{2,1,0:T(8,128)(2,1)} %param.12, bf16[64,128]{1,0:T(8,128)(2,1)S(1)} %convert_element_type.75), kind=kLoop, calls=%fused_computation.51 | loop fusion | flops 1048576 | bytes 4210688 | tf_op jit(solution)/shard_map/mul | solution.py:43
  10.2 1.9 %copy.30 = bf16[4,8,16,16,128]{4,3,2,1,0:T(8,128)(2,1)} copy(bf16[4,8,16,16,128]{4,3,1,2,0:T(8,128)(2,1)S(1)} %bitcast.110) | data formatting | bytes 4194304 | tf_op jit(solution)/shard_map/transpose | solution.py:44
  12.1 4.1 %copy.31 = bf16[32,128,256]{2,1,0:T(8,128)(2,1)} copy(bf16[32,128,256]{1,2,0:T(8,128)(2,1)} %bitcast.106) | data formatting | bytes 4194304 | tf_op jit(solution)/shard_map/transpose | solution.py:46
  16.2 4.9 %copy.32 = bf16[256,16,256]{0,1,2:T(8,128)(2,1)} copy(bf16[256,16,256]{2,1,0:T(8,128)(2,1)} %bitcast.107) | data formatting | bytes 4194304 | tf_op jit(solution)/shard_map/reshape | solution.py:46
  21.1 0.7 copy.54
  21.7 1.1 reshape.106
  23.0 3.6 %fusion.43 = f32[256,384]{1,0:T(8,128)} fusion(bf16[256,16,256]{0,1,2:T(8,128)(2,1)} %copy.32, bf16[16,256,384]{2,0,1:T(8,128)(2,1)S(1)} %bitcast.103, f32[32,384]{1,0:T(8,128)S(1)} %fusion.80), kind=kOutput, calls=%fused_computation.48 | convolution fusion | flops 805404672 | bytes 5685248 | tf_op jit(solution)/shard_map/dot_general | solution.py:47
  26.6 0.8 reshape.111
  27.4 0.9 copy.53
  28.6 2.8 %collective-permute-done = bf16[64,128,128]{2,1,0:T(8,128)(2,1)} collective-permute-done((bf16[64,128,128]{2,1,0:T(8,128)(2,1)}, bf16[64,128,128]{2,1,0:T(8,128)(2,1)}, u32[]{:S(2)}, u32[]{:S(2)}) %collective-permute-start) | collective-permute-done | bytes 2097184 | tf_op jit(solution)/shard_map/ppermute | solution.py:19
  31.5 2.5 %broadcast_multiply_fusion = bf16[64,128,128]{2,1,0:T(8,128)(2,1)S(1)} fusion(bf16[64,128,128]{2,1,0:T(8,128)(2,1)} %collective-permute-done, bf16[64,128]{1,0:T(8,128)(2,1)S(1)} %collective-permute-done.1), kind=kLoop, calls=%fused_computation.50 | loop fusion | flops 1048576 | bytes 4210688 | tf_op jit(solution)/shard_map/mul | solution.py:43
  33.9 1.9 %copy.34 = bf16[4,8,16,16,128]{4,3,2,1,0:T(8,128)(2,1)} copy(bf16[4,8,16,16,128]{4,3,1,2,0:T(8,128)(2,1)S(1)} %bitcast.105) | data formatting | bytes 4194304 | tf_op jit(solution)/shard_map/transpose | solution.py:44
  35.8 4.1 %copy.35 = bf16[32,128,256]{2,1,0:T(8,128)(2,1)} copy(bf16[32,128,256]{1,2,0:T(8,128)(2,1)} %bitcast.108) | data formatting | bytes 4194304 | tf_op jit(solution)/shard_map/transpose | solution.py:46
  39.9 4.8 %copy.36 = bf16[256,16,256]{0,1,2:T(8,128)(2,1)} copy(bf16[256,16,256]{2,1,0:T(8,128)(2,1)} %bitcast.109) | data formatting | bytes 4194304 | tf_op jit(solution)/shard_map/reshape | solution.py:46
  44.8 3.0 %fusion.44 = f32[256,384]{1,0:T(8,128)S(1)} fusion(bf16[256,16,256]{0,1,2:T(8,128)(2,1)} %copy.36, bf16[16,256,384]{2,0,1:T(8,128)(2,1)S(1)} %bitcast.104, f32[32,384]{1,0:T(8,128)S(1)} %fusion.81), kind=kOutput, calls=%fused_computation.49 | convolution fusion | flops 805404672 | bytes 5685248 | tf_op jit(solution)/shard_map/dot_general | solution.py:47
  47.8 2.2 %collective-permute-start.2 = (bf16[512,384]{1,0:T(8,128)(2,1)S(1)}, bf16[512,384]{1,0:T(8,128)(2,1)}, u32[]{:S(2)}, u32[]{:S(2)}) collective-permute-start(bf16[512,384]{1,0:T(8,128)(2,1)S(1)} %fusion.51), channel_id=1, source_target_pairs={{0,1},{1,0},{2,3},{3,2},{4,5},{5,4},{6,7},{7,6},{8,9},{9,8},{10,11... | collective-permute-start | bytes 1179656 | tf_op jit(solution)/shard_map/ppermute | solution.py:90
  50.0 1.5 slice_reduce_fusion
  51.5 7.6 %collective-permute-done.2 = bf16[512,384]{1,0:T(8,128)(2,1)} collective-permute-done((bf16[512,384]{1,0:T(8,128)(2,1)S(1)}, bf16[512,384]{1,0:T(8,128)(2,1)}, u32[]{:S(2)}, u32[]{:S(2)}) %collective-permute-start.2) | collective-permute-done | bytes 393248 | tf_op jit(solution)/shard_map/ppermute | solution.py:90
  59.1 1.4 convert_reduce_fusion
  60.4 1.5 fusion.29
  62.0 3.1 %fusion.36 = bf16[3,512,384]{1,2,0:T(8,128)(2,1)S(1)} fusion(bf16[1,3,768,384]{3,2,1,0:T(8,128)(2,1)} %param.19, f32[768]{0:T(1024)S(1)} %get-tuple-element.9, f32[768]{0:T(1024)S(1)} %get-tuple-element.19, f32[512]{0:T(512)S(1)} %add_rsqrt_fusion.2, f32[512]{0:T(512)S(1)} %broadcast_multiply_fusion.4, bf16[512,384]{1,0:T(8,128)(2,1)} %collective-permute-done.2, ...), kind=kOutput, calls=%fused_computation.42 | convolution fusion | flops 912457728 | bytes 3745793 | tf_op jit(solution)/shard_map/td,sde->ste/dot_general | solution.py:98
  65.0 1.0 fusion.78
  66.1 6.5 %fusion.79 = (f32[6,512]{1,0:T(8,128)}, f32[6,512,512]{1,2,0:T(8,128)}) fusion(bf16[512,6,64]{0,2,1:T(8,128)(2,1)} %bitcast.119, bf16[512,6,64]{0,2,1:T(8,128)(2,1)} %bitcast.118), kind=kOutput, calls=%fused_computation.103 | convolution fusion | flops 206045696 | bytes 7090176 | tf_op jit(solution)/shard_map/sub | solution.py:107
  72.6 3.5 %fusion.42 = bf16[6,64,512]{2,1,0:T(8,128)(2,1)S(1)} fusion(bf16[512,6,64]{0,2,1:T(8,128)(2,1)} %bitcast.117, f32[6,512,512]{1,2,0:T(8,128)} %get-tuple-element.17, f32[6,512]{1,0:T(8,128)} %get-tuple-element.16), kind=kOutput, calls=%fused_computation.45 | convolution fusion | flops 204668928 | bytes 7090176 | tf_op jit(solution)/shard_map/hts,shd->thd/dot_general | solution.py:108
  76.8 1.8 collective-permute-start.3
  78.6 16.7 %collective-permute-done.3 = bf16[512,768]{1,0:T(8,128)(2,1)S(1)} collective-permute-done((bf16[512,768]{1,0:T(8,128)(2,1)S(1)}, bf16[512,768]{1,0:T(8,128)(2,1)S(1)}, u32[]{:S(2)}, u32[]{:S(2)}) %collective-permute-start.3) | collective-permute-done | bytes 786464 | tf_op jit(solution)/shard_map/ppermute | solution.py:24
  95.3 1.9 %fusion.76 = f32[512]{0:T(512)S(1)} fusion(bf16[512,768]{1,0:T(8,128)(2,1)S(1)} %collective-permute-done.3, bf16[512,768]{1,0:T(8,128)(2,1)S(1)} %convolution_convert_fusion, bf16[512,384]{1,0:T(8,128)(2,1)S(1)} %fusion.51, bf16[512,384]{1,0:T(8,128)(2,1)} %collective-permute-done.2, pred[]{:T(512)S(6)} %eq.4), kind=kLoop, calls=%fused_computation.100 | loop fusion | flops 5897728 | bytes 2361345 | tf_op jit(solution)/shard_map/reduce_sum | solution.py:29
  97.2 1.7 multiply_reduce_fusion.2
  99.6 7.2 %fusion.39 = bf16[512,768]{1,0:T(8,128)(2,1)} fusion(bf16[1,1536,768]{2,1,0:T(8,128)(2,1)} %param.22, bf16[1,768,1536]{2,1,0:T(8,128)(2,1)} %param.21, f32[768]{0:T(1024)S(1)} %copy-done.11, f32[768]{0:T(1024)S(1)} %copy-done.12, f32[512]{0:T(512)} %add_rsqrt_fusion.1, f32[512]{0:T(512)S(1)} %broadcast_multiply_fusion.3, bf16[512,768]{1,0:T(8,128)(2,1)} %copy-done.2, ...), kind=kOutput, calls=%fused_computation.43 | convolution fusion | flops 2430861312 | bytes 7874561 | tf_op jit(solution)/shard_map/dot_general | solution.py:118
  106.8 1.6 collective-permute-start.4
  108.4 4.6 %copy.40 = bf16[768,2048]{0,1:T(8,128)(2,1)} copy(bf16[768,2048]{1,0:T(8,128)(2,1)} %param.23) | data formatting | bytes 6291456 | tf_op args[11]
  113.0 11.7 %collective-permute-done.4 = bf16[512,768]{1,0:T(8,128)(2,1)} collective-permute-done((bf16[512,768]{1,0:T(8,128)(2,1)}, bf16[512,768]{1,0:T(8,128)(2,1)}, u32[]{:S(2)}, u32[]{:S(2)}) %collective-permute-start.4) | collective-permute-done | bytes 786464 | tf_op jit(solution)/shard_map/ppermute | solution.py:24
  124.7 2.7 %fusion.77 = (f32[512]{0:T(512)S(1)}, f32[512,768]{1,0:T(8,128)S(1)}) fusion(bf16[512,768]{1,0:T(8,128)(2,1)} %collective-permute-done.4, bf16[512,768]{1,0:T(8,128)(2,1)} %fusion.39, bf16[512,768]{1,0:T(8,128)(2,1)} %copy-done.2, bf16[512,768]{1,0:T(8,128)(2,1)} %copy-done.1, bf16[512,384]{1,0:T(8,128)(2,1)S(1)} %fusion.51, ...), kind=kLoop, calls=%fused_computation.101 | loop fusion | flops 7470592 | bytes 5507073 | tf_op jit(solution)/shard_map/reduce_sum | solution.py:29
  127.7 3.3 %fusion.22 = bf16[512,16,128]{2,0,1:T(8,128)(2,1)S(1)} fusion(bf16[16,128,768]{2,0,1:T(8,128)(2,1)S(1)} %bitcast.114, f32[512,768]{1,0:T(8,128)S(1)} %get-tuple-element.12, f32[768]{0:T(1024)S(1)} %get-tuple-element.8, f32[768]{0:T(1024)S(1)} %copy-done.10, f32[512]{0:T(512)S(1)} %add_rsqrt_fusion, f32[512]{0:T(512)S(1)} %broadcast_multiply_fusion.2), kind=kOutput, calls=%fused_computation.27 | convolution fusion | flops 1613627392 | bytes 6825984 | tf_op jit(solution)/shard_map/dot_general | solution.py:128
  131.1 1.3 copy-done.4
  132.4 1.1 slice.48
  133.5 1.9 %collective-permute-start.5 = (bf16[256,16,128]{2,0,1:T(8,128)(2,1)}, bf16[256,16,128]{2,0,1:T(8,128)(2,1)}, u32[]{:S(2)}, u32[]{:S(2)}) collective-permute-start(bf16[256,16,128]{2,0,1:T(8,128)(2,1)} %slice.48), channel_id=1, source_target_pairs={{0,2},{2,4},{4,6},{6,8},{8,10},{10,12},{12,14},{14,16},{16,18},{18... | collective-permute-start | bytes 3145736 | tf_op jit(solution)/shard_map/ppermute | solution.py:19
  135.5 16.6 %collective-permute-done.5 = bf16[256,16,128]{2,0,1:T(8,128)(2,1)} collective-permute-done((bf16[256,16,128]{2,0,1:T(8,128)(2,1)}, bf16[256,16,128]{2,0,1:T(8,128)(2,1)}, u32[]{:S(2)}, u32[]{:S(2)}) %collective-permute-start.5) | collective-permute-done | bytes 1048608 | tf_op jit(solution)/shard_map/ppermute | solution.py:19
  152.0 2.2 %divide_convert_fusion.2 = bf16[256,16,128]{2,0,1:T(8,128)(2,1)S(1)} fusion(bf16[256,16,128]{2,0,1:T(8,128)(2,1)} %collective-permute-done.5, bf16[512,16,128]{2,0,1:T(8,128)(2,1)} %copy-done.4, f32[]{:T(128)S(6)} %convert_element_type.98, s32[128]{0:T(128)S(1)} %get-tuple-element.23, s32[128]{0:T(128)S(1)} %get-tuple-element.24, s32[]{:T(128)S(6)} %mul.166, ...), kind=kLoop, calls=%fused_computation.26 | loop fusion | flops 12058624 | bytes 3149192 | tf_op jit(solution)/shard_map/convert_element_type | solution.py:146
  154.2 1.6 copy.42
  155.8 2.3 %copy.43 = bf16[32,128,128]{2,1,0:T(8,128)(2,1)} copy(bf16[32,128,128]{1,2,0:T(8,128)(2,1)} %bitcast.113) | data formatting | bytes 2097152 | tf_op jit(solution)/shard_map/transpose | solution.py:149
  158.1 1.4 collective-permute-start.6
  159.5 22.9 %collective-permute-done.6 = bf16[4,8,8,16,128]{4,3,1,2,0:T(8,128)(2,1)S(1)} collective-permute-done((bf16[4,8,8,16,128]{4,3,1,2,0:T(8,128)(2,1)}, bf16[4,8,8,16,128]{4,3,1,2,0:T(8,128)(2,1)S(1)}, u32[]{:S(2)}, u32[]{:S(2)}) %collective-permute-start.6) | collective-permute-done | bytes 1048608 | tf_op jit(solution)/shard_map/ppermute | solution.py:151
  182.4 1.8 maximum_select_fusion
  184.2 1.9 %copy.44 = bf16[4,16,8,16,128]{4,3,2,1,0:T(8,128)(2,1)} copy(bf16[4,16,8,16,128]{4,3,1,2,0:T(8,128)(2,1)S(1)} %maximum_select_fusion) | data formatting | bytes 4194304 | tf_op jit(solution)/shard_map/jit(_where)/select_n | solution.py:152
  (43 shorter events, 2.3 us)
Async XLA Ops:
  0.0 23.0 %copy-start = (bf16[4096,384]{1,0:T(8,128)(2,1)S(1)}, bf16[4096,384]{1,0:T(8,128)(2,1)}, u32[]{:S(2)}) copy-start(bf16[4096,384]{1,0:T(8,128)(2,1)} %param.14) | copy-start | bytes 9437188
  0.9 25.7 %collective-permute-start.1 = (bf16[64,128]{1,0:T(8,128)(2,1)S(1)}, bf16[64,128]{1,0:T(8,128)(2,1)S(1)}, u32[]{:S(2)}, u32[]{:S(2)}) collective-permute-start(bf16[64,128]{1,0:T(8,128)(2,1)S(1)} %convert_element_type.75), channel_id=1, source_target_pairs={{2,0},{4,2},{6,4},{8,6},{10,8},{12,10},{14,12},{16,14},{18,16},{20... | collective-permute-start | bytes 49160 | tf_op jit(solution)/shard_map/ppermute | solution.py:19
  5.0 26.4 %collective-permute-start = (bf16[64,128,128]{2,1,0:T(8,128)(2,1)}, bf16[64,128,128]{2,1,0:T(8,128)(2,1)}, u32[]{:S(2)}, u32[]{:S(2)}) collective-permute-start(bf16[64,128,128]{2,1,0:T(8,128)(2,1)} %param.12), channel_id=1, source_target_pairs={{2,0},{4,2},{6,4},{8,6},{10,8},{12,10},{14,12},{16,14},{18,16},{20... | collective-permute-start | bytes 6291464 | tf_op jit(solution)/shard_map/ppermute | solution.py:19
  16.2 6.6 %copy-start.5 = (bf16[256,384]{1,0:T(8,128)(2,1)S(1)}, bf16[256,384]{1,0:T(8,128)(2,1)}, u32[]{:S(2)}) copy-start(bf16[256,384]{1,0:T(8,128)(2,1)} %param.15) | copy-start | bytes 589828
  44.8 3.0 %copy-start.7 = (bf16[512,384]{1,0:T(8,128)(2,1)S(1)}, bf16[512,384]{1,0:T(8,128)(2,1)}, u32[]{:S(2)}) copy-start(bf16[512,384]{1,0:T(8,128)(2,1)} %param.16) | copy-start | bytes 1179652
  44.8 3.0 %copy-start.8 = (f32[256,384]{1,0:T(8,128)S(1)}, f32[256,384]{1,0:T(8,128)}, u32[]{:S(2)}) copy-start(f32[256,384]{1,0:T(8,128)} %fusion.43) | copy-start | bytes 1179652
  44.8 5.3 %copy-start.9 = (f32[3,768]{1,0:T(4,128)S(1)}, f32[3,768]{1,0:T(4,128)}, u32[]{:S(2)}) copy-start(f32[3,768]{1,0:T(4,128)} %param.18) | copy-start | bytes 27652
  47.8 11.2 %collective-permute-start.2 = (bf16[512,384]{1,0:T(8,128)(2,1)S(1)}, bf16[512,384]{1,0:T(8,128)(2,1)}, u32[]{:S(2)}, u32[]{:S(2)}) collective-permute-start(bf16[512,384]{1,0:T(8,128)(2,1)S(1)} %fusion.51), channel_id=1, source_target_pairs={{0,1},{1,0},{2,3},{3,2},{4,5},{5,4},{6,7},{7,6},{8,9},{9,8},{10,11... | collective-permute-start | bytes 1179656 | tf_op jit(solution)/shard_map/ppermute | solution.py:90
  72.6 3.6 %copy-start.6 = (bf16[1,384,768]{2,1,0:T(8,128)(2,1)S(1)}, bf16[1,384,768]{2,1,0:T(8,128)(2,1)}, u32[]{:S(2)}) copy-start(bf16[1,384,768]{2,1,0:T(8,128)(2,1)} %param.20) | copy-start | bytes 1769476
  76.8 22.2 %copy-start.1 = (bf16[512,768]{1,0:T(8,128)(2,1)}, bf16[512,768]{1,0:T(8,128)(2,1)S(1)}, u32[]{:S(2)}) copy-start(bf16[512,768]{1,0:T(8,128)(2,1)S(1)} %convolution_convert_fusion) | copy-start | bytes 2359300
  76.8 22.8 %copy-start.11 = (f32[768]{0:T(1024)S(1)}, f32[768]{0:T(1024)}, u32[]{:S(2)}) copy-start(f32[768]{0:T(1024)} %get-tuple-element.10) | copy-start | bytes 9220
  76.8 22.8 %copy-start.12 = (f32[768]{0:T(1024)S(1)}, f32[768]{0:T(1024)}, u32[]{:S(2)}) copy-start(f32[768]{0:T(1024)} %get-tuple-element.18) | copy-start | bytes 9220
  76.8 18.5 %collective-permute-start.3 = (bf16[512,768]{1,0:T(8,128)(2,1)S(1)}, bf16[512,768]{1,0:T(8,128)(2,1)S(1)}, u32[]{:S(2)}, u32[]{:S(2)}) collective-permute-start(bf16[512,768]{1,0:T(8,128)(2,1)S(1)} %convolution_convert_fusion), channel_id=1, source_target_pairs={{0,1},{1,0},{2,3},{3,2},{4,5},{5,4},{6,7},{7,6},{8,9},{9,8},{10,11... | collective-permute-start | bytes 2359304 | tf_op jit(solution)/shard_map/ppermute | solution.py:24
  95.3 3.6 %copy-start.2 = (bf16[512,768]{1,0:T(8,128)(2,1)}, bf16[512,768]{1,0:T(8,128)(2,1)S(1)}, u32[]{:S(2)}) copy-start(bf16[512,768]{1,0:T(8,128)(2,1)S(1)} %collective-permute-done.3) | copy-start | bytes 2359300
  106.8 17.9 %collective-permute-start.4 = (bf16[512,768]{1,0:T(8,128)(2,1)}, bf16[512,768]{1,0:T(8,128)(2,1)}, u32[]{:S(2)}, u32[]{:S(2)}) collective-permute-start(bf16[512,768]{1,0:T(8,128)(2,1)} %fusion.39), channel_id=1, source_target_pairs={{0,1},{1,0},{2,3},{3,2},{4,5},{5,4},{6,7},{7,6},{8,9},{9,8},{10,11... | collective-permute-start | bytes 2359304 | tf_op jit(solution)/shard_map/ppermute | solution.py:24
  113.0 14.7 %copy-start.3 = (bf16[768,2048]{0,1:T(8,128)(2,1)S(1)}, bf16[768,2048]{0,1:T(8,128)(2,1)}, u32[]{:S(2)}) copy-start(bf16[768,2048]{0,1:T(8,128)(2,1)} %copy.40) | copy-start | bytes 9437188
  113.0 14.7 %copy-start.10 = (f32[768]{0:T(1024)S(1)}, f32[768]{0:T(1024)}, u32[]{:S(2)}) copy-start(f32[768]{0:T(1024)} %get-tuple-element.20) | copy-start | bytes 9220
  131.1 1.3 copy-start.4
  133.5 18.5 %collective-permute-start.5 = (bf16[256,16,128]{2,0,1:T(8,128)(2,1)}, bf16[256,16,128]{2,0,1:T(8,128)(2,1)}, u32[]{:S(2)}, u32[]{:S(2)}) collective-permute-start(bf16[256,16,128]{2,0,1:T(8,128)(2,1)} %slice.48), channel_id=1, source_target_pairs={{0,2},{2,4},{4,6},{6,8},{8,10},{10,12},{12,14},{14,16},{16,18},{18... | collective-permute-start | bytes 3145736 | tf_op jit(solution)/shard_map/ppermute | solution.py:19
  158.1 24.3 %collective-permute-start.6 = (bf16[4,8,8,16,128]{4,3,1,2,0:T(8,128)(2,1)}, bf16[4,8,8,16,128]{4,3,1,2,0:T(8,128)(2,1)S(1)}, u32[]{:S(2)}, u32[]{:S(2)}) collective-permute-start(bf16[4,8,8,16,128]{4,3,1,2,0:T(8,128)(2,1)} %bitcast.111), channel_id=1, source_target_pairs={{0,1},{1,0},{2,3},{3,2},{4,5},{5,4},{6,7},{7,6},{8,9},{9,8},{10,11... | collective-permute-start | bytes 3145736 | tf_op jit(solution)/shard_map/ppermute | solution.py:151

commit v2 on v1

--- a/solution.py
+++ b/solution.py
@@ -83,41 +83,26 @@
     next_traces, next_live = from_behind((traces, own_live), "tile", -1)
     local_width = embed_voxel.shape[1]
     embed_by_depth = embed_voxel.reshape(PATCH * PATCH, PATCH, local_width).transpose(1, 0, 2)
-    own_embedded = embed_planes(traces, own_live, embed_by_depth, embed_mask)
-    arrived_rows = embed_planes(next_traces, next_live, embed_by_depth, embed_mask)
-    embedded = jnp.concatenate([own_embedded, arrived_rows], 0)
-    embedded = (embedded + position.astype(jnp.float32)).astype(jnp.bfloat16)
-    other_columns = lax.ppermute(embedded, "head", [(0, 1), (1, 0)])
-    stream = jnp.where(
-        head_index == 0,
-        jnp.concatenate([embedded, other_columns], 1),
-        jnp.concatenate([other_columns, embedded], 1),
-    ).astype(jnp.float32)
+    position = position.astype(jnp.float32)
+    halves = []
+    for rows, (amplitudes, live) in enumerate(((traces, own_live), (next_traces, next_live))):
+        embedded = embed_planes(amplitudes, live, embed_by_depth, embed_mask)
+        embedded = embedded + position[rows * half_tokens:(rows + 1) * half_tokens]
+        embedded = embedded.astype(jnp.bfloat16)
+        other_columns = lax.ppermute(embedded, "head", [(0, 1), (1, 0)])
+        halves.append(jnp.where(
+            head_index == 0,
+            jnp.concatenate([embedded, other_columns], 1),
+            jnp.concatenate([other_columns, embedded], 1),
+        ).astype(jnp.float32))
+    stream = jnp.concatenate(halves, 0)
     local_heads = w_qkv.shape[3] // HEAD_DIM
     normed = layer_norm(stream, norm_gain[0], norm_bias[0]).astype(jnp.bfloat16)
     projected = jnp.einsum(
         "td,sde->ste", normed, w_qkv[0], preferred_element_type=jnp.float32
     ).astype(jnp.bfloat16)
-    query = projected[0].reshape(tokens, local_heads, HEAD_DIM)
     keys = projected[1].reshape(tokens, local_heads, HEAD_DIM)
     values = projected[2].reshape(tokens, local_heads, HEAD_DIM)
-    scores = jnp.einsum(
-        "thd,shd->hts", query, keys, preferred_element_type=jnp.float32
-    ) * HEAD_DIM ** (-0.5)
-    weights = jax.nn.softmax(scores, axis=-1).astype(jnp.bfloat16)
-    attended = jnp.einsum(
-        "hts,shd->thd", weights, values, preferred_element_type=jnp.float32
-    ).astype(jnp.bfloat16)
-    attended = attended.reshape(tokens, local_heads * HEAD_DIM)
-    partial_attention = jnp.dot(attended, w_out[0], preferred_element_type=jnp.float32)
-    stream = stream + partner_sum(partial_attention)
-    normed = layer_norm(stream, norm_gain[1], norm_bias[1]).astype(jnp.bfloat16)
-    hidden = jax.nn.gelu(
-        jnp.dot(normed, w_up[0], preferred_element_type=jnp.float32), approximate=True
-    ).astype(jnp.bfloat16)
-    partial_forward = jnp.dot(hidden, w_down[0], preferred_element_type=jnp.float32)
-    stream = stream + partner_sum(partial_forward)
-    latent = layer_norm(stream, norm_gain[2 * LAYERS], norm_bias[2 * LAYERS]).astype(jnp.bfloat16)
     inner_rows = w_decode.shape[1] // (PATCH * PATCH)
     cell_cols = inner_rows * PATCH
     decode_by_depth = (
@@ -125,12 +110,33 @@
         .transpose(2, 0, 1, 3)
         .reshape(PATCH, cell_cols, -1)
     )
-    decoded = lax.dot_general(
-        latent, decode_by_depth, (((1,), (2,)), ((), ())),
-        preferred_element_type=jnp.float32,
-    ).astype(jnp.bfloat16)
-    upper_part = from_behind(decoded[half_tokens:], "tile", 1)
-    lower_part = decoded[:half_tokens]
+    decoded_chunks = {}
+    for chunk in (1, 0):
+        span = slice(chunk * half_tokens, (chunk + 1) * half_tokens)
+        query = projected[0][span].reshape(half_tokens, local_heads, HEAD_DIM)
+        scores = jnp.einsum(
+            "thd,shd->hts", query, keys, preferred_element_type=jnp.float32
+        ) * HEAD_DIM ** (-0.5)
+        weights = jax.nn.softmax(scores, axis=-1).astype(jnp.bfloat16)
+        attended = jnp.einsum(
+            "hts,shd->thd", weights, values, preferred_element_type=jnp.float32
+        ).astype(jnp.bfloat16)
+        attended = attended.reshape(half_tokens, local_heads * HEAD_DIM)
+        partial_attention = jnp.dot(attended, w_out[0], preferred_element_type=jnp.float32)
+        part = stream[span] + partner_sum(partial_attention)
+        normed = layer_norm(part, norm_gain[1], norm_bias[1]).astype(jnp.bfloat16)
+        hidden = jax.nn.gelu(
+            jnp.dot(normed, w_up[0], preferred_element_type=jnp.float32), approximate=True
+        ).astype(jnp.bfloat16)
+        partial_forward = jnp.dot(hidden, w_down[0], preferred_element_type=jnp.float32)
+        part = part + partner_sum(partial_forward)
+        latent = layer_norm(part, norm_gain[2 * LAYERS], norm_bias[2 * LAYERS]).astype(jnp.bfloat16)
+        decoded_chunks[chunk] = lax.dot_general(
+            latent, decode_by_depth, (((1,), (2,)), ((), ())),
+            preferred_element_type=jnp.float32,
+        ).astype(jnp.bfloat16)
+    upper_part = from_behind(decoded_chunks[1], "tile", 1)
+    lower_part = decoded_chunks[0]
     shape = lower_part.shape
     token_a = lax.broadcasted_iota(jnp.int32, shape, 0) // (side * side)
     inner = lax.broadcasted_iota(jnp.int32, shape, 2) // PATCH

time: 187 us -> 176 us (0.941)
  the two profiles are of different devices: /device:TPU:8 before, /device:TPU:31 now
where the time goes in v2:
time: 176 us; the launch traced here: 175 us
  waiting for transfers between devices  44.1 us (25%)
  local copies, waits for them, and re-layouts  44 us (25%)
  matrix products  41.8 us (24%)
  starting transfers between devices  24.2 us (14%)
  other arithmetic  20.7 us (12%)
    ppermute x1, waiting for transfers between devices, body(): other_rows = lax.ppermute(arranged, 'head', [(0, 1), (1, 0)])  20.9 us
    ppermute x3, starting transfers between devices, from_behind(): return lax.ppermute(block, axis, route)  19 us
    dot_general x2, matrix products, body(): lax.dot_general(latent, decode_by_depth, (((1,), (2,)), ((), ())), prefer...  10.5 us
    ppermute x4, waiting for transfers between devices, partner_sum(): other = lax.ppermute(rounded, 'head', [(0, 1), (1, 0)])  10.5 us
    reshape x2, local copies, waits for them, and re-layouts, embed_planes(): voxels = jnp.swapaxes(grouped, 1, 2).reshape(rows, PATCH, PATCH * PATCH)  9.74 us
    dot_general x2, matrix products, body(): jnp.dot(hidden, w_down[0], preferred_element_type=jnp.float32)  9.27 us
    ppermute x3, waiting for transfers between devices, from_behind(): return lax.ppermute(block, axis, route)  8.96 us
    transpose x2, local copies, waits for them, and re-layouts, embed_planes(): voxels = jnp.swapaxes(grouped, 1, 2).reshape(rows, PATCH, PATCH * PATCH)  8.15 us
  transfers between devices with their start and end apart: 10, of which 6 were waited for; matrix products, arithmetic and copies ran while one was open for 43% of the time, Pallas kernels for 0%

profile of v2, /device:TPU:31, one launch (start us, length us, event | category | flops | bytes accessed | tf_op | source)
XLA Modules:
  0.0 175.2 jit_solution(2716897032943158796)
XLA Ops:
  0.0 0.9 convert_element_type.120
  0.9 2.7 %collective-permute-start.2 = (bf16[64,128]{1,0:T(8,128)(2,1)S(1)}, bf16[64,128]{1,0:T(8,128)(2,1)}, u32[]{:S(2)}, u32[]{:S(2)}) collective-permute-start(bf16[64,128]{1,0:T(8,128)(2,1)S(1)} %convert_element_type.120), channel_id=1, source_target_pairs={{2,0},{4,2},{6,4},{8,6},{10,8},{12,10},{14,12},{16,14},{18,16},{20... | collective-permute-start | bytes 49160 | tf_op jit(solution)/shard_map/ppermute | solution.py:19
  3.6 2.2 %collective-permute-start.1 = (bf16[64,128,128]{2,1,0:T(8,128)(2,1)}, bf16[64,128,128]{2,1,0:T(8,128)(2,1)}, u32[]{:S(2)}, u32[]{:S(2)}) collective-permute-start(bf16[64,128,128]{2,1,0:T(8,128)(2,1)} %param.12), channel_id=1, source_target_pairs={{2,0},{4,2},{6,4},{8,6},{10,8},{12,10},{14,12},{16,14},{18,16},{20... | collective-permute-start | bytes 6291464 | tf_op jit(solution)/shard_map/ppermute | solution.py:19
  5.8 3.4 %broadcast_multiply_fusion.1 = bf16[64,128,128]{2,1,0:T(8,128)(2,1)} fusion(bf16[64,128,128]{2,1,0:T(8,128)(2,1)} %param.12, bf16[64,128]{1,0:T(8,128)(2,1)S(1)} %convert_element_type.120), kind=kLoop, calls=%fused_computation.70 | loop fusion | flops 1048576 | bytes 4210688 | tf_op jit(solution)/shard_map/mul | solution.py:43
  9.4 2.0 %convert_element_type.121 = f32[512,384]{1,0:T(8,128)} convert(bf16[512,384]{1,0:T(8,128)(2,1)} %param.16) | non-fusion elementwise | flops 196608 | bytes 1179648 | tf_op jit(solution)/shard_map/convert_element_type | solution.py:86
  11.3 3.5 %copy.29 = bf16[4,8,16,16,128]{4,3,2,1,0:T(8,128)(2,1)} copy(bf16[4,8,16,16,128]{4,3,1,2,0:T(8,128)(2,1)} %bitcast.142) | data formatting | bytes 4194304 | tf_op jit(solution)/shard_map/transpose | solution.py:44
  14.8 4.1 %copy.30 = bf16[32,128,256]{2,1,0:T(8,128)(2,1)} copy(bf16[32,128,256]{1,2,0:T(8,128)(2,1)} %bitcast.144) | data formatting | bytes 4194304 | tf_op jit(solution)/shard_map/transpose | solution.py:46
  18.9 4.9 %copy.31 = bf16[256,16,256]{0,1,2:T(8,128)(2,1)} copy(bf16[256,16,256]{2,1,0:T(8,128)(2,1)} %bitcast.145) | data formatting | bytes 4194304 | tf_op jit(solution)/shard_map/reshape | solution.py:46
  24.5 1.1 reshape.145
  25.8 2.9 %fusion.73 = bf16[256,384]{1,0:T(8,128)(2,1)S(1)} fusion(bf16[256,16,256]{0,1,2:T(8,128)(2,1)} %copy.31, bf16[16,256,384]{2,0,1:T(8,128)(2,1)S(1)} %bitcast.140, f32[512,384]{1,0:T(8,128)} %convert_element_type.121, f32[32,384]{1,0:T(8,128)S(1)} %fusion.152), kind=kOutput, calls=%fused_computation.66 | convolution fusion | flops 805601280 | bytes 5881856 | tf_op jit(solution)/shard_map/dot_general | solution.py:47
  28.7 1.7 collective-permute-start
  31.1 4.6 %copy.38 = bf16[768,2048]{0,1:T(8,128)(2,1)} copy(bf16[768,2048]{1,0:T(8,128)(2,1)} %param.23) | data formatting | bytes 6291456 | tf_op args[11]
  35.7 1.5 reshape.150
  37.2 1.6 copy.57
  38.8 1.1 reshape.151
  40.6 2.5 %broadcast_multiply_fusion = bf16[64,128,128]{2,1,0:T(8,128)(2,1)S(1)} fusion(bf16[64,128,128]{2,1,0:T(8,128)(2,1)} %collective-permute-done.1, bf16[64,128]{1,0:T(8,128)(2,1)} %collective-permute-done.2), kind=kLoop, calls=%fused_computation.69 | loop fusion | flops 1048576 | bytes 4210688 | tf_op jit(solution)/shard_map/mul | solution.py:43
  43.1 1.9 %copy.33 = bf16[4,8,16,16,128]{4,3,2,1,0:T(8,128)(2,1)} copy(bf16[4,8,16,16,128]{4,3,1,2,0:T(8,128)(2,1)S(1)} %bitcast.143) | data formatting | bytes 4194304 | tf_op jit(solution)/shard_map/transpose | solution.py:44
  45.0 4.1 %copy.34 = bf16[32,128,256]{2,1,0:T(8,128)(2,1)} copy(bf16[32,128,256]{1,2,0:T(8,128)(2,1)} %bitcast.146) | data formatting | bytes 4194304 | tf_op jit(solution)/shard_map/transpose | solution.py:46
  49.1 4.8 %copy.35 = bf16[256,16,256]{0,1,2:T(8,128)(2,1)} copy(bf16[256,16,256]{2,1,0:T(8,128)(2,1)} %bitcast.147) | data formatting | bytes 4194304 | tf_op jit(solution)/shard_map/reshape | solution.py:46
  53.9 2.9 %fusion.72 = bf16[256,384]{1,0:T(8,128)(2,1)S(1)} fusion(bf16[256,16,256]{0,1,2:T(8,128)(2,1)} %copy.35, bf16[16,256,384]{2,0,1:T(8,128)(2,1)S(1)} %bitcast.141, f32[512,384]{1,0:T(8,128)} %convert_element_type.121, f32[32,384]{1,0:T(8,128)S(1)} %copy-done.15), kind=kOutput, calls=%fused_computation.65 | convolution fusion | flops 805601280 | bytes 5881856 | tf_op jit(solution)/shard_map/dot_general | solution.py:47
  57.6 1.1 fusion.103
  58.7 3.8 %collective-permute-done.3 = bf16[256,384]{1,0:T(8,128)(2,1)S(1)} collective-permute-done((bf16[256,384]{1,0:T(8,128)(2,1)S(1)}, bf16[256,384]{1,0:T(8,128)(2,1)S(1)}, u32[]{:S(2)}, u32[]{:S(2)}) %collective-permute-start.3) | collective-permute-done | bytes 196640 | tf_op jit(solution)/shard_map/ppermute | solution.py:92
  63.1 1.3 fusion.59
  66.1 3.9 %fusion.151 = (f32[6,256]{1,0:T(8,128)S(1)}, f32[6,256,512]{2,1,0:T(8,128)}) fusion(bf16[256,6,64]{0,2,1:T(8,128)(2,1)} %bitcast.162, bf16[512,6,64]{0,2,1:T(8,128)(2,1)} %bitcast.157), kind=kOutput, calls=%fused_computation.169 | convolution fusion | flops 103023104 | bytes 3741696 | tf_op jit(solution)/shard_map/sub | solution.py:120
  70.0 2.6 %fusion.75 = bf16[6,64,256]{2,1,0:T(8,128)(2,1)S(1)} fusion(bf16[512,6,64]{0,2,1:T(8,128)(2,1)S(1)} %bitcast.155, f32[6,256,512]{2,1,0:T(8,128)} %get-tuple-element.22, f32[6,256]{1,0:T(8,128)S(1)} %get-tuple-element.21), kind=kOutput, calls=%fused_computation.68 | convolution fusion | flops 102334464 | bytes 3741696 | tf_op jit(solution)/shard_map/hts,shd->thd/dot_general | solution.py:121
  73.5 3.9 %fusion.150 = (f32[6,256]{1,0:T(8,128)S(1)}, f32[6,256,512]{2,1,0:T(8,128)}) fusion(bf16[256,6,64]{0,2,1:T(8,128)(2,1)} %bitcast.161, bf16[512,6,64]{0,2,1:T(8,128)(2,1)} %bitcast.158), kind=kOutput, calls=%fused_computation.168 | convolution fusion | flops 103023104 | bytes 3741696 | tf_op jit(solution)/shard_map/sub | solution.py:120
  77.4 2.8 %fusion.74 = bf16[6,64,256]{2,1,0:T(8,128)(2,1)S(1)} fusion(bf16[512,6,64]{0,2,1:T(8,128)(2,1)} %bitcast.156, f32[6,256,512]{2,1,0:T(8,128)} %get-tuple-element.20, f32[6,256]{1,0:T(8,128)S(1)} %get-tuple-element.19), kind=kOutput, calls=%fused_computation.67 | convolution fusion | flops 102334464 | bytes 3741696 | tf_op jit(solution)/shard_map/hts,shd->thd/dot_general | solution.py:121
  80.6 1.3 collective-permute-start.6
  82.2 1.4 fusion.146
  84.8 6.7 %collective-permute-done.6 = bf16[256,768]{1,0:T(8,128)(2,1)S(1)} collective-permute-done((bf16[256,768]{1,0:T(8,128)(2,1)S(1)}, bf16[256,768]{1,0:T(8,128)(2,1)S(1)}, u32[]{:S(2)}, u32[]{:S(2)}) %collective-permute-start.6) | collective-permute-done | bytes 393248 | tf_op jit(solution)/shard_map/ppermute | solution.py:24
  91.8 0.9 copy-done.3
  92.9 5.0 %fusion.65 = bf16[256,768]{1,0:T(8,128)(2,1)} fusion(bf16[1,1536,768]{2,1,0:T(8,128)(2,1)} %param.22, bf16[1,768,1536]{2,1,0:T(8,128)(2,1)} %param.21, f32[256,768]{1,0:T(8,128)} %copy-done.3, f32[256]{0:T(256)S(1)} %add_rsqrt_fusion.2, f32[256]{0:T(256)S(1)} %broadcast_multiply_fusion.4, f32[768]{0:T(1024)S(1)} %copy-done.20, f32[768]{0:T(1024)S(1)} %copy-done.21), kind=kOutput, calls=%fused_computation.56 | convolution fusion | flops 1212678144 | bytes 5906432 | tf_op jit(solution)/shard_map/dot_general | solution.py:131
  97.9 4.3 %fusion.62 = bf16[256,768]{1,0:T(8,128)(2,1)S(1)} fusion(bf16[1,1536,768]{2,1,0:T(8,128)(2,1)} %param.22, bf16[1,768,1536]{2,1,0:T(8,128)(2,1)} %param.21, f32[256,768]{1,0:T(8,128)} %copy-done.1, f32[768]{0:T(1024)S(1)} %copy-done.20, f32[768]{0:T(1024)S(1)} %copy-done.21, f32[256]{0:T(256)S(1)} %add_rsqrt_fusion.4, f32[256]{0:T(256)S(1)} %broadcast_multiply_fusion.6), kind=kOutput, calls=%fused_computation.55 | convolution fusion | flops 1212678144 | bytes 5906432 | tf_op jit(solution)/shard_map/dot_general | solution.py:131
  102.2 1.5 collective-permute-start.5
  103.8 3.4 %collective-permute-done.7 = bf16[256,768]{1,0:T(8,128)(2,1)} collective-permute-done((bf16[256,768]{1,0:T(8,128)(2,1)}, bf16[256,768]{1,0:T(8,128)(2,1)}, u32[]{:S(2)}, u32[]{:S(2)}) %collective-permute-start.7) | collective-permute-done | bytes 393248 | tf_op jit(solution)/shard_map/ppermute | solution.py:24
  107.2 1.6 fusion.145
  108.8 1.4 multiply_reduce_fusion.3
  110.2 5.6 %fusion.56 = bf16[256,16,128]{2,0,1:T(8,128)(2,1)} fusion(bf16[16,128,768]{2,0,1:T(8,128)(2,1)} %bitcast.151, f32[256]{0:T(256)S(1)} %add_rsqrt_fusion.1, f32[256]{0:T(256)S(1)} %broadcast_multiply_fusion.3, f32[768]{0:T(1024)S(1)} %copy-done.18, f32[768]{0:T(1024)S(1)} %copy-done.19, f32[256,768]{1,0:T(8,128)S(1)} %copy-done.4, ...), kind=kOutput, calls=%fused_computation.53 | convolution fusion | flops 807600128 | bytes 5775360 | tf_op jit(solution)/shard_map/dot_general | solution.py:134
  115.8 14.1 %collective-permute-start.8 = (bf16[256,16,128]{2,0,1:T(8,128)(2,1)}, bf16[256,16,128]{2,0,1:T(8,128)(2,1)}, u32[]{:S(2)}, u32[]{:S(2)}) collective-permute-start(bf16[256,16,128]{2,0,1:T(8,128)(2,1)} %fusion.56), channel_id=1, source_target_pairs={{0,2},{2,4},{4,6},{6,8},{8,10},{10,12},{12,14},{14,16},{16,18},{18... | collective-permute-start | bytes 3145736 | tf_op jit(solution)/shard_map/ppermute | solution.py:19
  130.0 1.5 fusion.144
  131.5 1.3 multiply_reduce_fusion.5
  132.8 9.0 %collective-permute-done.8 = bf16[256,16,128]{2,0,1:T(8,128)(2,1)} collective-permute-done((bf16[256,16,128]{2,0,1:T(8,128)(2,1)}, bf16[256,16,128]{2,0,1:T(8,128)(2,1)}, u32[]{:S(2)}, u32[]{:S(2)}) %collective-permute-start.8) | collective-permute-done | bytes 1048608 | tf_op jit(solution)/shard_map/ppermute | solution.py:19
  141.8 4.9 %divide_convert_fusion.2 = bf16[256,16,128]{2,0,1:T(8,128)(2,1)S(1)} fusion(bf16[256,16,128]{2,0,1:T(8,128)(2,1)} %collective-permute-done.8, f32[]{:T(128)S(6)} %convert_element_type.158, s32[128]{0:T(128)S(1)} %get-tuple-element.28, s32[128]{0:T(128)S(1)} %get-tuple-element.29, s32[]{:T(128)S(6)} %mul.199, s32[256]{0:T(256)S(1)} %get-tuple-element.26, ...), kind=kOutput, calls=%fused_computation.25 | convolution fusion | flops 819658752 | bytes 6827400 | tf_op jit(solution)/shard_map/dot_general | solution.py:134
  146.7 1.6 copy.41
  148.3 2.3 %copy.42 = bf16[32,128,128]{2,1,0:T(8,128)(2,1)} copy(bf16[32,128,128]{1,2,0:T(8,128)(2,1)} %bitcast.150) | data formatting | bytes 2097152 | tf_op jit(solution)/shard_map/transpose | solution.py:155
  150.6 20.9 %collective-permute-done.9 = bf16[4,8,8,16,128]{4,3,1,2,0:T(8,128)(2,1)S(1)} collective-permute-done((bf16[4,8,8,16,128]{4,3,1,2,0:T(8,128)(2,1)}, bf16[4,8,8,16,128]{4,3,1,2,0:T(8,128)(2,1)S(1)}, u32[]{:S(2)}, u32[]{:S(2)}) %collective-permute-start.9) | collective-permute-done | bytes 1048608 | tf_op jit(solution)/shard_map/ppermute | solution.py:157
  171.5 1.8 %maximum_select_fusion = bf16[4,16,8,16,128]{4,3,1,2,0:T(8,128)(2,1)S(1)} fusion(bf16[4,8,8,16,128]{4,3,1,2,0:T(8,128)(2,1)S(1)} %collective-permute-done.9, bf16[4,8,8,16,128]{4,3,1,2,0:T(8,128)(2,1)} %bitcast.149, pred[]{:T(512)S(6)} %eq.2), kind=kLoop, calls=%fused_computation.24 | loop fusion | flops 3145728 | bytes 4194305 | tf_op jit(solution)/shard_map/jit(_where)/select_n | solution.py:158
  173.3 1.9 %copy.43 = bf16[4,16,8,16,128]{4,3,2,1,0:T(8,128)(2,1)} copy(bf16[4,16,8,16,128]{4,3,1,2,0:T(8,128)(2,1)S(1)} %maximum_select_fusion) | data formatting | bytes 4194304 | tf_op jit(solution)/shard_map/jit(_where)/select_n | solution.py:158
  (89 shorter events, 8.7 us)
Async XLA Ops:
  0.0 25.7 %copy-start = (bf16[4096,384]{1,0:T(8,128)(2,1)S(1)}, bf16[4096,384]{1,0:T(8,128)(2,1)}, u32[]{:S(2)}) copy-start(bf16[4096,384]{1,0:T(8,128)(2,1)} %param.14) | copy-start | bytes 9437188
  0.9 34.8 %collective-permute-start.2 = (bf16[64,128]{1,0:T(8,128)(2,1)S(1)}, bf16[64,128]{1,0:T(8,128)(2,1)}, u32[]{:S(2)}, u32[]{:S(2)}) collective-permute-start(bf16[64,128]{1,0:T(8,128)(2,1)S(1)} %convert_element_type.120), channel_id=1, source_target_pairs={{2,0},{4,2},{6,4},{8,6},{10,8},{12,10},{14,12},{16,14},{18,16},{20... | collective-permute-start | bytes 49160 | tf_op jit(solution)/shard_map/ppermute | solution.py:19
  3.6 37.0 %collective-permute-start.1 = (bf16[64,128,128]{2,1,0:T(8,128)(2,1)}, bf16[64,128,128]{2,1,0:T(8,128)(2,1)}, u32[]{:S(2)}, u32[]{:S(2)}) collective-permute-start(bf16[64,128,128]{2,1,0:T(8,128)(2,1)} %param.12), channel_id=1, source_target_pairs={{2,0},{4,2},{6,4},{8,6},{10,8},{12,10},{14,12},{16,14},{18,16},{20... | collective-permute-start | bytes 6291464 | tf_op jit(solution)/shard_map/ppermute | solution.py:19
  18.9 6.7 %copy-start.7 = (bf16[256,384]{1,0:T(8,128)(2,1)S(1)}, bf16[256,384]{1,0:T(8,128)(2,1)}, u32[]{:S(2)}) copy-start(bf16[256,384]{1,0:T(8,128)(2,1)} %param.15) | copy-start | bytes 589828
  25.7 4.7 %copy-start.16 = (f32[3,768]{1,0:T(4,128)S(1)}, f32[3,768]{1,0:T(4,128)}, u32[]{:S(2)}) copy-start(f32[3,768]{1,0:T(4,128)} %param.18) | copy-start | bytes 27652
  25.7 4.7 %copy-start.17 = (f32[3,768]{1,0:T(4,128)S(1)}, f32[3,768]{1,0:T(4,128)}, u32[]{:S(2)}) copy-start(f32[3,768]{1,0:T(4,128)} %param.17) | copy-start | bytes 27652
  28.7 28.9 %copy-start.8 = (bf16[256,384]{1,0:T(8,128)(2,1)}, bf16[256,384]{1,0:T(8,128)(2,1)S(1)}, u32[]{:S(2)}) copy-start(bf16[256,384]{1,0:T(8,128)(2,1)S(1)} %fusion.73) | copy-start | bytes 589828
  28.7 28.8 %collective-permute-start = (bf16[256,384]{1,0:T(8,128)(2,1)S(1)}, bf16[256,384]{1,0:T(8,128)(2,1)}, u32[]{:S(2)}, u32[]{:S(2)}) collective-permute-start(bf16[256,384]{1,0:T(8,128)(2,1)S(1)} %fusion.73), channel_id=1, source_target_pairs={{0,1},{1,0},{2,3},{3,2},{4,5},{5,4},{6,7},{7,6},{8,9},{9,8},{10,11... | collective-permute-start | bytes 589832 | tf_op jit(solution)/shard_map/ppermute | solution.py:92
  49.1 4.8 %copy-start.15 = (f32[32,384]{1,0:T(8,128)S(1)}, f32[32,384]{1,0:T(8,128)}, u32[]{:S(2)}) copy-start(f32[32,384]{1,0:T(8,128)} %fusion.153) | copy-start | bytes 147460
  56.9 6.1 %copy-start.10 = (bf16[256,384]{1,0:T(8,128)(2,1)}, bf16[256,384]{1,0:T(8,128)(2,1)S(1)}, u32[]{:S(2)}) copy-start(bf16[256,384]{1,0:T(8,128)(2,1)S(1)} %fusion.72) | copy-start | bytes 589828
  56.9 5.6 %collective-permute-start.3 = (bf16[256,384]{1,0:T(8,128)(2,1)S(1)}, bf16[256,384]{1,0:T(8,128)(2,1)S(1)}, u32[]{:S(2)}, u32[]{:S(2)}) collective-permute-start(bf16[256,384]{1,0:T(8,128)(2,1)S(1)} %fusion.72), channel_id=1, source_target_pairs={{0,1},{1,0},{2,3},{3,2},{4,5},{5,4},{6,7},{7,6},{8,9},{9,8},{10,11... | collective-permute-start | bytes 589832 | tf_op jit(solution)/shard_map/ppermute | solution.py:92
  58.7 4.5 %copy-start.22 = (f32[768]{0:T(1024)S(1)}, f32[768]{0:T(1024)}, u32[]{:S(2)}) copy-start(f32[768]{0:T(1024)} %get-tuple-element.9) | copy-start | bytes 9220
  58.7 4.5 %copy-start.23 = (f32[768]{0:T(1024)S(1)}, f32[768]{0:T(1024)}, u32[]{:S(2)}) copy-start(f32[768]{0:T(1024)} %get-tuple-element.24) | copy-start | bytes 9220
  58.7 4.4 %copy-start.24 = (bf16[1,3,768,384]{3,2,1,0:T(8,128)(2,1)S(1)}, bf16[1,3,768,384]{3,2,1,0:T(8,128)(2,1)}, u32[]{:S(2)}) copy-start(bf16[1,3,768,384]{3,2,1,0:T(8,128)(2,1)} %param.19) | copy-start | bytes 5308420
  62.4 0.7 copy-start.12
  65.3 4.7 %copy-start.14 = (bf16[1,512,384]{1,2,0:T(8,128)(2,1)}, bf16[1,512,384]{1,2,0:T(8,128)(2,1)S(1)}, u32[]{:S(2)}) copy-start(bf16[1,512,384]{1,2,0:T(8,128)(2,1)S(1)} %get-tuple-element.18) | copy-start | bytes 1179652
  70.0 2.6 %copy-start.5 = (bf16[1,384,768]{2,1,0:T(8,128)(2,1)S(1)}, bf16[1,384,768]{2,1,0:T(8,128)(2,1)}, u32[]{:S(2)}) copy-start(bf16[1,384,768]{2,1,0:T(8,128)(2,1)} %param.20) | copy-start | bytes 1769476
  73.0 9.2 %collective-permute-start.4 = (bf16[256,768]{1,0:T(8,128)(2,1)S(1)}, bf16[256,768]{1,0:T(8,128)(2,1)}, u32[]{:S(2)}, u32[]{:S(2)}) collective-permute-start(bf16[256,768]{1,0:T(8,128)(2,1)S(1)} %convolution_convert_fusion.1), channel_id=1, source_target_pairs={{0,1},{1,0},{2,3},{3,2},{4,5},{5,4},{6,7},{7,6},{8,9},{9,8},{10,11... | collective-permute-start | bytes 1179656 | tf_op jit(solution)/shard_map/ppermute | solution.py:24
  77.4 2.8 %copy-start.6 = (bf16[1,384,768]{2,1,0:T(8,128)(2,1)S(1)}, bf16[1,384,768]{2,1,0:T(8,128)(2,1)}, u32[]{:S(2)}) copy-start(bf16[1,384,768]{2,1,0:T(8,128)(2,1)} %param.20) | copy-start | bytes 1769476
  77.4 4.8 %copy-start.9 = (bf16[256,384]{1,0:T(8,128)(2,1)S(1)}, bf16[256,384]{1,0:T(8,128)(2,1)}, u32[]{:S(2)}) copy-start(bf16[256,384]{1,0:T(8,128)(2,1)} %copy-done.8) | copy-start | bytes 589828
  80.2 11.3 %copy-start.11 = (bf16[256,384]{1,0:T(8,128)(2,1)S(1)}, bf16[256,384]{1,0:T(8,128)(2,1)}, u32[]{:S(2)}) copy-start(bf16[256,384]{1,0:T(8,128)(2,1)} %copy-done.10) | copy-start | bytes 589828
  80.2 11.3 %copy-start.13 = (bf16[256,384]{1,0:T(8,128)(2,1)S(1)}, bf16[256,384]{1,0:T(8,128)(2,1)}, u32[]{:S(2)}) copy-start(bf16[256,384]{1,0:T(8,128)(2,1)} %copy-done.12) | copy-start | bytes 589828
  80.6 10.9 %collective-permute-start.6 = (bf16[256,768]{1,0:T(8,128)(2,1)S(1)}, bf16[256,768]{1,0:T(8,128)(2,1)S(1)}, u32[]{:S(2)}, u32[]{:S(2)}) collective-permute-start(bf16[256,768]{1,0:T(8,128)(2,1)S(1)} %convolution_convert_fusion), channel_id=1, source_target_pairs={{0,1},{1,0},{2,3},{3,2},{4,5},{5,4},{6,7},{7,6},{8,9},{9,8},{10,11... | collective-permute-start | bytes 1179656 | tf_op jit(solution)/shard_map/ppermute | solution.py:24
  83.7 0.9 copy-start.1
  83.7 9.2 %copy-start.20 = (f32[768]{0:T(1024)S(1)}, f32[768]{0:T(1024)}, u32[]{:S(2)}) copy-start(f32[768]{0:T(1024)} %get-tuple-element.10) | copy-start | bytes 9220
  83.7 9.2 %copy-start.21 = (f32[768]{0:T(1024)S(1)}, f32[768]{0:T(1024)}, u32[]{:S(2)}) copy-start(f32[768]{0:T(1024)} %get-tuple-element.23) | copy-start | bytes 9220
  91.8 0.9 copy-start.3
  97.9 9.3 %collective-permute-start.7 = (bf16[256,768]{1,0:T(8,128)(2,1)}, bf16[256,768]{1,0:T(8,128)(2,1)}, u32[]{:S(2)}, u32[]{:S(2)}) collective-permute-start(bf16[256,768]{1,0:T(8,128)(2,1)} %fusion.65), channel_id=1, source_target_pairs={{0,1},{1,0},{2,3},{3,2},{4,5},{5,4},{6,7},{7,6},{8,9},{9,8},{10,11... | collective-permute-start | bytes 1179656 | tf_op jit(solution)/shard_map/ppermute | solution.py:24
  102.2 6.6 %copy-start.4 = (f32[256,768]{1,0:T(8,128)S(1)}, f32[256,768]{1,0:T(8,128)}, u32[]{:S(2)}) copy-start(f32[256,768]{1,0:T(8,128)} %copy-done.3) | copy-start | bytes 2359300
  102.2 8.0 %copy-start.18 = (f32[768]{0:T(1024)S(1)}, f32[768]{0:T(1024)}, u32[]{:S(2)}) copy-start(f32[768]{0:T(1024)} %get-tuple-element.8) | copy-start | bytes 9220
  102.2 8.0 %copy-start.19 = (f32[768]{0:T(1024)S(1)}, f32[768]{0:T(1024)}, u32[]{:S(2)}) copy-start(f32[768]{0:T(1024)} %get-tuple-element.25) | copy-start | bytes 9220
  102.2 27.8 %collective-permute-start.5 = (bf16[256,768]{1,0:T(8,128)(2,1)S(1)}, bf16[256,768]{1,0:T(8,128)(2,1)}, u32[]{:S(2)}, u32[]{:S(2)}) collective-permute-start(bf16[256,768]{1,0:T(8,128)(2,1)S(1)} %fusion.62), channel_id=1, source_target_pairs={{0,1},{1,0},{2,3},{3,2},{4,5},{5,4},{6,7},{7,6},{8,9},{9,8},{10,11... | collective-permute-start | bytes 1179656 | tf_op jit(solution)/shard_map/ppermute | solution.py:24
  115.8 26.0 %copy-start.25 = (pred[128]{0:T(512)(128)(4,1)S(1)}, pred[128]{0:T(512)(128)(4,1)}, u32[]{:S(2)}) copy-start(pred[128]{0:T(512)(128)(4,1)} %compare_and_fusion) | copy-start | bytes 388
  115.8 26.0 %collective-permute-start.8 = (bf16[256,16,128]{2,0,1:T(8,128)(2,1)}, bf16[256,16,128]{2,0,1:T(8,128)(2,1)}, u32[]{:S(2)}, u32[]{:S(2)}) collective-permute-start(bf16[256,16,128]{2,0,1:T(8,128)(2,1)} %fusion.56), channel_id=1, source_target_pairs={{0,2},{2,4},{4,6},{6,8},{8,10},{10,12},{12,14},{14,16},{16,18},{18... | collective-permute-start | bytes 3145736 | tf_op jit(solution)/shard_map/ppermute | solution.py:19
  130.0 1.6 copy-start.2
  150.6 20.9 %collective-permute-start.9 = (bf16[4,8,8,16,128]{4,3,1,2,0:T(8,128)(2,1)}, bf16[4,8,8,16,128]{4,3,1,2,0:T(8,128)(2,1)S(1)}, u32[]{:S(2)}, u32[]{:S(2)}) collective-permute-start(bf16[4,8,8,16,128]{4,3,1,2,0:T(8,128)(2,1)} %bitcast.148), channel_id=1, source_target_pairs={{0,1},{1,0},{2,3},{3,2},{4,5},{5,4},{6,7},{7,6},{8,9},{9,8},{10,11... | collective-permute-start | bytes 3145736 | tf_op jit(solution)/shard_map/ppermute | solution.py:157

commit v3 on v2

--- a/solution.py
+++ b/solution.py
@@ -110,10 +110,17 @@
         .transpose(2, 0, 1, 3)
         .reshape(PATCH, cell_cols, -1)
     )
-    decoded_chunks = {}
-    for chunk in (1, 0):
-        span = slice(chunk * half_tokens, (chunk + 1) * half_tokens)
-        query = projected[0][span].reshape(half_tokens, local_heads, HEAD_DIM)
+    chunks = 4
+    chunk_tokens = tokens // chunks
+    half_chunks = chunks // 2
+    chunk_planes = (side // 2) // half_chunks
+    later = (tile_index > 0).astype(jnp.float32)
+    pieces = {}
+    order = list(range(half_chunks, chunks)) + list(range(half_chunks))
+    arrived_upper = {}
+    for chunk in order:
+        span = slice(chunk * chunk_tokens, (chunk + 1) * chunk_tokens)
+        query = projected[0][span].reshape(chunk_tokens, local_heads, HEAD_DIM)
         scores = jnp.einsum(
             "thd,shd->hts", query, keys, preferred_element_type=jnp.float32
         ) * HEAD_DIM ** (-0.5)
@@ -121,7 +128,7 @@
         attended = jnp.einsum(
             "hts,shd->thd", weights, values, preferred_element_type=jnp.float32
         ).astype(jnp.bfloat16)
-        attended = attended.reshape(half_tokens, local_heads * HEAD_DIM)
+        attended = attended.reshape(chunk_tokens, local_heads * HEAD_DIM)
         partial_attention = jnp.dot(attended, w_out[0], preferred_element_type=jnp.float32)
         part = stream[span] + partner_sum(partial_attention)
         normed = layer_norm(part, norm_gain[1], norm_bias[1]).astype(jnp.bfloat16)
@@ -131,36 +138,37 @@
         partial_forward = jnp.dot(hidden, w_down[0], preferred_element_type=jnp.float32)
         part = part + partner_sum(partial_forward)
         latent = layer_norm(part, norm_gain[2 * LAYERS], norm_bias[2 * LAYERS]).astype(jnp.bfloat16)
-        decoded_chunks[chunk] = lax.dot_general(
+        decoded = lax.dot_general(
             latent, decode_by_depth, (((1,), (2,)), ((), ())),
             preferred_element_type=jnp.float32,
         ).astype(jnp.bfloat16)
-    upper_part = from_behind(decoded_chunks[1], "tile", 1)
-    lower_part = decoded_chunks[0]
-    shape = lower_part.shape
-    token_a = lax.broadcasted_iota(jnp.int32, shape, 0) // (side * side)
-    inner = lax.broadcasted_iota(jnp.int32, shape, 2) // PATCH
-    places = (token_a * PATCH + head_index * inner_rows + inner).astype(jnp.float32)
-    lower_profile = profile_of(places)
-    upper_profile = profile_of(places + HALF)
-    later = (tile_index > 0).astype(jnp.float32)
-    numerator = (
-        lower_part.astype(jnp.float32) * lower_profile
-        + upper_part.astype(jnp.float32) * upper_profile
-    )
-    denominator = lower_profile + later * upper_profile
-    blended = (numerator / denominator).astype(jnp.bfloat16)
-    half_side = side // 2
-    arranged = blended.reshape(half_side * side, WIN, cell_cols)
-    arranged = jnp.swapaxes(arranged, 1, 2).reshape(half_side, side, inner_rows, PATCH, WIN)
-    arranged = arranged.transpose(0, 2, 1, 3, 4)
-    other_rows = lax.ppermute(arranged, "head", [(0, 1), (1, 0)])
-    whole = jnp.where(
-        head_index == 0,
-        jnp.concatenate([arranged, other_rows], 1),
-        jnp.concatenate([other_rows, arranged], 1),
-    )
-    return whole.reshape(HALF, WIN, WIN)
+        if chunk >= half_chunks:
+            arrived_upper[chunk - half_chunks] = from_behind(decoded, "tile", 1)
+            continue
+        upper_part = arrived_upper[chunk]
+        shape = decoded.shape
+        token_a = lax.broadcasted_iota(jnp.int32, shape, 0) // (side * side) + chunk * chunk_planes
+        inner = lax.broadcasted_iota(jnp.int32, shape, 2) // PATCH
+        places = (token_a * PATCH + head_index * inner_rows + inner).astype(jnp.float32)
+        lower_profile = profile_of(places)
+        upper_profile = profile_of(places + HALF)
+        numerator = (
+            decoded.astype(jnp.float32) * lower_profile
+            + upper_part.astype(jnp.float32) * upper_profile
+        )
+        denominator = lower_profile + later * upper_profile
+        blended = (numerator / denominator).astype(jnp.bfloat16)
+        arranged = blended.reshape(chunk_planes * side, WIN, cell_cols)
+        arranged = jnp.swapaxes(arranged, 1, 2).reshape(chunk_planes, side, inner_rows, PATCH, WIN)
+        arranged = arranged.transpose(0, 2, 1, 3, 4)
+        other_rows = lax.ppermute(arranged, "head", [(0, 1), (1, 0)])
+        whole = jnp.where(
+            head_index == 0,
+            jnp.concatenate([arranged, other_rows], 1),
+            jnp.concatenate([other_rows, arranged], 1),
+        )
+        pieces[chunk] = whole.reshape(chunk_planes * PATCH, WIN, WIN)
+    return jnp.concatenate([pieces[c] for c in range(half_chunks)], 0)
 
 
 def solution(mesh):

time: 176 us -> 197 us (1.12)
  waiting for transfers between devices: 44.1 us -> 18.9 us
  matrix products: 41.8 us -> 66.2 us
  other arithmetic: 20.7 us -> 35.1 us
  starting transfers between devices: 24.2 us -> 29.4 us
    ppermute x4 -> x8, waiting for transfers between devices: 10.5 us -> 0.02 us  [partner_sum(): other = lax.ppermute(rounded, 'head', [(0, 1), (1, 0)])]
    ppermute x3 -> x4, waiting for transfers between devices: 8.96 us -> 0.01 us  [from_behind(): return lax.ppermute(block, axis, route)]
    dot_general x2 -> x4, matrix products: 9.27 us -> 16.7 us  [body(): jnp.dot(hidden, w_down[0], preferred_element_type=jnp.float32)]
    dot_general x2 -> x4, matrix products: 0.78 us -> 7.03 us  [body(): jnp.dot(attended, w_out[0], preferred_element_type=jnp.float32)]
    ppermute x1 -> x2, waiting for transfers between devices: 20.9 us -> 15.3 us  [body(): other_rows = lax.ppermute(arranged, 'head', [(0, 1), (1, 0)])]
    dot_general x2 -> x4, matrix products: 5.37 us -> 10.6 us  [body(): jnp.einsum('hts,shd->thd', weights, values, preferred_element_type=jnp.fl...]
    dot_general x2 -> x4, matrix products: 10.5 us -> 15.1 us  [body(): lax.dot_general(latent, decode_by_depth, (((1,), (2,)), ((), ())), prefer...]
    reduce_sum x5 -> x7, other arithmetic: 4.88 us -> 8.75 us  [layer_norm(): average = jnp.mean(values, axis=-1, keepdims=True)]
  transfers between devices with their start and end apart: 10 -> 16, of which waited for: 6 -> 3; matrix products, arithmetic and copies ran while one was open for 43% -> 65% of each run, Pallas kernels for 0% -> 0%
where the time goes in v3:
time: 197 us; the launch traced here: 195 us
  matrix products  66.2 us (34%)
  local copies, waits for them, and re-layouts  44.3 us (22%)
  other arithmetic  35.1 us (18%)
  starting transfers between devices  29.4 us (15%)
  waiting for transfers between devices  18.9 us (10%)
    ppermute x4, starting transfers between devices, from_behind(): return lax.ppermute(block, axis, route)  20 us
    dot_general x4, matrix products, body(): jnp.dot(hidden, w_down[0], preferred_element_type=jnp.float32)  16.7 us
    ppermute x2, waiting for transfers between devices, body(): other_rows = lax.ppermute(arranged, 'head', [(0, 1), (1, 0)])  15.3 us
    dot_general x4, matrix products, body(): lax.dot_general(latent, decode_by_depth, (((1,), (2,)), ((), ())), prefer...  15.1 us
    dot_general x4, matrix products, body(): jnp.einsum('hts,shd->thd', weights, values, preferred_element_type=jnp.fl...  10.6 us
    reshape x2, local copies, waits for them, and re-layouts, embed_planes(): voxels = jnp.swapaxes(grouped, 1, 2).reshape(rows, PATCH, PATCH * PATCH)  9.74 us
    reduce_sum x7, other arithmetic, layer_norm(): average = jnp.mean(values, axis=-1, keepdims=True)  8.75 us
    sub x4, matrix products, body(): weights = jax.nn.softmax(scores, axis=-1).astype(jnp.bfloat16)  8.74 us
  transfers between devices with their start and end apart: 16, of which 3 were waited for; matrix products, arithmetic and copies ran while one was open for 65% of the time, Pallas kernels for 0%

profile of v3, /device:TPU:31, one launch (start us, length us, event | category | flops | bytes accessed | tf_op | source)
XLA Modules:
  0.0 194.6 jit_solution(3734795561569424830)
XLA Ops:
  0.9 2.7 %collective-permute-start.2 = (bf16[64,128]{1,0:T(8,128)(2,1)S(1)}, bf16[64,128]{1,0:T(8,128)(2,1)S(1)}, u32[]{:S(2)}, u32[]{:S(2)}) collective-permute-start(bf16[64,128]{1,0:T(8,128)(2,1)S(1)} %convert_element_type.210), channel_id=1, source_target_pairs={{2,0},{4,2},{6,4},{8,6},{10,8},{12,10},{14,12},{16,14},{18,16},{20... | collective-permute-start | bytes 49160 | tf_op jit(solution)/shard_map/ppermute | solution.py:19
  3.6 2.2 %collective-permute-start.1 = (bf16[64,128,128]{2,1,0:T(8,128)(2,1)}, bf16[64,128,128]{2,1,0:T(8,128)(2,1)}, u32[]{:S(2)}, u32[]{:S(2)}) collective-permute-start(bf16[64,128,128]{2,1,0:T(8,128)(2,1)} %param.12), channel_id=1, source_target_pairs={{2,0},{4,2},{6,4},{8,6},{10,8},{12,10},{14,12},{16,14},{18,16},{20... | collective-permute-start | bytes 6291464 | tf_op jit(solution)/shard_map/ppermute | solution.py:19
  5.8 3.4 %broadcast_multiply_fusion.1 = bf16[64,128,128]{2,1,0:T(8,128)(2,1)} fusion(bf16[64,128,128]{2,1,0:T(8,128)(2,1)} %param.12, bf16[64,128]{1,0:T(8,128)(2,1)S(1)} %convert_element_type.210), kind=kLoop, calls=%fused_computation.118 | loop fusion | flops 1048576 | bytes 4210688 | tf_op jit(solution)/shard_map/mul | solution.py:43
  9.4 1.9 convert_element_type.211
  11.3 3.5 %copy.33 = bf16[4,8,16,16,128]{4,3,2,1,0:T(8,128)(2,1)} copy(bf16[4,8,16,16,128]{4,3,1,2,0:T(8,128)(2,1)} %bitcast.203) | data formatting | bytes 4194304 | tf_op jit(solution)/shard_map/transpose | solution.py:44
  14.8 4.1 %copy.34 = bf16[32,128,256]{2,1,0:T(8,128)(2,1)} copy(bf16[32,128,256]{1,2,0:T(8,128)(2,1)} %bitcast.205) | data formatting | bytes 4194304 | tf_op jit(solution)/shard_map/transpose | solution.py:46
  18.9 4.9 %copy.35 = bf16[256,16,256]{0,1,2:T(8,128)(2,1)} copy(bf16[256,16,256]{2,1,0:T(8,128)(2,1)} %bitcast.206) | data formatting | bytes 4194304 | tf_op jit(solution)/shard_map/reshape | solution.py:46
  25.7 3.6 %fusion.73 = bf16[256,384]{1,0:T(8,128)(2,1)} fusion(bf16[256,16,256]{0,1,2:T(8,128)(2,1)} %copy.35, bf16[16,256,384]{2,0,1:T(8,128)(2,1)S(1)} %bitcast.201, f32[512,384]{1,0:T(8,128)} %convert_element_type.211, f32[32,384]{1,0:T(8,128)S(1)} %fusion.307), kind=kOutput, calls=%fused_computation.75 | convolution fusion | flops 805601280 | bytes 5881856 | tf_op jit(solution)/shard_map/dot_general | solution.py:47
  29.3 1.6 collective-permute-start
  33.7 4.6 %copy.42 = bf16[768,2048]{0,1:T(8,128)(2,1)} copy(bf16[768,2048]{1,0:T(8,128)(2,1)} %param.23) | data formatting | bytes 6291456 | tf_op args[11]
  40.4 2.5 %broadcast_multiply_fusion = bf16[64,128,128]{2,1,0:T(8,128)(2,1)S(1)} fusion(bf16[64,128,128]{2,1,0:T(8,128)(2,1)} %collective-permute-done.1, bf16[64,128]{1,0:T(8,128)(2,1)S(1)} %collective-permute-done.2), kind=kLoop, calls=%fused_computation.117 | loop fusion | flops 1048576 | bytes 4210688 | tf_op jit(solution)/shard_map/mul | solution.py:43
  42.8 1.9 copy.37
  44.7 4.1 %copy.38 = bf16[32,128,256]{2,1,0:T(8,128)(2,1)} copy(bf16[32,128,256]{1,2,0:T(8,128)(2,1)} %bitcast.207) | data formatting | bytes 4194304 | tf_op jit(solution)/shard_map/transpose | solution.py:46
  48.8 4.8 %copy.39 = bf16[256,16,256]{0,1,2:T(8,128)(2,1)} copy(bf16[256,16,256]{2,1,0:T(8,128)(2,1)} %bitcast.208) | data formatting | bytes 4194304 | tf_op jit(solution)/shard_map/reshape | solution.py:46
  53.6 2.9 %fusion.72 = bf16[256,384]{1,0:T(8,128)(2,1)S(1)} fusion(bf16[256,16,256]{0,1,2:T(8,128)(2,1)} %copy.39, bf16[16,256,384]{2,0,1:T(8,128)(2,1)S(1)} %bitcast.202, f32[512,384]{1,0:T(8,128)} %convert_element_type.211, f32[32,384]{1,0:T(8,128)S(1)} %fusion.308), kind=kOutput, calls=%fused_computation.74 | convolution fusion | flops 805601280 | bytes 5881856 | tf_op jit(solution)/shard_map/dot_general | solution.py:47
  58.5 3.6 %collective-permute-done.3 = bf16[256,384]{1,0:T(8,128)(2,1)S(1)} collective-permute-done((bf16[256,384]{1,0:T(8,128)(2,1)S(1)}, bf16[256,384]{1,0:T(8,128)(2,1)S(1)}, u32[]{:S(2)}, u32[]{:S(2)}) %collective-permute-start.3) | collective-permute-done | bytes 196640 | tf_op jit(solution)/shard_map/ppermute | solution.py:92
  67.0 2.2 %fusion.306 = f32[6,128]{1,0:T(8,128)} fusion(bf16[128,6,64]{0,2,1:T(8,128)(2,1)} %bitcast.241, bf16[512,6,64]{0,2,1:T(8,128)(2,1)S(1)} %bitcast.223), kind=kOutput, calls=%fused_computation.322 | convolution fusion | flops 51511808 | bytes 494592 | tf_op jit(solution)/shard_map/sub | solution.py:127
  69.2 2.6 %convolution_convert_fusion.5 = bf16[6,64,128]{2,1,0:T(8,128)(2,1)} fusion(bf16[512,6,64]{0,2,1:T(8,128)(2,1)} %bitcast.231, f32[6,128]{1,0:T(8,128)} %fusion.306, bf16[128,6,64]{0,2,1:T(8,128)(2,1)} %bitcast.242, bf16[512,6,64]{0,2,1:T(8,128)(2,1)S(1)} %bitcast.224), kind=kOutput, calls=%fused_computation.85 | convolution fusion | flops 102286592 | bytes 986112 | tf_op jit(solution)/shard_map/hts,shd->thd/dot_general | solution.py:128
  71.8 1.4 convolution_convert_fusion.1
  73.7 1.8 fusion.305
  75.5 2.6 %convolution_convert_fusion.7 = bf16[6,64,128]{2,1,0:T(8,128)(2,1)} fusion(bf16[512,6,64]{0,2,1:T(8,128)(2,1)} %bitcast.232, f32[6,128]{1,0:T(8,128)S(1)} %fusion.305, bf16[128,6,64]{0,2,1:T(8,128)(2,1)S(1)} %bitcast.240, bf16[512,6,64]{0,2,1:T(8,128)(2,1)} %bitcast.226), kind=kOutput, calls=%fused_computation.87 | convolution fusion | flops 102286592 | bytes 986112 | tf_op jit(solution)/shard_map/hts,shd->thd/dot_general | solution.py:128
  78.1 1.4 convolution_convert_fusion.3
  79.5 1.4 collective-permute-start.4
  80.9 2.4 %fusion.304 = f32[6,128]{1,0:T(8,128)} fusion(bf16[128,6,64]{0,2,1:T(8,128)(2,1)} %bitcast.237, bf16[512,6,64]{0,2,1:T(8,128)(2,1)} %bitcast.227), kind=kOutput, calls=%fused_computation.320 | convolution fusion | flops 51511808 | bytes 494592 | tf_op jit(solution)/shard_map/sub | solution.py:127
  83.3 2.7 %convolution_convert_fusion.4 = bf16[6,64,128]{2,1,0:T(8,128)(2,1)} fusion(bf16[512,6,64]{0,2,1:T(8,128)(2,1)} %bitcast.233, f32[6,128]{1,0:T(8,128)} %fusion.304, bf16[128,6,64]{0,2,1:T(8,128)(2,1)} %bitcast.238, bf16[512,6,64]{0,2,1:T(8,128)(2,1)} %bitcast.228), kind=kOutput, calls=%fused_computation.84 | convolution fusion | flops 102286592 | bytes 986112 | tf_op jit(solution)/shard_map/hts,shd->thd/dot_general | solution.py:128
  86.0 2.1 %convolution_convert_fusion = bf16[128,768]{1,0:T(8,128)(2,1)} fusion(bf16[128,384]{0,1:T(8,128)(2,1)} %bitcast.246, bf16[1,384,768]{2,1,0:T(8,128)(2,1)} %param.20), kind=kOutput, calls=%fused_computation.80 | convolution fusion | flops 75595776 | bytes 884736 | tf_op jit(solution)/shard_map/dot_general | solution.py:132
  88.2 2.4 %fusion.303 = f32[6,128]{1,0:T(8,128)} fusion(bf16[128,6,64]{0,2,1:T(8,128)(2,1)} %bitcast.235, bf16[512,6,64]{0,2,1:T(8,128)(2,1)} %bitcast.229), kind=kOutput, calls=%fused_computation.319 | convolution fusion | flops 51511808 | bytes 494592 | tf_op jit(solution)/shard_map/sub | solution.py:127
  90.6 2.7 %convolution_convert_fusion.6 = bf16[6,64,128]{2,1,0:T(8,128)(2,1)} fusion(bf16[512,6,64]{0,2,1:T(8,128)(2,1)} %bitcast.234, f32[6,128]{1,0:T(8,128)} %fusion.303, bf16[128,6,64]{0,2,1:T(8,128)(2,1)} %bitcast.236, bf16[512,6,64]{0,2,1:T(8,128)(2,1)} %bitcast.230), kind=kOutput, calls=%fused_computation.86 | convolution fusion | flops 102286592 | bytes 986112 | tf_op jit(solution)/shard_map/hts,shd->thd/dot_general | solution.py:128
  93.3 2.1 %convolution_convert_fusion.2 = bf16[128,768]{1,0:T(8,128)(2,1)} fusion(bf16[128,384]{0,1:T(8,128)(2,1)} %bitcast.243, bf16[1,384,768]{2,1,0:T(8,128)(2,1)} %param.20), kind=kOutput, calls=%fused_computation.82 | convolution fusion | flops 75595776 | bytes 884736 | tf_op jit(solution)/shard_map/dot_general | solution.py:132
  96.7 2.2 %fusion.297 = (f32[128]{0:T(128)}, f32[128,768]{1,0:T(8,128)S(1)}, f32[128]{0:T(128)S(1)}, f32[128,768]{1,0:T(8,128)S(1)}) fusion(bf16[128,768]{1,0:T(8,128)(2,1)} %collective-permute-done.4, bf16[128,768]{1,0:T(8,128)(2,1)} %copy-done.10, f32[256,768]{1,0:T(8,128)} %copy-done.2, bf16[128,768]{1,0:T(8,128)(2,1)} %collective-permute-done.10, ...), kind=kLoop, calls=%fused_computation.313 | loop fusion | flops 982784 | bytes 2360320 | tf_op jit(solution)/shard_map/reduce_sum | solution.py:29
  100.3 4.2 %fusion.80 = bf16[128,768]{1,0:T(8,128)(2,1)} fusion(bf16[1,1536,768]{2,1,0:T(8,128)(2,1)} %param.22, bf16[1,768,1536]{2,1,0:T(8,128)(2,1)} %param.21, f32[128,768]{1,0:T(8,128)} %copy-done.3, f32[128]{0:T(128)} %add_rsqrt_fusion.4, f32[128]{0:T(128)} %copy-done.22, f32[768]{0:T(1024)S(1)} %get-tuple-element.10, f32[768]{0:T(1024)S(1)} %get-tuple-element.7), kind=kOutput, calls=%fused_computation.78 | convolution fusion | flops 606339072 | bytes 5315584 | tf_op jit(solution)/shard_map/dot_general | solution.py:138
  104.7 2.8 %fusion.298 = (f32[128]{0:T(128)}, f32[128,768]{1,0:T(8,128)}, f32[128]{0:T(128)S(1)}, f32[128,768]{1,0:T(8,128)S(1)}) fusion(bf16[128,768]{1,0:T(8,128)(2,1)} %collective-permute-done.6, bf16[128,768]{1,0:T(8,128)(2,1)} %convolution_convert_fusion.2, f32[256,768]{1,0:T(8,128)} %copy-done.1, bf16[128,768]{1,0:T(8,128)(2,1)} %collective-permute-done.12, ...), kind=kLoop, calls=%fused_computation.314 | loop fusion | flops 982784 | bytes 2360320 | tf_op jit(solution)/shard_map/reduce_sum | solution.py:29
  109.0 4.2 %fusion.83 = bf16[128,768]{1,0:T(8,128)(2,1)} fusion(bf16[1,1536,768]{2,1,0:T(8,128)(2,1)} %param.22, bf16[1,768,1536]{2,1,0:T(8,128)(2,1)} %param.21, f32[128,768]{1,0:T(8,128)} %copy-done.6, f32[128]{0:T(128)} %add_rsqrt_fusion.2, f32[128]{0:T(128)} %copy-done.23, f32[768]{0:T(1024)S(1)} %get-tuple-element.10, f32[768]{0:T(1024)S(1)} %get-tuple-element.7), kind=kOutput, calls=%fused_computation.79 | convolution fusion | flops 606339072 | bytes 5315584 | tf_op jit(solution)/shard_map/dot_general | solution.py:138
  116.5 4.1 %fusion.74 = bf16[128,768]{1,0:T(8,128)(2,1)} fusion(bf16[1,1536,768]{2,1,0:T(8,128)(2,1)} %param.22, bf16[1,768,1536]{2,1,0:T(8,128)(2,1)} %param.21, f32[128,768]{1,0:T(8,128)S(1)} %get-tuple-element.12, f32[768]{0:T(1024)S(1)} %get-tuple-element.10, f32[768]{0:T(1024)S(1)} %get-tuple-element.7, f32[128]{0:T(128)} %add_rsqrt_fusion.8, f32[128]{0:T(128)} %copy-done.21), kind=kOutput, calls=%fused_computation.76 | convolution fusion | flops 606339072 | bytes 5315584 | tf_op jit(solution)/shard_map/dot_general | solution.py:138
  123.7 4.2 %fusion.77 = bf16[128,768]{1,0:T(8,128)(2,1)} fusion(bf16[1,1536,768]{2,1,0:T(8,128)(2,1)} %param.22, bf16[1,768,1536]{2,1,0:T(8,128)(2,1)} %param.21, f32[128,768]{1,0:T(8,128)} %get-tuple-element.14, f32[128]{0:T(128)} %add_rsqrt_fusion.6, f32[128]{0:T(128)} %copy-done.20, f32[768]{0:T(1024)S(1)} %get-tuple-element.10, f32[768]{0:T(1024)S(1)} %get-tuple-element.7), kind=kOutput, calls=%fused_computation.77 | convolution fusion | flops 606339072 | bytes 5315584 | tf_op jit(solution)/shard_map/dot_general | solution.py:138
  131.9 4.3 %fusion.65 = bf16[128,16,128]{2,0,1:T(8,128)(2,1)S(1)} fusion(bf16[16,128,768]{2,0,1:T(8,128)(2,1)} %bitcast.211, f32[128]{0:T(128)S(1)} %add_rsqrt_fusion.1, f32[128]{0:T(128)S(1)} %broadcast_multiply_fusion.3, f32[768]{0:T(1024)S(1)} %get-tuple-element.8, f32[768]{0:T(1024)S(1)} %get-tuple-element.5, f32[128,768]{1,0:T(8,128)S(1)} %copy-done.7, ...), kind=kOutput, calls=%fused_computation.63 | convolution fusion | flops 403800064 | bytes 4463616 | tf_op jit(solution)/shard_map/dot_general | solution.py:141
  136.2 13.2 %collective-permute-start.14 = (bf16[128,16,128]{2,0,1:T(8,128)(2,1)S(1)}, bf16[128,16,128]{2,0,1:T(8,128)(2,1)S(1)}, u32[]{:S(2)}, u32[]{:S(2)}) collective-permute-start(bf16[128,16,128]{2,0,1:T(8,128)(2,1)S(1)} %fusion.65), channel_id=1, source_target_pairs={{0,2},{2,4},{4,6},{6,8},{8,10},{10,12},{12,14},{14,16},{16,18},{18... | collective-permute-start | bytes 1572872 | tf_op jit(solution)/shard_map/ppermute | solution.py:19
  152.1 3.0 %fusion.53 = bf16[128,16,128]{2,0,1:T(8,128)(2,1)} fusion(bf16[16,128,768]{2,0,1:T(8,128)(2,1)S(1)} %bitcast.213, f32[128]{0:T(128)S(1)} %add_rsqrt_fusion.5, f32[128]{0:T(128)S(1)} %broadcast_multiply_fusion.7, f32[768]{0:T(1024)S(1)} %get-tuple-element.8, f32[768]{0:T(1024)S(1)} %get-tuple-element.5, f32[128,768]{1,0:T(8,128)S(1)} %copy-done.5, ...), kind=kOutput, calls=%fused_computation.59 | convolution fusion | flops 403800064 | bytes 4463616 | tf_op jit(solution)/shard_map/dot_general | solution.py:141
  155.1 1.9 collective-permute-start.8
  159.4 3.3 %divide_convert_fusion.4 = bf16[128,16,128]{2,0,1:T(8,128)(2,1)S(1)} fusion(bf16[128,16,128]{2,0,1:T(8,128)(2,1)S(1)} %collective-permute-done.14, bf16[16,128,768]{2,0,1:T(8,128)(2,1)S(1)} %bitcast.214, f32[]{:T(128)S(6)} %convert_element_type.248, s32[128]{0:T(128)S(1)} %copy-done.30, s32[128]{0:T(128)S(1)} %copy-done.25, s32[]{:T(128)S(6)} %mul.313, ...), kind=kOutput, calls=%fused_computation.115 | convolution fusion | flops 410091520 | bytes 4990216 | tf_op jit(solution)/shard_map/dot_general | solution.py:141
  163.8 2.0 %copy.51 = bf16[16,128,128]{2,1,0:T(8,128)(2,1)} copy(bf16[16,128,128]{1,2,0:T(8,128)(2,1)} %bitcast.219) | data formatting | bytes 1048576 | tf_op jit(solution)/shard_map/transpose | solution.py:162
  165.9 4.5 %divide_convert_fusion.5 = bf16[128,16,128]{2,0,1:T(8,128)(2,1)S(1)} fusion(bf16[128,16,128]{2,0,1:T(8,128)(2,1)} %collective-permute-done.8, bf16[16,128,768]{2,0,1:T(8,128)(2,1)} %bitcast.212, f32[]{:T(128)S(6)} %convert_element_type.248, s32[128]{0:T(128)} %iota_shift-right-logical_fusion.1, s32[128]{0:T(128)} %broadcast_add_fusion, s32[]{:T(128)S(6)} %mul.313, ...), kind=kOutput, calls=%fused_computation.116 | convolution fusion | flops 409829376 | bytes 4990216 | tf_op jit(solution)/shard_map/dot_general | solution.py:141
  171.5 2.0 %copy.46 = bf16[16,128,128]{2,1,0:T(8,128)(2,1)} copy(bf16[16,128,128]{1,2,0:T(8,128)(2,1)} %bitcast.220) | data formatting | bytes 1048576 | tf_op jit(solution)/shard_map/transpose | solution.py:162
  173.5 1.5 collective-permute-start.9
  175.0 4.2 %collective-permute-done.15 = bf16[2,8,8,16,128]{4,3,1,2,0:T(8,128)(2,1)} collective-permute-done((bf16[2,8,8,16,128]{4,3,1,2,0:T(8,128)(2,1)}, bf16[2,8,8,16,128]{4,3,1,2,0:T(8,128)(2,1)}, u32[]{:S(2)}, u32[]{:S(2)}) %collective-permute-start.15) | collective-permute-done | bytes 524320 | tf_op jit(solution)/shard_map/ppermute | solution.py:164
  179.2 11.1 %collective-permute-done.9 = bf16[2,8,8,16,128]{4,3,1,2,0:T(8,128)(2,1)S(1)} collective-permute-done((bf16[2,8,8,16,128]{4,3,1,2,0:T(8,128)(2,1)}, bf16[2,8,8,16,128]{4,3,1,2,0:T(8,128)(2,1)S(1)}, u32[]{:S(2)}, u32[]{:S(2)}) %collective-permute-start.9) | collective-permute-done | bytes 524320 | tf_op jit(solution)/shard_map/ppermute | solution.py:164
  190.3 2.2 %maximum_select_fusion = (bf16[2,16,8,16,128]{4,3,1,2,0:T(8,128)(2,1)S(1)}, bf16[2,16,8,16,128]{4,3,1,2,0:T(8,128)(2,1)S(1)}) fusion(bf16[2,8,8,16,128]{4,3,1,2,0:T(8,128)(2,1)S(1)} %collective-permute-done.9, bf16[2,8,8,16,128]{4,3,1,2,0:T(8,128)(2,1)} %bitcast.218, pred[]{:T(512)S(6)} %eq.2, bf16[2,8,8,16,128]{4,3,1,2,0:T(8,128)(2,1)} %bitcast.216, ...), kind=kLoop, calls=%fused_computation.113 | loop fusion | flops 3145728 | bytes 4194305 | tf_op jit(solution)/shard_map/jit(_where)/select_n | solution.py:165
  193.1 1.5 pad_maximum_fusion
  (142 shorter events, 37.4 us)
Async XLA Ops:
  0.0 25.7 %copy-start = (bf16[4096,384]{1,0:T(8,128)(2,1)S(1)}, bf16[4096,384]{1,0:T(8,128)(2,1)}, u32[]{:S(2)}) copy-start(bf16[4096,384]{1,0:T(8,128)(2,1)} %param.14) | copy-start | bytes 9437188
  0.9 37.4 %collective-permute-start.2 = (bf16[64,128]{1,0:T(8,128)(2,1)S(1)}, bf16[64,128]{1,0:T(8,128)(2,1)S(1)}, u32[]{:S(2)}, u32[]{:S(2)}) collective-permute-start(bf16[64,128]{1,0:T(8,128)(2,1)S(1)} %convert_element_type.210), channel_id=1, source_target_pairs={{2,0},{4,2},{6,4},{8,6},{10,8},{12,10},{14,12},{16,14},{18,16},{20... | collective-permute-start | bytes 49160 | tf_op jit(solution)/shard_map/ppermute | solution.py:19
  3.6 36.7 %collective-permute-start.1 = (bf16[64,128,128]{2,1,0:T(8,128)(2,1)}, bf16[64,128,128]{2,1,0:T(8,128)(2,1)}, u32[]{:S(2)}, u32[]{:S(2)}) collective-permute-start(bf16[64,128,128]{2,1,0:T(8,128)(2,1)} %param.12), channel_id=1, source_target_pairs={{2,0},{4,2},{6,4},{8,6},{10,8},{12,10},{14,12},{16,14},{18,16},{20... | collective-permute-start | bytes 6291464 | tf_op jit(solution)/shard_map/ppermute | solution.py:19
  18.9 6.7 %copy-start.11 = (bf16[256,384]{1,0:T(8,128)(2,1)S(1)}, bf16[256,384]{1,0:T(8,128)(2,1)}, u32[]{:S(2)}) copy-start(bf16[256,384]{1,0:T(8,128)(2,1)} %param.15) | copy-start | bytes 589828
  25.7 7.4 %copy-start.18 = (f32[3,768]{1,0:T(4,128)S(1)}, f32[3,768]{1,0:T(4,128)}, u32[]{:S(2)}) copy-start(f32[3,768]{1,0:T(4,128)} %param.17) | copy-start | bytes 27652
  25.7 7.4 %copy-start.19 = (f32[3,768]{1,0:T(4,128)S(1)}, f32[3,768]{1,0:T(4,128)}, u32[]{:S(2)}) copy-start(f32[3,768]{1,0:T(4,128)} %param.18) | copy-start | bytes 27652
  29.3 27.9 %collective-permute-start = (bf16[256,384]{1,0:T(8,128)(2,1)}, bf16[256,384]{1,0:T(8,128)(2,1)}, u32[]{:S(2)}, u32[]{:S(2)}) collective-permute-start(bf16[256,384]{1,0:T(8,128)(2,1)} %fusion.73), channel_id=1, source_target_pairs={{0,1},{1,0},{2,3},{3,2},{4,5},{5,4},{6,7},{7,6},{8,9},{9,8},{10,11... | collective-permute-start | bytes 589832 | tf_op jit(solution)/shard_map/ppermute | solution.py:92
  56.6 5.6 %collective-permute-start.3 = (bf16[256,384]{1,0:T(8,128)(2,1)S(1)}, bf16[256,384]{1,0:T(8,128)(2,1)S(1)}, u32[]{:S(2)}, u32[]{:S(2)}) collective-permute-start(bf16[256,384]{1,0:T(8,128)(2,1)S(1)} %fusion.72), channel_id=1, source_target_pairs={{0,1},{1,0},{2,3},{3,2},{4,5},{5,4},{6,7},{7,6},{8,9},{9,8},{10,11... | collective-permute-start | bytes 589832 | tf_op jit(solution)/shard_map/ppermute | solution.py:92
  58.5 4.2 %copy-start.2 = (f32[256,768]{1,0:T(8,128)}, f32[256,768]{1,0:T(8,128)S(1)}, u32[]{:S(2)}) copy-start(f32[256,768]{1,0:T(8,128)S(1)} %fusion.182) | copy-start | bytes 2359300
  62.2 0.9 copy-start.1
  62.2 1.8 copy-start.24
  66.1 5.7 %copy-start.16 = (bf16[1,512,384]{1,2,0:T(8,128)(2,1)}, bf16[1,512,384]{1,2,0:T(8,128)(2,1)S(1)}, u32[]{:S(2)}) copy-start(bf16[1,512,384]{1,2,0:T(8,128)(2,1)S(1)} %get-tuple-element.23) | copy-start | bytes 1179652
  71.8 3.7 %copy-start.17 = (bf16[1,128,384]{1,2,0:T(8,128)(2,1)S(1)}, bf16[1,128,384]{1,2,0:T(8,128)(2,1)}, u32[]{:S(2)}) copy-start(bf16[1,128,384]{1,2,0:T(8,128)(2,1)} %get-tuple-element.19) | copy-start | bytes 294916
  73.2 4.9 %copy-start.9 = (bf16[128,768]{1,0:T(8,128)(2,1)}, bf16[128,768]{1,0:T(8,128)(2,1)S(1)}, u32[]{:S(2)}) copy-start(bf16[128,768]{1,0:T(8,128)(2,1)S(1)} %convolution_convert_fusion.1) | copy-start | bytes 589828
  73.2 23.4 %collective-permute-start.10 = (bf16[128,768]{1,0:T(8,128)(2,1)S(1)}, bf16[128,768]{1,0:T(8,128)(2,1)}, u32[]{:S(2)}, u32[]{:S(2)}) collective-permute-start(bf16[128,768]{1,0:T(8,128)(2,1)S(1)} %convolution_convert_fusion.1), channel_id=1, source_target_pairs={{0,1},{1,0},{2,3},{3,2},{4,5},{5,4},{6,7},{7,6},{8,9},{9,8},{10,11... | collective-permute-start | bytes 589832 | tf_op jit(solution)/shard_map/ppermute | solution.py:24
  79.5 6.4 %copy-start.10 = (bf16[128,768]{1,0:T(8,128)(2,1)}, bf16[128,768]{1,0:T(8,128)(2,1)S(1)}, u32[]{:S(2)}) copy-start(bf16[128,768]{1,0:T(8,128)(2,1)S(1)} %convolution_convert_fusion.3) | copy-start | bytes 589828
  79.5 17.2 %collective-permute-start.4 = (bf16[128,768]{1,0:T(8,128)(2,1)S(1)}, bf16[128,768]{1,0:T(8,128)(2,1)}, u32[]{:S(2)}, u32[]{:S(2)}) collective-permute-start(bf16[128,768]{1,0:T(8,128)(2,1)S(1)} %convolution_convert_fusion.3), channel_id=1, source_target_pairs={{0,1},{1,0},{2,3},{3,2},{4,5},{5,4},{6,7},{7,6},{8,9},{9,8},{10,11... | collective-permute-start | bytes 589832 | tf_op jit(solution)/shard_map/ppermute | solution.py:24
  88.0 16.7 %collective-permute-start.12 = (bf16[128,768]{1,0:T(8,128)(2,1)}, bf16[128,768]{1,0:T(8,128)(2,1)}, u32[]{:S(2)}, u32[]{:S(2)}) collective-permute-start(bf16[128,768]{1,0:T(8,128)(2,1)} %convolution_convert_fusion), channel_id=1, source_target_pairs={{0,1},{1,0},{2,3},{3,2},{4,5},{5,4},{6,7},{7,6},{8,9},{9,8},{10,11... | collective-permute-start | bytes 589832 | tf_op jit(solution)/shard_map/ppermute | solution.py:24
  95.4 9.3 %collective-permute-start.6 = (bf16[128,768]{1,0:T(8,128)(2,1)}, bf16[128,768]{1,0:T(8,128)(2,1)}, u32[]{:S(2)}, u32[]{:S(2)}) collective-permute-start(bf16[128,768]{1,0:T(8,128)(2,1)} %convolution_convert_fusion.2), channel_id=1, source_target_pairs={{0,1},{1,0},{2,3},{3,2},{4,5},{5,4},{6,7},{7,6},{8,9},{9,8},{10,11... | collective-permute-start | bytes 589832 | tf_op jit(solution)/shard_map/ppermute | solution.py:24
  98.9 0.7 copy-start.3
  98.9 0.9 copy-start.22
  104.5 45.0 %collective-permute-start.11 = (bf16[128,768]{1,0:T(8,128)(2,1)}, bf16[128,768]{1,0:T(8,128)(2,1)}, u32[]{:S(2)}, u32[]{:S(2)}) collective-permute-start(bf16[128,768]{1,0:T(8,128)(2,1)} %fusion.80), channel_id=1, source_target_pairs={{0,1},{1,0},{2,3},{3,2},{4,5},{5,4},{6,7},{7,6},{8,9},{9,8},{10,11... | collective-permute-start | bytes 589832 | tf_op jit(solution)/shard_map/ppermute | solution.py:24
  107.5 0.7 copy-start.6
  107.5 0.9 copy-start.23
  113.2 15.9 %collective-permute-start.13 = (bf16[128,768]{1,0:T(8,128)(2,1)}, bf16[128,768]{1,0:T(8,128)(2,1)}, u32[]{:S(2)}, u32[]{:S(2)}) collective-permute-start(bf16[128,768]{1,0:T(8,128)(2,1)} %fusion.83), channel_id=1, source_target_pairs={{0,1},{1,0},{2,3},{3,2},{4,5},{5,4},{6,7},{7,6},{8,9},{9,8},{10,11... | collective-permute-start | bytes 589832 | tf_op jit(solution)/shard_map/ppermute | solution.py:24
  115.2 0.6 copy-start.21
  120.6 30.0 %collective-permute-start.5 = (bf16[128,768]{1,0:T(8,128)(2,1)}, bf16[128,768]{1,0:T(8,128)(2,1)}, u32[]{:S(2)}, u32[]{:S(2)}) collective-permute-start(bf16[128,768]{1,0:T(8,128)(2,1)} %fusion.74), channel_id=1, source_target_pairs={{0,1},{1,0},{2,3},{3,2},{4,5},{5,4},{6,7},{7,6},{8,9},{9,8},{10,11... | collective-permute-start | bytes 589832 | tf_op jit(solution)/shard_map/ppermute | solution.py:24
  121.4 0.6 copy-start.20
  127.9 3.9 %copy-start.7 = (f32[128,768]{1,0:T(8,128)S(1)}, f32[128,768]{1,0:T(8,128)}, u32[]{:S(2)}) copy-start(f32[128,768]{1,0:T(8,128)} %copy-done.6) | copy-start | bytes 1179652
  127.9 3.9 %copy-start.15 = (bf16[128,768]{1,0:T(8,128)(2,1)S(1)}, bf16[128,768]{1,0:T(8,128)(2,1)}, u32[]{:S(2)}) copy-start(bf16[128,768]{1,0:T(8,128)(2,1)} %fusion.83) | copy-start | bytes 589828
  127.9 23.8 %collective-permute-start.7 = (bf16[128,768]{1,0:T(8,128)(2,1)}, bf16[128,768]{1,0:T(8,128)(2,1)S(1)}, u32[]{:S(2)}, u32[]{:S(2)}) collective-permute-start(bf16[128,768]{1,0:T(8,128)(2,1)} %fusion.77), channel_id=1, source_target_pairs={{0,1},{1,0},{2,3},{3,2},{4,5},{5,4},{6,7},{7,6},{8,9},{9,8},{10,11... | collective-permute-start | bytes 589832 | tf_op jit(solution)/shard_map/ppermute | solution.py:24
  131.9 17.6 %copy-start.4 = (f32[128,768]{1,0:T(8,128)S(1)}, f32[128,768]{1,0:T(8,128)}, u32[]{:S(2)}) copy-start(f32[128,768]{1,0:T(8,128)} %copy-done.3) | copy-start | bytes 1179652
  131.9 17.6 %copy-start.12 = (bf16[128,768]{1,0:T(8,128)(2,1)S(1)}, bf16[128,768]{1,0:T(8,128)(2,1)}, u32[]{:S(2)}) copy-start(bf16[128,768]{1,0:T(8,128)(2,1)} %fusion.80) | copy-start | bytes 589828
  131.9 18.7 %copy-start.13 = (bf16[128,768]{1,0:T(8,128)(2,1)S(1)}, bf16[128,768]{1,0:T(8,128)(2,1)}, u32[]{:S(2)}) copy-start(bf16[128,768]{1,0:T(8,128)(2,1)} %fusion.74) | copy-start | bytes 589828
  131.9 20.2 %copy-start.8 = (bf16[768,2048]{0,1:T(8,128)(2,1)S(1)}, bf16[768,2048]{0,1:T(8,128)(2,1)}, u32[]{:S(2)}) copy-start(bf16[768,2048]{0,1:T(8,128)(2,1)} %copy.42) | copy-start | bytes 9437188
  136.2 15.5 %copy-start.5 = (f32[128,768]{1,0:T(8,128)S(1)}, f32[128,768]{1,0:T(8,128)}, u32[]{:S(2)}) copy-start(f32[128,768]{1,0:T(8,128)} %get-tuple-element.14) | copy-start | bytes 1179652
  136.2 15.5 %copy-start.14 = (bf16[128,768]{1,0:T(8,128)(2,1)S(1)}, bf16[128,768]{1,0:T(8,128)(2,1)}, u32[]{:S(2)}) copy-start(bf16[128,768]{1,0:T(8,128)(2,1)} %fusion.77) | copy-start | bytes 589828
  136.2 23.1 %collective-permute-start.14 = (bf16[128,16,128]{2,0,1:T(8,128)(2,1)S(1)}, bf16[128,16,128]{2,0,1:T(8,128)(2,1)S(1)}, u32[]{:S(2)}, u32[]{:S(2)}) collective-permute-start(bf16[128,16,128]{2,0,1:T(8,128)(2,1)S(1)} %fusion.65), channel_id=1, source_target_pairs={{0,2},{2,4},{4,6},{6,8},{8,10},{10,12},{12,14},{14,16},{16,18},{18... | collective-permute-start | bytes 1572872 | tf_op jit(solution)/shard_map/ppermute | solution.py:19
  155.1 4.2 %copy-start.25 = (s32[128]{0:T(128)S(1)}, s32[128]{0:T(128)}, u32[]{:S(2)}) copy-start(s32[128]{0:T(128)} %broadcast_add_fusion) | copy-start | bytes 1540
  155.1 4.2 %copy-start.26 = (s32[128]{0:T(128)S(1)}, s32[128]{0:T(128)}, u32[]{:S(2)}) copy-start(s32[128]{0:T(128)} %broadcast_add_fusion.1) | copy-start | bytes 1540
  155.1 4.3 %copy-start.27 = (pred[128]{0:T(512)(128)(4,1)S(1)}, pred[128]{0:T(512)(128)(4,1)}, u32[]{:S(2)}) copy-start(pred[128]{0:T(512)(128)(4,1)} %compare_and_fusion) | copy-start | bytes 388
  155.1 4.3 %copy-start.28 = (pred[128]{0:T(512)(128)(4,1)S(1)}, pred[128]{0:T(512)(128)(4,1)}, u32[]{:S(2)}) copy-start(pred[128]{0:T(512)(128)(4,1)} %compare_and_fusion.1) | copy-start | bytes 388
  155.1 4.3 %copy-start.29 = (s32[128]{0:T(128)S(1)}, s32[128]{0:T(128)}, u32[]{:S(2)}) copy-start(s32[128]{0:T(128)} %iota_shift-right-logical_fusion) | copy-start | bytes 1540
  155.1 4.3 %copy-start.30 = (s32[128]{0:T(128)S(1)}, s32[128]{0:T(128)}, u32[]{:S(2)}) copy-start(s32[128]{0:T(128)} %iota_shift-right-logical_fusion.1) | copy-start | bytes 1540
  155.1 10.8 %collective-permute-start.8 = (bf16[128,16,128]{2,0,1:T(8,128)(2,1)}, bf16[128,16,128]{2,0,1:T(8,128)(2,1)}, u32[]{:S(2)}, u32[]{:S(2)}) collective-permute-start(bf16[128,16,128]{2,0,1:T(8,128)(2,1)} %fusion.53), channel_id=1, source_target_pairs={{0,2},{2,4},{4,6},{6,8},{8,10},{10,12},{12,14},{14,16},{16,18},{18... | collective-permute-start | bytes 1572872 | tf_op jit(solution)/shard_map/ppermute | solution.py:19
  165.9 13.3 %collective-permute-start.15 = (bf16[2,8,8,16,128]{4,3,1,2,0:T(8,128)(2,1)}, bf16[2,8,8,16,128]{4,3,1,2,0:T(8,128)(2,1)}, u32[]{:S(2)}, u32[]{:S(2)}) collective-permute-start(bf16[2,8,8,16,128]{4,3,1,2,0:T(8,128)(2,1)} %bitcast.215), channel_id=1, source_target_pairs={{0,1},{1,0},{2,3},{3,2},{4,5},{5,4},{6,7},{7,6},{8,9},{9,8},{10,11... | collective-permute-start | bytes 1572872 | tf_op jit(solution)/shard_map/ppermute | solution.py:164
  173.5 16.8 %collective-permute-start.9 = (bf16[2,8,8,16,128]{4,3,1,2,0:T(8,128)(2,1)}, bf16[2,8,8,16,128]{4,3,1,2,0:T(8,128)(2,1)S(1)}, u32[]{:S(2)}, u32[]{:S(2)}) collective-permute-start(bf16[2,8,8,16,128]{4,3,1,2,0:T(8,128)(2,1)} %bitcast.217), channel_id=1, source_target_pairs={{0,1},{1,0},{2,3},{3,2},{4,5},{5,4},{6,7},{7,6},{8,9},{9,8},{10,11... | collective-permute-start | bytes 1572872 | tf_op jit(solution)/shard_map/ppermute | solution.py:164

commit v4 on v2

--- a/solution.py
+++ b/solution.py
@@ -129,6 +129,10 @@
             jnp.dot(normed, w_up[0], preferred_element_type=jnp.float32), approximate=True
         ).astype(jnp.bfloat16)
         partial_forward = jnp.dot(hidden, w_down[0], preferred_element_type=jnp.float32)
+        if chunk == 0:
+            decoded_chunks[1], partial_forward = lax.optimization_barrier(
+                (decoded_chunks[1], partial_forward)
+            )
         part = part + partner_sum(partial_forward)
         latent = layer_norm(part, norm_gain[2 * LAYERS], norm_bias[2 * LAYERS]).astype(jnp.bfloat16)
         decoded_chunks[chunk] = lax.dot_general(

time: 176 us -> 174 us (0.989)
  starting transfers between devices: 24.2 us -> 21.8 us
  waiting for transfers between devices: 44.1 us -> 45.9 us
    ppermute x3, starting transfers between devices: 19 us -> 13 us  [from_behind(): return lax.ppermute(block, axis, route)]
    ppermute x1, waiting for transfers between devices: 20.9 us -> 23.5 us  [body(): other_rows = lax.ppermute(arranged, 'head', [(0, 1), (1, 0)])]
    unnamed x53 -> x43, local copies, waits for them, and re-layouts: 6.57 us -> 6.55 us
  transfers between devices with their start and end apart: 10 -> 10, of which waited for: 6 -> 6; matrix products, arithmetic and copies ran while one was open for 43% -> 38% of each run, Pallas kernels for 0% -> 0%
where the time goes in v4:
time: 174 us; the launch traced here: 173 us
  waiting for transfers between devices  45.9 us (26%)
  matrix products  43 us (25%)
  local copies, waits for them, and re-layouts  42.3 us (24%)
  starting transfers between devices  21.8 us (13%)
  other arithmetic  20.2 us (12%)
    ppermute x1, waiting for transfers between devices, body(): other_rows = lax.ppermute(arranged, 'head', [(0, 1), (1, 0)])  23.5 us
    ppermute x3, starting transfers between devices, from_behind(): return lax.ppermute(block, axis, route)  13 us
    ppermute x4, waiting for transfers between devices, partner_sum(): other = lax.ppermute(rounded, 'head', [(0, 1), (1, 0)])  11 us
    dot_general x2, matrix products, body(): lax.dot_general(latent, decode_by_depth, (((1,), (2,)), ((), ())), prefer...  10.5 us
    reshape x2, local copies, waits for them, and re-layouts, embed_planes(): voxels = jnp.swapaxes(grouped, 1, 2).reshape(rows, PATCH, PATCH * PATCH)  9.69 us
    dot_general x2, matrix products, body(): jnp.dot(hidden, w_down[0], preferred_element_type=jnp.float32)  9.29 us
    sub x2, matrix products, body(): weights = jax.nn.softmax(scores, axis=-1).astype(jnp.bfloat16)  9 us
    ppermute x3, waiting for transfers between devices, from_behind(): return lax.ppermute(block, axis, route)  8.48 us
  transfers between devices with their start and end apart: 10, of which 6 were waited for; matrix products, arithmetic and copies ran while one was open for 38% of the time, Pallas kernels for 0%

profile of v4, /device:TPU:31, one launch (start us, length us, event | category | flops | bytes accessed | tf_op | source)
XLA Modules:
  0.0 173.5 jit_solution(11306345219532970751)
XLA Ops:
  0.9 2.7 %collective-permute-start.2 = (bf16[64,128]{1,0:T(8,128)(2,1)S(1)}, bf16[64,128]{1,0:T(8,128)(2,1)}, u32[]{:S(2)}, u32[]{:S(2)}) collective-permute-start(bf16[64,128]{1,0:T(8,128)(2,1)S(1)} %convert_element_type.120), channel_id=1, source_target_pairs={{2,0},{4,2},{6,4},{8,6},{10,8},{12,10},{14,12},{16,14},{18,16},{20... | collective-permute-start | bytes 49160 | tf_op jit(solution)/shard_map/ppermute | solution.py:19
  3.6 2.2 %collective-permute-start.1 = (bf16[64,128,128]{2,1,0:T(8,128)(2,1)}, bf16[64,128,128]{2,1,0:T(8,128)(2,1)}, u32[]{:S(2)}, u32[]{:S(2)}) collective-permute-start(bf16[64,128,128]{2,1,0:T(8,128)(2,1)} %param.12), channel_id=1, source_target_pairs={{2,0},{4,2},{6,4},{8,6},{10,8},{12,10},{14,12},{16,14},{18,16},{20... | collective-permute-start | bytes 6291464 | tf_op jit(solution)/shard_map/ppermute | solution.py:19
  6.0 2.0 %convert_element_type.121 = f32[512,384]{1,0:T(8,128)} convert(bf16[512,384]{1,0:T(8,128)(2,1)} %param.16) | non-fusion elementwise | flops 196608 | bytes 1179648 | tf_op jit(solution)/shard_map/convert_element_type | solution.py:86
  7.9 2.5 %broadcast_multiply_fusion.1 = bf16[64,128,128]{2,1,0:T(8,128)(2,1)S(1)} fusion(bf16[64,128,128]{2,1,0:T(8,128)(2,1)} %param.12, bf16[64,128]{1,0:T(8,128)(2,1)S(1)} %convert_element_type.120), kind=kLoop, calls=%fused_computation.69 | loop fusion | flops 1048576 | bytes 4210688 | tf_op jit(solution)/shard_map/mul | solution.py:43
  10.4 1.9 %copy.29 = bf16[4,8,16,16,128]{4,3,2,1,0:T(8,128)(2,1)} copy(bf16[4,8,16,16,128]{4,3,1,2,0:T(8,128)(2,1)S(1)} %bitcast.145) | data formatting | bytes 4194304 | tf_op jit(solution)/shard_map/transpose | solution.py:44
  12.3 4.1 %copy.30 = bf16[32,128,256]{2,1,0:T(8,128)(2,1)} copy(bf16[32,128,256]{1,2,0:T(8,128)(2,1)} %bitcast.141) | data formatting | bytes 4194304 | tf_op jit(solution)/shard_map/transpose | solution.py:46
  16.4 4.9 %copy.31 = bf16[256,16,256]{0,1,2:T(8,128)(2,1)} copy(bf16[256,16,256]{2,1,0:T(8,128)(2,1)} %bitcast.142) | data formatting | bytes 4194304 | tf_op jit(solution)/shard_map/reshape | solution.py:46
  21.9 1.1 reshape.145
  23.1 2.9 %fusion.70 = bf16[256,384]{1,0:T(8,128)(2,1)S(1)} fusion(bf16[256,16,256]{0,1,2:T(8,128)(2,1)} %copy.31, bf16[16,256,384]{2,0,1:T(8,128)(2,1)S(1)} %bitcast.138, f32[512,384]{1,0:T(8,128)} %convert_element_type.121, f32[32,384]{1,0:T(8,128)S(1)} %fusion.149), kind=kOutput, calls=%fused_computation.65 | convolution fusion | flops 805601280 | bytes 5881856 | tf_op jit(solution)/shard_map/dot_general | solution.py:47
  26.1 1.7 collective-permute-start
  27.8 4.6 %copy.38 = bf16[768,2048]{0,1:T(8,128)(2,1)} copy(bf16[768,2048]{1,0:T(8,128)(2,1)} %param.23) | data formatting | bytes 6291456 | tf_op args[11]
  32.4 1.5 reshape.150
  33.9 1.6 copy.57
  35.5 1.1 reshape.151
  37.3 2.5 %broadcast_multiply_fusion = bf16[64,128,128]{2,1,0:T(8,128)(2,1)S(1)} fusion(bf16[64,128,128]{2,1,0:T(8,128)(2,1)} %collective-permute-done.1, bf16[64,128]{1,0:T(8,128)(2,1)} %collective-permute-done.2), kind=kLoop, calls=%fused_computation.68 | loop fusion | flops 1048576 | bytes 4210688 | tf_op jit(solution)/shard_map/mul | solution.py:43
  39.8 1.9 %copy.33 = bf16[4,8,16,16,128]{4,3,2,1,0:T(8,128)(2,1)} copy(bf16[4,8,16,16,128]{4,3,1,2,0:T(8,128)(2,1)S(1)} %bitcast.140) | data formatting | bytes 4194304 | tf_op jit(solution)/shard_map/transpose | solution.py:44
  41.7 4.1 %copy.34 = bf16[32,128,256]{2,1,0:T(8,128)(2,1)} copy(bf16[32,128,256]{1,2,0:T(8,128)(2,1)} %bitcast.143) | data formatting | bytes 4194304 | tf_op jit(solution)/shard_map/transpose | solution.py:46
  45.8 4.8 %copy.35 = bf16[256,16,256]{0,1,2:T(8,128)(2,1)} copy(bf16[256,16,256]{2,1,0:T(8,128)(2,1)} %bitcast.144) | data formatting | bytes 4194304 | tf_op jit(solution)/shard_map/reshape | solution.py:46
  50.6 2.9 %fusion.69 = bf16[256,384]{1,0:T(8,128)(2,1)S(1)} fusion(bf16[256,16,256]{0,1,2:T(8,128)(2,1)} %copy.35, bf16[16,256,384]{2,0,1:T(8,128)(2,1)S(1)} %bitcast.139, f32[512,384]{1,0:T(8,128)} %convert_element_type.121, f32[32,384]{1,0:T(8,128)S(1)} %copy-done.15), kind=kOutput, calls=%fused_computation.64 | convolution fusion | flops 805601280 | bytes 5881856 | tf_op jit(solution)/shard_map/dot_general | solution.py:47
  53.6 1.5 collective-permute-start.3
  55.7 1.1 fusion.100
  56.9 2.8 %collective-permute-done.3 = bf16[256,384]{1,0:T(8,128)(2,1)S(1)} collective-permute-done((bf16[256,384]{1,0:T(8,128)(2,1)S(1)}, bf16[256,384]{1,0:T(8,128)(2,1)S(1)}, u32[]{:S(2)}, u32[]{:S(2)}) %collective-permute-start.3) | collective-permute-done | bytes 196640 | tf_op jit(solution)/shard_map/ppermute | solution.py:92
  60.4 1.3 fusion.59
  63.3 4.5 %fusion.148 = (f32[6,256]{1,0:T(8,128)}, f32[6,256,512]{2,1,0:T(8,128)}) fusion(bf16[256,6,64]{0,2,1:T(8,128)(2,1)} %bitcast.160, bf16[512,6,64]{0,2,1:T(8,128)(2,1)} %bitcast.155), kind=kOutput, calls=%fused_computation.168 | convolution fusion | flops 103023104 | bytes 3741696 | tf_op jit(solution)/shard_map/sub | solution.py:120
  67.8 2.6 %fusion.72 = bf16[6,64,256]{2,1,0:T(8,128)(2,1)S(1)} fusion(bf16[512,6,64]{0,2,1:T(8,128)(2,1)S(1)} %bitcast.153, f32[6,256,512]{2,1,0:T(8,128)} %get-tuple-element.26, f32[6,256]{1,0:T(8,128)} %get-tuple-element.25), kind=kOutput, calls=%fused_computation.67 | convolution fusion | flops 102334464 | bytes 3741696 | tf_op jit(solution)/shard_map/hts,shd->thd/dot_general | solution.py:121
  70.8 2.2 %collective-permute-start.4 = (bf16[256,768]{1,0:T(8,128)(2,1)S(1)}, bf16[256,768]{1,0:T(8,128)(2,1)}, u32[]{:S(2)}, u32[]{:S(2)}) collective-permute-start(bf16[256,768]{1,0:T(8,128)(2,1)S(1)} %convolution_convert_fusion.1), channel_id=1, source_target_pairs={{0,1},{1,0},{2,3},{3,2},{4,5},{5,4},{6,7},{7,6},{8,9},{9,8},{10,11... | collective-permute-start | bytes 1179656 | tf_op jit(solution)/shard_map/ppermute | solution.py:24
  73.1 4.5 %fusion.147 = (f32[6,256]{1,0:T(8,128)}, f32[6,256,512]{2,1,0:T(8,128)}) fusion(bf16[256,6,64]{0,2,1:T(8,128)(2,1)} %bitcast.159, bf16[512,6,64]{0,2,1:T(8,128)(2,1)} %bitcast.156), kind=kOutput, calls=%fused_computation.167 | convolution fusion | flops 103023104 | bytes 3741696 | tf_op jit(solution)/shard_map/sub | solution.py:120
  77.6 2.7 %fusion.71 = bf16[6,64,256]{2,1,0:T(8,128)(2,1)S(1)} fusion(bf16[512,6,64]{0,2,1:T(8,128)(2,1)} %bitcast.154, f32[6,256,512]{2,1,0:T(8,128)} %get-tuple-element.24, f32[6,256]{1,0:T(8,128)} %get-tuple-element.23), kind=kOutput, calls=%fused_computation.66 | convolution fusion | flops 102334464 | bytes 3741696 | tf_op jit(solution)/shard_map/hts,shd->thd/dot_general | solution.py:121
  81.6 1.4 fusion.143
  84.7 6.1 %collective-permute-done.5 = bf16[256,768]{1,0:T(8,128)(2,1)S(1)} collective-permute-done((bf16[256,768]{1,0:T(8,128)(2,1)S(1)}, bf16[256,768]{1,0:T(8,128)(2,1)S(1)}, u32[]{:S(2)}, u32[]{:S(2)}) %collective-permute-start.5) | collective-permute-done | bytes 393248 | tf_op jit(solution)/shard_map/ppermute | solution.py:24
  92.2 5.0 %fusion.62 = bf16[256,768]{1,0:T(8,128)(2,1)} fusion(bf16[1,1536,768]{2,1,0:T(8,128)(2,1)} %param.22, bf16[1,768,1536]{2,1,0:T(8,128)(2,1)} %param.21, f32[256,768]{1,0:T(8,128)} %copy-done.3, f32[768]{0:T(1024)S(1)} %get-tuple-element.12, f32[768]{0:T(1024)S(1)} %copy-done.18, f32[256]{0:T(256)S(1)} %add_rsqrt_fusion.4, f32[256]{0:T(256)S(1)} %broadcast_multiply_fusion.6), kind=kOutput, calls=%fused_computation.55 | convolution fusion | flops 1212678144 | bytes 5906432 | tf_op jit(solution)/shard_map/dot_general | solution.py:131
  97.2 1.0 collective-permute-start.6
  98.2 4.3 %fusion.12 = bf16[256,768]{1,0:T(8,128)(2,1)S(1)} fusion(bf16[1,1536,768]{2,1,0:T(8,128)(2,1)} %param.22, bf16[1,768,1536]{2,1,0:T(8,128)(2,1)} %param.21, f32[256,768]{1,0:T(8,128)} %copy-done.1, f32[256]{0:T(256)} %add_rsqrt_fusion.2, f32[256]{0:T(256)S(1)} %broadcast_multiply_fusion.4, f32[768]{0:T(1024)S(1)} %get-tuple-element.12, ...), kind=kOutput, calls=%fused_computation.16 | convolution fusion | flops 1212481536 | bytes 5906432 | tf_op jit(solution)/shard_map/dot_general | solution.py:131
  102.5 4.2 %collective-permute-done.6 = bf16[256,768]{1,0:T(8,128)(2,1)} collective-permute-done((bf16[256,768]{1,0:T(8,128)(2,1)}, bf16[256,768]{1,0:T(8,128)(2,1)}, u32[]{:S(2)}, u32[]{:S(2)}) %collective-permute-start.6) | collective-permute-done | bytes 393248 | tf_op jit(solution)/shard_map/ppermute | solution.py:24
  106.7 1.6 fusion.141
  108.2 1.4 multiply_reduce_fusion.5
  109.7 5.6 %fusion.53 = bf16[256,16,128]{2,0,1:T(8,128)(2,1)} fusion(bf16[16,128,768]{2,0,1:T(8,128)(2,1)} %bitcast.149, f32[768]{0:T(1024)S(1)} %get-tuple-element.14, f32[768]{0:T(1024)S(1)} %get-tuple-element.27, f32[256]{0:T(256)S(1)} %add_rsqrt_fusion.3, f32[256]{0:T(256)S(1)} %broadcast_multiply_fusion.5, f32[256,768]{1,0:T(8,128)S(1)} %copy-done.4, ...), kind=kOutput, calls=%fused_computation.52 | convolution fusion | flops 807600128 | bytes 5775360 | tf_op jit(solution)/shard_map/dot_general | solution.py:138
  115.2 1.3 collective-permute-start.7
  116.6 8.1 %collective-permute-start.8 = (bf16[256,16,128]{2,0,1:T(8,128)(2,1)}, bf16[256,16,128]{2,0,1:T(8,128)(2,1)}, u32[]{:S(2)}, u32[]{:S(2)}) collective-permute-start(bf16[256,16,128]{2,0,1:T(8,128)(2,1)} %fusion.53), channel_id=1, source_target_pairs={{0,2},{2,4},{4,6},{6,8},{8,10},{10,12},{12,14},{14,16},{16,18},{18... | collective-permute-start | bytes 3145736 | tf_op jit(solution)/shard_map/ppermute | solution.py:19
  125.3 1.5 fusion.142
  126.8 1.3 multiply_reduce_fusion.3
  128.1 8.5 %collective-permute-done.8 = bf16[256,16,128]{2,0,1:T(8,128)(2,1)} collective-permute-done((bf16[256,16,128]{2,0,1:T(8,128)(2,1)}, bf16[256,16,128]{2,0,1:T(8,128)(2,1)}, u32[]{:S(2)}, u32[]{:S(2)}) %collective-permute-start.8) | collective-permute-done | bytes 1048608 | tf_op jit(solution)/shard_map/ppermute | solution.py:19
  136.6 4.9 %divide_convert_fusion.2 = bf16[256,16,128]{2,0,1:T(8,128)(2,1)S(1)} fusion(bf16[256,16,128]{2,0,1:T(8,128)(2,1)} %collective-permute-done.8, f32[]{:T(128)S(6)} %convert_element_type.158, s32[128]{0:T(128)S(1)} %get-tuple-element.32, s32[128]{0:T(128)S(1)} %get-tuple-element.33, s32[]{:T(128)S(6)} %mul.212, s32[256]{0:T(256)S(1)} %get-tuple-element.30, ...), kind=kOutput, calls=%fused_computation.25 | convolution fusion | flops 819658752 | bytes 6827400 | tf_op jit(solution)/shard_map/dot_general | solution.py:138
  141.4 1.6 copy.41
  143.1 2.3 %copy.42 = bf16[32,128,128]{2,1,0:T(8,128)(2,1)} copy(bf16[32,128,128]{1,2,0:T(8,128)(2,1)} %bitcast.148) | data formatting | bytes 2097152 | tf_op jit(solution)/shard_map/transpose | solution.py:159
  146.2 23.5 %collective-permute-done.9 = bf16[4,8,8,16,128]{4,3,1,2,0:T(8,128)(2,1)S(1)} collective-permute-done((bf16[4,8,8,16,128]{4,3,1,2,0:T(8,128)(2,1)}, bf16[4,8,8,16,128]{4,3,1,2,0:T(8,128)(2,1)S(1)}, u32[]{:S(2)}, u32[]{:S(2)}) %collective-permute-start.9) | collective-permute-done | bytes 1048608 | tf_op jit(solution)/shard_map/ppermute | solution.py:161
  169.7 1.8 %maximum_select_fusion = bf16[4,16,8,16,128]{4,3,1,2,0:T(8,128)(2,1)S(1)} fusion(bf16[4,8,8,16,128]{4,3,1,2,0:T(8,128)(2,1)S(1)} %collective-permute-done.9, bf16[4,8,8,16,128]{4,3,1,2,0:T(8,128)(2,1)} %bitcast.147, pred[]{:T(512)S(6)} %eq.2), kind=kLoop, calls=%fused_computation.24 | loop fusion | flops 3145728 | bytes 4194305 | tf_op jit(solution)/shard_map/jit(_where)/select_n | solution.py:162
  171.5 1.9 %copy.43 = bf16[4,16,8,16,128]{4,3,2,1,0:T(8,128)(2,1)} copy(bf16[4,16,8,16,128]{4,3,1,2,0:T(8,128)(2,1)S(1)} %maximum_select_fusion) | data formatting | bytes 4194304 | tf_op jit(solution)/shard_map/jit(_where)/select_n | solution.py:162
  (79 shorter events, 11.7 us)
Async XLA Ops:
  0.0 23.1 %copy-start = (bf16[4096,384]{1,0:T(8,128)(2,1)S(1)}, bf16[4096,384]{1,0:T(8,128)(2,1)}, u32[]{:S(2)}) copy-start(bf16[4096,384]{1,0:T(8,128)(2,1)} %param.14) | copy-start | bytes 9437188
  0.9 31.5 %collective-permute-start.2 = (bf16[64,128]{1,0:T(8,128)(2,1)S(1)}, bf16[64,128]{1,0:T(8,128)(2,1)}, u32[]{:S(2)}, u32[]{:S(2)}) collective-permute-start(bf16[64,128]{1,0:T(8,128)(2,1)S(1)} %convert_element_type.120), channel_id=1, source_target_pairs={{2,0},{4,2},{6,4},{8,6},{10,8},{12,10},{14,12},{16,14},{18,16},{20... | collective-permute-start | bytes 49160 | tf_op jit(solution)/shard_map/ppermute | solution.py:19
  3.6 33.7 %collective-permute-start.1 = (bf16[64,128,128]{2,1,0:T(8,128)(2,1)}, bf16[64,128,128]{2,1,0:T(8,128)(2,1)}, u32[]{:S(2)}, u32[]{:S(2)}) collective-permute-start(bf16[64,128,128]{2,1,0:T(8,128)(2,1)} %param.12), channel_id=1, source_target_pairs={{2,0},{4,2},{6,4},{8,6},{10,8},{12,10},{14,12},{16,14},{18,16},{20... | collective-permute-start | bytes 6291464 | tf_op jit(solution)/shard_map/ppermute | solution.py:19
  16.4 6.6 %copy-start.7 = (bf16[256,384]{1,0:T(8,128)(2,1)S(1)}, bf16[256,384]{1,0:T(8,128)(2,1)}, u32[]{:S(2)}) copy-start(bf16[256,384]{1,0:T(8,128)(2,1)} %param.15) | copy-start | bytes 589828
  26.0 29.7 %copy-start.8 = (bf16[256,384]{1,0:T(8,128)(2,1)}, bf16[256,384]{1,0:T(8,128)(2,1)S(1)}, u32[]{:S(2)}) copy-start(bf16[256,384]{1,0:T(8,128)(2,1)S(1)} %fusion.70) | copy-start | bytes 589828
  26.1 29.7 %collective-permute-start = (bf16[256,384]{1,0:T(8,128)(2,1)S(1)}, bf16[256,384]{1,0:T(8,128)(2,1)}, u32[]{:S(2)}, u32[]{:S(2)}) collective-permute-start(bf16[256,384]{1,0:T(8,128)(2,1)S(1)} %fusion.70), channel_id=1, source_target_pairs={{0,1},{1,0},{2,3},{3,2},{4,5},{5,4},{6,7},{7,6},{8,9},{9,8},{10,11... | collective-permute-start | bytes 589832 | tf_op jit(solution)/shard_map/ppermute | solution.py:92
  45.8 4.8 %copy-start.15 = (f32[32,384]{1,0:T(8,128)S(1)}, f32[32,384]{1,0:T(8,128)}, u32[]{:S(2)}) copy-start(f32[32,384]{1,0:T(8,128)} %fusion.150) | copy-start | bytes 147460
  50.6 4.5 %copy-start.16 = (f32[3,768]{1,0:T(4,128)S(1)}, f32[3,768]{1,0:T(4,128)}, u32[]{:S(2)}) copy-start(f32[3,768]{1,0:T(4,128)} %param.18) | copy-start | bytes 27652
  50.6 4.5 %copy-start.17 = (f32[3,768]{1,0:T(4,128)S(1)}, f32[3,768]{1,0:T(4,128)}, u32[]{:S(2)}) copy-start(f32[3,768]{1,0:T(4,128)} %param.17) | copy-start | bytes 27652
  53.6 6.6 %copy-start.10 = (bf16[256,384]{1,0:T(8,128)(2,1)}, bf16[256,384]{1,0:T(8,128)(2,1)S(1)}, u32[]{:S(2)}) copy-start(bf16[256,384]{1,0:T(8,128)(2,1)S(1)} %fusion.69) | copy-start | bytes 589828
  53.6 6.1 %collective-permute-start.3 = (bf16[256,384]{1,0:T(8,128)(2,1)S(1)}, bf16[256,384]{1,0:T(8,128)(2,1)S(1)}, u32[]{:S(2)}, u32[]{:S(2)}) collective-permute-start(bf16[256,384]{1,0:T(8,128)(2,1)S(1)} %fusion.69), channel_id=1, source_target_pairs={{0,1},{1,0},{2,3},{3,2},{4,5},{5,4},{6,7},{7,6},{8,9},{9,8},{10,11... | collective-permute-start | bytes 589832 | tf_op jit(solution)/shard_map/ppermute | solution.py:92
  56.8 3.5 %copy-start.19 = (bf16[1,3,768,384]{3,2,1,0:T(8,128)(2,1)S(1)}, bf16[1,3,768,384]{3,2,1,0:T(8,128)(2,1)}, u32[]{:S(2)}) copy-start(bf16[1,3,768,384]{3,2,1,0:T(8,128)(2,1)} %param.19) | copy-start | bytes 5308420
  59.7 0.7 copy-start.12
  62.5 5.3 %copy-start.14 = (bf16[1,512,384]{1,2,0:T(8,128)(2,1)}, bf16[1,512,384]{1,2,0:T(8,128)(2,1)S(1)}, u32[]{:S(2)}) copy-start(bf16[1,512,384]{1,2,0:T(8,128)(2,1)S(1)} %get-tuple-element.22) | copy-start | bytes 1179652
  67.8 2.6 %copy-start.5 = (bf16[1,384,768]{2,1,0:T(8,128)(2,1)S(1)}, bf16[1,384,768]{2,1,0:T(8,128)(2,1)}, u32[]{:S(2)}) copy-start(bf16[1,384,768]{2,1,0:T(8,128)(2,1)} %param.20) | copy-start | bytes 1769476
  70.8 10.8 %collective-permute-start.4 = (bf16[256,768]{1,0:T(8,128)(2,1)S(1)}, bf16[256,768]{1,0:T(8,128)(2,1)}, u32[]{:S(2)}, u32[]{:S(2)}) collective-permute-start(bf16[256,768]{1,0:T(8,128)(2,1)S(1)} %convolution_convert_fusion.1), channel_id=1, source_target_pairs={{0,1},{1,0},{2,3},{3,2},{4,5},{5,4},{6,7},{7,6},{8,9},{9,8},{10,11... | collective-permute-start | bytes 1179656 | tf_op jit(solution)/shard_map/ppermute | solution.py:24
  77.6 2.7 %copy-start.6 = (bf16[1,384,768]{2,1,0:T(8,128)(2,1)S(1)}, bf16[1,384,768]{2,1,0:T(8,128)(2,1)}, u32[]{:S(2)}) copy-start(bf16[1,384,768]{2,1,0:T(8,128)(2,1)} %param.20) | copy-start | bytes 1769476
  77.6 4.0 %copy-start.9 = (bf16[256,384]{1,0:T(8,128)(2,1)S(1)}, bf16[256,384]{1,0:T(8,128)(2,1)}, u32[]{:S(2)}) copy-start(bf16[256,384]{1,0:T(8,128)(2,1)} %copy-done.8) | copy-start | bytes 589828
  80.3 10.5 %copy-start.11 = (bf16[256,384]{1,0:T(8,128)(2,1)S(1)}, bf16[256,384]{1,0:T(8,128)(2,1)}, u32[]{:S(2)}) copy-start(bf16[256,384]{1,0:T(8,128)(2,1)} %copy-done.10) | copy-start | bytes 589828
  80.3 10.5 %copy-start.13 = (bf16[256,384]{1,0:T(8,128)(2,1)S(1)}, bf16[256,384]{1,0:T(8,128)(2,1)}, u32[]{:S(2)}) copy-start(bf16[256,384]{1,0:T(8,128)(2,1)} %copy-done.12) | copy-start | bytes 589828
  80.7 10.1 %collective-permute-start.5 = (bf16[256,768]{1,0:T(8,128)(2,1)S(1)}, bf16[256,768]{1,0:T(8,128)(2,1)S(1)}, u32[]{:S(2)}, u32[]{:S(2)}) collective-permute-start(bf16[256,768]{1,0:T(8,128)(2,1)S(1)} %convolution_convert_fusion), channel_id=1, source_target_pairs={{0,1},{1,0},{2,3},{3,2},{4,5},{5,4},{6,7},{7,6},{8,9},{9,8},{10,11... | collective-permute-start | bytes 1179656 | tf_op jit(solution)/shard_map/ppermute | solution.py:24
  83.0 0.9 copy-start.1
  83.0 9.1 %copy-start.18 = (f32[768]{0:T(1024)S(1)}, f32[768]{0:T(1024)}, u32[]{:S(2)}) copy-start(f32[768]{0:T(1024)} %get-tuple-element.29) | copy-start | bytes 9220
  91.1 0.9 copy-start.3
  97.2 9.5 %collective-permute-start.6 = (bf16[256,768]{1,0:T(8,128)(2,1)}, bf16[256,768]{1,0:T(8,128)(2,1)}, u32[]{:S(2)}, u32[]{:S(2)}) collective-permute-start(bf16[256,768]{1,0:T(8,128)(2,1)} %fusion.62), channel_id=1, source_target_pairs={{0,1},{1,0},{2,3},{3,2},{4,5},{5,4},{6,7},{7,6},{8,9},{9,8},{10,11... | collective-permute-start | bytes 1179656 | tf_op jit(solution)/shard_map/ppermute | solution.py:24
  102.5 5.7 %copy-start.4 = (f32[256,768]{1,0:T(8,128)S(1)}, f32[256,768]{1,0:T(8,128)}, u32[]{:S(2)}) copy-start(f32[256,768]{1,0:T(8,128)} %copy-done.3) | copy-start | bytes 2359300
  115.2 10.0 %collective-permute-start.7 = (bf16[256,768]{1,0:T(8,128)(2,1)S(1)}, bf16[256,768]{1,0:T(8,128)(2,1)}, u32[]{:S(2)}, u32[]{:S(2)}) collective-permute-start(bf16[256,768]{1,0:T(8,128)(2,1)S(1)} %fusion.12), channel_id=1, source_target_pairs={{0,1},{1,0},{2,3},{3,2},{4,5},{5,4},{6,7},{7,6},{8,9},{9,8},{10,11... | collective-permute-start | bytes 1179656 | tf_op jit(solution)/shard_map/ppermute | solution.py:24
  116.6 20.0 %collective-permute-start.8 = (bf16[256,16,128]{2,0,1:T(8,128)(2,1)}, bf16[256,16,128]{2,0,1:T(8,128)(2,1)}, u32[]{:S(2)}, u32[]{:S(2)}) collective-permute-start(bf16[256,16,128]{2,0,1:T(8,128)(2,1)} %fusion.53), channel_id=1, source_target_pairs={{0,2},{2,4},{4,6},{6,8},{8,10},{10,12},{12,14},{14,16},{16,18},{18... | collective-permute-start | bytes 3145736 | tf_op jit(solution)/shard_map/ppermute | solution.py:19
  125.3 1.5 copy-start.2
  125.3 11.3 %copy-start.20 = (pred[256]{0:T(512)(128)(4,1)S(1)}, pred[256]{0:T(512)(128)(4,1)}, u32[]{:S(2)}) copy-start(pred[256]{0:T(512)(128)(4,1)} %compare_and_fusion.1) | copy-start | bytes 772
  145.4 24.4 %collective-permute-start.9 = (bf16[4,8,8,16,128]{4,3,1,2,0:T(8,128)(2,1)}, bf16[4,8,8,16,128]{4,3,1,2,0:T(8,128)(2,1)S(1)}, u32[]{:S(2)}, u32[]{:S(2)}) collective-permute-start(bf16[4,8,8,16,128]{4,3,1,2,0:T(8,128)(2,1)} %bitcast.146), channel_id=1, source_target_pairs={{0,1},{1,0},{2,3},{3,2},{4,5},{5,4},{6,7},{7,6},{8,9},{9,8},{10,11... | collective-permute-start | bytes 3145736 | tf_op jit(solution)/shard_map/ppermute | solution.py:161

commit v5 on v4

--- a/solution.py
+++ b/solution.py
@@ -97,10 +97,14 @@
         ).astype(jnp.float32))
     stream = jnp.concatenate(halves, 0)
     local_heads = w_qkv.shape[3] // HEAD_DIM
-    normed = layer_norm(stream, norm_gain[0], norm_bias[0]).astype(jnp.bfloat16)
-    projected = jnp.einsum(
-        "td,sde->ste", normed, w_qkv[0], preferred_element_type=jnp.float32
-    ).astype(jnp.bfloat16)
+    projected = jnp.concatenate([
+        jnp.einsum(
+            "td,sde->ste",
+            layer_norm(half, norm_gain[0], norm_bias[0]).astype(jnp.bfloat16),
+            w_qkv[0], preferred_element_type=jnp.float32,
+        ).astype(jnp.bfloat16)
+        for half in halves
+    ], 1)
     keys = projected[1].reshape(tokens, local_heads, HEAD_DIM)
     values = projected[2].reshape(tokens, local_heads, HEAD_DIM)
     inner_rows = w_decode.shape[1] // (PATCH * PATCH)
@@ -141,30 +145,36 @@
         ).astype(jnp.bfloat16)
     upper_part = from_behind(decoded_chunks[1], "tile", 1)
     lower_part = decoded_chunks[0]
-    shape = lower_part.shape
-    token_a = lax.broadcasted_iota(jnp.int32, shape, 0) // (side * side)
-    inner = lax.broadcasted_iota(jnp.int32, shape, 2) // PATCH
-    places = (token_a * PATCH + head_index * inner_rows + inner).astype(jnp.float32)
-    lower_profile = profile_of(places)
-    upper_profile = profile_of(places + HALF)
     later = (tile_index > 0).astype(jnp.float32)
-    numerator = (
-        lower_part.astype(jnp.float32) * lower_profile
-        + upper_part.astype(jnp.float32) * upper_profile
-    )
-    denominator = lower_profile + later * upper_profile
-    blended = (numerator / denominator).astype(jnp.bfloat16)
     half_side = side // 2
-    arranged = blended.reshape(half_side * side, WIN, cell_cols)
-    arranged = jnp.swapaxes(arranged, 1, 2).reshape(half_side, side, inner_rows, PATCH, WIN)
-    arranged = arranged.transpose(0, 2, 1, 3, 4)
-    other_rows = lax.ppermute(arranged, "head", [(0, 1), (1, 0)])
-    whole = jnp.where(
-        head_index == 0,
-        jnp.concatenate([arranged, other_rows], 1),
-        jnp.concatenate([other_rows, arranged], 1),
-    )
-    return whole.reshape(HALF, WIN, WIN)
+    pieces = []
+    piece_planes = half_side // 2
+    piece_tokens = piece_planes * side * side
+    for piece in range(half_side // piece_planes):
+        span = slice(piece * piece_tokens, (piece + 1) * piece_tokens)
+        lower_piece = lower_part[span]
+        shape = lower_piece.shape
+        token_a = lax.broadcasted_iota(jnp.int32, shape, 0) // (side * side) + piece * piece_planes
+        inner = lax.broadcasted_iota(jnp.int32, shape, 2) // PATCH
+        places = (token_a * PATCH + head_index * inner_rows + inner).astype(jnp.float32)
+        lower_profile = profile_of(places)
+        upper_profile = profile_of(places + HALF)
+        numerator = (
+            lower_piece.astype(jnp.float32) * lower_profile
+            + upper_part[span].astype(jnp.float32) * upper_profile
+        )
+        denominator = lower_profile + later * upper_profile
+        blended = (numerator / denominator).astype(jnp.bfloat16)
+        arranged = blended.reshape(piece_planes * side, WIN, cell_cols)
+        arranged = jnp.swapaxes(arranged, 1, 2).reshape(piece_planes, side, inner_rows, PATCH, WIN)
+        other_rows = lax.ppermute(arranged, "head", [(0, 1), (1, 0)])
+        whole = jnp.where(
+            head_index == 0,
+            jnp.concatenate([arranged, other_rows], 2),
+            jnp.concatenate([other_rows, arranged], 2),
+        )
+        pieces.append(whole.transpose(0, 2, 1, 3, 4).reshape(piece_planes * PATCH, WIN, WIN))
+    return jnp.concatenate(pieces, 0)
 
 
 def solution(mesh):

time: 174 us -> 174 us (level)
  the two profiles are of different devices: /device:TPU:31 before, /device:TPU:1 now
where the time goes in v5:
time: 174 us; the launch traced here: 173 us
  waiting for transfers between devices  59.2 us (34%)
  local copies, waits for them, and re-layouts  39.7 us (23%)
  matrix products  36.9 us (21%)
  other arithmetic  21.7 us (12%)
  starting transfers between devices  15.3 us (9%)
    ppermute x2, waiting for transfers between devices, body(): other_rows = lax.ppermute(arranged, 'head', [(0, 1), (1, 0)])  29.1 us
    ppermute x4, waiting for transfers between devices, partner_sum(): other = lax.ppermute(rounded, 'head', [(0, 1), (1, 0)])  20.6 us
    reshape x2, local copies, waits for them, and re-layouts, embed_planes(): voxels = jnp.swapaxes(grouped, 1, 2).reshape(rows, PATCH, PATCH * PATCH)  9.74 us
    ppermute x3, starting transfers between devices, from_behind(): return lax.ppermute(block, axis, route)  9.01 us
    dot_general x2, matrix products, body(): jnp.dot(hidden, w_down[0], preferred_element_type=jnp.float32)  8.52 us
    transpose x2, local copies, waits for them, and re-layouts, embed_planes(): voxels = jnp.swapaxes(grouped, 1, 2).reshape(rows, PATCH, PATCH * PATCH)  8.15 us
    dot_general x2, matrix products, embed_planes(): lax.dot_general(voxels, embed_by_depth, (((1, 2), (0, 1)), ((), ())), pre...  6.83 us
    unnamed x45, local copies, waits for them, and re-layouts  6.67 us
  transfers between devices with their start and end apart: 11, of which 8 were waited for; matrix products, arithmetic and copies ran while one was open for 29% of the time, Pallas kernels for 0%

profile of v5, /device:TPU:1, one launch (start us, length us, event | category | flops | bytes accessed | tf_op | source)
XLA Modules:
  0.0 173.4 jit_solution(2579652568259190446)
XLA Ops:
  0.9 3.4 %collective-permute-start.2 = (bf16[64,128]{1,0:T(8,128)(2,1)S(1)}, bf16[64,128]{1,0:T(8,128)(2,1)}, u32[]{:S(2)}, u32[]{:S(2)}) collective-permute-start(bf16[64,128]{1,0:T(8,128)(2,1)S(1)} %convert_element_type.141), channel_id=1, source_target_pairs={{2,0},{4,2},{6,4},{8,6},{10,8},{12,10},{14,12},{16,14},{18,16},{20... | collective-permute-start | bytes 49160 | tf_op jit(solution)/shard_map/ppermute | solution.py:19
  4.3 1.9 %collective-permute-start.1 = (bf16[64,128,128]{2,1,0:T(8,128)(2,1)}, bf16[64,128,128]{2,1,0:T(8,128)(2,1)}, u32[]{:S(2)}, u32[]{:S(2)}) collective-permute-start(bf16[64,128,128]{2,1,0:T(8,128)(2,1)} %param.12), channel_id=1, source_target_pairs={{2,0},{4,2},{6,4},{8,6},{10,8},{12,10},{14,12},{16,14},{18,16},{20... | collective-permute-start | bytes 6291464 | tf_op jit(solution)/shard_map/ppermute | solution.py:19
  6.3 3.4 %broadcast_multiply_fusion.1 = bf16[64,128,128]{2,1,0:T(8,128)(2,1)} fusion(bf16[64,128,128]{2,1,0:T(8,128)(2,1)} %param.12, bf16[64,128]{1,0:T(8,128)(2,1)S(1)} %convert_element_type.141), kind=kLoop, calls=%fused_computation.110 | loop fusion | flops 1048576 | bytes 4210688 | tf_op jit(solution)/shard_map/mul | solution.py:43
  9.8 3.5 %copy.39 = bf16[4,8,16,16,128]{4,3,2,1,0:T(8,128)(2,1)} copy(bf16[4,8,16,16,128]{4,3,1,2,0:T(8,128)(2,1)} %bitcast.159) | data formatting | bytes 4194304 | tf_op jit(solution)/shard_map/transpose | solution.py:44
  13.3 4.1 %copy.40 = bf16[32,128,256]{2,1,0:T(8,128)(2,1)} copy(bf16[32,128,256]{1,2,0:T(8,128)(2,1)} %bitcast.160) | data formatting | bytes 4194304 | tf_op jit(solution)/shard_map/transpose | solution.py:46
  17.4 4.9 %copy.41 = bf16[256,16,256]{0,1,2:T(8,128)(2,1)} copy(bf16[256,16,256]{2,1,0:T(8,128)(2,1)} %bitcast.161) | data formatting | bytes 4194304 | tf_op jit(solution)/shard_map/reshape | solution.py:46
  23.0 1.1 reshape.164
  24.1 1.0 convert_element_type.142
  25.3 3.0 %fusion.78 = bf16[256,384]{1,0:T(8,128)(2,1)S(1)} fusion(bf16[256,16,256]{0,1,2:T(8,128)(2,1)} %copy.41, bf16[16,256,384]{2,0,1:T(8,128)(2,1)S(1)} %bitcast.156, f32[512,384]{1,0:T(8,128)S(1)} %convert_element_type.142, f32[32,384]{1,0:T(8,128)S(1)} %fusion.194), kind=kOutput, calls=%fused_computation.75 | convolution fusion | flops 805601280 | bytes 5881856 | tf_op jit(solution)/shard_map/dot_general | solution.py:47
  28.4 1.8 %collective-permute-start = (bf16[256,384]{1,0:T(8,128)(2,1)S(1)}, bf16[256,384]{1,0:T(8,128)(2,1)S(1)}, u32[]{:S(2)}, u32[]{:S(2)}) collective-permute-start(bf16[256,384]{1,0:T(8,128)(2,1)S(1)} %fusion.78), channel_id=1, source_target_pairs={{0,1},{1,0},{2,3},{3,2},{4,5},{5,4},{6,7},{7,6},{8,9},{9,8},{10,11... | collective-permute-start | bytes 589832 | tf_op jit(solution)/shard_map/ppermute | solution.py:92
  32.5 4.6 %copy.51 = bf16[768,2048]{0,1:T(8,128)(2,1)} copy(bf16[768,2048]{1,0:T(8,128)(2,1)} %param.23) | data formatting | bytes 6291456 | tf_op args[11]
  37.1 1.5 reshape.169
  38.6 1.6 copy.70
  40.2 1.1 reshape.170
  41.3 1.7 fusion.195
  43.5 2.5 %broadcast_multiply_fusion = bf16[64,128,128]{2,1,0:T(8,128)(2,1)S(1)} fusion(bf16[64,128,128]{2,1,0:T(8,128)(2,1)} %collective-permute-done.1, bf16[64,128]{1,0:T(8,128)(2,1)} %collective-permute-done.2), kind=kLoop, calls=%fused_computation.109 | loop fusion | flops 1048576 | bytes 4210688 | tf_op jit(solution)/shard_map/mul | solution.py:43
  46.0 1.9 %copy.43 = bf16[4,8,16,16,128]{4,3,2,1,0:T(8,128)(2,1)} copy(bf16[4,8,16,16,128]{4,3,1,2,0:T(8,128)(2,1)S(1)} %bitcast.158) | data formatting | bytes 4194304 | tf_op jit(solution)/shard_map/transpose | solution.py:44
  47.9 4.1 %copy.44 = bf16[32,128,256]{2,1,0:T(8,128)(2,1)} copy(bf16[32,128,256]{1,2,0:T(8,128)(2,1)} %bitcast.162) | data formatting | bytes 4194304 | tf_op jit(solution)/shard_map/transpose | solution.py:46
  52.0 4.8 %copy.45 = bf16[256,16,256]{0,1,2:T(8,128)(2,1)} copy(bf16[256,16,256]{2,1,0:T(8,128)(2,1)} %bitcast.163) | data formatting | bytes 4194304 | tf_op jit(solution)/shard_map/reshape | solution.py:46
  56.8 3.8 %fusion.77 = bf16[256,384]{1,0:T(8,128)(2,1)} fusion(bf16[256,16,256]{0,1,2:T(8,128)(2,1)} %copy.45, bf16[16,256,384]{2,0,1:T(8,128)(2,1)S(1)} %bitcast.157, f32[512,384]{1,0:T(8,128)} %copy-done.5, f32[32,384]{1,0:T(8,128)} %fusion.195), kind=kOutput, calls=%fused_computation.74 | convolution fusion | flops 805601280 | bytes 5881856 | tf_op jit(solution)/shard_map/dot_general | solution.py:47
  61.6 5.3 %collective-permute-done.3 = bf16[256,384]{1,0:T(8,128)(2,1)S(1)} collective-permute-done((bf16[256,384]{1,0:T(8,128)(2,1)}, bf16[256,384]{1,0:T(8,128)(2,1)S(1)}, u32[]{:S(2)}, u32[]{:S(2)}) %collective-permute-start.3) | collective-permute-done | bytes 196640 | tf_op jit(solution)/shard_map/ppermute | solution.py:92
  66.9 1.2 convert_reduce_fusion
  68.1 1.3 fusion.116
  69.4 2.5 %fusion.64 = bf16[3,256,384]{2,1,0:T(8,128)(2,1)S(1)} fusion(bf16[1,3,768,384]{3,2,1,0:T(8,128)(2,1)} %param.19, f32[256]{0:T(256)S(1)} %add_rsqrt_fusion.4, f32[256]{0:T(256)S(1)} %broadcast_multiply_fusion.6, f32[768]{0:T(1024)S(1)} %copy-done.18, f32[768]{0:T(1024)S(1)} %copy-done.17, bf16[256,384]{1,0:T(8,128)(2,1)S(1)} %collective-permute-done.3, ...), kind=kOutput, calls=%fused_computation.57 | convolution fusion | flops 456228864 | bytes 2760705 | tf_op jit(solution)/shard_map/td,sde->ste/dot_general | solution.py:101
  72.4 2.8 %fusion.193 = (f32[6,256]{1,0:T(8,128)S(1)}, f32[6,256,512]{2,1,0:T(8,128)}) fusion(bf16[256,6,64]{0,2,1:T(8,128)(2,1)S(1)} %bitcast.182, bf16[512,6,64]{0,2,1:T(8,128)(2,1)S(1)} %bitcast.178), kind=kOutput, calls=%fused_computation.221 | convolution fusion | flops 103023104 | bytes 3741696 | tf_op jit(solution)/shard_map/sub | solution.py:124
  75.2 2.6 %fusion.80 = bf16[6,64,256]{2,1,0:T(8,128)(2,1)S(1)} fusion(bf16[512,6,64]{0,2,1:T(8,128)(2,1)S(1)} %bitcast.176, f32[6,256,512]{2,1,0:T(8,128)} %get-tuple-element.26, f32[6,256]{1,0:T(8,128)S(1)} %get-tuple-element.25), kind=kOutput, calls=%fused_computation.77 | convolution fusion | flops 102334464 | bytes 3741696 | tf_op jit(solution)/shard_map/hts,shd->thd/dot_general | solution.py:125
  78.6 2.8 %fusion.192 = (f32[6,256]{1,0:T(8,128)S(1)}, f32[6,256,512]{2,1,0:T(8,128)}) fusion(bf16[256,6,64]{0,2,1:T(8,128)(2,1)S(1)} %bitcast.183, bf16[512,6,64]{0,2,1:T(8,128)(2,1)S(1)} %bitcast.179), kind=kOutput, calls=%fused_computation.220 | convolution fusion | flops 103023104 | bytes 3741696 | tf_op jit(solution)/shard_map/sub | solution.py:124
  81.4 2.6 %fusion.79 = bf16[6,64,256]{2,1,0:T(8,128)(2,1)S(1)} fusion(bf16[512,6,64]{0,2,1:T(8,128)(2,1)S(1)} %bitcast.177, f32[6,256,512]{2,1,0:T(8,128)} %get-tuple-element.24, f32[6,256]{1,0:T(8,128)S(1)} %get-tuple-element.23), kind=kOutput, calls=%fused_computation.76 | convolution fusion | flops 102334464 | bytes 3741696 | tf_op jit(solution)/shard_map/hts,shd->thd/dot_general | solution.py:125
  84.3 1.5 collective-permute-start.5
  85.9 3.0 %collective-permute-done.4 = bf16[256,768]{1,0:T(8,128)(2,1)S(1)} collective-permute-done((bf16[256,768]{1,0:T(8,128)(2,1)S(1)}, bf16[256,768]{1,0:T(8,128)(2,1)S(1)}, u32[]{:S(2)}, u32[]{:S(2)}) %collective-permute-start.4) | collective-permute-done | bytes 393248 | tf_op jit(solution)/shard_map/ppermute | solution.py:24
  89.5 7.8 %collective-permute-done.5 = bf16[256,768]{1,0:T(8,128)(2,1)S(1)} collective-permute-done((bf16[256,768]{1,0:T(8,128)(2,1)S(1)}, bf16[256,768]{1,0:T(8,128)(2,1)S(1)}, u32[]{:S(2)}, u32[]{:S(2)}) %collective-permute-start.5) | collective-permute-done | bytes 393248 | tf_op jit(solution)/shard_map/ppermute | solution.py:24
  97.3 1.3 fusion.189
  98.6 1.4 multiply_reduce_fusion.5
  100.0 4.4 %fusion.70 = bf16[256,768]{1,0:T(8,128)(2,1)S(1)} fusion(bf16[1,1536,768]{2,1,0:T(8,128)(2,1)} %param.22, bf16[1,768,1536]{2,1,0:T(8,128)(2,1)} %param.21, f32[768]{0:T(1024)S(1)} %copy-done.16, f32[768]{0:T(1024)S(1)} %copy-done.15, f32[256]{0:T(256)S(1)} %add_rsqrt_fusion.3, f32[256]{0:T(256)S(1)} %broadcast_multiply_fusion.5, ...), kind=kOutput, calls=%fused_computation.59 | convolution fusion | flops 1215430656 | bytes 6299649 | tf_op jit(solution)/shard_map/dot_general | solution.py:135
  105.0 4.1 %fusion.12 = bf16[256,768]{1,0:T(8,128)(2,1)S(1)} fusion(bf16[1,1536,768]{2,1,0:T(8,128)(2,1)} %param.22, bf16[1,768,1536]{2,1,0:T(8,128)(2,1)} %param.21, f32[256]{0:T(256)S(1)} %add_rsqrt_fusion.1, f32[256]{0:T(256)S(1)} %broadcast_multiply_fusion.3, f32[768]{0:T(1024)S(1)} %copy-done.16, f32[768]{0:T(1024)S(1)} %copy-done.15, ...), kind=kOutput, calls=%fused_computation.16 | convolution fusion | flops 1215234048 | bytes 6299649 | tf_op jit(solution)/shard_map/dot_general | solution.py:135
  109.2 5.3 %collective-permute-done.6 = bf16[256,768]{1,0:T(8,128)(2,1)} collective-permute-done((bf16[256,768]{1,0:T(8,128)(2,1)S(1)}, bf16[256,768]{1,0:T(8,128)(2,1)}, u32[]{:S(2)}, u32[]{:S(2)}) %collective-permute-start.6) | collective-permute-done | bytes 393248 | tf_op jit(solution)/shard_map/ppermute | solution.py:24
  114.4 1.6 fusion.191
  116.3 2.4 %fusion.52 = bf16[256,16,128]{2,0,1:T(8,128)(2,1)S(1)} fusion(bf16[16,128,768]{2,0,1:T(8,128)(2,1)S(1)} %bitcast.166, f32[256,768]{1,0:T(8,128)S(1)} %get-tuple-element.18, f32[768]{0:T(1024)S(1)} %copy-done.14, f32[768]{0:T(1024)S(1)} %copy-done.13, f32[256]{0:T(256)S(1)} %add_rsqrt_fusion.2, f32[256]{0:T(256)S(1)} %broadcast_multiply_fusion.4), kind=kOutput, calls=%fused_computation.53 | convolution fusion | flops 806813696 | bytes 4988928 | tf_op jit(solution)/shard_map/dot_general | solution.py:142
  119.4 3.7 %collective-permute-start.8 = (bf16[256,16,128]{2,0,1:T(8,128)(2,1)S(1)}, bf16[256,16,128]{2,0,1:T(8,128)(2,1)S(1)}, u32[]{:S(2)}, u32[]{:S(2)}) collective-permute-start(bf16[256,16,128]{2,0,1:T(8,128)(2,1)S(1)} %fusion.52), channel_id=1, source_target_pairs={{0,2},{2,4},{4,6},{6,8},{8,10},{10,12},{12,14},{14,16},{16,18},{18... | collective-permute-start | bytes 3145736 | tf_op jit(solution)/shard_map/ppermute | solution.py:19
  123.1 4.5 %collective-permute-done.7 = bf16[256,768]{1,0:T(8,128)(2,1)S(1)} collective-permute-done((bf16[256,768]{1,0:T(8,128)(2,1)S(1)}, bf16[256,768]{1,0:T(8,128)(2,1)S(1)}, u32[]{:S(2)}, u32[]{:S(2)}) %collective-permute-start.7) | collective-permute-done | bytes 393248 | tf_op jit(solution)/shard_map/ppermute | solution.py:24
  128.2 2.4 %fusion.55 = bf16[256,16,128]{2,0,1:T(8,128)(2,1)S(1)} fusion(bf16[16,128,768]{2,0,1:T(8,128)(2,1)S(1)} %bitcast.167, f32[256,768]{1,0:T(8,128)S(1)} %get-tuple-element.16, f32[256]{0:T(256)S(1)} %add_rsqrt_fusion, f32[256]{0:T(256)S(1)} %broadcast_multiply_fusion.2, f32[768]{0:T(1024)S(1)} %copy-done.14, f32[768]{0:T(1024)S(1)} %copy-done.13), kind=kOutput, calls=%fused_computation.54 | convolution fusion | flops 806813696 | bytes 4988928 | tf_op jit(solution)/shard_map/dot_general | solution.py:142
  130.6 4.2 %collective-permute-done.8 = bf16[256,16,128]{2,0,1:T(8,128)(2,1)S(1)} collective-permute-done((bf16[256,16,128]{2,0,1:T(8,128)(2,1)S(1)}, bf16[256,16,128]{2,0,1:T(8,128)(2,1)S(1)}, u32[]{:S(2)}, u32[]{:S(2)}) %collective-permute-start.8) | collective-permute-done | bytes 1048608 | tf_op jit(solution)/shard_map/ppermute | solution.py:19
  137.4 1.2 collective-permute-start.9
  138.6 18.9 %collective-permute-done.10 = bf16[2,8,8,16,128]{4,3,2,1,0:T(8,128)(2,1)S(1)} collective-permute-done((bf16[2,8,8,16,128]{4,3,2,1,0:T(8,128)(2,1)S(1)}, bf16[2,8,8,16,128]{4,3,2,1,0:T(8,128)(2,1)S(1)}, u32[]{:S(2)}, u32[]{:S(2)}) %collective-permute-start.10) | collective-permute-done | bytes 524320 | tf_op jit(solution)/shard_map/ppermute | solution.py:170
  158.3 10.3 %collective-permute-done.9 = bf16[2,8,8,16,128]{4,3,2,1,0:T(8,128)(2,1)S(1)} collective-permute-done((bf16[2,8,8,16,128]{4,3,2,1,0:T(8,128)(2,1)S(1)}, bf16[2,8,8,16,128]{4,3,2,1,0:T(8,128)(2,1)S(1)}, u32[]{:S(2)}, u32[]{:S(2)}) %collective-permute-start.9) | collective-permute-done | bytes 524320 | tf_op jit(solution)/shard_map/ppermute | solution.py:170
  168.6 1.6 fusion.106
  170.7 1.5 pad_maximum_fusion
  172.2 1.1 copy-done.1
  (100 shorter events, 13.9 us)
Async XLA Ops:
  0.0 25.3 %copy-start = (bf16[4096,384]{1,0:T(8,128)(2,1)S(1)}, bf16[4096,384]{1,0:T(8,128)(2,1)}, u32[]{:S(2)}) copy-start(bf16[4096,384]{1,0:T(8,128)(2,1)} %param.14) | copy-start | bytes 9437188
  0.9 36.2 %collective-permute-start.2 = (bf16[64,128]{1,0:T(8,128)(2,1)S(1)}, bf16[64,128]{1,0:T(8,128)(2,1)}, u32[]{:S(2)}, u32[]{:S(2)}) collective-permute-start(bf16[64,128]{1,0:T(8,128)(2,1)S(1)} %convert_element_type.141), channel_id=1, source_target_pairs={{2,0},{4,2},{6,4},{8,6},{10,8},{12,10},{14,12},{16,14},{18,16},{20... | collective-permute-start | bytes 49160 | tf_op jit(solution)/shard_map/ppermute | solution.py:19
  4.3 39.2 %collective-permute-start.1 = (bf16[64,128,128]{2,1,0:T(8,128)(2,1)}, bf16[64,128,128]{2,1,0:T(8,128)(2,1)}, u32[]{:S(2)}, u32[]{:S(2)}) collective-permute-start(bf16[64,128,128]{2,1,0:T(8,128)(2,1)} %param.12), channel_id=1, source_target_pairs={{2,0},{4,2},{6,4},{8,6},{10,8},{12,10},{14,12},{16,14},{18,16},{20... | collective-permute-start | bytes 6291464 | tf_op jit(solution)/shard_map/ppermute | solution.py:19
  17.4 7.7 %copy-start.6 = (bf16[256,384]{1,0:T(8,128)(2,1)S(1)}, bf16[256,384]{1,0:T(8,128)(2,1)}, u32[]{:S(2)}) copy-start(bf16[256,384]{1,0:T(8,128)(2,1)} %param.15) | copy-start | bytes 589828
  25.1 3.2 %copy-start.5 = (f32[512,384]{1,0:T(8,128)}, f32[512,384]{1,0:T(8,128)S(1)}, u32[]{:S(2)}) copy-start(f32[512,384]{1,0:T(8,128)S(1)} %convert_element_type.142) | copy-start | bytes 2359300
  25.3 5.4 %copy-start.11 = (f32[3,768]{1,0:T(4,128)S(1)}, f32[3,768]{1,0:T(4,128)}, u32[]{:S(2)}) copy-start(f32[3,768]{1,0:T(4,128)} %param.17) | copy-start | bytes 27652
  25.3 6.0 %copy-start.12 = (f32[3,768]{1,0:T(4,128)S(1)}, f32[3,768]{1,0:T(4,128)}, u32[]{:S(2)}) copy-start(f32[3,768]{1,0:T(4,128)} %param.18) | copy-start | bytes 27652
  28.4 14.6 %collective-permute-start = (bf16[256,384]{1,0:T(8,128)(2,1)S(1)}, bf16[256,384]{1,0:T(8,128)(2,1)S(1)}, u32[]{:S(2)}, u32[]{:S(2)}) collective-permute-start(bf16[256,384]{1,0:T(8,128)(2,1)S(1)} %fusion.78), channel_id=1, source_target_pairs={{0,1},{1,0},{2,3},{3,2},{4,5},{5,4},{6,7},{7,6},{8,9},{9,8},{10,11... | collective-permute-start | bytes 589832 | tf_op jit(solution)/shard_map/ppermute | solution.py:92
  56.8 3.8 %copy-start.17 = (f32[768]{0:T(1024)S(1)}, f32[768]{0:T(1024)}, u32[]{:S(2)}) copy-start(f32[768]{0:T(1024)} %get-tuple-element.10) | copy-start | bytes 9220
  56.8 3.8 %copy-start.18 = (f32[768]{0:T(1024)S(1)}, f32[768]{0:T(1024)}, u32[]{:S(2)}) copy-start(f32[768]{0:T(1024)} %get-tuple-element.13) | copy-start | bytes 9220
  56.8 3.8 %copy-start.21 = (bf16[1,3,768,384]{3,2,1,0:T(8,128)(2,1)S(1)}, bf16[1,3,768,384]{3,2,1,0:T(8,128)(2,1)}, u32[]{:S(2)}) copy-start(bf16[1,3,768,384]{3,2,1,0:T(8,128)(2,1)} %param.19) | copy-start | bytes 5308420
  60.6 6.3 %collective-permute-start.3 = (bf16[256,384]{1,0:T(8,128)(2,1)}, bf16[256,384]{1,0:T(8,128)(2,1)S(1)}, u32[]{:S(2)}, u32[]{:S(2)}) collective-permute-start(bf16[256,384]{1,0:T(8,128)(2,1)} %fusion.77), channel_id=1, source_target_pairs={{0,1},{1,0},{2,3},{3,2},{4,5},{5,4},{6,7},{7,6},{8,9},{9,8},{10,11... | collective-permute-start | bytes 589832 | tf_op jit(solution)/shard_map/ppermute | solution.py:92
  71.9 3.3 %copy-start.4 = (bf16[3,256,384]{2,1,0:T(8,128)(2,1)}, bf16[3,256,384]{2,1,0:T(8,128)(2,1)S(1)}, u32[]{:S(2)}) copy-start(bf16[3,256,384]{2,1,0:T(8,128)(2,1)S(1)} %fusion.64) | copy-start | bytes 1769476
  72.2 3.0 %copy-start.8 = (bf16[1,512,384]{1,2,0:T(8,128)(2,1)}, bf16[1,512,384]{1,2,0:T(8,128)(2,1)S(1)}, u32[]{:S(2)}) copy-start(bf16[1,512,384]{1,2,0:T(8,128)(2,1)S(1)} %copy.49) | copy-start | bytes 1179652
  75.2 2.7 %copy-start.3 = (bf16[1,384,768]{2,1,0:T(8,128)(2,1)S(1)}, bf16[1,384,768]{2,1,0:T(8,128)(2,1)}, u32[]{:S(2)}) copy-start(bf16[1,384,768]{2,1,0:T(8,128)(2,1)} %param.20) | copy-start | bytes 1769476
  75.2 3.2 %slice-start = ((bf16[3,256,384]{2,1,0:T(8,128)(2,1)}), bf16[1,256,384]{2,1,0:T(8,128)(2,1)S(1)}, s32[]{:S(2)}) async-start(bf16[3,256,384]{2,1,0:T(8,128)(2,1)} %copy-done.4), calls=%async_computation | async-start | bytes 393216 | tf_op jit(solution)/shard_map/slice | solution.py:120
  75.2 3.3 %copy-start.9 = (bf16[1,512,384]{1,2,0:T(8,128)(2,1)S(1)}, bf16[1,512,384]{1,2,0:T(8,128)(2,1)}, u32[]{:S(2)}) copy-start(bf16[1,512,384]{1,2,0:T(8,128)(2,1)} %copy-done.8) | copy-start | bytes 1179652
  78.3 10.6 %collective-permute-start.4 = (bf16[256,768]{1,0:T(8,128)(2,1)S(1)}, bf16[256,768]{1,0:T(8,128)(2,1)S(1)}, u32[]{:S(2)}, u32[]{:S(2)}) collective-permute-start(bf16[256,768]{1,0:T(8,128)(2,1)S(1)} %convolution_convert_fusion.1), channel_id=1, source_target_pairs={{0,1},{1,0},{2,3},{3,2},{4,5},{5,4},{6,7},{7,6},{8,9},{9,8},{10,11... | collective-permute-start | bytes 1179656 | tf_op jit(solution)/shard_map/ppermute | solution.py:24
  84.3 15.7 %copy-start.15 = (f32[768]{0:T(1024)S(1)}, f32[768]{0:T(1024)}, u32[]{:S(2)}) copy-start(f32[768]{0:T(1024)} %get-tuple-element.11) | copy-start | bytes 9220
  84.3 15.7 %copy-start.16 = (f32[768]{0:T(1024)S(1)}, f32[768]{0:T(1024)}, u32[]{:S(2)}) copy-start(f32[768]{0:T(1024)} %get-tuple-element.14) | copy-start | bytes 9220
  84.3 13.0 %collective-permute-start.5 = (bf16[256,768]{1,0:T(8,128)(2,1)S(1)}, bf16[256,768]{1,0:T(8,128)(2,1)S(1)}, u32[]{:S(2)}, u32[]{:S(2)}) collective-permute-start(bf16[256,768]{1,0:T(8,128)(2,1)S(1)} %convolution_convert_fusion), channel_id=1, source_target_pairs={{0,1},{1,0},{2,3},{3,2},{4,5},{5,4},{6,7},{7,6},{8,9},{9,8},{10,11... | collective-permute-start | bytes 1179656 | tf_op jit(solution)/shard_map/ppermute | solution.py:24
  104.4 4.7 %copy-start.10 = (bf16[256,768]{1,0:T(8,128)(2,1)}, bf16[256,768]{1,0:T(8,128)(2,1)S(1)}, u32[]{:S(2)}) copy-start(bf16[256,768]{1,0:T(8,128)(2,1)S(1)} %fusion.70) | copy-start | bytes 1179652
  104.4 10.0 %collective-permute-start.6 = (bf16[256,768]{1,0:T(8,128)(2,1)S(1)}, bf16[256,768]{1,0:T(8,128)(2,1)}, u32[]{:S(2)}, u32[]{:S(2)}) collective-permute-start(bf16[256,768]{1,0:T(8,128)(2,1)S(1)} %fusion.70), channel_id=1, source_target_pairs={{0,1},{1,0},{2,3},{3,2},{4,5},{5,4},{6,7},{7,6},{8,9},{9,8},{10,11... | collective-permute-start | bytes 1179656 | tf_op jit(solution)/shard_map/ppermute | solution.py:24
  109.1 7.1 %copy-start.2 = (bf16[768,2048]{0,1:T(8,128)(2,1)S(1)}, bf16[768,2048]{0,1:T(8,128)(2,1)}, u32[]{:S(2)}) copy-start(bf16[768,2048]{0,1:T(8,128)(2,1)} %copy.51) | copy-start | bytes 9437188
  109.1 7.1 %copy-start.13 = (f32[768]{0:T(1024)S(1)}, f32[768]{0:T(1024)}, u32[]{:S(2)}) copy-start(f32[768]{0:T(1024)} %get-tuple-element.9) | copy-start | bytes 9220
  109.1 7.1 %copy-start.14 = (f32[768]{0:T(1024)S(1)}, f32[768]{0:T(1024)}, u32[]{:S(2)}) copy-start(f32[768]{0:T(1024)} %get-tuple-element.12) | copy-start | bytes 9220
  118.7 8.9 %collective-permute-start.7 = (bf16[256,768]{1,0:T(8,128)(2,1)S(1)}, bf16[256,768]{1,0:T(8,128)(2,1)S(1)}, u32[]{:S(2)}, u32[]{:S(2)}) collective-permute-start(bf16[256,768]{1,0:T(8,128)(2,1)S(1)} %fusion.12), channel_id=1, source_target_pairs={{0,1},{1,0},{2,3},{3,2},{4,5},{5,4},{6,7},{7,6},{8,9},{9,8},{10,11... | collective-permute-start | bytes 1179656 | tf_op jit(solution)/shard_map/ppermute | solution.py:24
  119.4 15.4 %collective-permute-start.8 = (bf16[256,16,128]{2,0,1:T(8,128)(2,1)S(1)}, bf16[256,16,128]{2,0,1:T(8,128)(2,1)S(1)}, u32[]{:S(2)}, u32[]{:S(2)}) collective-permute-start(bf16[256,16,128]{2,0,1:T(8,128)(2,1)S(1)} %fusion.52), channel_id=1, source_target_pairs={{0,2},{2,4},{4,6},{6,8},{8,10},{10,12},{12,14},{14,16},{16,18},{18... | collective-permute-start | bytes 3145736 | tf_op jit(solution)/shard_map/ppermute | solution.py:19
  128.2 6.6 %copy-start.19 = (s32[128]{0:T(128)S(1)}, s32[128]{0:T(128)}, u32[]{:S(2)}) copy-start(s32[128]{0:T(128)} %broadcast_add_fusion) | copy-start | bytes 1540
  128.2 6.6 %copy-start.20 = (s32[128]{0:T(128)S(1)}, s32[128]{0:T(128)}, u32[]{:S(2)}) copy-start(s32[128]{0:T(128)} %broadcast_add_fusion.1) | copy-start | bytes 1540
  136.4 21.1 %collective-permute-start.10 = (bf16[2,8,8,16,128]{4,3,2,1,0:T(8,128)(2,1)S(1)}, bf16[2,8,8,16,128]{4,3,2,1,0:T(8,128)(2,1)S(1)}, u32[]{:S(2)}, u32[]{:S(2)}) collective-permute-start(bf16[2,8,8,16,128]{4,3,2,1,0:T(8,128)(2,1)S(1)} %bitcast.168), channel_id=1, source_target_pairs={{0,1},{1,0},{2,3},{3,2},{4,5},{5,4},{6,7},{7,6},{8,9},{9,8},{10,11... | collective-permute-start | bytes 1572872 | tf_op jit(solution)/shard_map/ppermute | solution.py:170
  137.4 31.1 %collective-permute-start.9 = (bf16[2,8,8,16,128]{4,3,2,1,0:T(8,128)(2,1)S(1)}, bf16[2,8,8,16,128]{4,3,2,1,0:T(8,128)(2,1)S(1)}, u32[]{:S(2)}, u32[]{:S(2)}) collective-permute-start(bf16[2,8,8,16,128]{4,3,2,1,0:T(8,128)(2,1)S(1)} %bitcast.170), channel_id=1, source_target_pairs={{0,1},{1,0},{2,3},{3,2},{4,5},{5,4},{6,7},{7,6},{8,9},{9,8},{10,11... | collective-permute-start | bytes 1572872 | tf_op jit(solution)/shard_map/ppermute | solution.py:170
  157.5 0.8 copy-start.7
  170.7 2.7 %copy-start.1 = (bf16[4096,384]{1,0:T(8,128)(2,1)S(1)}, bf16[4096,384]{1,0:T(8,128)(2,1)}, u32[]{:S(2)}) copy-start(bf16[4096,384]{1,0:T(8,128)(2,1)} %param.14) | copy-start | bytes 9437188

commit v6 on v4

--- a/solution.py
+++ b/solution.py
@@ -81,6 +81,7 @@
     head_index = lax.axis_index("head")
     own_live = trace_mask.astype(jnp.bfloat16)
     next_traces, next_live = from_behind((traces, own_live), "tile", -1)
+    other_w_out = lax.ppermute(w_out[0], "head", [(0, 1), (1, 0)])
     local_width = embed_voxel.shape[1]
     embed_by_depth = embed_voxel.reshape(PATCH * PATCH, PATCH, local_width).transpose(1, 0, 2)
     position = position.astype(jnp.float32)
@@ -122,8 +123,13 @@
             "hts,shd->thd", weights, values, preferred_element_type=jnp.float32
         ).astype(jnp.bfloat16)
         attended = attended.reshape(half_tokens, local_heads * HEAD_DIM)
-        partial_attention = jnp.dot(attended, w_out[0], preferred_element_type=jnp.float32)
-        part = stream[span] + partner_sum(partial_attention)
+        other_attended = lax.ppermute(attended, "head", [(0, 1), (1, 0)])
+        own_term = jnp.dot(attended, w_out[0], preferred_element_type=jnp.float32)
+        other_term = jnp.dot(other_attended, other_w_out, preferred_element_type=jnp.float32)
+        part = stream[span] + (
+            own_term.astype(jnp.bfloat16).astype(jnp.float32)
+            + other_term.astype(jnp.bfloat16).astype(jnp.float32)
+        )
         normed = layer_norm(part, norm_gain[1], norm_bias[1]).astype(jnp.bfloat16)
         hidden = jax.nn.gelu(
             jnp.dot(normed, w_up[0], preferred_element_type=jnp.float32), approximate=True

time: 174 us -> 155 us (0.89)
  other arithmetic: 20.2 us -> 13.1 us
  local copies, waits for them, and re-layouts: 42.3 us -> 35.2 us
  matrix products: 43 us -> 40.5 us
  starting transfers between devices: 21.8 us -> 19.9 us
    ppermute x4 -> x2, waiting for transfers between devices: 11 us -> 4.89 us  [partner_sum(): other = lax.ppermute(rounded, 'head', [(0, 1), (1, 0)])]
    dot_general x2 -> x4, matrix products: 0.78 us -> 6.27 us  [the longest x2 3.37 us: body(): jnp.dot(other_attended, other_w_out, preferred_element_type=jnp.float32)]
    ppermute x3, waiting for transfers between devices: 8.48 us -> 13.3 us  [from_behind(): return lax.ppermute(block, axis, route)]
    reduce_sum x5 -> x3, other arithmetic: 4.89 us -> 0.57 us  [layer_norm(): average = jnp.mean(values, axis=-1, keepdims=True)]
    sub x2, matrix products: 9 us -> 5.59 us  [body(): weights = jax.nn.softmax(scores, axis=-1).astype(jnp.bfloat16)]
    ppermute x4 -> x2, starting transfers between devices: 4.68 us -> 1.43 us  [partner_sum(): other = lax.ppermute(rounded, 'head', [(0, 1), (1, 0)])]
    dot_general x2, matrix products: 10.5 us -> 7.35 us  [body(): lax.dot_general(latent, decode_by_depth, (((1,), (2,)), ((), ())), prefer...]
    reduce_sum x5, other arithmetic: 3.39 us -> 1.29 us  [layer_norm(): variance = jnp.mean(centered * centered, axis=-1, keepdims=True)]
  transfers between devices with their start and end apart: 10 -> 11, of which waited for: 6 -> 6; matrix products, arithmetic and copies ran while one was open for 38% -> 44% of each run, Pallas kernels for 0% -> 0%
where the time goes in v6:
time: 155 us; the launch traced here: 154 us
  waiting for transfers between devices  45.1 us (29%)
  matrix products  40.5 us (26%)
  local copies, waits for them, and re-layouts  35.2 us (23%)
  starting transfers between devices  19.9 us (13%)
  other arithmetic  13.1 us (8%)
    ppermute x1, waiting for transfers between devices, body(): other_rows = lax.ppermute(arranged, 'head', [(0, 1), (1, 0)])  22.8 us
    ppermute x3, waiting for transfers between devices, from_behind(): return lax.ppermute(block, axis, route)  13.3 us
    ppermute x3, starting transfers between devices, from_behind(): return lax.ppermute(block, axis, route)  13 us
    reshape x2, local copies, waits for them, and re-layouts, embed_planes(): voxels = jnp.swapaxes(grouped, 1, 2).reshape(rows, PATCH, PATCH * PATCH)  9.68 us
    transpose x2, local copies, waits for them, and re-layouts, embed_planes(): voxels = jnp.swapaxes(grouped, 1, 2).reshape(rows, PATCH, PATCH * PATCH)  8.19 us
    dot_general x2, matrix products, body(): jnp.dot(hidden, w_down[0], preferred_element_type=jnp.float32)  8.05 us
    dot_general x2, matrix products, body(): lax.dot_general(latent, decode_by_depth, (((1,), (2,)), ((), ())), prefer...  7.35 us
    dot_general x2, matrix products, embed_planes(): lax.dot_general(voxels, embed_by_depth, (((1, 2), (0, 1)), ((), ())), pre...  6.56 us
  transfers between devices with their start and end apart: 11, of which 6 were waited for; matrix products, arithmetic and copies ran while one was open for 44% of the time, Pallas kernels for 0%

profile of v6, /device:TPU:31, one launch (start us, length us, event | category | flops | bytes accessed | tf_op | source)
XLA Modules:
  0.0 154.2 jit_solution(14221078746954664872)
XLA Ops:
  0.0 0.9 convert_element_type.126
  0.9 2.7 %collective-permute-start.2 = (bf16[64,128]{1,0:T(8,128)(2,1)S(1)}, bf16[64,128]{1,0:T(8,128)(2,1)S(1)}, u32[]{:S(2)}, u32[]{:S(2)}) collective-permute-start(bf16[64,128]{1,0:T(8,128)(2,1)S(1)} %convert_element_type.126), channel_id=1, source_target_pairs={{2,0},{4,2},{6,4},{8,6},{10,8},{12,10},{14,12},{16,14},{18,16},{20... | collective-permute-start | bytes 49160 | tf_op jit(solution)/shard_map/ppermute | solution.py:19
  3.6 2.2 %collective-permute-start.1 = (bf16[64,128,128]{2,1,0:T(8,128)(2,1)}, bf16[64,128,128]{2,1,0:T(8,128)(2,1)}, u32[]{:S(2)}, u32[]{:S(2)}) collective-permute-start(bf16[64,128,128]{2,1,0:T(8,128)(2,1)} %param.12), channel_id=1, source_target_pairs={{2,0},{4,2},{6,4},{8,6},{10,8},{12,10},{14,12},{16,14},{18,16},{20... | collective-permute-start | bytes 6291464 | tf_op jit(solution)/shard_map/ppermute | solution.py:19
  6.0 2.0 %convert_element_type.127 = f32[512,384]{1,0:T(8,128)} convert(bf16[512,384]{1,0:T(8,128)(2,1)} %param.16) | non-fusion elementwise | flops 196608 | bytes 1179648 | tf_op jit(solution)/shard_map/convert_element_type | solution.py:87
  7.9 2.5 %broadcast_multiply_fusion.1 = bf16[64,128,128]{2,1,0:T(8,128)(2,1)S(1)} fusion(bf16[64,128,128]{2,1,0:T(8,128)(2,1)} %param.12, bf16[64,128]{1,0:T(8,128)(2,1)S(1)} %convert_element_type.126), kind=kLoop, calls=%fused_computation.79 | loop fusion | flops 1048576 | bytes 4210688 | tf_op jit(solution)/shard_map/mul | solution.py:43
  10.4 1.9 %copy.29 = bf16[4,8,16,16,128]{4,3,2,1,0:T(8,128)(2,1)} copy(bf16[4,8,16,16,128]{4,3,1,2,0:T(8,128)(2,1)S(1)} %bitcast.149) | data formatting | bytes 4194304 | tf_op jit(solution)/shard_map/transpose | solution.py:44
  12.3 4.1 %copy.30 = bf16[32,128,256]{2,1,0:T(8,128)(2,1)} copy(bf16[32,128,256]{1,2,0:T(8,128)(2,1)} %bitcast.145) | data formatting | bytes 4194304 | tf_op jit(solution)/shard_map/transpose | solution.py:46
  16.4 4.9 %copy.31 = bf16[256,16,256]{0,1,2:T(8,128)(2,1)} copy(bf16[256,16,256]{2,1,0:T(8,128)(2,1)} %bitcast.146) | data formatting | bytes 4194304 | tf_op jit(solution)/shard_map/reshape | solution.py:46
  21.9 1.1 reshape.145
  23.1 3.6 %fusion.78 = bf16[256,384]{1,0:T(8,128)(2,1)} fusion(bf16[256,16,256]{0,1,2:T(8,128)(2,1)} %copy.31, bf16[16,256,384]{2,0,1:T(8,128)(2,1)S(1)} %bitcast.142, f32[512,384]{1,0:T(8,128)} %convert_element_type.127, f32[32,384]{1,0:T(8,128)S(1)} %fusion.157), kind=kOutput, calls=%fused_computation.75 | convolution fusion | flops 805601280 | bytes 5881856 | tf_op jit(solution)/shard_map/dot_general | solution.py:47
  26.7 1.6 %collective-permute-start = (bf16[256,384]{1,0:T(8,128)(2,1)}, bf16[256,384]{1,0:T(8,128)(2,1)}, u32[]{:S(2)}, u32[]{:S(2)}) collective-permute-start(bf16[256,384]{1,0:T(8,128)(2,1)} %fusion.78), channel_id=1, source_target_pairs={{0,1},{1,0},{2,3},{3,2},{4,5},{5,4},{6,7},{7,6},{8,9},{9,8},{10,11... | collective-permute-start | bytes 589832 | tf_op jit(solution)/shard_map/ppermute | solution.py:93
  28.4 4.6 %copy.38 = bf16[768,2048]{0,1:T(8,128)(2,1)} copy(bf16[768,2048]{1,0:T(8,128)(2,1)} %param.23) | data formatting | bytes 6291456 | tf_op args[11]
  33.0 0.8 reshape.150
  33.8 0.9 copy.57
  35.1 2.1 %collective-permute-done.1 = bf16[64,128,128]{2,1,0:T(8,128)(2,1)} collective-permute-done((bf16[64,128,128]{2,1,0:T(8,128)(2,1)}, bf16[64,128,128]{2,1,0:T(8,128)(2,1)}, u32[]{:S(2)}, u32[]{:S(2)}) %collective-permute-start.1) | collective-permute-done | bytes 2097184 | tf_op jit(solution)/shard_map/ppermute | solution.py:19
  37.1 2.5 %broadcast_multiply_fusion = bf16[64,128,128]{2,1,0:T(8,128)(2,1)S(1)} fusion(bf16[64,128,128]{2,1,0:T(8,128)(2,1)} %collective-permute-done.1, bf16[64,128]{1,0:T(8,128)(2,1)S(1)} %collective-permute-done.2), kind=kLoop, calls=%fused_computation.78 | loop fusion | flops 1048576 | bytes 4210688 | tf_op jit(solution)/shard_map/mul | solution.py:43
  39.6 1.9 %copy.33 = bf16[4,8,16,16,128]{4,3,2,1,0:T(8,128)(2,1)} copy(bf16[4,8,16,16,128]{4,3,1,2,0:T(8,128)(2,1)S(1)} %bitcast.144) | data formatting | bytes 4194304 | tf_op jit(solution)/shard_map/transpose | solution.py:44
  41.5 4.1 %copy.34 = bf16[32,128,256]{2,1,0:T(8,128)(2,1)} copy(bf16[32,128,256]{1,2,0:T(8,128)(2,1)} %bitcast.147) | data formatting | bytes 4194304 | tf_op jit(solution)/shard_map/transpose | solution.py:46
  45.6 4.8 %copy.35 = bf16[256,16,256]{0,1,2:T(8,128)(2,1)} copy(bf16[256,16,256]{2,1,0:T(8,128)(2,1)} %bitcast.148) | data formatting | bytes 4194304 | tf_op jit(solution)/shard_map/reshape | solution.py:46
  50.4 2.9 %fusion.77 = bf16[256,384]{1,0:T(8,128)(2,1)S(1)} fusion(bf16[256,16,256]{0,1,2:T(8,128)(2,1)} %copy.35, bf16[16,256,384]{2,0,1:T(8,128)(2,1)S(1)} %bitcast.143, f32[512,384]{1,0:T(8,128)} %convert_element_type.127, f32[32,384]{1,0:T(8,128)S(1)} %fusion.158), kind=kOutput, calls=%fused_computation.74 | convolution fusion | flops 805601280 | bytes 5881856 | tf_op jit(solution)/shard_map/dot_general | solution.py:47
  53.3 1.7 %collective-permute-start.3 = (bf16[256,384]{1,0:T(8,128)(2,1)S(1)}, bf16[256,384]{1,0:T(8,128)(2,1)S(1)}, u32[]{:S(2)}, u32[]{:S(2)}) collective-permute-start(bf16[256,384]{1,0:T(8,128)(2,1)S(1)} %fusion.77), channel_id=1, source_target_pairs={{0,1},{1,0},{2,3},{3,2},{4,5},{5,4},{6,7},{7,6},{8,9},{9,8},{10,11... | collective-permute-start | bytes 589832 | tf_op jit(solution)/shard_map/ppermute | solution.py:93
  55.1 1.3 fusion.106
  56.4 3.1 %collective-permute-done.3 = bf16[256,384]{1,0:T(8,128)(2,1)S(1)} collective-permute-done((bf16[256,384]{1,0:T(8,128)(2,1)S(1)}, bf16[256,384]{1,0:T(8,128)(2,1)S(1)}, u32[]{:S(2)}, u32[]{:S(2)}) %collective-permute-start.3) | collective-permute-done | bytes 196640 | tf_op jit(solution)/shard_map/ppermute | solution.py:93
  60.1 1.3 fusion.59
  61.5 2.8 %fusion.155 = (f32[6,256]{1,0:T(8,128)S(1)}, f32[6,256,512]{2,1,0:T(8,128)}) fusion(bf16[256,6,64]{0,2,1:T(8,128)(2,1)S(1)} %bitcast.166, bf16[512,6,64]{0,2,1:T(8,128)(2,1)S(1)} %bitcast.159), kind=kOutput, calls=%fused_computation.175 | convolution fusion | flops 103023104 | bytes 3741696 | tf_op jit(solution)/shard_map/sub | solution.py:121
  64.3 2.6 %fusion.80 = bf16[6,64,256]{2,1,0:T(8,128)(2,1)S(1)} fusion(bf16[512,6,64]{0,2,1:T(8,128)(2,1)S(1)} %bitcast.157, f32[6,256,512]{2,1,0:T(8,128)} %get-tuple-element.24, f32[6,256]{1,0:T(8,128)S(1)} %get-tuple-element.23), kind=kOutput, calls=%fused_computation.77 | convolution fusion | flops 102334464 | bytes 3741696 | tf_op jit(solution)/shard_map/hts,shd->thd/dot_general | solution.py:122
  66.8 1.9 %collective-permute-start.4 = (bf16[256,384]{0,1:T(8,128)(2,1)S(1)}, bf16[256,384]{0,1:T(8,128)(2,1)}, u32[]{:S(2)}, u32[]{:S(2)}) collective-permute-start(bf16[256,384]{0,1:T(8,128)(2,1)S(1)} %bitcast.163), channel_id=1, source_target_pairs={{0,1},{1,0},{2,3},{3,2},{4,5},{5,4},{6,7},{7,6},{8,9},{9,8},{10,11... | collective-permute-start | bytes 589832 | tf_op jit(solution)/shard_map/ppermute | solution.py:126
  68.7 2.8 %fusion.153 = (f32[6,256]{1,0:T(8,128)S(1)}, f32[6,256,512]{2,1,0:T(8,128)}) fusion(bf16[256,6,64]{0,2,1:T(8,128)(2,1)S(1)} %bitcast.165, bf16[512,6,64]{0,2,1:T(8,128)(2,1)S(1)} %bitcast.160), kind=kOutput, calls=%fused_computation.173 | convolution fusion | flops 103023104 | bytes 3741696 | tf_op jit(solution)/shard_map/sub | solution.py:121
  71.5 2.6 %fusion.79 = bf16[6,64,256]{2,1,0:T(8,128)(2,1)S(1)} fusion(bf16[512,6,64]{0,2,1:T(8,128)(2,1)S(1)} %bitcast.158, f32[6,256,512]{2,1,0:T(8,128)} %get-tuple-element.20, f32[6,256]{1,0:T(8,128)S(1)} %get-tuple-element.19), kind=kOutput, calls=%fused_computation.76 | convolution fusion | flops 102334464 | bytes 3741696 | tf_op jit(solution)/shard_map/hts,shd->thd/dot_general | solution.py:122
  74.2 1.4 fusion.72
  75.6 1.5 fusion.68
  77.1 1.8 %fusion.156 = (f32[256]{0:T(256)S(1)}, f32[256,768]{1,0:T(8,128)S(1)}) fusion(f32[256,768]{1,0:T(8,128)S(1)} %fusion.72, bf16[256,384]{0,1:T(8,128)(2,1)} %collective-permute-done.4, bf16[384,768]{1,0:T(8,128)(2,1)} %collective-permute-done.5, bf16[256,384]{1,0:T(8,128)(2,1)} %fusion.78, bf16[256,384]{1,0:T(8,128)(2,1)} %collective-permute-done, pred[]{:T(512)S(6)} %eq.2), kind=kOutput, calls=%fused_computation.176 | convolution fusion | flops 153943808 | bytes 2753537 | tf_op jit(solution)/shard_map/dot_general | solution.py:128
  79.2 1.0 collective-permute-done.6
  80.2 1.5 fusion.154
  82.0 4.0 %fusion.62 = bf16[256,768]{1,0:T(8,128)(2,1)S(1)} fusion(bf16[1,1536,768]{2,1,0:T(8,128)(2,1)} %param.22, bf16[1,768,1536]{2,1,0:T(8,128)(2,1)} %param.21, f32[256,768]{1,0:T(8,128)S(1)} %get-tuple-element.22, f32[768]{0:T(1024)S(1)} %get-tuple-element.12, f32[768]{0:T(1024)S(1)} %get-tuple-element.29, f32[256]{0:T(256)S(1)} %add_rsqrt_fusion.4, ...), kind=kOutput, calls=%fused_computation.55 | convolution fusion | flops 1212678144 | bytes 5906432 | tf_op jit(solution)/shard_map/dot_general | solution.py:137
  86.6 4.0 %fusion.12 = bf16[256,768]{1,0:T(8,128)(2,1)S(1)} fusion(bf16[1,1536,768]{2,1,0:T(8,128)(2,1)} %param.22, bf16[1,768,1536]{2,1,0:T(8,128)(2,1)} %param.21, f32[256,768]{1,0:T(8,128)S(1)} %get-tuple-element.26, f32[256]{0:T(256)S(1)} %add_rsqrt_fusion.2, f32[256]{0:T(256)S(1)} %broadcast_multiply_fusion.4, f32[768]{0:T(1024)S(1)} %get-tuple-element.12, ...), kind=kOutput, calls=%fused_computation.16 | convolution fusion | flops 1212481536 | bytes 5906432 | tf_op jit(solution)/shard_map/dot_general | solution.py:137
  90.6 4.9 %collective-permute-done.7 = bf16[256,768]{1,0:T(8,128)(2,1)S(1)} collective-permute-done((bf16[256,768]{1,0:T(8,128)(2,1)S(1)}, bf16[256,768]{1,0:T(8,128)(2,1)S(1)}, u32[]{:S(2)}, u32[]{:S(2)}) %collective-permute-start.7) | collective-permute-done | bytes 393248 | tf_op jit(solution)/shard_map/ppermute | solution.py:24
  96.0 3.5 %fusion.53 = bf16[256,16,128]{2,0,1:T(8,128)(2,1)} fusion(bf16[16,128,768]{2,0,1:T(8,128)(2,1)S(1)} %bitcast.153, f32[768]{0:T(1024)S(1)} %get-tuple-element.14, f32[768]{0:T(1024)S(1)} %get-tuple-element.27, f32[256]{0:T(256)S(1)} %add_rsqrt_fusion.3, f32[256]{0:T(256)S(1)} %broadcast_multiply_fusion.5, f32[256,768]{1,0:T(8,128)S(1)} %get-tuple-element.22, ...), kind=kOutput, calls=%fused_computation.52 | convolution fusion | flops 807600128 | bytes 5775360 | tf_op jit(solution)/shard_map/dot_general | solution.py:144
  99.5 0.9 collective-permute-start.8
  100.4 8.1 %collective-permute-start.9 = (bf16[256,16,128]{2,0,1:T(8,128)(2,1)}, bf16[256,16,128]{2,0,1:T(8,128)(2,1)S(1)}, u32[]{:S(2)}, u32[]{:S(2)}) collective-permute-start(bf16[256,16,128]{2,0,1:T(8,128)(2,1)} %fusion.53), channel_id=1, source_target_pairs={{0,2},{2,4},{4,6},{6,8},{8,10},{10,12},{12,14},{14,16},{16,18},{18... | collective-permute-start | bytes 3145736 | tf_op jit(solution)/shard_map/ppermute | solution.py:19
  109.1 11.2 %collective-permute-done.9 = bf16[256,16,128]{2,0,1:T(8,128)(2,1)S(1)} collective-permute-done((bf16[256,16,128]{2,0,1:T(8,128)(2,1)}, bf16[256,16,128]{2,0,1:T(8,128)(2,1)S(1)}, u32[]{:S(2)}, u32[]{:S(2)}) %collective-permute-start.9) | collective-permute-done | bytes 1048608 | tf_op jit(solution)/shard_map/ppermute | solution.py:19
  120.4 1.0 copy-done.9
  121.4 3.8 %divide_convert_fusion.2 = bf16[256,16,128]{2,0,1:T(8,128)(2,1)S(1)} fusion(bf16[256,16,128]{2,0,1:T(8,128)(2,1)} %copy-done.9, f32[]{:T(128)S(6)} %convert_element_type.166, s32[128]{0:T(128)S(1)} %get-tuple-element.32, s32[128]{0:T(128)S(1)} %get-tuple-element.33, s32[]{:T(128)S(6)} %mul.212, s32[256]{0:T(256)S(1)} %get-tuple-element.30, ...), kind=kOutput, calls=%fused_computation.25 | convolution fusion | flops 819658752 | bytes 6827400 | tf_op jit(solution)/shard_map/dot_general | solution.py:144
  125.2 0.7 copy.41
  126.7 0.9 copy-done.2
  127.5 22.8 %collective-permute-done.10 = bf16[4,8,8,16,128]{4,3,1,2,0:T(8,128)(2,1)S(1)} collective-permute-done((bf16[4,8,8,16,128]{4,3,1,2,0:T(8,128)(2,1)S(1)}, bf16[4,8,8,16,128]{4,3,1,2,0:T(8,128)(2,1)S(1)}, u32[]{:S(2)}, u32[]{:S(2)}) %collective-permute-start.10) | collective-permute-done | bytes 1048608 | tf_op jit(solution)/shard_map/ppermute | solution.py:167
  150.3 1.9 %maximum_select_fusion = bf16[4,16,8,16,128]{4,3,1,2,0:T(8,128)(2,1)S(1)} fusion(bf16[4,8,8,16,128]{4,3,1,2,0:T(8,128)(2,1)S(1)} %collective-permute-done.10, bf16[4,8,8,16,128]{4,3,1,2,0:T(8,128)(2,1)} %bitcast.151, pred[]{:T(512)S(6)} %eq.2), kind=kLoop, calls=%fused_computation.24 | loop fusion | flops 3145728 | bytes 4194305 | tf_op jit(solution)/shard_map/jit(_where)/select_n | solution.py:168
  152.3 1.9 %copy.43 = bf16[4,16,8,16,128]{4,3,2,1,0:T(8,128)(2,1)} copy(bf16[4,16,8,16,128]{4,3,1,2,0:T(8,128)(2,1)S(1)} %maximum_select_fusion) | data formatting | bytes 4194304 | tf_op jit(solution)/shard_map/jit(_where)/select_n | solution.py:168
  (59 shorter events, 4.8 us)
Async XLA Ops:
  0.0 23.1 %copy-start = (bf16[4096,384]{1,0:T(8,128)(2,1)S(1)}, bf16[4096,384]{1,0:T(8,128)(2,1)}, u32[]{:S(2)}) copy-start(bf16[4096,384]{1,0:T(8,128)(2,1)} %param.14) | copy-start | bytes 9437188
  0.9 32.1 %collective-permute-start.2 = (bf16[64,128]{1,0:T(8,128)(2,1)S(1)}, bf16[64,128]{1,0:T(8,128)(2,1)S(1)}, u32[]{:S(2)}, u32[]{:S(2)}) collective-permute-start(bf16[64,128]{1,0:T(8,128)(2,1)S(1)} %convert_element_type.126), channel_id=1, source_target_pairs={{2,0},{4,2},{6,4},{8,6},{10,8},{12,10},{14,12},{16,14},{18,16},{20... | collective-permute-start | bytes 49160 | tf_op jit(solution)/shard_map/ppermute | solution.py:19
  3.6 33.5 %collective-permute-start.1 = (bf16[64,128,128]{2,1,0:T(8,128)(2,1)}, bf16[64,128,128]{2,1,0:T(8,128)(2,1)}, u32[]{:S(2)}, u32[]{:S(2)}) collective-permute-start(bf16[64,128,128]{2,1,0:T(8,128)(2,1)} %param.12), channel_id=1, source_target_pairs={{2,0},{4,2},{6,4},{8,6},{10,8},{12,10},{14,12},{16,14},{18,16},{20... | collective-permute-start | bytes 6291464 | tf_op jit(solution)/shard_map/ppermute | solution.py:19
  16.4 6.6 %copy-start.5 = (bf16[256,384]{1,0:T(8,128)(2,1)S(1)}, bf16[256,384]{1,0:T(8,128)(2,1)}, u32[]{:S(2)}) copy-start(bf16[256,384]{1,0:T(8,128)(2,1)} %param.15) | copy-start | bytes 589828
  26.7 28.4 %collective-permute-start = (bf16[256,384]{1,0:T(8,128)(2,1)}, bf16[256,384]{1,0:T(8,128)(2,1)}, u32[]{:S(2)}, u32[]{:S(2)}) collective-permute-start(bf16[256,384]{1,0:T(8,128)(2,1)} %fusion.78), channel_id=1, source_target_pairs={{0,1},{1,0},{2,3},{3,2},{4,5},{5,4},{6,7},{7,6},{8,9},{9,8},{10,11... | collective-permute-start | bytes 589832 | tf_op jit(solution)/shard_map/ppermute | solution.py:93
  28.4 48.7 %collective-permute-start.5 = (bf16[384,768]{1,0:T(8,128)(2,1)}, bf16[384,768]{1,0:T(8,128)(2,1)}, u32[]{:S(2)}, u32[]{:S(2)}) collective-permute-start(bf16[384,768]{1,0:T(8,128)(2,1)} %bitcast.27), channel_id=1, source_target_pairs={{0,1},{1,0},{2,3},{3,2},{4,5},{5,4},{6,7},{7,6},{8,9},{9,8},{10,11... | collective-permute-start | bytes 1769480 | tf_op jit(solution)/shard_map/ppermute | solution.py:84
  50.4 4.7 %copy-start.6 = (f32[3,768]{1,0:T(4,128)S(1)}, f32[3,768]{1,0:T(4,128)}, u32[]{:S(2)}) copy-start(f32[3,768]{1,0:T(4,128)} %param.18) | copy-start | bytes 27652
  50.4 4.7 %copy-start.7 = (f32[3,768]{1,0:T(4,128)S(1)}, f32[3,768]{1,0:T(4,128)}, u32[]{:S(2)}) copy-start(f32[3,768]{1,0:T(4,128)} %param.17) | copy-start | bytes 27652
  53.3 6.2 %collective-permute-start.3 = (bf16[256,384]{1,0:T(8,128)(2,1)S(1)}, bf16[256,384]{1,0:T(8,128)(2,1)S(1)}, u32[]{:S(2)}, u32[]{:S(2)}) collective-permute-start(bf16[256,384]{1,0:T(8,128)(2,1)S(1)} %fusion.77), channel_id=1, source_target_pairs={{0,1},{1,0},{2,3},{3,2},{4,5},{5,4},{6,7},{7,6},{8,9},{9,8},{10,11... | collective-permute-start | bytes 589832 | tf_op jit(solution)/shard_map/ppermute | solution.py:93
  56.4 3.6 %copy-start.8 = (bf16[1,3,768,384]{3,2,1,0:T(8,128)(2,1)S(1)}, bf16[1,3,768,384]{3,2,1,0:T(8,128)(2,1)}, u32[]{:S(2)}) copy-start(bf16[1,3,768,384]{3,2,1,0:T(8,128)(2,1)} %param.19) | copy-start | bytes 5308420
  66.8 10.3 %collective-permute-start.4 = (bf16[256,384]{0,1:T(8,128)(2,1)S(1)}, bf16[256,384]{0,1:T(8,128)(2,1)}, u32[]{:S(2)}, u32[]{:S(2)}) collective-permute-start(bf16[256,384]{0,1:T(8,128)(2,1)S(1)} %bitcast.163), channel_id=1, source_target_pairs={{0,1},{1,0},{2,3},{3,2},{4,5},{5,4},{6,7},{7,6},{8,9},{9,8},{10,11... | collective-permute-start | bytes 589832 | tf_op jit(solution)/shard_map/ppermute | solution.py:126
  74.1 6.1 %collective-permute-start.6 = (bf16[256,384]{0,1:T(8,128)(2,1)S(1)}, bf16[256,384]{0,1:T(8,128)(2,1)S(1)}, u32[]{:S(2)}, u32[]{:S(2)}) collective-permute-start(bf16[256,384]{0,1:T(8,128)(2,1)S(1)} %bitcast.161), channel_id=1, source_target_pairs={{0,1},{1,0},{2,3},{3,2},{4,5},{5,4},{6,7},{7,6},{8,9},{9,8},{10,11... | collective-permute-start | bytes 589832 | tf_op jit(solution)/shard_map/ppermute | solution.py:126
  86.0 9.5 %collective-permute-start.7 = (bf16[256,768]{1,0:T(8,128)(2,1)S(1)}, bf16[256,768]{1,0:T(8,128)(2,1)S(1)}, u32[]{:S(2)}, u32[]{:S(2)}) collective-permute-start(bf16[256,768]{1,0:T(8,128)(2,1)S(1)} %fusion.62), channel_id=1, source_target_pairs={{0,1},{1,0},{2,3},{3,2},{4,5},{5,4},{6,7},{7,6},{8,9},{9,8},{10,11... | collective-permute-start | bytes 1179656 | tf_op jit(solution)/shard_map/ppermute | solution.py:24
  90.6 5.4 %copy-start.3 = (bf16[768,2048]{0,1:T(8,128)(2,1)S(1)}, bf16[768,2048]{0,1:T(8,128)(2,1)}, u32[]{:S(2)}) copy-start(bf16[768,2048]{0,1:T(8,128)(2,1)} %copy.38) | copy-start | bytes 9437188
  99.5 9.1 %collective-permute-start.8 = (bf16[256,768]{1,0:T(8,128)(2,1)S(1)}, bf16[256,768]{1,0:T(8,128)(2,1)S(1)}, u32[]{:S(2)}, u32[]{:S(2)}) collective-permute-start(bf16[256,768]{1,0:T(8,128)(2,1)S(1)} %fusion.12), channel_id=1, source_target_pairs={{0,1},{1,0},{2,3},{3,2},{4,5},{5,4},{6,7},{7,6},{8,9},{9,8},{10,11... | collective-permute-start | bytes 1179656 | tf_op jit(solution)/shard_map/ppermute | solution.py:24
  100.4 20.0 %collective-permute-start.9 = (bf16[256,16,128]{2,0,1:T(8,128)(2,1)}, bf16[256,16,128]{2,0,1:T(8,128)(2,1)S(1)}, u32[]{:S(2)}, u32[]{:S(2)}) collective-permute-start(bf16[256,16,128]{2,0,1:T(8,128)(2,1)} %fusion.53), channel_id=1, source_target_pairs={{0,2},{2,4},{4,6},{6,8},{8,10},{10,12},{12,14},{14,16},{16,18},{18... | collective-permute-start | bytes 3145736 | tf_op jit(solution)/shard_map/ppermute | solution.py:19
  108.6 12.8 %copy-start.4 = (bf16[768,2048]{0,1:T(8,128)(2,1)S(1)}, bf16[768,2048]{0,1:T(8,128)(2,1)}, u32[]{:S(2)}) copy-start(bf16[768,2048]{0,1:T(8,128)(2,1)} %copy.38) | copy-start | bytes 9437188
  120.4 1.0 copy-start.9
  126.6 1.0 copy-start.2
  126.6 23.8 %collective-permute-start.10 = (bf16[4,8,8,16,128]{4,3,1,2,0:T(8,128)(2,1)S(1)}, bf16[4,8,8,16,128]{4,3,1,2,0:T(8,128)(2,1)S(1)}, u32[]{:S(2)}, u32[]{:S(2)}) collective-permute-start(bf16[4,8,8,16,128]{4,3,1,2,0:T(8,128)(2,1)S(1)} %bitcast.150), channel_id=1, source_target_pairs={{0,1},{1,0},{2,3},{3,2},{4,5},{5,4},{6,7},{7,6},{8,9},{9,8},{10,11... | collective-permute-start | bytes 3145736 | tf_op jit(solution)/shard_map/ppermute | solution.py:167
  150.3 3.9 %copy-start.1 = (bf16[4096,384]{1,0:T(8,128)(2,1)S(1)}, bf16[4096,384]{1,0:T(8,128)(2,1)}, u32[]{:S(2)}) copy-start(bf16[4096,384]{1,0:T(8,128)(2,1)} %param.14) | copy-start | bytes 9437188

commit v7 on v6

--- a/solution.py
+++ b/solution.py
@@ -80,14 +80,14 @@
     tile_index = lax.axis_index("tile")
     head_index = lax.axis_index("head")
     own_live = trace_mask.astype(jnp.bfloat16)
-    next_traces, next_live = from_behind((traces, own_live), "tile", -1)
     other_w_out = lax.ppermute(w_out[0], "head", [(0, 1), (1, 0)])
     local_width = embed_voxel.shape[1]
     embed_by_depth = embed_voxel.reshape(PATCH * PATCH, PATCH, local_width).transpose(1, 0, 2)
     position = position.astype(jnp.float32)
+    own_embedded = embed_planes(traces, own_live, embed_by_depth, embed_mask)
+    next_embedded = from_behind(own_embedded, "tile", -1)
     halves = []
-    for rows, (amplitudes, live) in enumerate(((traces, own_live), (next_traces, next_live))):
-        embedded = embed_planes(amplitudes, live, embed_by_depth, embed_mask)
+    for rows, embedded in enumerate((own_embedded, next_embedded)):
         embedded = embedded + position[rows * half_tokens:(rows + 1) * half_tokens]
         embedded = embedded.astype(jnp.bfloat16)
         other_columns = lax.ppermute(embedded, "head", [(0, 1), (1, 0)])
@@ -136,16 +136,23 @@
         ).astype(jnp.bfloat16)
         partial_forward = jnp.dot(hidden, w_down[0], preferred_element_type=jnp.float32)
         if chunk == 0:
-            decoded_chunks[1], partial_forward = lax.optimization_barrier(
-                (decoded_chunks[1], partial_forward)
+            sent_latent, partial_forward = lax.optimization_barrier(
+                (sent_latent, partial_forward)
             )
         part = part + partner_sum(partial_forward)
         latent = layer_norm(part, norm_gain[2 * LAYERS], norm_bias[2 * LAYERS]).astype(jnp.bfloat16)
+        if chunk == 1:
+            sent_latent = latent
+            continue
         decoded_chunks[chunk] = lax.dot_general(
             latent, decode_by_depth, (((1,), (2,)), ((), ())),
             preferred_element_type=jnp.float32,
         ).astype(jnp.bfloat16)
-    upper_part = from_behind(decoded_chunks[1], "tile", 1)
+    arrived_latent = from_behind(sent_latent, "tile", 1)
+    upper_part = lax.dot_general(
+        arrived_latent, decode_by_depth, (((1,), (2,)), ((), ())),
+        preferred_element_type=jnp.float32,
+    ).astype(jnp.bfloat16)
     lower_part = decoded_chunks[0]
     shape = lower_part.shape
     token_a = lax.broadcasted_iota(jnp.int32, shape, 0) // (side * side)

time: 155 us -> 148 us (0.955)
  the two profiles are of different devices: /device:TPU:31 before, /device:TPU:22 now
where the time goes in v7:
time: 148 us
  waiting for transfers between devices  53.9 us (36%)
  matrix products  39.8 us (27%)
  local copies, waits for them, and re-layouts  26.4 us (18%)
  starting transfers between devices  13.9 us (9%)
  other arithmetic  13.2 us (9%)
    ppermute x1, waiting for transfers between devices, body(): other_rows = lax.ppermute(arranged, 'head', [(0, 1), (1, 0)])  23.4 us
    ppermute x2, waiting for transfers between devices, partner_sum(): other = lax.ppermute(rounded, 'head', [(0, 1), (1, 0)])  13.8 us
    ppermute x2, waiting for transfers between devices, body(): other_columns = lax.ppermute(embedded, 'head', [(0, 1), (1, 0)])  10.7 us
    dot_general x2, matrix products, body(): jnp.dot(hidden, w_down[0], preferred_element_type=jnp.float32)  9.32 us
    sub x2, matrix products, body(): weights = jax.nn.softmax(scores, axis=-1).astype(jnp.bfloat16)  7.81 us
    unnamed x23, local copies, waits for them, and re-layouts  6.32 us
    dot_general x2, matrix products, body(): jnp.einsum('hts,shd->thd', weights, values, preferred_element_type=jnp.fl...  6.07 us
    ppermute x2, waiting for transfers between devices, from_behind(): return lax.ppermute(block, axis, route)  5.2 us
  transfers between devices with their start and end apart: 10, of which 6 were waited for; matrix products, arithmetic and copies ran while one was open for 26% of the time, Pallas kernels for 0%

profile of v7, /device:TPU:22, one launch (start us, length us, event | category | flops | bytes accessed | tf_op | source)
XLA Modules:
  0.0 147.7 jit_solution(3088732356808395156)
XLA Ops:
  0.0 0.9 convert_element_type.126
  1.1 2.5 %broadcast_multiply_fusion = bf16[64,128,128]{2,1,0:T(8,128)(2,1)S(1)} fusion(bf16[64,128,128]{2,1,0:T(8,128)(2,1)} %param.12, bf16[64,128]{1,0:T(8,128)(2,1)S(1)} %convert_element_type.126), kind=kLoop, calls=%fused_computation.72 | loop fusion | flops 1048576 | bytes 4210688 | tf_op jit(solution)/shard_map/mul | solution.py:43
  3.5 1.9 %copy.26 = bf16[4,8,16,16,128]{4,3,2,1,0:T(8,128)(2,1)} copy(bf16[4,8,16,16,128]{4,3,1,2,0:T(8,128)(2,1)S(1)} %bitcast.113) | data formatting | bytes 4194304 | tf_op jit(solution)/shard_map/transpose | solution.py:44
  5.4 4.1 %copy.27 = bf16[32,128,256]{2,1,0:T(8,128)(2,1)} copy(bf16[32,128,256]{1,2,0:T(8,128)(2,1)} %bitcast.114) | data formatting | bytes 4194304 | tf_op jit(solution)/shard_map/transpose | solution.py:46
  9.5 4.8 %copy.28 = bf16[256,16,256]{0,1,2:T(8,128)(2,1)} copy(bf16[256,16,256]{2,1,0:T(8,128)(2,1)} %bitcast.115) | data formatting | bytes 4194304 | tf_op jit(solution)/shard_map/reshape | solution.py:46
  14.5 1.1 fusion.149
  15.6 2.9 %fusion.73 = f32[256,384]{1,0:T(8,128)S(1)} fusion(bf16[256,16,256]{0,1,2:T(8,128)(2,1)} %copy.28, bf16[16,256,384]{2,0,1:T(8,128)(2,1)S(1)} %bitcast.112, f32[32,384]{1,0:T(8,128)S(1)} %fusion.149), kind=kOutput, calls=%fused_computation.69 | convolution fusion | flops 805404672 | bytes 5685248 | tf_op jit(solution)/shard_map/dot_general | solution.py:47
  18.6 2.2 %collective-permute-start.1 = (f32[256,384]{1,0:T(8,128)S(1)}, f32[256,384]{1,0:T(8,128)S(1)}, u32[]{:S(2)}, u32[]{:S(2)}) collective-permute-start(f32[256,384]{1,0:T(8,128)S(1)} %fusion.73), channel_id=1, source_target_pairs={{2,0},{4,2},{6,4},{8,6},{10,8},{12,10},{14,12},{16,14},{18,16},{20... | collective-permute-start | bytes 1179656 | tf_op jit(solution)/shard_map/ppermute | solution.py:19
  20.8 5.2 %collective-permute-done.1 = f32[256,384]{1,0:T(8,128)S(1)} collective-permute-done((f32[256,384]{1,0:T(8,128)S(1)}, f32[256,384]{1,0:T(8,128)S(1)}, u32[]{:S(2)}, u32[]{:S(2)}) %collective-permute-start.1) | collective-permute-done | bytes 393248 | tf_op jit(solution)/shard_map/ppermute | solution.py:19
  26.1 2.0 %collective-permute-start = (bf16[256,384]{1,0:T(8,128)(2,1)S(1)}, bf16[256,384]{1,0:T(8,128)(2,1)}, u32[]{:S(2)}, u32[]{:S(2)}) collective-permute-start(bf16[256,384]{1,0:T(8,128)(2,1)S(1)} %get-tuple-element.19), channel_id=1, source_target_pairs={{0,1},{1,0},{2,3},{3,2},{4,5},{5,4},{6,7},{7,6},{8,9},{9,8},{10,11... | collective-permute-start | bytes 589832 | tf_op jit(solution)/shard_map/ppermute | solution.py:93
  28.2 4.6 %copy.31 = bf16[768,2048]{0,1:T(8,128)(2,1)} copy(bf16[768,2048]{1,0:T(8,128)(2,1)} %param.23) | data formatting | bytes 6291456 | tf_op args[11]
  32.9 1.9 %collective-permute-start.2 = (bf16[256,384]{1,0:T(8,128)(2,1)S(1)}, bf16[256,384]{1,0:T(8,128)(2,1)S(1)}, u32[]{:S(2)}, u32[]{:S(2)}) collective-permute-start(bf16[256,384]{1,0:T(8,128)(2,1)S(1)} %get-tuple-element.20), channel_id=1, source_target_pairs={{0,1},{1,0},{2,3},{3,2},{4,5},{5,4},{6,7},{7,6},{8,9},{9,8},{10,11... | collective-permute-start | bytes 589832 | tf_op jit(solution)/shard_map/ppermute | solution.py:93
  34.8 1.5 slice_reduce_fusion.2
  36.3 1.1 fusion.101
  37.4 10.7 %collective-permute-done.2 = bf16[256,384]{1,0:T(8,128)(2,1)S(1)} collective-permute-done((bf16[256,384]{1,0:T(8,128)(2,1)S(1)}, bf16[256,384]{1,0:T(8,128)(2,1)S(1)}, u32[]{:S(2)}, u32[]{:S(2)}) %collective-permute-start.2) | collective-permute-done | bytes 196640 | tf_op jit(solution)/shard_map/ppermute | solution.py:93
  48.1 0.7 copy-done.8
  49.3 1.3 fusion.59
  50.6 0.9 fusion.144
  51.6 0.8 fusion.143
  52.4 3.9 %fusion.145 = (f32[6,256]{1,0:T(8,128)S(1)}, f32[6,256,512]{2,1,0:T(8,128)}) fusion(bf16[256,6,64]{0,2,1:T(8,128)(2,1)} %bitcast.129, bf16[512,6,64]{0,2,1:T(8,128)(2,1)} %bitcast.124), kind=kOutput, calls=%fused_computation.165 | convolution fusion | flops 103023104 | bytes 3741696 | tf_op jit(solution)/shard_map/sub | solution.py:121
  56.3 3.4 %fusion.75 = bf16[6,64,256]{2,1,0:T(8,128)(2,1)} fusion(bf16[512,6,64]{0,2,1:T(8,128)(2,1)} %bitcast.122, f32[6,256,512]{2,1,0:T(8,128)} %get-tuple-element.22, f32[6,256]{1,0:T(8,128)S(1)} %get-tuple-element.21), kind=kOutput, calls=%fused_computation.71 | convolution fusion | flops 102334464 | bytes 3741696 | tf_op jit(solution)/shard_map/hts,shd->thd/dot_general | solution.py:122
  59.6 2.1 %collective-permute-start.3 = (bf16[256,384]{0,1:T(8,128)(2,1)}, bf16[256,384]{0,1:T(8,128)(2,1)}, u32[]{:S(2)}, u32[]{:S(2)}) collective-permute-start(bf16[256,384]{0,1:T(8,128)(2,1)} %bitcast.17), channel_id=1, source_target_pairs={{0,1},{1,0},{2,3},{3,2},{4,5},{5,4},{6,7},{7,6},{8,9},{9,8},{10,11... | collective-permute-start | bytes 589832 | tf_op jit(solution)/shard_map/ppermute | solution.py:126
  61.7 3.9 %fusion.146 = (f32[6,256]{1,0:T(8,128)S(1)}, f32[6,256,512]{2,1,0:T(8,128)}) fusion(bf16[256,6,64]{0,2,1:T(8,128)(2,1)} %bitcast.128, bf16[512,6,64]{0,2,1:T(8,128)(2,1)} %bitcast.125), kind=kOutput, calls=%fused_computation.166 | convolution fusion | flops 103023104 | bytes 3741696 | tf_op jit(solution)/shard_map/sub | solution.py:121
  65.6 2.7 %fusion.74 = bf16[6,64,256]{2,1,0:T(8,128)(2,1)S(1)} fusion(bf16[512,6,64]{0,2,1:T(8,128)(2,1)} %bitcast.123, f32[6,256,512]{2,1,0:T(8,128)} %get-tuple-element.24, f32[6,256]{1,0:T(8,128)S(1)} %get-tuple-element.23), kind=kOutput, calls=%fused_computation.70 | convolution fusion | flops 102334464 | bytes 3741696 | tf_op jit(solution)/shard_map/hts,shd->thd/dot_general | solution.py:122
  68.6 1.6 %fusion.72 = f32[256,768]{1,0:T(8,128)S(1)} fusion(bf16[256,384]{0,1:T(8,128)(2,1)} %bitcast.17, bf16[1,384,768]{2,1,0:T(8,128)(2,1)} %param.20), kind=kOutput, calls=%fused_computation.67 | convolution fusion | flops 151388160 | bytes 1572864 | tf_op jit(solution)/shard_map/dot_general | solution.py:127
  70.1 1.5 fusion.68
  71.6 1.8 %fusion.148 = (f32[256]{0:T(256)S(1)}, f32[256,768]{1,0:T(8,128)S(1)}) fusion(f32[256,768]{1,0:T(8,128)S(1)} %fusion.72, bf16[256,384]{0,1:T(8,128)(2,1)} %collective-permute-done.3, bf16[384,768]{1,0:T(8,128)(2,1)} %collective-permute-done.4, bf16[256,384]{1,0:T(8,128)(2,1)S(1)} %get-tuple-element.19, bf16[256,384]{1,0:T(8,128)(2,1)} %collective-permute-done, ...), kind=kOutput, calls=%fused_computation.168 | convolution fusion | flops 153943808 | bytes 2753537 | tf_op jit(solution)/shard_map/dot_general | solution.py:128
  74.3 0.9 collective-permute-done.5
  75.2 1.6 %fusion.147 = (f32[256]{0:T(256)S(1)}, f32[256,768]{1,0:T(8,128)S(1)}) fusion(f32[256,768]{1,0:T(8,128)S(1)} %fusion.68, bf16[256,384]{0,1:T(8,128)(2,1)S(1)} %collective-permute-done.5, bf16[384,768]{1,0:T(8,128)(2,1)} %collective-permute-done.4, bf16[256,384]{1,0:T(8,128)(2,1)S(1)} %get-tuple-element.20, bf16[256,384]{1,0:T(8,128)(2,1)S(1)} %copy-done.9, ...), kind=kOutput, calls=%fused_computation.167 | convolution fusion | flops 153943808 | bytes 2753537 | tf_op jit(solution)/shard_map/dot_general | solution.py:128
  76.7 0.9 copy-done.1
  78.4 4.3 %fusion.62 = bf16[256,768]{1,0:T(8,128)(2,1)S(1)} fusion(bf16[1,1536,768]{2,1,0:T(8,128)(2,1)} %param.22, bf16[1,768,1536]{2,1,0:T(8,128)(2,1)} %param.21, f32[256,768]{1,0:T(8,128)} %copy-done.1, f32[768]{0:T(1024)} %get-tuple-element.12, f32[768]{0:T(1024)} %get-tuple-element.31, f32[256]{0:T(256)} %add_rsqrt_fusion.4, f32[256]{0:T(256)S(1)} %broadcast_multiply_fusion.5), kind=kOutput, calls=%fused_computation.55 | convolution fusion | flops 1212678144 | bytes 5906432 | tf_op jit(solution)/shard_map/dot_general | solution.py:137
  82.7 1.2 collective-permute-start.6
  83.9 5.0 %fusion.12 = bf16[256,768]{1,0:T(8,128)(2,1)} fusion(bf16[1,1536,768]{2,1,0:T(8,128)(2,1)} %param.22, bf16[1,768,1536]{2,1,0:T(8,128)(2,1)} %param.21, f32[256,768]{1,0:T(8,128)} %copy-done.3, f32[256]{0:T(256)} %add_rsqrt_fusion.2, f32[256]{0:T(256)S(1)} %broadcast_multiply_fusion.3, f32[768]{0:T(1024)} %get-tuple-element.12, f32[768]{0:T(1024)} %get-tuple-element.31), kind=kOutput, calls=%fused_computation.16 | convolution fusion | flops 1212481536 | bytes 5906432 | tf_op jit(solution)/shard_map/dot_general | solution.py:137
  88.9 5.6 %collective-permute-done.6 = bf16[256,768]{1,0:T(8,128)(2,1)} collective-permute-done((bf16[256,768]{1,0:T(8,128)(2,1)S(1)}, bf16[256,768]{1,0:T(8,128)(2,1)}, u32[]{:S(2)}, u32[]{:S(2)}) %collective-permute-start.6) | collective-permute-done | bytes 393248 | tf_op jit(solution)/shard_map/ppermute | solution.py:24
  94.5 1.4 fusion.141
  96.0 1.3 multiply_reduce_fusion.5
  97.4 1.4 add_convert_fusion.3
  98.7 0.7 collective-permute-start.7
  99.4 2.3 %collective-permute-start.8 = (bf16[256,768]{1,0:T(8,128)(2,1)S(1)}, bf16[256,768]{1,0:T(8,128)(2,1)S(1)}, u32[]{:S(2)}, u32[]{:S(2)}) collective-permute-start(bf16[256,768]{1,0:T(8,128)(2,1)S(1)} %add_convert_fusion.3), channel_id=1, source_target_pairs={{0,2},{2,4},{4,6},{6,8},{8,10},{10,12},{12,14},{14,16},{16,18},{18... | collective-permute-start | bytes 1179656 | tf_op jit(solution)/shard_map/ppermute | solution.py:19
  101.8 8.2 %collective-permute-done.7 = bf16[256,768]{1,0:T(8,128)(2,1)S(1)} collective-permute-done((bf16[256,768]{1,0:T(8,128)(2,1)S(1)}, bf16[256,768]{1,0:T(8,128)(2,1)S(1)}, u32[]{:S(2)}, u32[]{:S(2)}) %collective-permute-start.7) | collective-permute-done | bytes 393248 | tf_op jit(solution)/shard_map/ppermute | solution.py:24
  110.5 2.5 %fusion.53 = bf16[256,16,128]{2,0,1:T(8,128)(2,1)S(1)} fusion(bf16[16,128,768]{2,0,1:T(8,128)(2,1)S(1)} %bitcast.119, f32[256]{0:T(256)S(1)} %add_rsqrt_fusion.1, f32[256]{0:T(256)S(1)} %broadcast_multiply_fusion.2, f32[768]{0:T(1024)S(1)} %get-tuple-element.14, f32[768]{0:T(1024)S(1)} %get-tuple-element.29, f32[256,768]{1,0:T(8,128)S(1)} %copy-done.4, ...), kind=kOutput, calls=%fused_computation.52 | convolution fusion | flops 807600128 | bytes 5775360 | tf_op jit(solution)/shard_map/dot_general | solution.py:147
  113.0 2.5 %divide_convert_fusion.2 = bf16[256,16,128]{2,0,1:T(8,128)(2,1)S(1)} fusion(bf16[256,16,128]{2,0,1:T(8,128)(2,1)S(1)} %fusion.53, f32[]{:T(128)S(6)} %convert_element_type.166, s32[128]{0:T(128)S(1)} %get-tuple-element.34, s32[128]{0:T(128)S(1)} %get-tuple-element.35, s32[]{:T(128)S(6)} %mul.202, s32[256]{0:T(256)S(1)} %get-tuple-element.32, ...), kind=kOutput, calls=%fused_computation.25 | convolution fusion | flops 817889280 | bytes 5639560 | tf_op jit(solution)/shard_map/dot_general | solution.py:152
  115.5 1.6 %copy.34 = bf16[256,16,128]{2,1,0:T(8,128)(2,1)} copy(bf16[256,16,128]{2,0,1:T(8,128)(2,1)S(1)} %divide_convert_fusion.2) | data formatting | bytes 2097152 | tf_op jit(solution)/shard_map/convert_element_type | solution.py:169
  117.1 2.3 %copy.35 = bf16[32,128,128]{2,1,0:T(8,128)(2,1)} copy(bf16[32,128,128]{1,2,0:T(8,128)(2,1)} %bitcast.118) | data formatting | bytes 2097152 | tf_op jit(solution)/shard_map/transpose | solution.py:172
  119.4 1.2 collective-permute-start.9
  120.6 23.4 %collective-permute-done.9 = bf16[4,8,8,16,128]{4,3,1,2,0:T(8,128)(2,1)S(1)} collective-permute-done((bf16[4,8,8,16,128]{4,3,1,2,0:T(8,128)(2,1)}, bf16[4,8,8,16,128]{4,3,1,2,0:T(8,128)(2,1)S(1)}, u32[]{:S(2)}, u32[]{:S(2)}) %collective-permute-start.9) | collective-permute-done | bytes 1048608 | tf_op jit(solution)/shard_map/ppermute | solution.py:174
  144.0 1.8 %maximum_select_fusion = bf16[4,16,8,16,128]{4,3,1,2,0:T(8,128)(2,1)S(1)} fusion(bf16[4,8,8,16,128]{4,3,1,2,0:T(8,128)(2,1)S(1)} %collective-permute-done.9, bf16[4,8,8,16,128]{4,3,1,2,0:T(8,128)(2,1)} %bitcast.117, pred[]{:T(512)S(6)} %eq.2), kind=kLoop, calls=%fused_computation.24 | loop fusion | flops 3145728 | bytes 4194305 | tf_op jit(solution)/shard_map/jit(_where)/select_n | solution.py:175
  145.8 1.9 %copy.36 = bf16[4,16,8,16,128]{4,3,2,1,0:T(8,128)(2,1)} copy(bf16[4,16,8,16,128]{4,3,1,2,0:T(8,128)(2,1)S(1)} %maximum_select_fusion) | data formatting | bytes 4194304 | tf_op jit(solution)/shard_map/jit(_where)/select_n | solution.py:175
  (52 shorter events, 3.6 us)
Async XLA Ops:
  0.0 15.6 %copy-start = (bf16[4096,384]{1,0:T(8,128)(2,1)S(1)}, bf16[4096,384]{1,0:T(8,128)(2,1)}, u32[]{:S(2)}) copy-start(bf16[4096,384]{1,0:T(8,128)(2,1)} %param.14) | copy-start | bytes 9437188
  15.6 5.2 %copy-start.7 = (bf16[512,384]{1,0:T(8,128)(2,1)S(1)}, bf16[512,384]{1,0:T(8,128)(2,1)}, u32[]{:S(2)}) copy-start(bf16[512,384]{1,0:T(8,128)(2,1)} %param.16) | copy-start | bytes 1179652
  18.6 7.5 %collective-permute-start.1 = (f32[256,384]{1,0:T(8,128)S(1)}, f32[256,384]{1,0:T(8,128)S(1)}, u32[]{:S(2)}, u32[]{:S(2)}) collective-permute-start(f32[256,384]{1,0:T(8,128)S(1)} %fusion.73), channel_id=1, source_target_pairs={{2,0},{4,2},{6,4},{8,6},{10,8},{12,10},{14,12},{16,14},{18,16},{20... | collective-permute-start | bytes 1179656 | tf_op jit(solution)/shard_map/ppermute | solution.py:19
  26.1 10.1 %collective-permute-start = (bf16[256,384]{1,0:T(8,128)(2,1)S(1)}, bf16[256,384]{1,0:T(8,128)(2,1)}, u32[]{:S(2)}, u32[]{:S(2)}) collective-permute-start(bf16[256,384]{1,0:T(8,128)(2,1)S(1)} %get-tuple-element.19), channel_id=1, source_target_pairs={{0,1},{1,0},{2,3},{3,2},{4,5},{5,4},{6,7},{7,6},{8,9},{9,8},{10,11... | collective-permute-start | bytes 589832 | tf_op jit(solution)/shard_map/ppermute | solution.py:93
  28.1 43.5 %collective-permute-start.4 = (bf16[384,768]{1,0:T(8,128)(2,1)}, bf16[384,768]{1,0:T(8,128)(2,1)}, u32[]{:S(2)}, u32[]{:S(2)}) collective-permute-start(bf16[384,768]{1,0:T(8,128)(2,1)} %bitcast.18), channel_id=1, source_target_pairs={{0,1},{1,0},{2,3},{3,2},{4,5},{5,4},{6,7},{7,6},{8,9},{9,8},{10,11... | collective-permute-start | bytes 1769480 | tf_op jit(solution)/shard_map/ppermute | solution.py:83
  32.9 15.2 %collective-permute-start.2 = (bf16[256,384]{1,0:T(8,128)(2,1)S(1)}, bf16[256,384]{1,0:T(8,128)(2,1)S(1)}, u32[]{:S(2)}, u32[]{:S(2)}) collective-permute-start(bf16[256,384]{1,0:T(8,128)(2,1)S(1)} %get-tuple-element.20), channel_id=1, source_target_pairs={{0,1},{1,0},{2,3},{3,2},{4,5},{5,4},{6,7},{7,6},{8,9},{9,8},{10,11... | collective-permute-start | bytes 589832 | tf_op jit(solution)/shard_map/ppermute | solution.py:93
  37.4 11.9 %copy-start.10 = (bf16[1,3,768,384]{3,2,1,0:T(8,128)(2,1)S(1)}, bf16[1,3,768,384]{3,2,1,0:T(8,128)(2,1)}, u32[]{:S(2)}) copy-start(bf16[1,3,768,384]{3,2,1,0:T(8,128)(2,1)} %param.19) | copy-start | bytes 5308420
  48.1 0.7 copy-start.8
  59.6 12.0 %collective-permute-start.3 = (bf16[256,384]{0,1:T(8,128)(2,1)}, bf16[256,384]{0,1:T(8,128)(2,1)}, u32[]{:S(2)}, u32[]{:S(2)}) collective-permute-start(bf16[256,384]{0,1:T(8,128)(2,1)} %bitcast.17), channel_id=1, source_target_pairs={{0,1},{1,0},{2,3},{3,2},{4,5},{5,4},{6,7},{7,6},{8,9},{9,8},{10,11... | collective-permute-start | bytes 589832 | tf_op jit(solution)/shard_map/ppermute | solution.py:126
  68.3 6.9 %collective-permute-start.5 = (bf16[256,384]{0,1:T(8,128)(2,1)S(1)}, bf16[256,384]{0,1:T(8,128)(2,1)S(1)}, u32[]{:S(2)}, u32[]{:S(2)}) collective-permute-start(bf16[256,384]{0,1:T(8,128)(2,1)S(1)} %bitcast.126), channel_id=1, source_target_pairs={{0,1},{1,0},{2,3},{3,2},{4,5},{5,4},{6,7},{7,6},{8,9},{9,8},{10,11... | collective-permute-start | bytes 589832 | tf_op jit(solution)/shard_map/ppermute | solution.py:126
  71.6 3.6 %copy-start.9 = (bf16[256,384]{1,0:T(8,128)(2,1)S(1)}, bf16[256,384]{1,0:T(8,128)(2,1)}, u32[]{:S(2)}) copy-start(bf16[256,384]{1,0:T(8,128)(2,1)} %copy-done.8) | copy-start | bytes 589828
  73.4 0.9 copy-start.3
  76.7 0.9 copy-start.1
  82.7 11.9 %collective-permute-start.6 = (bf16[256,768]{1,0:T(8,128)(2,1)S(1)}, bf16[256,768]{1,0:T(8,128)(2,1)}, u32[]{:S(2)}, u32[]{:S(2)}) collective-permute-start(bf16[256,768]{1,0:T(8,128)(2,1)S(1)} %fusion.62), channel_id=1, source_target_pairs={{0,1},{1,0},{2,3},{3,2},{4,5},{5,4},{6,7},{7,6},{8,9},{9,8},{10,11... | collective-permute-start | bytes 1179656 | tf_op jit(solution)/shard_map/ppermute | solution.py:24
  88.9 7.1 %copy-start.2 = (f32[256,768]{1,0:T(8,128)S(1)}, f32[256,768]{1,0:T(8,128)}, u32[]{:S(2)}) copy-start(f32[256,768]{1,0:T(8,128)} %copy-done.1) | copy-start | bytes 2359300
  95.9 2.8 %copy-start.6 = (bf16[256,768]{1,0:T(8,128)(2,1)S(1)}, bf16[256,768]{1,0:T(8,128)(2,1)}, u32[]{:S(2)}) copy-start(bf16[256,768]{1,0:T(8,128)(2,1)} %fusion.12) | copy-start | bytes 1179652
  96.0 14.0 %copy-start.4 = (f32[256,768]{1,0:T(8,128)S(1)}, f32[256,768]{1,0:T(8,128)}, u32[]{:S(2)}) copy-start(f32[256,768]{1,0:T(8,128)} %copy-done.3) | copy-start | bytes 2359300
  97.3 13.2 %copy-start.5 = (bf16[768,2048]{0,1:T(8,128)(2,1)S(1)}, bf16[768,2048]{0,1:T(8,128)(2,1)}, u32[]{:S(2)}) copy-start(bf16[768,2048]{0,1:T(8,128)(2,1)} %copy.31) | copy-start | bytes 9437188
  98.7 11.2 %collective-permute-start.7 = (bf16[256,768]{1,0:T(8,128)(2,1)S(1)}, bf16[256,768]{1,0:T(8,128)(2,1)S(1)}, u32[]{:S(2)}, u32[]{:S(2)}) collective-permute-start(bf16[256,768]{1,0:T(8,128)(2,1)S(1)} %copy-done.6), channel_id=1, source_target_pairs={{0,1},{1,0},{2,3},{3,2},{4,5},{5,4},{6,7},{7,6},{8,9},{9,8},{10,11... | collective-permute-start | bytes 1179656 | tf_op jit(solution)/shard_map/ppermute | solution.py:24
  99.4 13.6 %collective-permute-start.8 = (bf16[256,768]{1,0:T(8,128)(2,1)S(1)}, bf16[256,768]{1,0:T(8,128)(2,1)S(1)}, u32[]{:S(2)}, u32[]{:S(2)}) collective-permute-start(bf16[256,768]{1,0:T(8,128)(2,1)S(1)} %add_convert_fusion.3), channel_id=1, source_target_pairs={{0,2},{2,4},{4,6},{6,8},{8,10},{10,12},{12,14},{14,16},{16,18},{18... | collective-permute-start | bytes 1179656 | tf_op jit(solution)/shard_map/ppermute | solution.py:19
  119.4 24.6 %collective-permute-start.9 = (bf16[4,8,8,16,128]{4,3,1,2,0:T(8,128)(2,1)}, bf16[4,8,8,16,128]{4,3,1,2,0:T(8,128)(2,1)S(1)}, u32[]{:S(2)}, u32[]{:S(2)}) collective-permute-start(bf16[4,8,8,16,128]{4,3,1,2,0:T(8,128)(2,1)} %bitcast.116), channel_id=1, source_target_pairs={{0,1},{1,0},{2,3},{3,2},{4,5},{5,4},{6,7},{7,6},{8,9},{9,8},{10,11... | collective-permute-start | bytes 3145736 | tf_op jit(solution)/shard_map/ppermute | solution.py:174

commit v8 on v7

--- a/solution.py
+++ b/solution.py
@@ -80,7 +80,6 @@
     tile_index = lax.axis_index("tile")
     head_index = lax.axis_index("head")
     own_live = trace_mask.astype(jnp.bfloat16)
-    other_w_out = lax.ppermute(w_out[0], "head", [(0, 1), (1, 0)])
     local_width = embed_voxel.shape[1]
     embed_by_depth = embed_voxel.reshape(PATCH * PATCH, PATCH, local_width).transpose(1, 0, 2)
     position = position.astype(jnp.float32)
@@ -96,6 +95,8 @@
             jnp.concatenate([embedded, other_columns], 1),
             jnp.concatenate([other_columns, embedded], 1),
         ).astype(jnp.float32))
+    own_w_out, halves = lax.optimization_barrier((w_out[0], halves))
+    other_w_out = lax.ppermute(own_w_out, "head", [(0, 1), (1, 0)])
     stream = jnp.concatenate(halves, 0)
     local_heads = w_qkv.shape[3] // HEAD_DIM
     normed = layer_norm(stream, norm_gain[0], norm_bias[0]).astype(jnp.bfloat16)
@@ -124,7 +125,7 @@
         ).astype(jnp.bfloat16)
         attended = attended.reshape(half_tokens, local_heads * HEAD_DIM)
         other_attended = lax.ppermute(attended, "head", [(0, 1), (1, 0)])
-        own_term = jnp.dot(attended, w_out[0], preferred_element_type=jnp.float32)
+        own_term = jnp.dot(attended, own_w_out, preferred_element_type=jnp.float32)
         other_term = jnp.dot(other_attended, other_w_out, preferred_element_type=jnp.float32)
         part = stream[span] + (
             own_term.astype(jnp.bfloat16).astype(jnp.float32)

time: 148 us -> 154 us (1.041)
  the two profiles are of different devices: /device:TPU:22 before, /device:TPU:31 now
where the time goes in v8:
time: 154 us; the launch traced here: 153 us
  waiting for transfers between devices  57.2 us (37%)
  matrix products  41.3 us (27%)
  local copies, waits for them, and re-layouts  28.3 us (18%)
  other arithmetic  16.1 us (10%)
  starting transfers between devices  9.4 us (6%)
    ppermute x1, waiting for transfers between devices, body(): other_rows = lax.ppermute(arranged, 'head', [(0, 1), (1, 0)])  25.3 us
    ppermute x2, waiting for transfers between devices, from_behind(): return lax.ppermute(block, axis, route)  12.3 us
    ppermute x2, waiting for transfers between devices, partner_sum(): other = lax.ppermute(rounded, 'head', [(0, 1), (1, 0)])  10.2 us
    dot_general x2, matrix products, body(): jnp.dot(hidden, w_down[0], preferred_element_type=jnp.float32)  9.32 us
    sub x2, matrix products, body(): weights = jax.nn.softmax(scores, axis=-1).astype(jnp.bfloat16)  7.82 us
    ppermute x1, waiting for transfers between devices, body(): other_w_out = lax.ppermute(own_w_out, 'head', [(0, 1), (1, 0)])  7.56 us
    unnamed x26, local copies, waits for them, and re-layouts  7.4 us
    dot_general x2, matrix products, body(): jnp.einsum('hts,shd->thd', weights, values, preferred_element_type=jnp.fl...  5.81 us
  transfers between devices with their start and end apart: 10, of which 6 were waited for; matrix products, arithmetic and copies ran while one was open for 18% of the time, Pallas kernels for 0%

profile of v8, /device:TPU:31, one launch (start us, length us, event | category | flops | bytes accessed | tf_op | source)
XLA Modules:
  0.0 152.8 jit_solution(12576921504254447104)
XLA Ops:
  0.0 0.9 convert_element_type.126
  1.1 2.5 %broadcast_multiply_fusion = bf16[64,128,128]{2,1,0:T(8,128)(2,1)S(1)} fusion(bf16[64,128,128]{2,1,0:T(8,128)(2,1)} %param.12, bf16[64,128]{1,0:T(8,128)(2,1)S(1)} %convert_element_type.126), kind=kLoop, calls=%fused_computation.71 | loop fusion | flops 1048576 | bytes 4210688 | tf_op jit(solution)/shard_map/mul | solution.py:43
  3.5 1.9 %copy.26 = bf16[4,8,16,16,128]{4,3,2,1,0:T(8,128)(2,1)} copy(bf16[4,8,16,16,128]{4,3,1,2,0:T(8,128)(2,1)S(1)} %bitcast.111) | data formatting | bytes 4194304 | tf_op jit(solution)/shard_map/transpose | solution.py:44
  5.4 4.1 %copy.27 = bf16[32,128,256]{2,1,0:T(8,128)(2,1)} copy(bf16[32,128,256]{1,2,0:T(8,128)(2,1)} %bitcast.112) | data formatting | bytes 4194304 | tf_op jit(solution)/shard_map/transpose | solution.py:46
  9.5 4.8 %copy.28 = bf16[256,16,256]{0,1,2:T(8,128)(2,1)} copy(bf16[256,16,256]{2,1,0:T(8,128)(2,1)} %bitcast.113) | data formatting | bytes 4194304 | tf_op jit(solution)/shard_map/reshape | solution.py:46
  14.5 1.1 fusion.145
  15.6 2.9 %fusion.73 = f32[256,384]{1,0:T(8,128)S(1)} fusion(bf16[256,16,256]{0,1,2:T(8,128)(2,1)} %copy.28, bf16[16,256,384]{2,0,1:T(8,128)(2,1)S(1)} %bitcast.110, f32[32,384]{1,0:T(8,128)S(1)} %fusion.145), kind=kOutput, calls=%fused_computation.68 | convolution fusion | flops 805404672 | bytes 5685248 | tf_op jit(solution)/shard_map/dot_general | solution.py:47
  18.6 2.6 %collective-permute-start.1 = (f32[256,384]{1,0:T(8,128)S(1)}, f32[256,384]{1,0:T(8,128)S(1)}, u32[]{:S(2)}, u32[]{:S(2)}) collective-permute-start(f32[256,384]{1,0:T(8,128)S(1)} %fusion.73), channel_id=1, source_target_pairs={{2,0},{4,2},{6,4},{8,6},{10,8},{12,10},{14,12},{16,14},{18,16},{20... | collective-permute-start | bytes 1179656 | tf_op jit(solution)/shard_map/ppermute | solution.py:19
  21.2 12.3 %collective-permute-done.1 = f32[256,384]{1,0:T(8,128)S(1)} collective-permute-done((f32[256,384]{1,0:T(8,128)S(1)}, f32[256,384]{1,0:T(8,128)S(1)}, u32[]{:S(2)}, u32[]{:S(2)}) %collective-permute-start.1) | collective-permute-done | bytes 393248 | tf_op jit(solution)/shard_map/ppermute | solution.py:19
  33.6 1.7 %collective-permute-start.2 = (bf16[256,384]{1,0:T(8,128)(2,1)S(1)}, bf16[256,384]{1,0:T(8,128)(2,1)}, u32[]{:S(2)}, u32[]{:S(2)}) collective-permute-start(bf16[256,384]{1,0:T(8,128)(2,1)S(1)} %get-tuple-element.25), channel_id=1, source_target_pairs={{0,1},{1,0},{2,3},{3,2},{4,5},{5,4},{6,7},{7,6},{8,9},{9,8},{10,11... | collective-permute-start | bytes 589832 | tf_op jit(solution)/shard_map/ppermute | solution.py:92
  35.3 4.6 %copy.31 = bf16[768,2048]{0,1:T(8,128)(2,1)} copy(bf16[768,2048]{1,0:T(8,128)(2,1)} %param.23) | data formatting | bytes 6291456 | tf_op args[11]
  40.0 1.5 slice_reduce_fusion.2
  41.5 1.1 fusion.101
  42.6 1.9 %collective-permute-done = bf16[256,384]{1,0:T(8,128)(2,1)S(1)} collective-permute-done((bf16[256,384]{1,0:T(8,128)(2,1)S(1)}, bf16[256,384]{1,0:T(8,128)(2,1)S(1)}, u32[]{:S(2)}, u32[]{:S(2)}) %collective-permute-start) | collective-permute-done | bytes 196640 | tf_op jit(solution)/shard_map/ppermute | solution.py:92
  44.6 0.9 copy-done.7
  45.4 0.9 constant_dynamic-update-slice_fusion.1
  46.4 0.9 constant_dynamic-update-slice_fusion
  47.3 1.6 %reduce_sum.108 = f32[512]{0:T(512)S(1)} reduce(f32[512,768]{1,0:T(8,128)} %constant_dynamic-update-slice_fusion, f32[]{:T(128)} %constant.70.clone.1), dimensions={1}, to_apply=%region_0.1 | reduce | flops 392704 | bytes 1574916 | tf_op jit(solution)/shard_map/reduce_sum | solution.py:29
  48.9 1.7 %multiply_reduce_fusion.2 = f32[512]{0:T(512)S(1)} fusion(f32[512,768]{1,0:T(8,128)} %constant_dynamic-update-slice_fusion, f32[512]{0:T(512)S(1)} %broadcast_multiply_fusion.1), kind=kLoop, calls=%fused_computation.47 | loop fusion | flops 1179136 | bytes 1576960 | tf_op jit(solution)/shard_map/reduce_sum | solution.py:31
  50.6 3.2 %fusion.59 = bf16[3,512,384]{1,2,0:T(8,128)(2,1)S(1)} fusion(bf16[1,3,768,384]{3,2,1,0:T(8,128)(2,1)} %param.19, f32[512,768]{1,0:T(8,128)} %constant_dynamic-update-slice_fusion, f32[768]{0:T(1024)S(1)} %get-tuple-element.19, f32[768]{0:T(1024)S(1)} %get-tuple-element.36, f32[512]{0:T(512)S(1)} %add_rsqrt_fusion, f32[512]{0:T(512)S(1)} %broadcast_multiply_fusion.1), kind=kOutput, calls=%fused_computation.53 | convolution fusion | flops 908525568 | bytes 4532224 | tf_op jit(solution)/shard_map/td,sde->ste/dot_general | solution.py:103
  53.8 0.8 fusion.140
  54.6 0.8 fusion.139
  55.4 3.9 %fusion.141 = (f32[6,256]{1,0:T(8,128)S(1)}, f32[6,256,512]{2,1,0:T(8,128)}) fusion(bf16[256,6,64]{0,2,1:T(8,128)(2,1)} %bitcast.127, bf16[512,6,64]{0,2,1:T(8,128)(2,1)} %bitcast.122), kind=kOutput, calls=%fused_computation.162 | convolution fusion | flops 103023104 | bytes 3741696 | tf_op jit(solution)/shard_map/sub | solution.py:122
  59.3 3.3 %fusion.75 = bf16[6,64,256]{2,1,0:T(8,128)(2,1)} fusion(bf16[512,6,64]{0,2,1:T(8,128)(2,1)S(1)} %bitcast.120, f32[6,256,512]{2,1,0:T(8,128)} %get-tuple-element.28, f32[6,256]{1,0:T(8,128)S(1)} %get-tuple-element.27), kind=kOutput, calls=%fused_computation.70 | convolution fusion | flops 102334464 | bytes 3741696 | tf_op jit(solution)/shard_map/hts,shd->thd/dot_general | solution.py:123
  62.6 1.4 collective-permute-start.4
  64.0 3.9 %fusion.142 = (f32[6,256]{1,0:T(8,128)S(1)}, f32[6,256,512]{2,1,0:T(8,128)}) fusion(bf16[256,6,64]{0,2,1:T(8,128)(2,1)} %bitcast.126, bf16[512,6,64]{0,2,1:T(8,128)(2,1)} %bitcast.123), kind=kOutput, calls=%fused_computation.163 | convolution fusion | flops 103023104 | bytes 3741696 | tf_op jit(solution)/shard_map/sub | solution.py:122
  67.9 2.6 %fusion.74 = bf16[6,64,256]{2,1,0:T(8,128)(2,1)S(1)} fusion(bf16[512,6,64]{0,2,1:T(8,128)(2,1)S(1)} %bitcast.121, f32[6,256,512]{2,1,0:T(8,128)} %get-tuple-element.30, f32[6,256]{1,0:T(8,128)S(1)} %get-tuple-element.29), kind=kOutput, calls=%fused_computation.69 | convolution fusion | flops 102334464 | bytes 3741696 | tf_op jit(solution)/shard_map/hts,shd->thd/dot_general | solution.py:123
  70.8 1.6 %fusion.72 = f32[256,768]{1,0:T(8,128)S(1)} fusion(bf16[256,384]{0,1:T(8,128)(2,1)} %bitcast.18, bf16[384,768]{1,0:T(8,128)(2,1)} %bitcast), kind=kOutput, calls=%fused_computation.66 | convolution fusion | flops 151388160 | bytes 1572864 | tf_op jit(solution)/shard_map/dot_general | solution.py:128
  72.4 1.5 fusion.68
  73.8 7.6 %collective-permute-done.4 = bf16[384,768]{1,0:T(8,128)(2,1)} collective-permute-done((bf16[384,768]{1,0:T(8,128)(2,1)}, bf16[384,768]{1,0:T(8,128)(2,1)}, u32[]{:S(2)}, u32[]{:S(2)}) %collective-permute-start.4) | collective-permute-done | bytes 589856 | tf_op jit(solution)/shard_map/ppermute | solution.py:99
  81.4 1.6 %fusion.144 = (f32[256]{0:T(256)S(1)}, f32[256,768]{1,0:T(8,128)S(1)}) fusion(f32[256,768]{1,0:T(8,128)S(1)} %copy-done.8, f32[256,768]{1,0:T(8,128)S(1)} %fusion.72, bf16[256,384]{0,1:T(8,128)(2,1)} %collective-permute-done.3, bf16[384,768]{1,0:T(8,128)(2,1)} %collective-permute-done.4), kind=kOutput, calls=%fused_computation.165 | convolution fusion | flops 151977728 | bytes 3146752 | tf_op jit(solution)/shard_map/dot_general | solution.py:129
  83.9 1.5 %fusion.143 = (f32[256]{0:T(256)S(1)}, f32[256,768]{1,0:T(8,128)S(1)}) fusion(f32[256,768]{1,0:T(8,128)S(1)} %copy-done.6, f32[256,768]{1,0:T(8,128)S(1)} %fusion.68, bf16[256,384]{0,1:T(8,128)(2,1)S(1)} %collective-permute-done.5, bf16[384,768]{1,0:T(8,128)(2,1)} %collective-permute-done.4), kind=kOutput, calls=%fused_computation.164 | convolution fusion | flops 151977728 | bytes 3146752 | tf_op jit(solution)/shard_map/dot_general | solution.py:129
  85.5 0.9 copy-done.1
  87.2 4.3 %fusion.62 = bf16[256,768]{1,0:T(8,128)(2,1)S(1)} fusion(bf16[1,1536,768]{2,1,0:T(8,128)(2,1)} %param.22, bf16[1,768,1536]{2,1,0:T(8,128)(2,1)} %param.21, f32[256,768]{1,0:T(8,128)} %copy-done.1, f32[768]{0:T(1024)} %get-tuple-element.18, f32[768]{0:T(1024)} %get-tuple-element.37, f32[256]{0:T(256)} %add_rsqrt_fusion.4, f32[256]{0:T(256)S(1)} %broadcast_multiply_fusion.5), kind=kOutput, calls=%fused_computation.54 | convolution fusion | flops 1212678144 | bytes 5906432 | tf_op jit(solution)/shard_map/dot_general | solution.py:138
  91.6 5.0 %fusion.12 = bf16[256,768]{1,0:T(8,128)(2,1)} fusion(bf16[1,1536,768]{2,1,0:T(8,128)(2,1)} %param.22, bf16[1,768,1536]{2,1,0:T(8,128)(2,1)} %param.21, f32[256,768]{1,0:T(8,128)} %copy-done.3, f32[256]{0:T(256)} %add_rsqrt_fusion.2, f32[256]{0:T(256)S(1)} %broadcast_multiply_fusion.3, f32[768]{0:T(1024)} %get-tuple-element.18, f32[768]{0:T(1024)} %get-tuple-element.37), kind=kOutput, calls=%fused_computation.16 | convolution fusion | flops 1212481536 | bytes 5906432 | tf_op jit(solution)/shard_map/dot_general | solution.py:138
  96.6 3.6 %collective-permute-done.6 = bf16[256,768]{1,0:T(8,128)(2,1)} collective-permute-done((bf16[256,768]{1,0:T(8,128)(2,1)S(1)}, bf16[256,768]{1,0:T(8,128)(2,1)}, u32[]{:S(2)}, u32[]{:S(2)}) %collective-permute-start.6) | collective-permute-done | bytes 393248 | tf_op jit(solution)/shard_map/ppermute | solution.py:24
  100.2 1.4 fusion.137
  101.7 1.3 multiply_reduce_fusion.5
  103.1 1.4 add_convert_fusion.3
  104.6 3.2 %collective-permute-start.8 = (bf16[256,768]{1,0:T(8,128)(2,1)S(1)}, bf16[256,768]{1,0:T(8,128)(2,1)S(1)}, u32[]{:S(2)}, u32[]{:S(2)}) collective-permute-start(bf16[256,768]{1,0:T(8,128)(2,1)S(1)} %add_convert_fusion.3), channel_id=1, source_target_pairs={{0,2},{2,4},{4,6},{6,8},{8,10},{10,12},{12,14},{14,16},{16,18},{18... | collective-permute-start | bytes 1179656 | tf_op jit(solution)/shard_map/ppermute | solution.py:19
  107.8 6.5 %collective-permute-done.7 = bf16[256,768]{1,0:T(8,128)(2,1)S(1)} collective-permute-done((bf16[256,768]{1,0:T(8,128)(2,1)S(1)}, bf16[256,768]{1,0:T(8,128)(2,1)S(1)}, u32[]{:S(2)}, u32[]{:S(2)}) %collective-permute-start.7) | collective-permute-done | bytes 393248 | tf_op jit(solution)/shard_map/ppermute | solution.py:24
  114.8 2.5 %fusion.53 = bf16[256,16,128]{2,0,1:T(8,128)(2,1)S(1)} fusion(bf16[16,128,768]{2,0,1:T(8,128)(2,1)S(1)} %bitcast.117, f32[256]{0:T(256)S(1)} %add_rsqrt_fusion.1, f32[256]{0:T(256)S(1)} %broadcast_multiply_fusion.2, f32[768]{0:T(1024)S(1)} %get-tuple-element.20, f32[768]{0:T(1024)S(1)} %get-tuple-element.35, f32[256,768]{1,0:T(8,128)S(1)} %copy-done.4, ...), kind=kOutput, calls=%fused_computation.51 | convolution fusion | flops 807600128 | bytes 5775360 | tf_op jit(solution)/shard_map/dot_general | solution.py:148
  117.3 2.5 %divide_convert_fusion.2 = bf16[256,16,128]{2,0,1:T(8,128)(2,1)S(1)} fusion(bf16[256,16,128]{2,0,1:T(8,128)(2,1)S(1)} %fusion.53, f32[]{:T(128)S(6)} %convert_element_type.166, s32[128]{0:T(128)S(1)} %get-tuple-element.40, s32[128]{0:T(128)S(1)} %get-tuple-element.41, s32[]{:T(128)S(6)} %mul.202, s32[256]{0:T(256)S(1)} %get-tuple-element.38, ...), kind=kOutput, calls=%fused_computation.25 | convolution fusion | flops 817889280 | bytes 5639560 | tf_op jit(solution)/shard_map/dot_general | solution.py:153
  119.8 1.6 %copy.34 = bf16[256,16,128]{2,1,0:T(8,128)(2,1)} copy(bf16[256,16,128]{2,0,1:T(8,128)(2,1)S(1)} %divide_convert_fusion.2) | data formatting | bytes 2097152 | tf_op jit(solution)/shard_map/convert_element_type | solution.py:170
  121.4 2.3 %copy.35 = bf16[32,128,128]{2,1,0:T(8,128)(2,1)} copy(bf16[32,128,128]{1,2,0:T(8,128)(2,1)} %bitcast.116) | data formatting | bytes 2097152 | tf_op jit(solution)/shard_map/transpose | solution.py:173
  123.7 25.3 %collective-permute-done.9 = bf16[4,8,8,16,128]{4,3,1,2,0:T(8,128)(2,1)S(1)} collective-permute-done((bf16[4,8,8,16,128]{4,3,1,2,0:T(8,128)(2,1)}, bf16[4,8,8,16,128]{4,3,1,2,0:T(8,128)(2,1)S(1)}, u32[]{:S(2)}, u32[]{:S(2)}) %collective-permute-start.9) | collective-permute-done | bytes 1048608 | tf_op jit(solution)/shard_map/ppermute | solution.py:175
  149.1 1.8 %maximum_select_fusion = bf16[4,16,8,16,128]{4,3,1,2,0:T(8,128)(2,1)S(1)} fusion(bf16[4,8,8,16,128]{4,3,1,2,0:T(8,128)(2,1)S(1)} %collective-permute-done.9, bf16[4,8,8,16,128]{4,3,1,2,0:T(8,128)(2,1)} %bitcast.115, pred[]{:T(512)S(6)} %eq.2), kind=kLoop, calls=%fused_computation.24 | loop fusion | flops 3145728 | bytes 4194305 | tf_op jit(solution)/shard_map/jit(_where)/select_n | solution.py:176
  150.9 1.9 %copy.36 = bf16[4,16,8,16,128]{4,3,2,1,0:T(8,128)(2,1)} copy(bf16[4,16,8,16,128]{4,3,1,2,0:T(8,128)(2,1)S(1)} %maximum_select_fusion) | data formatting | bytes 4194304 | tf_op jit(solution)/shard_map/jit(_where)/select_n | solution.py:176
  (56 shorter events, 3.3 us)
Async XLA Ops:
  0.0 15.6 %copy-start = (bf16[4096,384]{1,0:T(8,128)(2,1)S(1)}, bf16[4096,384]{1,0:T(8,128)(2,1)}, u32[]{:S(2)}) copy-start(bf16[4096,384]{1,0:T(8,128)(2,1)} %param.14) | copy-start | bytes 9437188
  15.6 5.6 %copy-start.11 = (bf16[512,384]{1,0:T(8,128)(2,1)S(1)}, bf16[512,384]{1,0:T(8,128)(2,1)}, u32[]{:S(2)}) copy-start(bf16[512,384]{1,0:T(8,128)(2,1)} %param.16) | copy-start | bytes 1179652
  18.6 14.9 %collective-permute-start.1 = (f32[256,384]{1,0:T(8,128)S(1)}, f32[256,384]{1,0:T(8,128)S(1)}, u32[]{:S(2)}, u32[]{:S(2)}) collective-permute-start(f32[256,384]{1,0:T(8,128)S(1)} %fusion.73), channel_id=1, source_target_pairs={{2,0},{4,2},{6,4},{8,6},{10,8},{12,10},{14,12},{16,14},{18,16},{20... | collective-permute-start | bytes 1179656 | tf_op jit(solution)/shard_map/ppermute | solution.py:19
  33.6 7.9 %collective-permute-start.2 = (bf16[256,384]{1,0:T(8,128)(2,1)S(1)}, bf16[256,384]{1,0:T(8,128)(2,1)}, u32[]{:S(2)}, u32[]{:S(2)}) collective-permute-start(bf16[256,384]{1,0:T(8,128)(2,1)S(1)} %get-tuple-element.25), channel_id=1, source_target_pairs={{0,1},{1,0},{2,3},{3,2},{4,5},{5,4},{6,7},{7,6},{8,9},{9,8},{10,11... | collective-permute-start | bytes 589832 | tf_op jit(solution)/shard_map/ppermute | solution.py:92
  40.0 4.5 %collective-permute-start = (bf16[256,384]{1,0:T(8,128)(2,1)S(1)}, bf16[256,384]{1,0:T(8,128)(2,1)S(1)}, u32[]{:S(2)}, u32[]{:S(2)}) collective-permute-start(bf16[256,384]{1,0:T(8,128)(2,1)S(1)} %get-tuple-element.26), channel_id=1, source_target_pairs={{0,1},{1,0},{2,3},{3,2},{4,5},{5,4},{6,7},{7,6},{8,9},{9,8},{10,11... | collective-permute-start | bytes 589832 | tf_op jit(solution)/shard_map/ppermute | solution.py:92
  42.6 3.8 %copy-start.5 = (f32[256,768]{1,0:T(8,128)}, f32[256,768]{1,0:T(8,128)S(1)}, u32[]{:S(2)}) copy-start(f32[256,768]{1,0:T(8,128)S(1)} %fusion.101) | copy-start | bytes 2359300
  44.6 0.9 copy-start.7
  62.6 11.3 %collective-permute-start.3 = (bf16[256,384]{0,1:T(8,128)(2,1)}, bf16[256,384]{0,1:T(8,128)(2,1)}, u32[]{:S(2)}, u32[]{:S(2)}) collective-permute-start(bf16[256,384]{0,1:T(8,128)(2,1)} %bitcast.18), channel_id=1, source_target_pairs={{0,1},{1,0},{2,3},{3,2},{4,5},{5,4},{6,7},{7,6},{8,9},{9,8},{10,11... | collective-permute-start | bytes 589832 | tf_op jit(solution)/shard_map/ppermute | solution.py:127
  62.6 18.8 %collective-permute-start.4 = (bf16[384,768]{1,0:T(8,128)(2,1)}, bf16[384,768]{1,0:T(8,128)(2,1)}, u32[]{:S(2)}, u32[]{:S(2)}) collective-permute-start(bf16[384,768]{1,0:T(8,128)(2,1)} %bitcast), channel_id=1, source_target_pairs={{0,1},{1,0},{2,3},{3,2},{4,5},{5,4},{6,7},{7,6},{8,9},{9,8},{10,11... | collective-permute-start | bytes 1769480 | tf_op jit(solution)/shard_map/ppermute | solution.py:99
  70.5 10.9 %copy-start.8 = (f32[256,768]{1,0:T(8,128)S(1)}, f32[256,768]{1,0:T(8,128)}, u32[]{:S(2)}) copy-start(f32[256,768]{1,0:T(8,128)} %copy-done.7) | copy-start | bytes 2359300
  70.5 13.4 %collective-permute-start.5 = (bf16[256,384]{0,1:T(8,128)(2,1)S(1)}, bf16[256,384]{0,1:T(8,128)(2,1)S(1)}, u32[]{:S(2)}, u32[]{:S(2)}) collective-permute-start(bf16[256,384]{0,1:T(8,128)(2,1)S(1)} %bitcast.124), channel_id=1, source_target_pairs={{0,1},{1,0},{2,3},{3,2},{4,5},{5,4},{6,7},{7,6},{8,9},{9,8},{10,11... | collective-permute-start | bytes 589832 | tf_op jit(solution)/shard_map/ppermute | solution.py:127
  73.8 10.1 %copy-start.6 = (f32[256,768]{1,0:T(8,128)S(1)}, f32[256,768]{1,0:T(8,128)}, u32[]{:S(2)}) copy-start(f32[256,768]{1,0:T(8,128)} %copy-done.5) | copy-start | bytes 2359300
  83.0 0.9 copy-start.3
  85.5 0.9 copy-start.1
  91.5 8.8 %collective-permute-start.6 = (bf16[256,768]{1,0:T(8,128)(2,1)S(1)}, bf16[256,768]{1,0:T(8,128)(2,1)}, u32[]{:S(2)}, u32[]{:S(2)}) collective-permute-start(bf16[256,768]{1,0:T(8,128)(2,1)S(1)} %fusion.62), channel_id=1, source_target_pairs={{0,1},{1,0},{2,3},{3,2},{4,5},{5,4},{6,7},{7,6},{8,9},{9,8},{10,11... | collective-permute-start | bytes 1179656 | tf_op jit(solution)/shard_map/ppermute | solution.py:24
  96.6 5.1 %copy-start.2 = (f32[256,768]{1,0:T(8,128)S(1)}, f32[256,768]{1,0:T(8,128)}, u32[]{:S(2)}) copy-start(f32[256,768]{1,0:T(8,128)} %copy-done.1) | copy-start | bytes 2359300
  101.7 2.8 %copy-start.10 = (bf16[256,768]{1,0:T(8,128)(2,1)S(1)}, bf16[256,768]{1,0:T(8,128)(2,1)}, u32[]{:S(2)}) copy-start(bf16[256,768]{1,0:T(8,128)(2,1)} %fusion.12) | copy-start | bytes 1179652
  101.7 12.6 %copy-start.4 = (f32[256,768]{1,0:T(8,128)S(1)}, f32[256,768]{1,0:T(8,128)}, u32[]{:S(2)}) copy-start(f32[256,768]{1,0:T(8,128)} %copy-done.3) | copy-start | bytes 2359300
  103.1 11.7 %copy-start.9 = (bf16[768,2048]{0,1:T(8,128)(2,1)S(1)}, bf16[768,2048]{0,1:T(8,128)(2,1)}, u32[]{:S(2)}) copy-start(bf16[768,2048]{0,1:T(8,128)(2,1)} %copy.31) | copy-start | bytes 9437188
  104.5 9.8 %collective-permute-start.7 = (bf16[256,768]{1,0:T(8,128)(2,1)S(1)}, bf16[256,768]{1,0:T(8,128)(2,1)S(1)}, u32[]{:S(2)}, u32[]{:S(2)}) collective-permute-start(bf16[256,768]{1,0:T(8,128)(2,1)S(1)} %copy-done.10), channel_id=1, source_target_pairs={{0,1},{1,0},{2,3},{3,2},{4,5},{5,4},{6,7},{7,6},{8,9},{9,8},{10,11... | collective-permute-start | bytes 1179656 | tf_op jit(solution)/shard_map/ppermute | solution.py:24
  104.6 12.7 %collective-permute-start.8 = (bf16[256,768]{1,0:T(8,128)(2,1)S(1)}, bf16[256,768]{1,0:T(8,128)(2,1)S(1)}, u32[]{:S(2)}, u32[]{:S(2)}) collective-permute-start(bf16[256,768]{1,0:T(8,128)(2,1)S(1)} %add_convert_fusion.3), channel_id=1, source_target_pairs={{0,2},{2,4},{4,6},{6,8},{8,10},{10,12},{12,14},{14,16},{16,18},{18... | collective-permute-start | bytes 1179656 | tf_op jit(solution)/shard_map/ppermute | solution.py:19
  123.7 25.3 %collective-permute-start.9 = (bf16[4,8,8,16,128]{4,3,1,2,0:T(8,128)(2,1)}, bf16[4,8,8,16,128]{4,3,1,2,0:T(8,128)(2,1)S(1)}, u32[]{:S(2)}, u32[]{:S(2)}) collective-permute-start(bf16[4,8,8,16,128]{4,3,1,2,0:T(8,128)(2,1)} %bitcast.114), channel_id=1, source_target_pairs={{0,1},{1,0},{2,3},{3,2},{4,5},{5,4},{6,7},{7,6},{8,9},{9,8},{10,11... | collective-permute-start | bytes 3145736 | tf_op jit(solution)/shard_map/ppermute | solution.py:175

commit v9 on v5

--- a/solution.py
+++ b/solution.py
@@ -80,13 +80,14 @@
     tile_index = lax.axis_index("tile")
     head_index = lax.axis_index("head")
     own_live = trace_mask.astype(jnp.bfloat16)
-    next_traces, next_live = from_behind((traces, own_live), "tile", -1)
+    other_w_out = lax.ppermute(w_out[0], "head", [(0, 1), (1, 0)])
     local_width = embed_voxel.shape[1]
     embed_by_depth = embed_voxel.reshape(PATCH * PATCH, PATCH, local_width).transpose(1, 0, 2)
     position = position.astype(jnp.float32)
+    own_embedded = embed_planes(traces, own_live, embed_by_depth, embed_mask)
+    next_embedded = from_behind(own_embedded, "tile", -1)
     halves = []
-    for rows, (amplitudes, live) in enumerate(((traces, own_live), (next_traces, next_live))):
-        embedded = embed_planes(amplitudes, live, embed_by_depth, embed_mask)
+    for rows, embedded in enumerate((own_embedded, next_embedded)):
         embedded = embedded + position[rows * half_tokens:(rows + 1) * half_tokens]
         embedded = embedded.astype(jnp.bfloat16)
         other_columns = lax.ppermute(embedded, "head", [(0, 1), (1, 0)])
@@ -97,14 +98,10 @@
         ).astype(jnp.float32))
     stream = jnp.concatenate(halves, 0)
     local_heads = w_qkv.shape[3] // HEAD_DIM
-    projected = jnp.concatenate([
-        jnp.einsum(
-            "td,sde->ste",
-            layer_norm(half, norm_gain[0], norm_bias[0]).astype(jnp.bfloat16),
-            w_qkv[0], preferred_element_type=jnp.float32,
-        ).astype(jnp.bfloat16)
-        for half in halves
-    ], 1)
+    normed = layer_norm(stream, norm_gain[0], norm_bias[0]).astype(jnp.bfloat16)
+    projected = jnp.einsum(
+        "td,sde->ste", normed, w_qkv[0], preferred_element_type=jnp.float32
+    ).astype(jnp.bfloat16)
     keys = projected[1].reshape(tokens, local_heads, HEAD_DIM)
     values = projected[2].reshape(tokens, local_heads, HEAD_DIM)
     inner_rows = w_decode.shape[1] // (PATCH * PATCH)
@@ -114,7 +111,6 @@
         .transpose(2, 0, 1, 3)
         .reshape(PATCH, cell_cols, -1)
     )
-    decoded_chunks = {}
     for chunk in (1, 0):
         span = slice(chunk * half_tokens, (chunk + 1) * half_tokens)
         query = projected[0][span].reshape(half_tokens, local_heads, HEAD_DIM)
@@ -126,33 +122,47 @@
             "hts,shd->thd", weights, values, preferred_element_type=jnp.float32
         ).astype(jnp.bfloat16)
         attended = attended.reshape(half_tokens, local_heads * HEAD_DIM)
-        partial_attention = jnp.dot(attended, w_out[0], preferred_element_type=jnp.float32)
-        part = stream[span] + partner_sum(partial_attention)
+        other_attended = lax.ppermute(attended, "head", [(0, 1), (1, 0)])
+        own_term = jnp.dot(attended, w_out[0], preferred_element_type=jnp.float32)
+        other_term = jnp.dot(other_attended, other_w_out, preferred_element_type=jnp.float32)
+        part = stream[span] + (
+            own_term.astype(jnp.bfloat16).astype(jnp.float32)
+            + other_term.astype(jnp.bfloat16).astype(jnp.float32)
+        )
         normed = layer_norm(part, norm_gain[1], norm_bias[1]).astype(jnp.bfloat16)
         hidden = jax.nn.gelu(
             jnp.dot(normed, w_up[0], preferred_element_type=jnp.float32), approximate=True
         ).astype(jnp.bfloat16)
         partial_forward = jnp.dot(hidden, w_down[0], preferred_element_type=jnp.float32)
         if chunk == 0:
-            decoded_chunks[1], partial_forward = lax.optimization_barrier(
-                (decoded_chunks[1], partial_forward)
+            sent_latent, partial_forward = lax.optimization_barrier(
+                (sent_latent, partial_forward)
             )
         part = part + partner_sum(partial_forward)
         latent = layer_norm(part, norm_gain[2 * LAYERS], norm_bias[2 * LAYERS]).astype(jnp.bfloat16)
-        decoded_chunks[chunk] = lax.dot_general(
-            latent, decode_by_depth, (((1,), (2,)), ((), ())),
-            preferred_element_type=jnp.float32,
-        ).astype(jnp.bfloat16)
-    upper_part = from_behind(decoded_chunks[1], "tile", 1)
-    lower_part = decoded_chunks[0]
+        if chunk == 1:
+            sent_latent = latent
+        else:
+            own_latent = latent
+    arrived_latent = from_behind(sent_latent, "tile", 1)
     later = (tile_index > 0).astype(jnp.float32)
     half_side = side // 2
-    pieces = []
     piece_planes = half_side // 2
     piece_tokens = piece_planes * side * side
+    pieces = []
+    gate = None
     for piece in range(half_side // piece_planes):
         span = slice(piece * piece_tokens, (piece + 1) * piece_tokens)
-        lower_piece = lower_part[span]
+        latents = (own_latent[span], arrived_latent[span])
+        if gate is not None:
+            gate, latents = lax.optimization_barrier((gate, latents))
+        lower_piece, upper_piece = [
+            lax.dot_general(
+                latent, decode_by_depth, (((1,), (2,)), ((), ())),
+                preferred_element_type=jnp.float32,
+            ).astype(jnp.bfloat16)
+            for latent in latents
+        ]
         shape = lower_piece.shape
         token_a = lax.broadcasted_iota(jnp.int32, shape, 0) // (side * side) + piece * piece_planes
         inner = lax.broadcasted_iota(jnp.int32, shape, 2) // PATCH
@@ -161,12 +171,13 @@
         upper_profile = profile_of(places + HALF)
         numerator = (
             lower_piece.astype(jnp.float32) * lower_profile
-            + upper_part[span].astype(jnp.float32) * upper_profile
+            + upper_piece.astype(jnp.float32) * upper_profile
         )
         denominator = lower_profile + later * upper_profile
         blended = (numerator / denominator).astype(jnp.bfloat16)
         arranged = blended.reshape(piece_planes * side, WIN, cell_cols)
         arranged = jnp.swapaxes(arranged, 1, 2).reshape(piece_planes, side, inner_rows, PATCH, WIN)
+        gate = arranged
         other_rows = lax.ppermute(arranged, "head", [(0, 1), (1, 0)])
         whole = jnp.where(
             head_index == 0,

time: 174 us -> 147 us (0.84)
  the two profiles are of different devices: /device:TPU:1 before, /device:TPU:126 now
where the time goes in v9:
time: 147 us; the launch traced here: 146 us
  matrix products  48 us (33%)
  waiting for transfers between devices  38.9 us (26%)
  local copies, waits for them, and re-layouts  29.2 us (20%)
  other arithmetic  17.8 us (12%)
  starting transfers between devices  11.6 us (8%)
    ppermute x2, waiting for transfers between devices, body(): other_columns = lax.ppermute(embedded, 'head', [(0, 1), (1, 0)])  17.6 us
    ppermute x2, waiting for transfers between devices, body(): other_rows = lax.ppermute(arranged, 'head', [(0, 1), (1, 0)])  11.5 us
    dot_general x4, matrix products, body(): lax.dot_general(latent, decode_by_depth, (((1,), (2,)), ((), ())), prefer...  10.5 us
    ppermute x2, waiting for transfers between devices, partner_sum(): other = lax.ppermute(rounded, 'head', [(0, 1), (1, 0)])  9.82 us
    dot_general x2, matrix products, body(): jnp.dot(hidden, w_down[0], preferred_element_type=jnp.float32)  9.32 us
    sub x2, matrix products, body(): weights = jax.nn.softmax(scores, axis=-1).astype(jnp.bfloat16)  9.01 us
    unnamed x57, local copies, waits for them, and re-layouts  8.76 us
    dot_general x2, matrix products, body(): jnp.einsum('hts,shd->thd', weights, values, preferred_element_type=jnp.fl...  6.58 us
  transfers between devices with their start and end apart: 11, of which 6 were waited for; matrix products, arithmetic and copies ran while one was open for 39% of the time, Pallas kernels for 0%

profile of v9, /device:TPU:126, one launch (start us, length us, event | category | flops | bytes accessed | tf_op | source)
XLA Modules:
  0.0 146.0 jit_solution(5598019761537093255)
XLA Ops:
  0.0 0.9 convert_element_type.144
  1.2 2.5 %broadcast_multiply_fusion = bf16[64,128,128]{2,1,0:T(8,128)(2,1)S(1)} fusion(bf16[64,128,128]{2,1,0:T(8,128)(2,1)} %param.12, bf16[64,128]{1,0:T(8,128)(2,1)S(1)} %convert_element_type.144), kind=kLoop, calls=%fused_computation.122 | loop fusion | flops 1048576 | bytes 4210688 | tf_op jit(solution)/shard_map/mul | solution.py:43
  3.7 1.9 %copy.30 = bf16[4,8,16,16,128]{4,3,2,1,0:T(8,128)(2,1)} copy(bf16[4,8,16,16,128]{4,3,1,2,0:T(8,128)(2,1)S(1)} %bitcast.126) | data formatting | bytes 4194304 | tf_op jit(solution)/shard_map/transpose | solution.py:44
  5.6 4.1 %copy.31 = bf16[32,128,256]{2,1,0:T(8,128)(2,1)} copy(bf16[32,128,256]{1,2,0:T(8,128)(2,1)} %bitcast.127) | data formatting | bytes 4194304 | tf_op jit(solution)/shard_map/transpose | solution.py:46
  9.7 4.9 %copy.32 = bf16[256,16,256]{0,1,2:T(8,128)(2,1)} copy(bf16[256,16,256]{2,1,0:T(8,128)(2,1)} %bitcast.128) | data formatting | bytes 4194304 | tf_op jit(solution)/shard_map/reshape | solution.py:46
  14.7 3.7 %fusion.113 = f32[256,384]{1,0:T(8,128)} fusion(bf16[256,16,256]{0,1,2:T(8,128)(2,1)} %copy.32, bf16[16,256,384]{2,0,1:T(8,128)(2,1)S(1)} %bitcast.125, f32[32,384]{1,0:T(8,128)S(1)} %fusion.213), kind=kOutput, calls=%fused_computation.88 | convolution fusion | flops 805404672 | bytes 5685248 | tf_op jit(solution)/shard_map/dot_general | solution.py:47
  18.4 2.2 %collective-permute-start.1 = (f32[256,384]{1,0:T(8,128)}, f32[256,384]{1,0:T(8,128)}, u32[]{:S(2)}, u32[]{:S(2)}) collective-permute-start(f32[256,384]{1,0:T(8,128)} %fusion.113), channel_id=1, source_target_pairs={{2,0},{4,2},{6,4},{8,6},{10,8},{12,10},{14,12},{16,14},{18,16},{20... | collective-permute-start | bytes 1179656 | tf_op jit(solution)/shard_map/ppermute | solution.py:19
  21.1 0.9 convert_element_type.145
  22.0 4.7 %copy.35 = bf16[768,2048]{0,1:T(8,128)(2,1)} copy(bf16[768,2048]{1,0:T(8,128)(2,1)} %param.23) | data formatting | bytes 6291456 | tf_op args[11]
  27.3 1.4 fusion.167
  28.8 1.7 %collective-permute-start.2 = (bf16[256,384]{1,0:T(8,128)(2,1)S(1)}, bf16[256,384]{1,0:T(8,128)(2,1)S(1)}, u32[]{:S(2)}, u32[]{:S(2)}) collective-permute-start(bf16[256,384]{1,0:T(8,128)(2,1)S(1)} %get-tuple-element.24), channel_id=1, source_target_pairs={{0,1},{1,0},{2,3},{3,2},{4,5},{5,4},{6,7},{7,6},{8,9},{9,8},{10,11... | collective-permute-start | bytes 589832 | tf_op jit(solution)/shard_map/ppermute | solution.py:93
  32.0 13.5 %collective-permute-done.2 = bf16[256,384]{1,0:T(8,128)(2,1)S(1)} collective-permute-done((bf16[256,384]{1,0:T(8,128)(2,1)S(1)}, bf16[256,384]{1,0:T(8,128)(2,1)S(1)}, u32[]{:S(2)}, u32[]{:S(2)}) %collective-permute-start.2) | collective-permute-done | bytes 196640 | tf_op jit(solution)/shard_map/ppermute | solution.py:93
  45.6 4.0 %collective-permute-done = bf16[256,384]{1,0:T(8,128)(2,1)S(1)} collective-permute-done((bf16[256,384]{1,0:T(8,128)(2,1)S(1)}, bf16[256,384]{1,0:T(8,128)(2,1)S(1)}, u32[]{:S(2)}, u32[]{:S(2)}) %collective-permute-start) | collective-permute-done | bytes 196640 | tf_op jit(solution)/shard_map/ppermute | solution.py:93
  50.9 1.3 fusion.57
  53.0 0.9 fusion.208
  53.9 4.5 %fusion.209 = (f32[6,256]{1,0:T(8,128)}, f32[6,256,512]{2,1,0:T(8,128)}) fusion(bf16[256,6,64]{0,2,1:T(8,128)(2,1)} %bitcast.147, bf16[512,6,64]{0,2,1:T(8,128)(2,1)} %bitcast.144), kind=kOutput, calls=%fused_computation.212 | convolution fusion | flops 103023104 | bytes 3741696 | tf_op jit(solution)/shard_map/sub | solution.py:120
  58.5 3.3 %fusion.114 = bf16[6,64,256]{2,1,0:T(8,128)(2,1)} fusion(bf16[512,6,64]{0,2,1:T(8,128)(2,1)} %bitcast.142, f32[6,256,512]{2,1,0:T(8,128)} %get-tuple-element.26, f32[6,256]{1,0:T(8,128)} %get-tuple-element.25), kind=kOutput, calls=%fused_computation.89 | convolution fusion | flops 102334464 | bytes 3741696 | tf_op jit(solution)/shard_map/hts,shd->thd/dot_general | solution.py:121
  62.1 4.5 %fusion.211 = (f32[6,256]{1,0:T(8,128)}, f32[6,256,512]{2,1,0:T(8,128)}) fusion(bf16[256,6,64]{0,2,1:T(8,128)(2,1)} %bitcast.146, bf16[512,6,64]{0,2,1:T(8,128)(2,1)} %bitcast.145), kind=kOutput, calls=%fused_computation.214 | convolution fusion | flops 103023104 | bytes 3741696 | tf_op jit(solution)/shard_map/sub | solution.py:120
  66.6 3.3 %fusion.115 = bf16[6,64,256]{2,1,0:T(8,128)(2,1)} fusion(bf16[512,6,64]{0,2,1:T(8,128)(2,1)} %bitcast.143, f32[6,256,512]{2,1,0:T(8,128)} %get-tuple-element.30, f32[6,256]{1,0:T(8,128)} %get-tuple-element.29), kind=kOutput, calls=%fused_computation.90 | convolution fusion | flops 102334464 | bytes 3741696 | tf_op jit(solution)/shard_map/hts,shd->thd/dot_general | solution.py:121
  69.9 1.6 %collective-permute-start.3 = (bf16[256,384]{0,1:T(8,128)(2,1)}, bf16[256,384]{0,1:T(8,128)(2,1)}, u32[]{:S(2)}, u32[]{:S(2)}) collective-permute-start(bf16[256,384]{0,1:T(8,128)(2,1)} %bitcast.17), channel_id=1, source_target_pairs={{0,1},{1,0},{2,3},{3,2},{4,5},{5,4},{6,7},{7,6},{8,9},{9,8},{10,11... | collective-permute-start | bytes 589832 | tf_op jit(solution)/shard_map/ppermute | solution.py:125
  71.6 1.6 %fusion.108 = f32[256,768]{1,0:T(8,128)S(1)} fusion(bf16[256,384]{0,1:T(8,128)(2,1)} %bitcast.22, bf16[1,384,768]{2,1,0:T(8,128)(2,1)} %param.20), kind=kOutput, calls=%fused_computation.80 | convolution fusion | flops 151388160 | bytes 1572864 | tf_op jit(solution)/shard_map/dot_general | solution.py:126
  73.1 2.4 %fusion.112 = f32[256,768]{1,0:T(8,128)} fusion(bf16[256,384]{0,1:T(8,128)(2,1)} %bitcast.17, bf16[1,384,768]{2,1,0:T(8,128)(2,1)} %param.20), kind=kOutput, calls=%fused_computation.86 | convolution fusion | flops 151388160 | bytes 1572864 | tf_op jit(solution)/shard_map/dot_general | solution.py:126
  75.6 1.7 %fusion.210 = (f32[256]{0:T(256)S(1)}, f32[256,768]{1,0:T(8,128)S(1)}) fusion(f32[256,768]{1,0:T(8,128)S(1)} %fusion.108, bf16[256,384]{0,1:T(8,128)(2,1)} %collective-permute-done.5, bf16[384,768]{1,0:T(8,128)(2,1)} %collective-permute-done.4, bf16[256,384]{1,0:T(8,128)(2,1)S(1)} %get-tuple-element.24, bf16[256,384]{1,0:T(8,128)(2,1)S(1)} %copy-done.14, ...), kind=kOutput, calls=%fused_computation.213 | convolution fusion | flops 153943808 | bytes 2753537 | tf_op jit(solution)/shard_map/dot_general | solution.py:127
  77.3 0.9 copy-done.3
  78.9 5.0 %fusion.102 = bf16[256,768]{1,0:T(8,128)(2,1)} fusion(bf16[1,1536,768]{2,1,0:T(8,128)(2,1)} %param.22, bf16[1,768,1536]{2,1,0:T(8,128)(2,1)} %param.21, f32[256,768]{1,0:T(8,128)} %copy-done.3, f32[768]{0:T(1024)} %get-tuple-element.16, f32[768]{0:T(1024)S(1)} %get-tuple-element.13, f32[256]{0:T(256)} %add_rsqrt_fusion.4, f32[256]{0:T(256)S(1)} %broadcast_multiply_fusion.5), kind=kOutput, calls=%fused_computation.74 | convolution fusion | flops 1212678144 | bytes 5906432 | tf_op jit(solution)/shard_map/dot_general | solution.py:136
  84.4 1.9 %fusion.212 = (f32[256]{0:T(256)S(1)}, f32[256,768]{1,0:T(8,128)S(1)}) fusion(f32[256,768]{1,0:T(8,128)} %fusion.112, bf16[256,384]{0,1:T(8,128)(2,1)} %collective-permute-done.3, bf16[384,768]{1,0:T(8,128)(2,1)} %collective-permute-done.4, bf16[256,384]{1,0:T(8,128)(2,1)S(1)} %get-tuple-element.23, bf16[256,384]{1,0:T(8,128)(2,1)S(1)} %copy-done.12, ...), kind=kOutput, calls=%fused_computation.215 | convolution fusion | flops 153943808 | bytes 2753537 | tf_op jit(solution)/shard_map/dot_general | solution.py:127
  86.2 0.9 copy-done.1
  87.9 4.3 %fusion.8 = bf16[256,768]{1,0:T(8,128)(2,1)S(1)} fusion(bf16[1,1536,768]{2,1,0:T(8,128)(2,1)} %param.22, bf16[1,768,1536]{2,1,0:T(8,128)(2,1)} %param.21, f32[256,768]{1,0:T(8,128)} %copy-done.1, f32[256]{0:T(256)} %add_rsqrt_fusion.2, f32[256]{0:T(256)S(1)} %broadcast_multiply_fusion.3, f32[768]{0:T(1024)} %get-tuple-element.16, f32[768]{0:T(1024)S(1)} %get-tuple-element.13), kind=kOutput, calls=%fused_computation.12 | convolution fusion | flops 1212481536 | bytes 5906432 | tf_op jit(solution)/shard_map/dot_general | solution.py:136
  92.2 2.6 %collective-permute-done.6 = bf16[256,768]{1,0:T(8,128)(2,1)} collective-permute-done((bf16[256,768]{1,0:T(8,128)(2,1)}, bf16[256,768]{1,0:T(8,128)(2,1)}, u32[]{:S(2)}, u32[]{:S(2)}) %collective-permute-start.6) | collective-permute-done | bytes 393248 | tf_op jit(solution)/shard_map/ppermute | solution.py:24
  94.8 1.6 %fusion.205 = f32[256]{0:T(256)S(1)} fusion(f32[256,768]{1,0:T(8,128)} %copy-done.3, bf16[256,768]{1,0:T(8,128)(2,1)} %collective-permute-done.6, bf16[256,768]{1,0:T(8,128)(2,1)} %fusion.102), kind=kLoop, calls=%fused_computation.208 | loop fusion | flops 982784 | bytes 1573888 | tf_op jit(solution)/shard_map/reduce_sum | solution.py:29
  96.4 1.4 multiply_reduce_fusion.5
  97.8 1.4 add_convert_fusion.3
  99.7 1.9 %collective-permute-start.8 = (bf16[256,768]{1,0:T(8,128)(2,1)S(1)}, bf16[256,768]{1,0:T(8,128)(2,1)S(1)}, u32[]{:S(2)}, u32[]{:S(2)}) collective-permute-start(bf16[256,768]{1,0:T(8,128)(2,1)S(1)} %add_convert_fusion.3), channel_id=1, source_target_pairs={{0,2},{2,4},{4,6},{6,8},{8,10},{10,12},{12,14},{14,16},{16,18},{18... | collective-permute-start | bytes 1179656 | tf_op jit(solution)/shard_map/ppermute | solution.py:19
  101.6 7.2 %collective-permute-done.7 = bf16[256,768]{1,0:T(8,128)(2,1)S(1)} collective-permute-done((bf16[256,768]{1,0:T(8,128)(2,1)S(1)}, bf16[256,768]{1,0:T(8,128)(2,1)S(1)}, u32[]{:S(2)}, u32[]{:S(2)}) %collective-permute-start.7) | collective-permute-done | bytes 393248 | tf_op jit(solution)/shard_map/ppermute | solution.py:24
  110.4 0.8 copy-done.5
  111.3 2.1 %fusion.78 = f32[128,16,128]{2,0,1:T(8,128)S(1)} fusion(bf16[16,128,768]{2,0,1:T(8,128)(2,1)S(1)} %bitcast.132, s32[128]{0:T(128)S(1)} %iota_shift-right-logical_fusion.1, s32[128]{0:T(128)S(1)} %copy-done.19, s32[]{:T(128)S(6)} %mul.218, s32[128]{0:T(128)S(1)} %iota_shift-right-logical_fusion, s32[128]{0:T(128)S(1)} %copy-done.18, ...), kind=kOutput, calls=%fused_computation.66 | convolution fusion | flops 406061056 | bytes 4393988 | tf_op jit(solution)/shard_map/dot_general | solution.py:160
  113.4 2.2 %divide_convert_fusion.9 = bf16[128,16,128]{2,0,1:T(8,128)(2,1)S(1)} fusion(f32[128,16,128]{2,0,1:T(8,128)S(1)} %fusion.78, bf16[16,128,768]{2,0,1:T(8,128)(2,1)S(1)} %bitcast.133, f32[]{:T(128)S(6)} %convert_element_type.184, s32[128]{0:T(128)S(1)} %iota_shift-right-logical_fusion.1, s32[128]{0:T(128)S(1)} %copy-done.19, s32[]{:T(128)S(6)} %mul.218, ...), kind=kOutput, calls=%fused_computation.121 | convolution fusion | flops 408420352 | bytes 4918280 | tf_op jit(solution)/shard_map/dot_general | solution.py:160
  115.6 1.1 copy.38
  116.7 2.0 %copy.39 = bf16[16,128,128]{2,1,0:T(8,128)(2,1)} copy(bf16[16,128,128]{1,2,0:T(8,128)(2,1)} %bitcast.139) | data formatting | bytes 1048576 | tf_op jit(solution)/shard_map/transpose | solution.py:179
  119.2 4.1 %fusion.99 = f32[128,16,128]{2,0,1:T(8,128)S(1)} fusion(bf16[16,128,768]{2,0,1:T(8,128)(2,1)} %bitcast.131, s32[128]{0:T(128)S(1)} %copy-done.21, s32[128]{0:T(128)S(1)} %copy-done.19, s32[]{:T(128)S(6)} %mul.218, s32[128]{0:T(128)S(1)} %copy-done.23, s32[128]{0:T(128)S(1)} %copy-done.18, pred[128]{0:T(512)(128)(4,1)S(1)} %copy-done.25, ...), kind=kOutput, calls=%fused_computation.73 | convolution fusion | flops 406323200 | bytes 4393220 | tf_op jit(solution)/shard_map/dot_general | solution.py:160
  123.3 2.2 %divide_convert_fusion.8 = bf16[128,16,128]{2,0,1:T(8,128)(2,1)S(1)} fusion(f32[128,16,128]{2,0,1:T(8,128)S(1)} %fusion.99, bf16[16,128,768]{2,0,1:T(8,128)(2,1)S(1)} %bitcast.134, f32[]{:T(128)S(6)} %convert_element_type.184, s32[128]{0:T(128)S(1)} %copy-done.21, s32[128]{0:T(128)S(1)} %copy-done.19, s32[]{:T(128)S(6)} %mul.218, s32[128]{0:T(128)S(1)} %copy-done.23, ...), kind=kOutput, calls=%fused_computation.120 | convolution fusion | flops 408682496 | bytes 4917512 | tf_op jit(solution)/shard_map/dot_general | solution.py:160
  125.5 1.1 copy.43
  126.6 2.0 %copy.44 = bf16[16,128,128]{2,1,0:T(8,128)(2,1)} copy(bf16[16,128,128]{1,2,0:T(8,128)(2,1)} %bitcast.140) | data formatting | bytes 1048576 | tf_op jit(solution)/shard_map/transpose | solution.py:179
  128.7 1.6 %collective-permute-start.10 = (bf16[2,8,8,16,128]{4,3,2,1,0:T(8,128)(2,1)}, bf16[2,8,8,16,128]{4,3,2,1,0:T(8,128)(2,1)S(1)}, u32[]{:S(2)}, u32[]{:S(2)}) collective-permute-start(bf16[2,8,8,16,128]{4,3,2,1,0:T(8,128)(2,1)} %bitcast.137), channel_id=1, source_target_pairs={{0,1},{1,0},{2,3},{3,2},{4,5},{5,4},{6,7},{7,6},{8,9},{9,8},{10,11... | collective-permute-start | bytes 1572872 | tf_op jit(solution)/shard_map/ppermute | solution.py:181
  130.3 2.0 %collective-permute-done.9 = bf16[2,8,8,16,128]{4,3,2,1,0:T(8,128)(2,1)} collective-permute-done((bf16[2,8,8,16,128]{4,3,2,1,0:T(8,128)(2,1)}, bf16[2,8,8,16,128]{4,3,2,1,0:T(8,128)(2,1)}, u32[]{:S(2)}, u32[]{:S(2)}) %collective-permute-start.9) | collective-permute-done | bytes 524320 | tf_op jit(solution)/shard_map/ppermute | solution.py:181
  132.3 9.5 %collective-permute-done.10 = bf16[2,8,8,16,128]{4,3,2,1,0:T(8,128)(2,1)S(1)} collective-permute-done((bf16[2,8,8,16,128]{4,3,2,1,0:T(8,128)(2,1)}, bf16[2,8,8,16,128]{4,3,2,1,0:T(8,128)(2,1)S(1)}, u32[]{:S(2)}, u32[]{:S(2)}) %collective-permute-start.10) | collective-permute-done | bytes 524320 | tf_op jit(solution)/shard_map/ppermute | solution.py:181
  141.8 2.1 %fusion.141 = (bf16[2,16,8,16,128]{4,3,1,2,0:T(8,128)(2,1)S(1)}, bf16[2,16,8,16,128]{4,3,1,2,0:T(8,128)(2,1)S(1)}) fusion(bf16[2,8,8,16,128]{4,3,2,1,0:T(8,128)(2,1)} %collective-permute-done.9, bf16[2,8,8,16,128]{4,3,2,1,0:T(8,128)(2,1)} %bitcast.136, pred[]{:T(512)S(6)} %eq.2, bf16[2,8,8,16,128]{4,3,2,1,0:T(8,128)(2,1)} %bitcast.138, ...), kind=kLoop, calls=%fused_computation.117 | loop fusion | flops 3145728 | bytes 4194305 | tf_op jit(solution)/shard_map/transpose | solution.py:187
  144.5 1.5 %pad_maximum_fusion = bf16[64,128,128]{2,1,0:T(8,128)(2,1)} fusion(bf16[32,128,128]{2,1,0:T(8,128)(2,1)S(1)} %bitcast.130, bf16[32,128,128]{2,1,0:T(8,128)(2,1)S(1)} %bitcast.129), kind=kLoop, calls=%fused_computation.20 | loop fusion | flops 1048576 | bytes 4194304 | tf_op jit(solution)/shard_map/concatenate | solution.py:188
  (102 shorter events, 10.6 us)
Async XLA Ops:
  0.0 14.7 %copy-start = (bf16[4096,384]{1,0:T(8,128)(2,1)S(1)}, bf16[4096,384]{1,0:T(8,128)(2,1)}, u32[]{:S(2)}) copy-start(bf16[4096,384]{1,0:T(8,128)(2,1)} %param.14) | copy-start | bytes 9437188
  9.7 4.9 %copy-start.10 = (bf16[256,384]{1,0:T(8,128)(2,1)S(1)}, bf16[256,384]{1,0:T(8,128)(2,1)}, u32[]{:S(2)}) copy-start(bf16[256,384]{1,0:T(8,128)(2,1)} %param.15) | copy-start | bytes 589828
  14.7 6.3 %copy-start.8 = (bf16[512,384]{1,0:T(8,128)(2,1)S(1)}, bf16[512,384]{1,0:T(8,128)(2,1)}, u32[]{:S(2)}) copy-start(bf16[512,384]{1,0:T(8,128)(2,1)} %param.16) | copy-start | bytes 1179652
  18.4 8.9 %collective-permute-start.1 = (f32[256,384]{1,0:T(8,128)}, f32[256,384]{1,0:T(8,128)}, u32[]{:S(2)}, u32[]{:S(2)}) collective-permute-start(f32[256,384]{1,0:T(8,128)} %fusion.113), channel_id=1, source_target_pairs={{2,0},{4,2},{6,4},{8,6},{10,8},{12,10},{14,12},{16,14},{18,16},{20... | collective-permute-start | bytes 1179656 | tf_op jit(solution)/shard_map/ppermute | solution.py:19
  20.6 55.0 %collective-permute-start.4 = (bf16[384,768]{1,0:T(8,128)(2,1)}, bf16[384,768]{1,0:T(8,128)(2,1)}, u32[]{:S(2)}, u32[]{:S(2)}) collective-permute-start(bf16[384,768]{1,0:T(8,128)(2,1)} %bitcast.18), channel_id=1, source_target_pairs={{0,1},{1,0},{2,3},{3,2},{4,5},{5,4},{6,7},{7,6},{8,9},{9,8},{10,11... | collective-permute-start | bytes 1769480 | tf_op jit(solution)/shard_map/ppermute | solution.py:83
  22.0 4.7 %copy-start.15 = (f32[3,768]{1,0:T(4,128)S(1)}, f32[3,768]{1,0:T(4,128)}, u32[]{:S(2)}) copy-start(f32[3,768]{1,0:T(4,128)} %param.17) | copy-start | bytes 27652
  22.0 4.7 %copy-start.16 = (f32[3,768]{1,0:T(4,128)S(1)}, f32[3,768]{1,0:T(4,128)}, u32[]{:S(2)}) copy-start(f32[3,768]{1,0:T(4,128)} %param.18) | copy-start | bytes 27652
  28.8 16.7 %collective-permute-start.2 = (bf16[256,384]{1,0:T(8,128)(2,1)S(1)}, bf16[256,384]{1,0:T(8,128)(2,1)S(1)}, u32[]{:S(2)}, u32[]{:S(2)}) collective-permute-start(bf16[256,384]{1,0:T(8,128)(2,1)S(1)} %get-tuple-element.24), channel_id=1, source_target_pairs={{0,1},{1,0},{2,3},{3,2},{4,5},{5,4},{6,7},{7,6},{8,9},{9,8},{10,11... | collective-permute-start | bytes 589832 | tf_op jit(solution)/shard_map/ppermute | solution.py:93
  31.0 18.6 %collective-permute-start = (bf16[256,384]{1,0:T(8,128)(2,1)S(1)}, bf16[256,384]{1,0:T(8,128)(2,1)S(1)}, u32[]{:S(2)}, u32[]{:S(2)}) collective-permute-start(bf16[256,384]{1,0:T(8,128)(2,1)S(1)} %get-tuple-element.23), channel_id=1, source_target_pairs={{0,1},{1,0},{2,3},{3,2},{4,5},{5,4},{6,7},{7,6},{8,9},{9,8},{10,11... | collective-permute-start | bytes 589832 | tf_op jit(solution)/shard_map/ppermute | solution.py:93
  45.5 4.1 %copy-start.13 = (bf16[256,384]{1,0:T(8,128)(2,1)}, bf16[256,384]{1,0:T(8,128)(2,1)S(1)}, u32[]{:S(2)}) copy-start(bf16[256,384]{1,0:T(8,128)(2,1)S(1)} %collective-permute-done.2) | copy-start | bytes 589828
  45.6 5.3 %copy-start.17 = (bf16[1,3,768,384]{3,2,1,0:T(8,128)(2,1)S(1)}, bf16[1,3,768,384]{3,2,1,0:T(8,128)(2,1)}, u32[]{:S(2)}) copy-start(bf16[1,3,768,384]{3,2,1,0:T(8,128)(2,1)} %param.19) | copy-start | bytes 5308420
  49.6 0.7 copy-start.11
  61.7 13.8 %collective-permute-start.5 = (bf16[256,384]{0,1:T(8,128)(2,1)}, bf16[256,384]{0,1:T(8,128)(2,1)}, u32[]{:S(2)}, u32[]{:S(2)}) collective-permute-start(bf16[256,384]{0,1:T(8,128)(2,1)} %bitcast.22), channel_id=1, source_target_pairs={{0,1},{1,0},{2,3},{3,2},{4,5},{5,4},{6,7},{7,6},{8,9},{9,8},{10,11... | collective-permute-start | bytes 589832 | tf_op jit(solution)/shard_map/ppermute | solution.py:125
  69.9 5.7 %copy-start.14 = (bf16[256,384]{1,0:T(8,128)(2,1)S(1)}, bf16[256,384]{1,0:T(8,128)(2,1)}, u32[]{:S(2)}) copy-start(bf16[256,384]{1,0:T(8,128)(2,1)} %copy-done.13) | copy-start | bytes 589828
  69.9 14.4 %collective-permute-start.3 = (bf16[256,384]{0,1:T(8,128)(2,1)}, bf16[256,384]{0,1:T(8,128)(2,1)}, u32[]{:S(2)}, u32[]{:S(2)}) collective-permute-start(bf16[256,384]{0,1:T(8,128)(2,1)} %bitcast.17), channel_id=1, source_target_pairs={{0,1},{1,0},{2,3},{3,2},{4,5},{5,4},{6,7},{7,6},{8,9},{9,8},{10,11... | collective-permute-start | bytes 589832 | tf_op jit(solution)/shard_map/ppermute | solution.py:125
  77.2 0.9 copy-start.3
  78.9 5.4 %copy-start.12 = (bf16[256,384]{1,0:T(8,128)(2,1)S(1)}, bf16[256,384]{1,0:T(8,128)(2,1)}, u32[]{:S(2)}) copy-start(bf16[256,384]{1,0:T(8,128)(2,1)} %copy-done.11) | copy-start | bytes 589828
  84.0 10.8 %collective-permute-start.6 = (bf16[256,768]{1,0:T(8,128)(2,1)}, bf16[256,768]{1,0:T(8,128)(2,1)}, u32[]{:S(2)}, u32[]{:S(2)}) collective-permute-start(bf16[256,768]{1,0:T(8,128)(2,1)} %fusion.102), channel_id=1, source_target_pairs={{0,1},{1,0},{2,3},{3,2},{4,5},{5,4},{6,7},{7,6},{8,9},{9,8},{10,11... | collective-permute-start | bytes 1179656 | tf_op jit(solution)/shard_map/ppermute | solution.py:24
  86.2 0.9 copy-start.1
  92.2 4.2 %copy-start.4 = (f32[256,768]{1,0:T(8,128)S(1)}, f32[256,768]{1,0:T(8,128)}, u32[]{:S(2)}) copy-start(f32[256,768]{1,0:T(8,128)} %copy-done.3) | copy-start | bytes 2359300
  96.3 12.5 %copy-start.2 = (f32[256,768]{1,0:T(8,128)S(1)}, f32[256,768]{1,0:T(8,128)}, u32[]{:S(2)}) copy-start(f32[256,768]{1,0:T(8,128)} %copy-done.1) | copy-start | bytes 2359300
  99.2 9.7 %collective-permute-start.7 = (bf16[256,768]{1,0:T(8,128)(2,1)S(1)}, bf16[256,768]{1,0:T(8,128)(2,1)S(1)}, u32[]{:S(2)}, u32[]{:S(2)}) collective-permute-start(bf16[256,768]{1,0:T(8,128)(2,1)S(1)} %fusion.8), channel_id=1, source_target_pairs={{0,1},{1,0},{2,3},{3,2},{4,5},{5,4},{6,7},{7,6},{8,9},{9,8},{10,11... | collective-permute-start | bytes 1179656 | tf_op jit(solution)/shard_map/ppermute | solution.py:24
  99.6 13.7 %copy-start.20 = (s32[128]{0:T(128)}, s32[128]{0:T(128)S(1)}, u32[]{:S(2)}) copy-start(s32[128]{0:T(128)S(1)} %iota_shift-right-logical_fusion.1) | copy-start | bytes 1540
  99.6 13.7 %copy-start.22 = (s32[128]{0:T(128)}, s32[128]{0:T(128)S(1)}, u32[]{:S(2)}) copy-start(s32[128]{0:T(128)S(1)} %iota_shift-right-logical_fusion) | copy-start | bytes 1540
  99.7 13.7 %copy-start.24 = (pred[128]{0:T(512)(128)(4,1)}, pred[128]{0:T(512)(128)(4,1)S(1)}, u32[]{:S(2)}) copy-start(pred[128]{0:T(512)(128)(4,1)S(1)} %compare_and_fusion.1) | copy-start | bytes 388
  99.7 13.7 %copy-start.26 = (pred[128]{0:T(512)(128)(4,1)}, pred[128]{0:T(512)(128)(4,1)S(1)}, u32[]{:S(2)}) copy-start(pred[128]{0:T(512)(128)(4,1)S(1)} %compare_and_fusion) | copy-start | bytes 388
  99.7 10.0 %collective-permute-start.8 = (bf16[256,768]{1,0:T(8,128)(2,1)S(1)}, bf16[256,768]{1,0:T(8,128)(2,1)S(1)}, u32[]{:S(2)}, u32[]{:S(2)}) collective-permute-start(bf16[256,768]{1,0:T(8,128)(2,1)S(1)} %add_convert_fusion.3), channel_id=1, source_target_pairs={{0,2},{2,4},{4,6},{6,8},{8,10},{10,12},{12,14},{14,16},{16,18},{18... | collective-permute-start | bytes 1179656 | tf_op jit(solution)/shard_map/ppermute | solution.py:19
  109.1 2.2 %copy-start.5 = (bf16[768,2048]{0,1:T(8,128)(2,1)S(1)}, bf16[768,2048]{0,1:T(8,128)(2,1)}, u32[]{:S(2)}) copy-start(bf16[768,2048]{0,1:T(8,128)(2,1)} %copy.35) | copy-start | bytes 9437188
  109.1 2.2 %copy-start.18 = (s32[128]{0:T(128)S(1)}, s32[128]{0:T(128)}, u32[]{:S(2)}) copy-start(s32[128]{0:T(128)} %broadcast_add_fusion.1) | copy-start | bytes 1540
  109.1 2.2 %copy-start.19 = (s32[128]{0:T(128)S(1)}, s32[128]{0:T(128)}, u32[]{:S(2)}) copy-start(s32[128]{0:T(128)} %broadcast_add_fusion) | copy-start | bytes 1540
  109.6 3.7 %copy-start.7 = (bf16[256,768]{1,0:T(8,128)(2,1)}, bf16[256,768]{1,0:T(8,128)(2,1)S(1)}, u32[]{:S(2)}) copy-start(bf16[256,768]{1,0:T(8,128)(2,1)S(1)} %add_convert_fusion.1) | copy-start | bytes 1179652
  109.7 0.8 copy-start.9
  115.5 3.6 %slice-start.1 = ((bf16[256,768]{1,0:T(8,128)(2,1)}), bf16[128,768]{1,0:T(8,128)(2,1)S(1)}, s32[]{:S(2)}) async-start(bf16[256,768]{1,0:T(8,128)(2,1)} %copy-done.9), calls=%async_computation.1 | async-start | bytes 393216 | tf_op jit(solution)/shard_map/slice | solution.py:156
  115.6 3.6 %copy-start.21 = (s32[128]{0:T(128)S(1)}, s32[128]{0:T(128)}, u32[]{:S(2)}) copy-start(s32[128]{0:T(128)} %copy-done.20) | copy-start | bytes 1540
  115.6 3.6 %copy-start.23 = (s32[128]{0:T(128)S(1)}, s32[128]{0:T(128)}, u32[]{:S(2)}) copy-start(s32[128]{0:T(128)} %copy-done.22) | copy-start | bytes 1540
  115.6 3.6 %copy-start.25 = (pred[128]{0:T(512)(128)(4,1)S(1)}, pred[128]{0:T(512)(128)(4,1)}, u32[]{:S(2)}) copy-start(pred[128]{0:T(512)(128)(4,1)} %copy-done.24) | copy-start | bytes 388
  115.6 3.6 %copy-start.27 = (pred[128]{0:T(512)(128)(4,1)S(1)}, pred[128]{0:T(512)(128)(4,1)}, u32[]{:S(2)}) copy-start(pred[128]{0:T(512)(128)(4,1)} %copy-done.26) | copy-start | bytes 388
  118.8 13.5 %collective-permute-start.9 = (bf16[2,8,8,16,128]{4,3,2,1,0:T(8,128)(2,1)}, bf16[2,8,8,16,128]{4,3,2,1,0:T(8,128)(2,1)}, u32[]{:S(2)}, u32[]{:S(2)}) collective-permute-start(bf16[2,8,8,16,128]{4,3,2,1,0:T(8,128)(2,1)} %bitcast.135), channel_id=1, source_target_pairs={{0,1},{1,0},{2,3},{3,2},{4,5},{5,4},{6,7},{7,6},{8,9},{9,8},{10,11... | collective-permute-start | bytes 1572872 | tf_op jit(solution)/shard_map/ppermute | solution.py:181
  119.2 4.1 %copy-start.6 = (bf16[768,2048]{0,1:T(8,128)(2,1)S(1)}, bf16[768,2048]{0,1:T(8,128)(2,1)}, u32[]{:S(2)}) copy-start(bf16[768,2048]{0,1:T(8,128)(2,1)} %copy.35) | copy-start | bytes 9437188
  119.2 4.1 %slice-start = ((bf16[256,768]{1,0:T(8,128)(2,1)}), bf16[128,768]{1,0:T(8,128)(2,1)S(1)}, s32[]{:S(2)}) async-start(bf16[256,768]{1,0:T(8,128)(2,1)} %copy-done.7), calls=%async_computation | async-start | bytes 393216 | tf_op jit(solution)/shard_map/slice | solution.py:156
  128.7 13.1 %collective-permute-start.10 = (bf16[2,8,8,16,128]{4,3,2,1,0:T(8,128)(2,1)}, bf16[2,8,8,16,128]{4,3,2,1,0:T(8,128)(2,1)S(1)}, u32[]{:S(2)}, u32[]{:S(2)}) collective-permute-start(bf16[2,8,8,16,128]{4,3,2,1,0:T(8,128)(2,1)} %bitcast.137), channel_id=1, source_target_pairs={{0,1},{1,0},{2,3},{3,2},{4,5},{5,4},{6,7},{7,6},{8,9},{9,8},{10,11... | collective-permute-start | bytes 1572872 | tf_op jit(solution)/shard_map/ppermute | solution.py:181

commit v10 on v9

--- a/solution.py
+++ b/solution.py
@@ -147,7 +147,7 @@
     arrived_latent = from_behind(sent_latent, "tile", 1)
     later = (tile_index > 0).astype(jnp.float32)
     half_side = side // 2
-    piece_planes = half_side // 2
+    piece_planes = half_side // 4
     piece_tokens = piece_planes * side * side
     pieces = []
     gate = None

time: 147 us -> 163 us (1.11)
  matrix products: 48 us -> 58.3 us
  local copies, waits for them, and re-layouts: 29.2 us -> 33.9 us
  starting transfers between devices: 11.6 us -> 14.2 us
    dot_general x4 -> x8, matrix products: 10.5 us -> 21.8 us  [body(): lax.dot_general(latent, decode_by_depth, (((1,), (2,)), ((), ())), prefer...]
    ppermute x2 -> x4, waiting for transfers between devices: 11.5 us -> 7.6 us  [body(): other_rows = lax.ppermute(arranged, 'head', [(0, 1), (1, 0)])]
    ppermute x2, waiting for transfers between devices: 9.82 us -> 13.4 us  [partner_sum(): other = lax.ppermute(rounded, 'head', [(0, 1), (1, 0)])]
    transpose x2 -> x4, local copies, waits for them, and re-layouts: 4.07 us -> 6.49 us  [body(): jnp.swapaxes(arranged, 1, 2)]
    slice x4 -> x2, local copies, waits for them, and re-layouts: 0.01 us -> 2.39 us  [body(): latents = (own_latent[span], arrived_latent[span])]
    ppermute x2 -> x4, starting transfers between devices: 2.03 us -> 4.35 us  [body(): other_rows = lax.ppermute(arranged, 'head', [(0, 1), (1, 0)])]
    convert_element_type x2 -> x4, local copies, waits for them, and re-layouts: 2.27 us -> 3.53 us  [body(): blended = (numerator / denominator).astype(jnp.bfloat16)]
    unnamed x57 -> x67, local copies, waits for them, and re-layouts: 8.76 us -> 7.89 us
  transfers between devices with their start and end apart: 11 -> 13, of which waited for: 6 -> 6; matrix products, arithmetic and copies ran while one was open for 39% -> 43% of each run, Pallas kernels for 0% -> 0%
where the time goes in v10:
time: 163 us
  matrix products  58.3 us (36%)
  waiting for transfers between devices  38.5 us (24%)
  local copies, waits for them, and re-layouts  33.9 us (21%)
  other arithmetic  16.9 us (10%)
  starting transfers between devices  14.2 us (9%)
    dot_general x8, matrix products, body(): lax.dot_general(latent, decode_by_depth, (((1,), (2,)), ((), ())), prefer...  21.8 us
    ppermute x2, waiting for transfers between devices, body(): other_columns = lax.ppermute(embedded, 'head', [(0, 1), (1, 0)])  17.6 us
    ppermute x2, waiting for transfers between devices, partner_sum(): other = lax.ppermute(rounded, 'head', [(0, 1), (1, 0)])  13.4 us
    dot_general x2, matrix products, body(): jnp.dot(hidden, w_down[0], preferred_element_type=jnp.float32)  9.28 us
    sub x2, matrix products, body(): weights = jax.nn.softmax(scores, axis=-1).astype(jnp.bfloat16)  9.01 us
    unnamed x67, local copies, waits for them, and re-layouts  7.89 us
    ppermute x4, waiting for transfers between devices, body(): other_rows = lax.ppermute(arranged, 'head', [(0, 1), (1, 0)])  7.6 us
    transpose x4, local copies, waits for them, and re-layouts, body(): jnp.swapaxes(arranged, 1, 2)  6.49 us
  transfers between devices with their start and end apart: 13, of which 6 were waited for; matrix products, arithmetic and copies ran while one was open for 43% of the time, Pallas kernels for 0%

profile of v10, /device:TPU:126, one launch (start us, length us, event | category | flops | bytes accessed | tf_op | source)
XLA Modules:
  0.0 162.5 jit_solution(11807387344881712776)
XLA Ops:
  1.1 2.5 %broadcast_multiply_fusion = bf16[64,128,128]{2,1,0:T(8,128)(2,1)S(1)} fusion(bf16[64,128,128]{2,1,0:T(8,128)(2,1)} %param.12, bf16[64,128]{1,0:T(8,128)(2,1)S(1)} %convert_element_type.180), kind=kLoop, calls=%fused_computation.109 | loop fusion | flops 1048576 | bytes 4210688 | tf_op jit(solution)/shard_map/mul | solution.py:43
  3.5 1.9 %copy.38 = bf16[4,8,16,16,128]{4,3,2,1,0:T(8,128)(2,1)} copy(bf16[4,8,16,16,128]{4,3,1,2,0:T(8,128)(2,1)S(1)} %bitcast.152) | data formatting | bytes 4194304 | tf_op jit(solution)/shard_map/transpose | solution.py:44
  5.4 4.1 %copy.39 = bf16[32,128,256]{2,1,0:T(8,128)(2,1)} copy(bf16[32,128,256]{1,2,0:T(8,128)(2,1)} %bitcast.153) | data formatting | bytes 4194304 | tf_op jit(solution)/shard_map/transpose | solution.py:46
  9.5 4.8 %copy.40 = bf16[256,16,256]{0,1,2:T(8,128)(2,1)} copy(bf16[256,16,256]{2,1,0:T(8,128)(2,1)} %bitcast.154) | data formatting | bytes 4194304 | tf_op jit(solution)/shard_map/reshape | solution.py:46
  15.6 3.7 %fusion.91 = f32[256,384]{1,0:T(8,128)} fusion(bf16[256,16,256]{0,1,2:T(8,128)(2,1)} %copy.40, bf16[16,256,384]{2,0,1:T(8,128)(2,1)S(1)} %bitcast.151, f32[32,384]{1,0:T(8,128)S(1)} %fusion.229), kind=kOutput, calls=%fused_computation.106 | convolution fusion | flops 805404672 | bytes 5685248 | tf_op jit(solution)/shard_map/dot_general | solution.py:47
  19.3 2.2 %collective-permute-start.1 = (f32[256,384]{1,0:T(8,128)}, f32[256,384]{1,0:T(8,128)}, u32[]{:S(2)}, u32[]{:S(2)}) collective-permute-start(f32[256,384]{1,0:T(8,128)} %fusion.91), channel_id=1, source_target_pairs={{2,0},{4,2},{6,4},{8,6},{10,8},{12,10},{14,12},{16,14},{18,16},{20... | collective-permute-start | bytes 1179656 | tf_op jit(solution)/shard_map/ppermute | solution.py:19
  22.9 4.7 %copy.43 = bf16[768,2048]{0,1:T(8,128)(2,1)} copy(bf16[768,2048]{1,0:T(8,128)(2,1)} %param.23) | data formatting | bytes 6291456 | tf_op args[11]
  28.2 1.4 fusion.177
  29.6 1.7 %collective-permute-start = (bf16[256,384]{1,0:T(8,128)(2,1)S(1)}, bf16[256,384]{1,0:T(8,128)(2,1)S(1)}, u32[]{:S(2)}, u32[]{:S(2)}) collective-permute-start(bf16[256,384]{1,0:T(8,128)(2,1)S(1)} %get-tuple-element.31), channel_id=1, source_target_pairs={{0,1},{1,0},{2,3},{3,2},{4,5},{5,4},{6,7},{7,6},{8,9},{9,8},{10,11... | collective-permute-start | bytes 589832 | tf_op jit(solution)/shard_map/ppermute | solution.py:93
  32.9 13.5 %collective-permute-done = bf16[256,384]{1,0:T(8,128)(2,1)S(1)} collective-permute-done((bf16[256,384]{1,0:T(8,128)(2,1)S(1)}, bf16[256,384]{1,0:T(8,128)(2,1)S(1)}, u32[]{:S(2)}, u32[]{:S(2)}) %collective-permute-start) | collective-permute-done | bytes 196640 | tf_op jit(solution)/shard_map/ppermute | solution.py:93
  46.5 4.0 %collective-permute-done.2 = bf16[256,384]{1,0:T(8,128)(2,1)S(1)} collective-permute-done((bf16[256,384]{1,0:T(8,128)(2,1)S(1)}, bf16[256,384]{1,0:T(8,128)(2,1)S(1)}, u32[]{:S(2)}, u32[]{:S(2)}) %collective-permute-start.2) | collective-permute-done | bytes 196640 | tf_op jit(solution)/shard_map/ppermute | solution.py:93
  51.8 1.3 fusion.49
  54.8 4.5 %fusion.225 = (f32[6,256]{1,0:T(8,128)}, f32[6,256,512]{2,1,0:T(8,128)}) fusion(bf16[256,6,64]{0,2,1:T(8,128)(2,1)} %bitcast.187, bf16[512,6,64]{0,2,1:T(8,128)(2,1)} %bitcast.182), kind=kOutput, calls=%fused_computation.273 | convolution fusion | flops 103023104 | bytes 3741696 | tf_op jit(solution)/shard_map/sub | solution.py:120
  59.3 3.3 %fusion.93 = bf16[6,64,256]{2,1,0:T(8,128)(2,1)} fusion(bf16[512,6,64]{0,2,1:T(8,128)(2,1)} %bitcast.180, f32[6,256,512]{2,1,0:T(8,128)} %get-tuple-element.40, f32[6,256]{1,0:T(8,128)} %get-tuple-element.39), kind=kOutput, calls=%fused_computation.108 | convolution fusion | flops 102334464 | bytes 3741696 | tf_op jit(solution)/shard_map/hts,shd->thd/dot_general | solution.py:121
  63.0 4.5 %fusion.226 = (f32[6,256]{1,0:T(8,128)}, f32[6,256,512]{2,1,0:T(8,128)}) fusion(bf16[256,6,64]{0,2,1:T(8,128)(2,1)} %bitcast.186, bf16[512,6,64]{0,2,1:T(8,128)(2,1)} %bitcast.183), kind=kOutput, calls=%fused_computation.274 | convolution fusion | flops 103023104 | bytes 3741696 | tf_op jit(solution)/shard_map/sub | solution.py:120
  67.5 2.6 %fusion.92 = bf16[6,64,256]{2,1,0:T(8,128)(2,1)S(1)} fusion(bf16[512,6,64]{0,2,1:T(8,128)(2,1)} %bitcast.181, f32[6,256,512]{2,1,0:T(8,128)} %get-tuple-element.42, f32[6,256]{1,0:T(8,128)} %get-tuple-element.41), kind=kOutput, calls=%fused_computation.107 | convolution fusion | flops 102334464 | bytes 3741696 | tf_op jit(solution)/shard_map/hts,shd->thd/dot_general | solution.py:121
  70.1 1.9 %collective-permute-start.5 = (bf16[256,384]{0,1:T(8,128)(2,1)S(1)}, bf16[256,384]{0,1:T(8,128)(2,1)S(1)}, u32[]{:S(2)}, u32[]{:S(2)}) collective-permute-start(bf16[256,384]{0,1:T(8,128)(2,1)S(1)} %bitcast.184), channel_id=1, source_target_pairs={{0,1},{1,0},{2,3},{3,2},{4,5},{5,4},{6,7},{7,6},{8,9},{9,8},{10,11... | collective-permute-start | bytes 589832 | tf_op jit(solution)/shard_map/ppermute | solution.py:125
  72.0 1.6 fusion.62
  73.6 1.5 fusion.58
  75.1 1.7 %fusion.228 = (f32[256]{0:T(256)S(1)}, f32[256,768]{1,0:T(8,128)S(1)}) fusion(f32[256,768]{1,0:T(8,128)S(1)} %fusion.62, bf16[256,384]{0,1:T(8,128)(2,1)} %collective-permute-done.3, bf16[384,768]{1,0:T(8,128)(2,1)} %collective-permute-done.4, bf16[256,384]{1,0:T(8,128)(2,1)S(1)} %get-tuple-element.31, bf16[256,384]{1,0:T(8,128)(2,1)S(1)} %copy-done.16, ...), kind=kOutput, calls=%fused_computation.276 | convolution fusion | flops 153943808 | bytes 2753537 | tf_op jit(solution)/shard_map/dot_general | solution.py:127
  78.4 1.6 fusion.227
  81.1 5.0 %fusion.52 = bf16[256,768]{1,0:T(8,128)(2,1)} fusion(bf16[1,1536,768]{2,1,0:T(8,128)(2,1)} %param.22, bf16[1,768,1536]{2,1,0:T(8,128)(2,1)} %param.21, f32[256,768]{1,0:T(8,128)} %copy-done.3, f32[768]{0:T(1024)S(1)} %copy-done.21, f32[768]{0:T(1024)S(1)} %get-tuple-element.21, f32[256]{0:T(256)S(1)} %add_rsqrt_fusion.4, f32[256]{0:T(256)S(1)} %broadcast_multiply_fusion.5), kind=kOutput, calls=%fused_computation.48 | convolution fusion | flops 1212678144 | bytes 5906432 | tf_op jit(solution)/shard_map/dot_general | solution.py:136
  86.5 4.3 %fusion.8 = bf16[256,768]{1,0:T(8,128)(2,1)S(1)} fusion(bf16[1,1536,768]{2,1,0:T(8,128)(2,1)} %param.22, bf16[1,768,1536]{2,1,0:T(8,128)(2,1)} %param.21, f32[256,768]{1,0:T(8,128)} %copy-done.1, f32[256]{0:T(256)} %add_rsqrt_fusion.2, f32[256]{0:T(256)S(1)} %broadcast_multiply_fusion.3, f32[768]{0:T(1024)} %get-tuple-element.24, f32[768]{0:T(1024)S(1)} %get-tuple-element.21), kind=kOutput, calls=%fused_computation.12 | convolution fusion | flops 1212481536 | bytes 5906432 | tf_op jit(solution)/shard_map/dot_general | solution.py:136
  90.8 6.1 %collective-permute-done.6 = bf16[256,768]{1,0:T(8,128)(2,1)} collective-permute-done((bf16[256,768]{1,0:T(8,128)(2,1)}, bf16[256,768]{1,0:T(8,128)(2,1)}, u32[]{:S(2)}, u32[]{:S(2)}) %collective-permute-start.6) | collective-permute-done | bytes 393248 | tf_op jit(solution)/shard_map/ppermute | solution.py:24
  96.9 1.6 fusion.219
  98.5 1.6 multiply_reduce_fusion.5
  100.1 1.3 add_convert_fusion.3
  102.0 1.9 %collective-permute-start.8 = (bf16[256,768]{1,0:T(8,128)(2,1)S(1)}, bf16[256,768]{1,0:T(8,128)(2,1)S(1)}, u32[]{:S(2)}, u32[]{:S(2)}) collective-permute-start(bf16[256,768]{1,0:T(8,128)(2,1)S(1)} %add_convert_fusion.3), channel_id=1, source_target_pairs={{0,2},{2,4},{4,6},{6,8},{8,10},{10,12},{12,14},{14,16},{16,18},{18... | collective-permute-start | bytes 1179656 | tf_op jit(solution)/shard_map/ppermute | solution.py:19
  104.0 7.2 %collective-permute-done.7 = bf16[256,768]{1,0:T(8,128)(2,1)S(1)} collective-permute-done((bf16[256,768]{1,0:T(8,128)(2,1)S(1)}, bf16[256,768]{1,0:T(8,128)(2,1)S(1)}, u32[]{:S(2)}, u32[]{:S(2)}) %collective-permute-start.7) | collective-permute-done | bytes 393248 | tf_op jit(solution)/shard_map/ppermute | solution.py:24
  113.4 1.9 %fusion.64 = f32[64,16,128]{2,0,1:T(8,128)S(1)} fusion(bf16[16,128,768]{2,0,1:T(8,128)(2,1)S(1)} %bitcast.158, s32[128]{0:T(128)S(1)} %iota_shift-right-logical_fusion, s32[128]{0:T(128)S(1)} %copy-done.23, s32[]{:T(128)S(6)} %mul.258, s32[64]{0:T(128)S(1)} %iota_shift-right-logical_fusion.1, s32[64]{0:T(128)S(1)} %copy-done.24, ...), kind=kOutput, calls=%fused_computation.78 | convolution fusion | flops 203030528 | bytes 3771396 | tf_op jit(solution)/shard_map/dot_general | solution.py:160
  115.4 2.0 %fusion.69 = bf16[64,16,128]{2,0,1:T(8,128)(2,1)S(1)} fusion(f32[64,16,128]{2,0,1:T(8,128)S(1)} %fusion.64, bf16[16,128,768]{2,0,1:T(8,128)(2,1)S(1)} %bitcast.159, f32[]{:T(128)S(6)} %convert_element_type.220, s32[128]{0:T(128)S(1)} %iota_shift-right-logical_fusion, s32[128]{0:T(128)S(1)} %copy-done.23, s32[]{:T(128)S(6)} %mul.258, ...), kind=kOutput, calls=%fused_computation.83 | convolution fusion | flops 204210176 | bytes 4033544 | tf_op jit(solution)/shard_map/dot_general | solution.py:160
  118.3 1.1 copy.47
  120.1 1.7 %fusion.223 = (bf16[64,768]{1,0:T(8,128)(2,1)}, bf16[64,768]{1,0:T(8,128)(2,1)}, bf16[64,768]{1,0:T(8,128)(2,1)S(1)}) fusion(bf16[256,768]{1,0:T(8,128)(2,1)} %copy-done.12), kind=kLoop, calls=%fused_computation.271 | loop fusion | bytes 589824 | tf_op jit(solution)/shard_map/slice | solution.py:156
  121.8 4.0 %fusion.76 = f32[64,16,128]{2,0,1:T(8,128)S(1)} fusion(bf16[16,128,768]{2,0,1:T(8,128)(2,1)} %bitcast.155, s32[128]{0:T(128)} %copy-done.29, s32[128]{0:T(128)S(1)} %copy-done.23, s32[]{:T(128)S(6)} %mul.258, s32[64]{0:T(128)} %copy-done.31, s32[64]{0:T(128)S(1)} %copy-done.24, pred[64]{0:T(512)(128)(4,1)} %copy-done.27, pred[128]{0:T(512)(128)(4,1)} %copy-done.25, ...), kind=kOutput, calls=%fused_computation.90 | convolution fusion | flops 203161600 | bytes 3770052 | tf_op jit(solution)/shard_map/dot_general | solution.py:160
  125.8 2.0 %fusion.74 = bf16[64,16,128]{2,0,1:T(8,128)(2,1)S(1)} fusion(f32[64,16,128]{2,0,1:T(8,128)S(1)} %fusion.76, bf16[16,128,768]{2,0,1:T(8,128)(2,1)S(1)} %bitcast.160, f32[]{:T(128)S(6)} %convert_element_type.220, s32[128]{0:T(128)S(1)} %copy-done.30, s32[128]{0:T(128)S(1)} %copy-done.23, s32[]{:T(128)S(6)} %mul.258, s32[64]{0:T(128)S(1)} %copy-done.32, ...), kind=kOutput, calls=%fused_computation.88 | convolution fusion | flops 204341248 | bytes 4032200 | tf_op jit(solution)/shard_map/dot_general | solution.py:160
  128.7 1.8 %copy.52 = bf16[8,128,128]{2,1,0:T(8,128)(2,1)} copy(bf16[8,128,128]{1,2,0:T(8,128)(2,1)} %bitcast.176) | data formatting | bytes 524288 | tf_op jit(solution)/shard_map/transpose | solution.py:179
  130.5 1.6 %collective-permute-start.10 = (bf16[1,8,8,16,128]{4,3,2,1,0:T(8,128)(2,1)}, bf16[1,8,8,16,128]{4,3,2,1,0:T(8,128)(2,1)}, u32[]{:S(2)}, u32[]{:S(2)}) collective-permute-start(bf16[1,8,8,16,128]{4,3,2,1,0:T(8,128)(2,1)} %bitcast.171), channel_id=1, source_target_pairs={{0,1},{1,0},{2,3},{3,2},{4,5},{5,4},{6,7},{7,6},{8,9},{9,8},{10,11... | collective-permute-start | bytes 786440 | tf_op jit(solution)/shard_map/ppermute | solution.py:181
  132.1 4.0 %fusion.83 = f32[64,16,128]{2,0,1:T(8,128)S(1)} fusion(bf16[16,128,768]{2,0,1:T(8,128)(2,1)} %bitcast.156, s32[128]{0:T(128)S(1)} %copy-done.30, s32[128]{0:T(128)S(1)} %copy-done.23, s32[]{:T(128)S(6)} %mul.258, s32[64]{0:T(128)S(1)} %copy-done.32, s32[64]{0:T(128)S(1)} %copy-done.24, pred[64]{0:T(512)(128)(4,1)S(1)} %copy-done.28, ...), kind=kOutput, calls=%fused_computation.97 | convolution fusion | flops 203161600 | bytes 3770052 | tf_op jit(solution)/shard_map/dot_general | solution.py:160
  136.2 2.0 %fusion.81 = bf16[64,16,128]{2,0,1:T(8,128)(2,1)S(1)} fusion(f32[64,16,128]{2,0,1:T(8,128)S(1)} %fusion.83, bf16[16,128,768]{2,0,1:T(8,128)(2,1)S(1)} %bitcast.161, f32[]{:T(128)S(6)} %convert_element_type.220, s32[128]{0:T(128)S(1)} %copy-done.30, s32[128]{0:T(128)S(1)} %copy-done.23, s32[]{:T(128)S(6)} %mul.258, s32[64]{0:T(128)S(1)} %copy-done.32, ...), kind=kOutput, calls=%fused_computation.95 | convolution fusion | flops 204341248 | bytes 4032200 | tf_op jit(solution)/shard_map/dot_general | solution.py:160
  139.0 1.8 %copy.57 = bf16[8,128,128]{2,1,0:T(8,128)(2,1)} copy(bf16[8,128,128]{1,2,0:T(8,128)(2,1)} %bitcast.177) | data formatting | bytes 524288 | tf_op jit(solution)/shard_map/transpose | solution.py:179
  140.8 4.0 %fusion.90 = f32[64,16,128]{2,0,1:T(8,128)S(1)} fusion(bf16[16,128,768]{2,0,1:T(8,128)(2,1)} %bitcast.157, s32[128]{0:T(128)S(1)} %copy-done.30, s32[128]{0:T(128)S(1)} %copy-done.23, s32[]{:T(128)S(6)} %mul.258, s32[64]{0:T(128)S(1)} %copy-done.32, s32[64]{0:T(128)S(1)} %copy-done.24, pred[64]{0:T(512)(128)(4,1)S(1)} %copy-done.28, ...), kind=kOutput, calls=%fused_computation.104 | convolution fusion | flops 203161600 | bytes 3770052 | tf_op jit(solution)/shard_map/dot_general | solution.py:160
  144.8 2.0 %fusion.88 = bf16[64,16,128]{2,0,1:T(8,128)(2,1)S(1)} fusion(f32[64,16,128]{2,0,1:T(8,128)S(1)} %fusion.90, bf16[16,128,768]{2,0,1:T(8,128)(2,1)S(1)} %bitcast.162, f32[]{:T(128)S(6)} %convert_element_type.220, s32[128]{0:T(128)S(1)} %copy-done.30, s32[128]{0:T(128)S(1)} %copy-done.23, s32[]{:T(128)S(6)} %mul.258, s32[64]{0:T(128)S(1)} %copy-done.32, ...), kind=kOutput, calls=%fused_computation.102 | convolution fusion | flops 204341248 | bytes 4032200 | tf_op jit(solution)/shard_map/dot_general | solution.py:160
  147.7 1.8 %copy.62 = bf16[8,128,128]{2,1,0:T(8,128)(2,1)} copy(bf16[8,128,128]{1,2,0:T(8,128)(2,1)} %bitcast.178) | data formatting | bytes 524288 | tf_op jit(solution)/shard_map/transpose | solution.py:179
  149.9 1.6 %collective-permute-start.11 = (bf16[1,8,8,16,128]{4,3,2,1,0:T(8,128)(2,1)}, bf16[1,8,8,16,128]{4,3,2,1,0:T(8,128)(2,1)S(1)}, u32[]{:S(2)}, u32[]{:S(2)}) collective-permute-start(bf16[1,8,8,16,128]{4,3,2,1,0:T(8,128)(2,1)} %bitcast.169), channel_id=1, source_target_pairs={{0,1},{1,0},{2,3},{3,2},{4,5},{5,4},{6,7},{7,6},{8,9},{9,8},{10,11... | collective-permute-start | bytes 786440 | tf_op jit(solution)/shard_map/ppermute | solution.py:181
  151.5 1.5 fusion.172
  153.1 4.8 %collective-permute-done.12 = bf16[1,8,8,16,128]{4,3,2,1,0:T(8,128)(2,1)S(1)} collective-permute-done((bf16[1,8,8,16,128]{4,3,2,1,0:T(8,128)(2,1)}, bf16[1,8,8,16,128]{4,3,2,1,0:T(8,128)(2,1)S(1)}, u32[]{:S(2)}, u32[]{:S(2)}) %collective-permute-start.12) | collective-permute-done | bytes 262176 | tf_op jit(solution)/shard_map/ppermute | solution.py:181
  157.9 2.8 %collective-permute-done.11 = bf16[1,8,8,16,128]{4,3,2,1,0:T(8,128)(2,1)S(1)} collective-permute-done((bf16[1,8,8,16,128]{4,3,2,1,0:T(8,128)(2,1)}, bf16[1,8,8,16,128]{4,3,2,1,0:T(8,128)(2,1)S(1)}, u32[]{:S(2)}, u32[]{:S(2)}) %collective-permute-start.11) | collective-permute-done | bytes 262176 | tf_op jit(solution)/shard_map/ppermute | solution.py:181
  160.9 1.6 pad_maximum_fusion
  (125 shorter events, 20.1 us)
Async XLA Ops:
  0.0 15.6 %copy-start = (bf16[4096,384]{1,0:T(8,128)(2,1)S(1)}, bf16[4096,384]{1,0:T(8,128)(2,1)}, u32[]{:S(2)}) copy-start(bf16[4096,384]{1,0:T(8,128)(2,1)} %param.14) | copy-start | bytes 9437188
  15.6 6.3 %copy-start.11 = (bf16[512,384]{1,0:T(8,128)(2,1)S(1)}, bf16[512,384]{1,0:T(8,128)(2,1)}, u32[]{:S(2)}) copy-start(bf16[512,384]{1,0:T(8,128)(2,1)} %param.16) | copy-start | bytes 1179652
  19.3 8.9 %collective-permute-start.1 = (f32[256,384]{1,0:T(8,128)}, f32[256,384]{1,0:T(8,128)}, u32[]{:S(2)}, u32[]{:S(2)}) collective-permute-start(f32[256,384]{1,0:T(8,128)} %fusion.91), channel_id=1, source_target_pairs={{2,0},{4,2},{6,4},{8,6},{10,8},{12,10},{14,12},{16,14},{18,16},{20... | collective-permute-start | bytes 1179656 | tf_op jit(solution)/shard_map/ppermute | solution.py:19
  21.5 53.6 %collective-permute-start.4 = (bf16[384,768]{1,0:T(8,128)(2,1)}, bf16[384,768]{1,0:T(8,128)(2,1)}, u32[]{:S(2)}, u32[]{:S(2)}) collective-permute-start(bf16[384,768]{1,0:T(8,128)(2,1)} %bitcast.18), channel_id=1, source_target_pairs={{0,1},{1,0},{2,3},{3,2},{4,5},{5,4},{6,7},{7,6},{8,9},{9,8},{10,11... | collective-permute-start | bytes 1769480 | tf_op jit(solution)/shard_map/ppermute | solution.py:83
  22.9 4.7 %copy-start.19 = (f32[3,768]{1,0:T(4,128)S(1)}, f32[3,768]{1,0:T(4,128)}, u32[]{:S(2)}) copy-start(f32[3,768]{1,0:T(4,128)} %param.17) | copy-start | bytes 27652
  22.9 4.7 %copy-start.20 = (f32[3,768]{1,0:T(4,128)S(1)}, f32[3,768]{1,0:T(4,128)}, u32[]{:S(2)}) copy-start(f32[3,768]{1,0:T(4,128)} %param.18) | copy-start | bytes 27652
  29.6 16.7 %collective-permute-start = (bf16[256,384]{1,0:T(8,128)(2,1)S(1)}, bf16[256,384]{1,0:T(8,128)(2,1)S(1)}, u32[]{:S(2)}, u32[]{:S(2)}) collective-permute-start(bf16[256,384]{1,0:T(8,128)(2,1)S(1)} %get-tuple-element.31), channel_id=1, source_target_pairs={{0,1},{1,0},{2,3},{3,2},{4,5},{5,4},{6,7},{7,6},{8,9},{9,8},{10,11... | collective-permute-start | bytes 589832 | tf_op jit(solution)/shard_map/ppermute | solution.py:93
  31.9 18.6 %collective-permute-start.2 = (bf16[256,384]{1,0:T(8,128)(2,1)S(1)}, bf16[256,384]{1,0:T(8,128)(2,1)S(1)}, u32[]{:S(2)}, u32[]{:S(2)}) collective-permute-start(bf16[256,384]{1,0:T(8,128)(2,1)S(1)} %get-tuple-element.32), channel_id=1, source_target_pairs={{0,1},{1,0},{2,3},{3,2},{4,5},{5,4},{6,7},{7,6},{8,9},{9,8},{10,11... | collective-permute-start | bytes 589832 | tf_op jit(solution)/shard_map/ppermute | solution.py:93
  46.4 4.1 %copy-start.15 = (bf16[256,384]{1,0:T(8,128)(2,1)}, bf16[256,384]{1,0:T(8,128)(2,1)S(1)}, u32[]{:S(2)}) copy-start(bf16[256,384]{1,0:T(8,128)(2,1)S(1)} %collective-permute-done) | copy-start | bytes 589828
  46.5 5.3 %copy-start.22 = (bf16[1,3,768,384]{3,2,1,0:T(8,128)(2,1)S(1)}, bf16[1,3,768,384]{3,2,1,0:T(8,128)(2,1)}, u32[]{:S(2)}) copy-start(bf16[1,3,768,384]{3,2,1,0:T(8,128)(2,1)} %param.19) | copy-start | bytes 5308420
  50.5 0.7 copy-start.13
  62.6 12.5 %collective-permute-start.3 = (bf16[256,384]{0,1:T(8,128)(2,1)}, bf16[256,384]{0,1:T(8,128)(2,1)}, u32[]{:S(2)}, u32[]{:S(2)}) collective-permute-start(bf16[256,384]{0,1:T(8,128)(2,1)} %bitcast.17), channel_id=1, source_target_pairs={{0,1},{1,0},{2,3},{3,2},{4,5},{5,4},{6,7},{7,6},{8,9},{9,8},{10,11... | collective-permute-start | bytes 589832 | tf_op jit(solution)/shard_map/ppermute | solution.py:125
  70.1 5.0 %copy-start.16 = (bf16[256,384]{1,0:T(8,128)(2,1)S(1)}, bf16[256,384]{1,0:T(8,128)(2,1)}, u32[]{:S(2)}) copy-start(bf16[256,384]{1,0:T(8,128)(2,1)} %copy-done.15) | copy-start | bytes 589828
  70.1 8.3 %collective-permute-start.5 = (bf16[256,384]{0,1:T(8,128)(2,1)S(1)}, bf16[256,384]{0,1:T(8,128)(2,1)S(1)}, u32[]{:S(2)}, u32[]{:S(2)}) collective-permute-start(bf16[256,384]{0,1:T(8,128)(2,1)S(1)} %bitcast.184), channel_id=1, source_target_pairs={{0,1},{1,0},{2,3},{3,2},{4,5},{5,4},{6,7},{7,6},{8,9},{9,8},{10,11... | collective-permute-start | bytes 589832 | tf_op jit(solution)/shard_map/ppermute | solution.py:125
  73.6 4.9 %copy-start.14 = (bf16[256,384]{1,0:T(8,128)(2,1)S(1)}, bf16[256,384]{1,0:T(8,128)(2,1)}, u32[]{:S(2)}) copy-start(bf16[256,384]{1,0:T(8,128)(2,1)} %copy-done.13) | copy-start | bytes 589828
  76.8 0.9 copy-start.1
  76.8 4.3 %copy-start.21 = (f32[768]{0:T(1024)S(1)}, f32[768]{0:T(1024)}, u32[]{:S(2)}) copy-start(f32[768]{0:T(1024)} %get-tuple-element.24) | copy-start | bytes 9220
  80.0 0.9 copy-start.3
  86.1 10.8 %collective-permute-start.6 = (bf16[256,768]{1,0:T(8,128)(2,1)}, bf16[256,768]{1,0:T(8,128)(2,1)}, u32[]{:S(2)}, u32[]{:S(2)}) collective-permute-start(bf16[256,768]{1,0:T(8,128)(2,1)} %fusion.52), channel_id=1, source_target_pairs={{0,1},{1,0},{2,3},{3,2},{4,5},{5,4},{6,7},{7,6},{8,9},{9,8},{10,11... | collective-permute-start | bytes 1179656 | tf_op jit(solution)/shard_map/ppermute | solution.py:24
  90.8 9.3 %copy-start.4 = (f32[256,768]{1,0:T(8,128)S(1)}, f32[256,768]{1,0:T(8,128)}, u32[]{:S(2)}) copy-start(f32[256,768]{1,0:T(8,128)} %copy-done.3) | copy-start | bytes 2359300
  90.8 20.4 %copy-start.2 = (f32[256,768]{1,0:T(8,128)S(1)}, f32[256,768]{1,0:T(8,128)}, u32[]{:S(2)}) copy-start(f32[256,768]{1,0:T(8,128)} %copy-done.1) | copy-start | bytes 2359300
  101.5 9.7 %collective-permute-start.7 = (bf16[256,768]{1,0:T(8,128)(2,1)S(1)}, bf16[256,768]{1,0:T(8,128)(2,1)S(1)}, u32[]{:S(2)}, u32[]{:S(2)}) collective-permute-start(bf16[256,768]{1,0:T(8,128)(2,1)S(1)} %fusion.8), channel_id=1, source_target_pairs={{0,1},{1,0},{2,3},{3,2},{4,5},{5,4},{6,7},{7,6},{8,9},{9,8},{10,11... | collective-permute-start | bytes 1179656 | tf_op jit(solution)/shard_map/ppermute | solution.py:24
  102.0 13.3 %copy-start.25 = (pred[128]{0:T(512)(128)(4,1)}, pred[128]{0:T(512)(128)(4,1)S(1)}, u32[]{:S(2)}) copy-start(pred[128]{0:T(512)(128)(4,1)S(1)} %compare_and_fusion) | copy-start | bytes 388
  102.0 13.3 %copy-start.27 = (pred[64]{0:T(512)(128)(4,1)}, pred[64]{0:T(512)(128)(4,1)S(1)}, u32[]{:S(2)}) copy-start(pred[64]{0:T(512)(128)(4,1)S(1)} %compare_and_fusion.1) | copy-start | bytes 196
  102.0 13.3 %copy-start.29 = (s32[128]{0:T(128)}, s32[128]{0:T(128)S(1)}, u32[]{:S(2)}) copy-start(s32[128]{0:T(128)S(1)} %iota_shift-right-logical_fusion) | copy-start | bytes 1540
  102.0 13.3 %copy-start.31 = (s32[64]{0:T(128)}, s32[64]{0:T(128)S(1)}, u32[]{:S(2)}) copy-start(s32[64]{0:T(128)S(1)} %iota_shift-right-logical_fusion.1) | copy-start | bytes 772
  102.0 13.3 %collective-permute-start.8 = (bf16[256,768]{1,0:T(8,128)(2,1)S(1)}, bf16[256,768]{1,0:T(8,128)(2,1)S(1)}, u32[]{:S(2)}, u32[]{:S(2)}) collective-permute-start(bf16[256,768]{1,0:T(8,128)(2,1)S(1)} %add_convert_fusion.3), channel_id=1, source_target_pairs={{0,2},{2,4},{4,6},{6,8},{8,10},{10,12},{12,14},{14,16},{16,18},{18... | collective-permute-start | bytes 1179656 | tf_op jit(solution)/shard_map/ppermute | solution.py:19
  111.4 2.0 %copy-start.5 = (bf16[768,2048]{0,1:T(8,128)(2,1)S(1)}, bf16[768,2048]{0,1:T(8,128)(2,1)}, u32[]{:S(2)}) copy-start(bf16[768,2048]{0,1:T(8,128)(2,1)} %copy.43) | copy-start | bytes 9437188
  111.4 2.0 %copy-start.23 = (s32[128]{0:T(128)S(1)}, s32[128]{0:T(128)}, u32[]{:S(2)}) copy-start(s32[128]{0:T(128)} %broadcast_add_fusion) | copy-start | bytes 1540
  111.4 1.9 %copy-start.24 = (s32[64]{0:T(128)S(1)}, s32[64]{0:T(128)}, u32[]{:S(2)}) copy-start(s32[64]{0:T(128)} %broadcast_add_fusion.1) | copy-start | bytes 772
  115.4 2.0 %copy-start.12 = (bf16[256,768]{1,0:T(8,128)(2,1)}, bf16[256,768]{1,0:T(8,128)(2,1)S(1)}, u32[]{:S(2)}) copy-start(bf16[256,768]{1,0:T(8,128)(2,1)S(1)} %collective-permute-done.8) | copy-start | bytes 1179652
  119.4 32.1 %collective-permute-start.9 = (bf16[1,8,8,16,128]{4,3,2,1,0:T(8,128)(2,1)S(1)}, bf16[1,8,8,16,128]{4,3,2,1,0:T(8,128)(2,1)}, u32[]{:S(2)}, u32[]{:S(2)}) collective-permute-start(bf16[1,8,8,16,128]{4,3,2,1,0:T(8,128)(2,1)S(1)} %bitcast.167), channel_id=1, source_target_pairs={{0,1},{1,0},{2,3},{3,2},{4,5},{5,4},{6,7},{7,6},{8,9},{9,8},{10,11... | collective-permute-start | bytes 786440 | tf_op jit(solution)/shard_map/ppermute | solution.py:181
  121.8 4.0 %copy-start.6 = (bf16[768,2048]{0,1:T(8,128)(2,1)S(1)}, bf16[768,2048]{0,1:T(8,128)(2,1)}, u32[]{:S(2)}) copy-start(bf16[768,2048]{0,1:T(8,128)(2,1)} %copy.43) | copy-start | bytes 9437188
  121.8 4.0 %copy-start.18 = (bf16[64,768]{1,0:T(8,128)(2,1)S(1)}, bf16[64,768]{1,0:T(8,128)(2,1)}, u32[]{:S(2)}) copy-start(bf16[64,768]{1,0:T(8,128)(2,1)} %get-tuple-element.15) | copy-start | bytes 294916
  121.8 4.0 %copy-start.26 = (pred[128]{0:T(512)(128)(4,1)S(1)}, pred[128]{0:T(512)(128)(4,1)}, u32[]{:S(2)}) copy-start(pred[128]{0:T(512)(128)(4,1)} %copy-done.25) | copy-start | bytes 388
  121.8 4.0 %copy-start.28 = (pred[64]{0:T(512)(128)(4,1)S(1)}, pred[64]{0:T(512)(128)(4,1)}, u32[]{:S(2)}) copy-start(pred[64]{0:T(512)(128)(4,1)} %copy-done.27) | copy-start | bytes 196
  121.8 4.0 %copy-start.30 = (s32[128]{0:T(128)S(1)}, s32[128]{0:T(128)}, u32[]{:S(2)}) copy-start(s32[128]{0:T(128)} %copy-done.29) | copy-start | bytes 1540
  121.8 4.0 %copy-start.32 = (s32[64]{0:T(128)S(1)}, s32[64]{0:T(128)}, u32[]{:S(2)}) copy-start(s32[64]{0:T(128)} %copy-done.31) | copy-start | bytes 772
  130.5 21.0 %collective-permute-start.10 = (bf16[1,8,8,16,128]{4,3,2,1,0:T(8,128)(2,1)}, bf16[1,8,8,16,128]{4,3,2,1,0:T(8,128)(2,1)}, u32[]{:S(2)}, u32[]{:S(2)}) collective-permute-start(bf16[1,8,8,16,128]{4,3,2,1,0:T(8,128)(2,1)} %bitcast.171), channel_id=1, source_target_pairs={{0,1},{1,0},{2,3},{3,2},{4,5},{5,4},{6,7},{7,6},{8,9},{9,8},{10,11... | collective-permute-start | bytes 786440 | tf_op jit(solution)/shard_map/ppermute | solution.py:181
  132.1 4.0 %copy-start.7 = (bf16[768,2048]{0,1:T(8,128)(2,1)S(1)}, bf16[768,2048]{0,1:T(8,128)(2,1)}, u32[]{:S(2)}) copy-start(bf16[768,2048]{0,1:T(8,128)(2,1)} %copy.43) | copy-start | bytes 9437188
  132.1 4.0 %copy-start.17 = (bf16[64,768]{1,0:T(8,128)(2,1)S(1)}, bf16[64,768]{1,0:T(8,128)(2,1)}, u32[]{:S(2)}) copy-start(bf16[64,768]{1,0:T(8,128)(2,1)} %get-tuple-element.17) | copy-start | bytes 294916
  140.8 4.0 %copy-start.8 = (bf16[768,2048]{0,1:T(8,128)(2,1)S(1)}, bf16[768,2048]{0,1:T(8,128)(2,1)}, u32[]{:S(2)}) copy-start(bf16[768,2048]{0,1:T(8,128)(2,1)} %copy.43) | copy-start | bytes 9437188
  149.5 11.2 %copy-start.9 = (bf16[8,128,128]{2,1,0:T(8,128)(2,1)S(1)}, bf16[8,128,128]{2,1,0:T(8,128)(2,1)}, u32[]{:S(2)}) copy-start(bf16[8,128,128]{2,1,0:T(8,128)(2,1)} %copy.57) | copy-start | bytes 786436
  149.5 11.2 %copy-start.10 = (bf16[8,128,128]{2,1,0:T(8,128)(2,1)S(1)}, bf16[8,128,128]{2,1,0:T(8,128)(2,1)}, u32[]{:S(2)}) copy-start(bf16[8,128,128]{2,1,0:T(8,128)(2,1)} %copy.62) | copy-start | bytes 786436
  149.5 8.4 %collective-permute-start.12 = (bf16[1,8,8,16,128]{4,3,2,1,0:T(8,128)(2,1)}, bf16[1,8,8,16,128]{4,3,2,1,0:T(8,128)(2,1)S(1)}, u32[]{:S(2)}, u32[]{:S(2)}) collective-permute-start(bf16[1,8,8,16,128]{4,3,2,1,0:T(8,128)(2,1)} %bitcast.173), channel_id=1, source_target_pairs={{0,1},{1,0},{2,3},{3,2},{4,5},{5,4},{6,7},{7,6},{8,9},{9,8},{10,11... | collective-permute-start | bytes 786440 | tf_op jit(solution)/shard_map/ppermute | solution.py:181
  149.9 10.8 %collective-permute-start.11 = (bf16[1,8,8,16,128]{4,3,2,1,0:T(8,128)(2,1)}, bf16[1,8,8,16,128]{4,3,2,1,0:T(8,128)(2,1)S(1)}, u32[]{:S(2)}, u32[]{:S(2)}) collective-permute-start(bf16[1,8,8,16,128]{4,3,2,1,0:T(8,128)(2,1)} %bitcast.169), channel_id=1, source_target_pairs={{0,1},{1,0},{2,3},{3,2},{4,5},{5,4},{6,7},{7,6},{8,9},{9,8},{10,11... | collective-permute-start | bytes 786440 | tf_op jit(solution)/shard_map/ppermute | solution.py:181

commit v11 on v9

--- a/solution.py
+++ b/solution.py
@@ -85,11 +85,15 @@
     embed_by_depth = embed_voxel.reshape(PATCH * PATCH, PATCH, local_width).transpose(1, 0, 2)
     position = position.astype(jnp.float32)
     own_embedded = embed_planes(traces, own_live, embed_by_depth, embed_mask)
-    next_embedded = from_behind(own_embedded, "tile", -1)
+    own_half = (own_embedded + position[:half_tokens]).astype(jnp.bfloat16)
+    for_previous = (own_embedded + position[half_tokens:]).astype(jnp.bfloat16)
+    next_half = jnp.where(
+        tile_index == lax.axis_size("tile") - 1,
+        position[half_tokens:].astype(jnp.bfloat16),
+        from_behind(for_previous, "tile", -1),
+    )
     halves = []
-    for rows, embedded in enumerate((own_embedded, next_embedded)):
-        embedded = embedded + position[rows * half_tokens:(rows + 1) * half_tokens]
-        embedded = embedded.astype(jnp.bfloat16)
+    for embedded in (own_half, next_half):
         other_columns = lax.ppermute(embedded, "head", [(0, 1), (1, 0)])
         halves.append(jnp.where(
             head_index == 0,

time: 147 us -> 137 us (0.932)
  the two profiles are of different devices: /device:TPU:126 before, /device:TPU:31 now
where the time goes in v11:
time: 137 us; the launch traced here: 135 us
  matrix products  46.2 us (34%)
  local copies, waits for them, and re-layouts  28.2 us (21%)
  waiting for transfers between devices  25.2 us (18%)
  other arithmetic  18.9 us (14%)
  starting transfers between devices  15.8 us (12%)
    ppermute x2, waiting for transfers between devices, body(): other_rows = lax.ppermute(arranged, 'head', [(0, 1), (1, 0)])  13.2 us
    dot_general x4, matrix products, body(): lax.dot_general(latent, decode_by_depth, (((1,), (2,)), ((), ())), prefer...  10.5 us
    dot_general x2, matrix products, body(): jnp.dot(hidden, w_down[0], preferred_element_type=jnp.float32)  9.28 us
    ppermute x2, starting transfers between devices, from_behind(): return lax.ppermute(block, axis, route)  9.07 us
    sub x2, matrix products, body(): weights = jax.nn.softmax(scores, axis=-1).astype(jnp.bfloat16)  8.89 us
    unnamed x57, local copies, waits for them, and re-layouts  7.91 us
    dot_general x2, matrix products, body(): jnp.einsum('hts,shd->thd', weights, values, preferred_element_type=jnp.fl...  5.97 us
    ppermute x2, waiting for transfers between devices, from_behind(): return lax.ppermute(block, axis, route)  4.89 us
  transfers between devices with their start and end apart: 11, of which 7 were waited for; matrix products, arithmetic and copies ran while one was open for 55% of the time, Pallas kernels for 0%

profile of v11, /device:TPU:31, one launch (start us, length us, event | category | flops | bytes accessed | tf_op | source)
XLA Modules:
  0.0 134.9 jit_solution(3345711264254359290)
XLA Ops:
  0.0 1.6 %collective-permute-start.4 = (bf16[384,768]{1,0:T(8,128)(2,1)}, bf16[384,768]{1,0:T(8,128)(2,1)}, u32[]{:S(2)}, u32[]{:S(2)}) collective-permute-start(bf16[384,768]{1,0:T(8,128)(2,1)} %bitcast.135), channel_id=1, source_target_pairs={{0,1},{1,0},{2,3},{3,2},{4,5},{5,4},{6,7},{7,6},{8,9},{9,8},{10,11... | collective-permute-start | bytes 1769480 | tf_op jit(solution)/shard_map/ppermute | solution.py:83
  2.7 1.9 %convert_element_type.148 = f32[512,384]{1,0:T(8,128)} convert(bf16[512,384]{1,0:T(8,128)(2,1)} %param.16) | non-fusion elementwise | flops 196608 | bytes 1179648 | tf_op jit(solution)/shard_map/convert_element_type | solution.py:86
  4.7 2.5 %broadcast_multiply_fusion = bf16[64,128,128]{2,1,0:T(8,128)(2,1)S(1)} fusion(bf16[64,128,128]{2,1,0:T(8,128)(2,1)} %param.12, bf16[64,128]{1,0:T(8,128)(2,1)S(1)} %convert_element_type.147), kind=kLoop, calls=%fused_computation.122 | loop fusion | flops 1048576 | bytes 4210688 | tf_op jit(solution)/shard_map/mul | solution.py:43
  7.1 1.9 %copy.30 = bf16[4,8,16,16,128]{4,3,2,1,0:T(8,128)(2,1)} copy(bf16[4,8,16,16,128]{4,3,1,2,0:T(8,128)(2,1)S(1)} %bitcast.126) | data formatting | bytes 4194304 | tf_op jit(solution)/shard_map/transpose | solution.py:44
  9.0 4.1 %copy.31 = bf16[32,128,256]{2,1,0:T(8,128)(2,1)} copy(bf16[32,128,256]{1,2,0:T(8,128)(2,1)} %bitcast.127) | data formatting | bytes 4194304 | tf_op jit(solution)/shard_map/transpose | solution.py:46
  13.1 4.9 %copy.32 = bf16[256,16,256]{0,1,2:T(8,128)(2,1)} copy(bf16[256,16,256]{2,1,0:T(8,128)(2,1)} %bitcast.128) | data formatting | bytes 4194304 | tf_op jit(solution)/shard_map/reshape | solution.py:46
  18.1 3.8 %fusion.166 = (bf16[256,384]{1,0:T(8,128)(2,1)}, bf16[256,384]{1,0:T(8,128)(2,1)}) fusion(f32[512,384]{1,0:T(8,128)} %convert_element_type.148, f32[32,384]{1,0:T(8,128)S(1)} %fusion.213, bf16[256,16,256]{0,1,2:T(8,128)(2,1)} %copy.32, bf16[16,256,384]{2,0,1:T(8,128)(2,1)S(1)} %bitcast.125), kind=kOutput, calls=%fused_computation.148 | convolution fusion | flops 805797888 | bytes 6471680 | tf_op jit(solution)/shard_map/dot_general | solution.py:47
  22.0 2.9 %collective-permute-start.1 = (bf16[256,384]{1,0:T(8,128)(2,1)}, bf16[256,384]{1,0:T(8,128)(2,1)S(1)}, u32[]{:S(2)}, u32[]{:S(2)}) collective-permute-start(bf16[256,384]{1,0:T(8,128)(2,1)} %get-tuple-element.24), channel_id=1, source_target_pairs={{2,0},{4,2},{6,4},{8,6},{10,8},{12,10},{14,12},{16,14},{18,16},{20... | collective-permute-start | bytes 589832 | tf_op jit(solution)/shard_map/ppermute | solution.py:19
  25.6 4.7 %copy.35 = bf16[768,2048]{0,1:T(8,128)(2,1)} copy(bf16[768,2048]{1,0:T(8,128)(2,1)} %param.23) | data formatting | bytes 6291456 | tf_op args[11]
  30.8 4.1 %collective-permute-done.1 = bf16[256,384]{1,0:T(8,128)(2,1)S(1)} collective-permute-done((bf16[256,384]{1,0:T(8,128)(2,1)}, bf16[256,384]{1,0:T(8,128)(2,1)S(1)}, u32[]{:S(2)}, u32[]{:S(2)}) %collective-permute-start.1) | collective-permute-done | bytes 196640 | tf_op jit(solution)/shard_map/ppermute | solution.py:19
  35.0 1.0 fusion.189
  36.8 1.3 fusion.167
  38.1 2.5 %collective-permute-done.2 = bf16[256,384]{1,0:T(8,128)(2,1)S(1)} collective-permute-done((bf16[256,384]{1,0:T(8,128)(2,1)S(1)}, bf16[256,384]{1,0:T(8,128)(2,1)S(1)}, u32[]{:S(2)}, u32[]{:S(2)}) %collective-permute-start.2) | collective-permute-done | bytes 196640 | tf_op jit(solution)/shard_map/ppermute | solution.py:97
  41.9 1.3 fusion.57
  43.9 0.9 fusion.208
  44.8 4.5 %fusion.209 = (f32[6,256]{1,0:T(8,128)}, f32[6,256,512]{2,1,0:T(8,128)}) fusion(bf16[256,6,64]{0,2,1:T(8,128)(2,1)} %bitcast.150, bf16[512,6,64]{0,2,1:T(8,128)(2,1)} %bitcast.145), kind=kOutput, calls=%fused_computation.213 | convolution fusion | flops 103023104 | bytes 3741696 | tf_op jit(solution)/shard_map/sub | solution.py:124
  49.3 3.3 %fusion.114 = bf16[6,64,256]{2,1,0:T(8,128)(2,1)} fusion(bf16[512,6,64]{0,2,1:T(8,128)(2,1)} %bitcast.143, f32[6,256,512]{2,1,0:T(8,128)} %get-tuple-element.26, f32[6,256]{1,0:T(8,128)} %get-tuple-element.25), kind=kOutput, calls=%fused_computation.89 | convolution fusion | flops 102334464 | bytes 3741696 | tf_op jit(solution)/shard_map/hts,shd->thd/dot_general | solution.py:125
  52.8 4.4 %fusion.211 = (f32[6,256]{1,0:T(8,128)}, f32[6,256,512]{2,1,0:T(8,128)}) fusion(bf16[256,6,64]{0,2,1:T(8,128)(2,1)S(1)} %bitcast.149, bf16[512,6,64]{0,2,1:T(8,128)(2,1)} %bitcast.146), kind=kOutput, calls=%fused_computation.215 | convolution fusion | flops 103023104 | bytes 3741696 | tf_op jit(solution)/shard_map/sub | solution.py:124
  57.2 2.7 %fusion.115 = bf16[6,64,256]{2,1,0:T(8,128)(2,1)S(1)} fusion(bf16[512,6,64]{0,2,1:T(8,128)(2,1)} %bitcast.144, f32[6,256,512]{2,1,0:T(8,128)} %get-tuple-element.30, f32[6,256]{1,0:T(8,128)} %get-tuple-element.29), kind=kOutput, calls=%fused_computation.90 | convolution fusion | flops 102334464 | bytes 3741696 | tf_op jit(solution)/shard_map/hts,shd->thd/dot_general | solution.py:125
  59.9 1.6 %collective-permute-start.3 = (bf16[256,384]{0,1:T(8,128)(2,1)S(1)}, bf16[256,384]{0,1:T(8,128)(2,1)}, u32[]{:S(2)}, u32[]{:S(2)}) collective-permute-start(bf16[256,384]{0,1:T(8,128)(2,1)S(1)} %bitcast.147), channel_id=1, source_target_pairs={{0,1},{1,0},{2,3},{3,2},{4,5},{5,4},{6,7},{7,6},{8,9},{9,8},{10,11... | collective-permute-start | bytes 589832 | tf_op jit(solution)/shard_map/ppermute | solution.py:129
  61.4 1.3 fusion.108
  62.8 1.3 fusion.112
  64.0 1.7 %fusion.210 = (f32[256]{0:T(256)S(1)}, f32[256,768]{1,0:T(8,128)S(1)}) fusion(f32[256,768]{1,0:T(8,128)S(1)} %fusion.108, bf16[256,384]{0,1:T(8,128)(2,1)} %collective-permute-done.5, bf16[384,768]{1,0:T(8,128)(2,1)} %collective-permute-done.4, bf16[256,384]{1,0:T(8,128)(2,1)S(1)} %fusion.189, bf16[256,384]{1,0:T(8,128)(2,1)S(1)} %copy-done.12, pred[]{:T(512)S(6)} %eq.4), kind=kOutput, calls=%fused_computation.214 | convolution fusion | flops 153943808 | bytes 2753537 | tf_op jit(solution)/shard_map/dot_general | solution.py:131
  65.7 0.9 copy-done.3
  66.8 5.0 %fusion.102 = bf16[256,768]{1,0:T(8,128)(2,1)} fusion(bf16[1,1536,768]{2,1,0:T(8,128)(2,1)} %param.22, bf16[1,768,1536]{2,1,0:T(8,128)(2,1)} %param.21, f32[256,768]{1,0:T(8,128)} %copy-done.3, f32[768]{0:T(1024)S(1)} %get-tuple-element.16, f32[768]{0:T(1024)S(1)} %get-tuple-element.13, f32[256]{0:T(256)S(1)} %add_rsqrt_fusion.4, ...), kind=kOutput, calls=%fused_computation.74 | convolution fusion | flops 1212678144 | bytes 5906432 | tf_op jit(solution)/shard_map/dot_general | solution.py:140
  72.0 2.1 %fusion.212 = (f32[256]{0:T(256)S(1)}, f32[256,768]{1,0:T(8,128)S(1)}) fusion(f32[256,768]{1,0:T(8,128)} %fusion.112, bf16[256,384]{0,1:T(8,128)(2,1)} %collective-permute-done.3, bf16[384,768]{1,0:T(8,128)(2,1)} %collective-permute-done.4, bf16[256,384]{1,0:T(8,128)(2,1)} %get-tuple-element.23, bf16[256,384]{1,0:T(8,128)(2,1)} %collective-permute-done, ...), kind=kOutput, calls=%fused_computation.216 | convolution fusion | flops 153943808 | bytes 2753537 | tf_op jit(solution)/shard_map/dot_general | solution.py:131
  74.1 0.9 copy-done.1
  75.7 4.3 %fusion.8 = bf16[256,768]{1,0:T(8,128)(2,1)S(1)} fusion(bf16[1,1536,768]{2,1,0:T(8,128)(2,1)} %param.22, bf16[1,768,1536]{2,1,0:T(8,128)(2,1)} %param.21, f32[256,768]{1,0:T(8,128)} %copy-done.1, f32[256]{0:T(256)} %add_rsqrt_fusion.2, f32[256]{0:T(256)S(1)} %broadcast_multiply_fusion.3, f32[768]{0:T(1024)} %copy-done.15, f32[768]{0:T(1024)S(1)} %get-tuple-element.13), kind=kOutput, calls=%fused_computation.12 | convolution fusion | flops 1212481536 | bytes 5906432 | tf_op jit(solution)/shard_map/dot_general | solution.py:140
  80.0 1.4 %collective-permute-done.6 = bf16[256,768]{1,0:T(8,128)(2,1)} collective-permute-done((bf16[256,768]{1,0:T(8,128)(2,1)}, bf16[256,768]{1,0:T(8,128)(2,1)}, u32[]{:S(2)}, u32[]{:S(2)}) %collective-permute-start.6) | collective-permute-done | bytes 393248 | tf_op jit(solution)/shard_map/ppermute | solution.py:24
  81.4 1.6 %fusion.205 = f32[256]{0:T(256)S(1)} fusion(f32[256,768]{1,0:T(8,128)} %copy-done.3, bf16[256,768]{1,0:T(8,128)(2,1)} %collective-permute-done.6, bf16[256,768]{1,0:T(8,128)(2,1)} %fusion.102), kind=kLoop, calls=%fused_computation.209 | loop fusion | flops 982784 | bytes 1573888 | tf_op jit(solution)/shard_map/reduce_sum | solution.py:29
  83.0 1.4 %multiply_reduce_fusion.5 = f32[256]{0:T(256)S(1)} fusion(f32[256]{0:T(256)S(1)} %broadcast_multiply_fusion.4, f32[256,768]{1,0:T(8,128)S(1)} %copy-done.4, bf16[256,768]{1,0:T(8,128)(2,1)} %collective-permute-done.6, bf16[256,768]{1,0:T(8,128)(2,1)} %fusion.102), kind=kLoop, calls=%fused_computation.131 | loop fusion | flops 1376000 | bytes 1574912 | tf_op jit(solution)/shard_map/reduce_sum | solution.py:31
  84.5 1.4 %add_convert_fusion.3 = bf16[256,768]{1,0:T(8,128)(2,1)S(1)} fusion(f32[768]{0:T(1024)S(1)} %get-tuple-element.18, f32[768]{0:T(1024)S(1)} %get-tuple-element.15, f32[256]{0:T(256)S(1)} %add_rsqrt_fusion.3, f32[256]{0:T(256)S(1)} %broadcast_multiply_fusion.4, f32[256,768]{1,0:T(8,128)S(1)} %copy-done.4, bf16[256,768]{1,0:T(8,128)(2,1)} %collective-permute-done.6, ...), kind=kLoop, calls=%fused_computation.130 | loop fusion | flops 1769472 | bytes 1974272 | tf_op jit(solution)/shard_map/convert_element_type | solution.py:146
  85.8 1.4 %collective-permute-start.7 = (bf16[256,768]{1,0:T(8,128)(2,1)S(1)}, bf16[256,768]{1,0:T(8,128)(2,1)S(1)}, u32[]{:S(2)}, u32[]{:S(2)}) collective-permute-start(bf16[256,768]{1,0:T(8,128)(2,1)S(1)} %fusion.8), channel_id=1, source_target_pairs={{0,1},{1,0},{2,3},{3,2},{4,5},{5,4},{6,7},{7,6},{8,9},{9,8},{10,11... | collective-permute-start | bytes 1179656 | tf_op jit(solution)/shard_map/ppermute | solution.py:24
  87.3 6.2 %collective-permute-start.8 = (bf16[256,768]{1,0:T(8,128)(2,1)S(1)}, bf16[256,768]{1,0:T(8,128)(2,1)S(1)}, u32[]{:S(2)}, u32[]{:S(2)}) collective-permute-start(bf16[256,768]{1,0:T(8,128)(2,1)S(1)} %add_convert_fusion.3), channel_id=1, source_target_pairs={{0,2},{2,4},{4,6},{6,8},{8,10},{10,12},{12,14},{14,16},{16,18},{18... | collective-permute-start | bytes 1179656 | tf_op jit(solution)/shard_map/ppermute | solution.py:19
  93.5 3.2 %collective-permute-done.7 = bf16[256,768]{1,0:T(8,128)(2,1)S(1)} collective-permute-done((bf16[256,768]{1,0:T(8,128)(2,1)S(1)}, bf16[256,768]{1,0:T(8,128)(2,1)S(1)}, u32[]{:S(2)}, u32[]{:S(2)}) %collective-permute-start.7) | collective-permute-done | bytes 393248 | tf_op jit(solution)/shard_map/ppermute | solution.py:24
  99.0 2.1 %fusion.78 = f32[128,16,128]{2,0,1:T(8,128)S(1)} fusion(bf16[16,128,768]{2,0,1:T(8,128)(2,1)S(1)} %bitcast.132, s32[128]{0:T(128)S(1)} %iota_shift-right-logical_fusion.1, s32[128]{0:T(128)S(1)} %copy-done.19, s32[]{:T(128)S(6)} %mul.218, s32[128]{0:T(128)S(1)} %iota_shift-right-logical_fusion, s32[128]{0:T(128)S(1)} %copy-done.18, ...), kind=kOutput, calls=%fused_computation.66 | convolution fusion | flops 406061056 | bytes 4393988 | tf_op jit(solution)/shard_map/dot_general | solution.py:164
  101.1 2.2 %divide_convert_fusion.9 = bf16[128,16,128]{2,0,1:T(8,128)(2,1)S(1)} fusion(f32[128,16,128]{2,0,1:T(8,128)S(1)} %fusion.78, bf16[16,128,768]{2,0,1:T(8,128)(2,1)S(1)} %bitcast.133, f32[]{:T(128)S(6)} %convert_element_type.188, s32[128]{0:T(128)S(1)} %iota_shift-right-logical_fusion.1, s32[128]{0:T(128)S(1)} %copy-done.19, s32[]{:T(128)S(6)} %mul.218, ...), kind=kOutput, calls=%fused_computation.121 | convolution fusion | flops 408420352 | bytes 4918280 | tf_op jit(solution)/shard_map/dot_general | solution.py:164
  103.3 1.1 copy.38
  104.4 2.0 %copy.39 = bf16[16,128,128]{2,1,0:T(8,128)(2,1)} copy(bf16[16,128,128]{1,2,0:T(8,128)(2,1)} %bitcast.140) | data formatting | bytes 1048576 | tf_op jit(solution)/shard_map/transpose | solution.py:183
  106.5 1.0 collective-permute-start.9
  107.6 4.1 %fusion.99 = f32[128,16,128]{2,0,1:T(8,128)S(1)} fusion(bf16[16,128,768]{2,0,1:T(8,128)(2,1)} %bitcast.131, s32[128]{0:T(128)S(1)} %copy-done.21, s32[128]{0:T(128)S(1)} %copy-done.19, s32[]{:T(128)S(6)} %mul.218, s32[128]{0:T(128)S(1)} %copy-done.23, s32[128]{0:T(128)S(1)} %copy-done.18, pred[128]{0:T(512)(128)(4,1)S(1)} %copy-done.25, ...), kind=kOutput, calls=%fused_computation.73 | convolution fusion | flops 406323200 | bytes 4393220 | tf_op jit(solution)/shard_map/dot_general | solution.py:164
  111.7 2.2 %divide_convert_fusion.8 = bf16[128,16,128]{2,0,1:T(8,128)(2,1)S(1)} fusion(f32[128,16,128]{2,0,1:T(8,128)S(1)} %fusion.99, bf16[16,128,768]{2,0,1:T(8,128)(2,1)S(1)} %bitcast.134, f32[]{:T(128)S(6)} %convert_element_type.188, s32[128]{0:T(128)S(1)} %copy-done.21, s32[128]{0:T(128)S(1)} %copy-done.19, s32[]{:T(128)S(6)} %mul.218, s32[128]{0:T(128)S(1)} %copy-done.23, ...), kind=kOutput, calls=%fused_computation.120 | convolution fusion | flops 408682496 | bytes 4917512 | tf_op jit(solution)/shard_map/dot_general | solution.py:164
  113.9 1.1 copy.43
  115.0 2.0 %copy.44 = bf16[16,128,128]{2,1,0:T(8,128)(2,1)} copy(bf16[16,128,128]{1,2,0:T(8,128)(2,1)} %bitcast.141) | data formatting | bytes 1048576 | tf_op jit(solution)/shard_map/transpose | solution.py:183
  117.5 2.0 %collective-permute-done.9 = bf16[2,8,8,16,128]{4,3,2,1,0:T(8,128)(2,1)} collective-permute-done((bf16[2,8,8,16,128]{4,3,2,1,0:T(8,128)(2,1)}, bf16[2,8,8,16,128]{4,3,2,1,0:T(8,128)(2,1)}, u32[]{:S(2)}, u32[]{:S(2)}) %collective-permute-start.9) | collective-permute-done | bytes 524320 | tf_op jit(solution)/shard_map/ppermute | solution.py:185
  119.4 11.2 %collective-permute-done.10 = bf16[2,8,8,16,128]{4,3,2,1,0:T(8,128)(2,1)S(1)} collective-permute-done((bf16[2,8,8,16,128]{4,3,2,1,0:T(8,128)(2,1)}, bf16[2,8,8,16,128]{4,3,2,1,0:T(8,128)(2,1)S(1)}, u32[]{:S(2)}, u32[]{:S(2)}) %collective-permute-start.10) | collective-permute-done | bytes 524320 | tf_op jit(solution)/shard_map/ppermute | solution.py:185
  130.7 2.1 %fusion.141 = (bf16[2,16,8,16,128]{4,3,1,2,0:T(8,128)(2,1)S(1)}, bf16[2,16,8,16,128]{4,3,1,2,0:T(8,128)(2,1)S(1)}) fusion(bf16[2,8,8,16,128]{4,3,2,1,0:T(8,128)(2,1)} %collective-permute-done.9, bf16[2,8,8,16,128]{4,3,2,1,0:T(8,128)(2,1)} %bitcast.137, pred[]{:T(512)S(6)} %eq.4, bf16[2,8,8,16,128]{4,3,2,1,0:T(8,128)(2,1)} %bitcast.139, ...), kind=kLoop, calls=%fused_computation.117 | loop fusion | flops 3145728 | bytes 4194305 | tf_op jit(solution)/shard_map/transpose | solution.py:191
  133.4 1.5 %pad_maximum_fusion = bf16[64,128,128]{2,1,0:T(8,128)(2,1)} fusion(bf16[32,128,128]{2,1,0:T(8,128)(2,1)S(1)} %bitcast.130, bf16[32,128,128]{2,1,0:T(8,128)(2,1)S(1)} %bitcast.129), kind=kLoop, calls=%fused_computation.20 | loop fusion | flops 1048576 | bytes 4194304 | tf_op jit(solution)/shard_map/concatenate | solution.py:192
  (102 shorter events, 9.9 us)
Async XLA Ops:
  0.0 18.1 %copy-start = (bf16[4096,384]{1,0:T(8,128)(2,1)S(1)}, bf16[4096,384]{1,0:T(8,128)(2,1)}, u32[]{:S(2)}) copy-start(bf16[4096,384]{1,0:T(8,128)(2,1)} %param.14) | copy-start | bytes 9437188
  0.0 64.0 %collective-permute-start.4 = (bf16[384,768]{1,0:T(8,128)(2,1)}, bf16[384,768]{1,0:T(8,128)(2,1)}, u32[]{:S(2)}, u32[]{:S(2)}) collective-permute-start(bf16[384,768]{1,0:T(8,128)(2,1)} %bitcast.135), channel_id=1, source_target_pairs={{0,1},{1,0},{2,3},{3,2},{4,5},{5,4},{6,7},{7,6},{8,9},{9,8},{10,11... | collective-permute-start | bytes 1769480 | tf_op jit(solution)/shard_map/ppermute | solution.py:83
  13.1 4.9 %copy-start.10 = (bf16[256,384]{1,0:T(8,128)(2,1)S(1)}, bf16[256,384]{1,0:T(8,128)(2,1)}, u32[]{:S(2)}) copy-start(bf16[256,384]{1,0:T(8,128)(2,1)} %param.15) | copy-start | bytes 589828
  18.1 6.8 %copy-start.13 = (f32[3,768]{1,0:T(4,128)S(1)}, f32[3,768]{1,0:T(4,128)}, u32[]{:S(2)}) copy-start(f32[3,768]{1,0:T(4,128)} %param.17) | copy-start | bytes 27652
  22.0 13.0 %collective-permute-start.1 = (bf16[256,384]{1,0:T(8,128)(2,1)}, bf16[256,384]{1,0:T(8,128)(2,1)S(1)}, u32[]{:S(2)}, u32[]{:S(2)}) collective-permute-start(bf16[256,384]{1,0:T(8,128)(2,1)} %get-tuple-element.24), channel_id=1, source_target_pairs={{2,0},{4,2},{6,4},{8,6},{10,8},{12,10},{14,12},{16,14},{18,16},{20... | collective-permute-start | bytes 589832 | tf_op jit(solution)/shard_map/ppermute | solution.py:19
  24.8 12.0 %collective-permute-start = (bf16[256,384]{1,0:T(8,128)(2,1)}, bf16[256,384]{1,0:T(8,128)(2,1)}, u32[]{:S(2)}, u32[]{:S(2)}) collective-permute-start(bf16[256,384]{1,0:T(8,128)(2,1)} %get-tuple-element.23), channel_id=1, source_target_pairs={{0,1},{1,0},{2,3},{3,2},{4,5},{5,4},{6,7},{7,6},{8,9},{9,8},{10,11... | collective-permute-start | bytes 589832 | tf_op jit(solution)/shard_map/ppermute | solution.py:97
  25.6 5.2 %copy-start.14 = (f32[3,768]{1,0:T(4,128)S(1)}, f32[3,768]{1,0:T(4,128)}, u32[]{:S(2)}) copy-start(f32[3,768]{1,0:T(4,128)} %param.18) | copy-start | bytes 27652
  30.8 36.0 %copy-start.15 = (f32[768]{0:T(1024)}, f32[768]{0:T(1024)S(1)}, u32[]{:S(2)}) copy-start(f32[768]{0:T(1024)S(1)} %get-tuple-element.16) | copy-start | bytes 9220
  36.0 4.6 %collective-permute-start.2 = (bf16[256,384]{1,0:T(8,128)(2,1)S(1)}, bf16[256,384]{1,0:T(8,128)(2,1)S(1)}, u32[]{:S(2)}, u32[]{:S(2)}) collective-permute-start(bf16[256,384]{1,0:T(8,128)(2,1)S(1)} %fusion.189), channel_id=1, source_target_pairs={{0,1},{1,0},{2,3},{3,2},{4,5},{5,4},{6,7},{7,6},{8,9},{9,8},{10,11... | collective-permute-start | bytes 589832 | tf_op jit(solution)/shard_map/ppermute | solution.py:97
  38.1 3.8 %copy-start.16 = (f32[768]{0:T(1024)S(1)}, f32[768]{0:T(1024)}, u32[]{:S(2)}) copy-start(f32[768]{0:T(1024)} %get-tuple-element.14) | copy-start | bytes 9220
  38.1 3.8 %copy-start.17 = (bf16[1,3,768,384]{3,2,1,0:T(8,128)(2,1)S(1)}, bf16[1,3,768,384]{3,2,1,0:T(8,128)(2,1)}, u32[]{:S(2)}) copy-start(bf16[1,3,768,384]{3,2,1,0:T(8,128)(2,1)} %param.19) | copy-start | bytes 5308420
  40.6 0.7 copy-start.11
  52.6 11.4 %collective-permute-start.5 = (bf16[256,384]{0,1:T(8,128)(2,1)}, bf16[256,384]{0,1:T(8,128)(2,1)}, u32[]{:S(2)}, u32[]{:S(2)}) collective-permute-start(bf16[256,384]{0,1:T(8,128)(2,1)} %bitcast.22), channel_id=1, source_target_pairs={{0,1},{1,0},{2,3},{3,2},{4,5},{5,4},{6,7},{7,6},{8,9},{9,8},{10,11... | collective-permute-start | bytes 589832 | tf_op jit(solution)/shard_map/ppermute | solution.py:129
  57.2 4.3 %copy-start.7 = (bf16[1,384,768]{2,1,0:T(8,128)(2,1)S(1)}, bf16[1,384,768]{2,1,0:T(8,128)(2,1)}, u32[]{:S(2)}) copy-start(bf16[1,384,768]{2,1,0:T(8,128)(2,1)} %param.20) | copy-start | bytes 1769476
  59.9 4.2 %copy-start.12 = (bf16[256,384]{1,0:T(8,128)(2,1)S(1)}, bf16[256,384]{1,0:T(8,128)(2,1)}, u32[]{:S(2)}) copy-start(bf16[256,384]{1,0:T(8,128)(2,1)} %copy-done.11) | copy-start | bytes 589828
  59.9 12.1 %collective-permute-start.3 = (bf16[256,384]{0,1:T(8,128)(2,1)S(1)}, bf16[256,384]{0,1:T(8,128)(2,1)}, u32[]{:S(2)}, u32[]{:S(2)}) collective-permute-start(bf16[256,384]{0,1:T(8,128)(2,1)S(1)} %bitcast.147), channel_id=1, source_target_pairs={{0,1},{1,0},{2,3},{3,2},{4,5},{5,4},{6,7},{7,6},{8,9},{9,8},{10,11... | collective-permute-start | bytes 589832 | tf_op jit(solution)/shard_map/ppermute | solution.py:129
  65.7 0.9 copy-start.3
  71.8 9.6 %collective-permute-start.6 = (bf16[256,768]{1,0:T(8,128)(2,1)}, bf16[256,768]{1,0:T(8,128)(2,1)}, u32[]{:S(2)}, u32[]{:S(2)}) collective-permute-start(bf16[256,768]{1,0:T(8,128)(2,1)} %fusion.102), channel_id=1, source_target_pairs={{0,1},{1,0},{2,3},{3,2},{4,5},{5,4},{6,7},{7,6},{8,9},{9,8},{10,11... | collective-permute-start | bytes 1179656 | tf_op jit(solution)/shard_map/ppermute | solution.py:24
  74.1 0.9 copy-start.1
  80.0 3.0 %copy-start.4 = (f32[256,768]{1,0:T(8,128)S(1)}, f32[256,768]{1,0:T(8,128)}, u32[]{:S(2)}) copy-start(f32[256,768]{1,0:T(8,128)} %copy-done.3) | copy-start | bytes 2359300
  83.0 13.7 %copy-start.2 = (f32[256,768]{1,0:T(8,128)S(1)}, f32[256,768]{1,0:T(8,128)}, u32[]{:S(2)}) copy-start(f32[256,768]{1,0:T(8,128)} %copy-done.1) | copy-start | bytes 2359300
  85.8 10.9 %collective-permute-start.7 = (bf16[256,768]{1,0:T(8,128)(2,1)S(1)}, bf16[256,768]{1,0:T(8,128)(2,1)S(1)}, u32[]{:S(2)}, u32[]{:S(2)}) collective-permute-start(bf16[256,768]{1,0:T(8,128)(2,1)S(1)} %fusion.8), channel_id=1, source_target_pairs={{0,1},{1,0},{2,3},{3,2},{4,5},{5,4},{6,7},{7,6},{8,9},{9,8},{10,11... | collective-permute-start | bytes 1179656 | tf_op jit(solution)/shard_map/ppermute | solution.py:24
  87.2 13.8 %copy-start.20 = (s32[128]{0:T(128)}, s32[128]{0:T(128)S(1)}, u32[]{:S(2)}) copy-start(s32[128]{0:T(128)S(1)} %iota_shift-right-logical_fusion.1) | copy-start | bytes 1540
  87.2 13.8 %copy-start.22 = (s32[128]{0:T(128)}, s32[128]{0:T(128)S(1)}, u32[]{:S(2)}) copy-start(s32[128]{0:T(128)S(1)} %iota_shift-right-logical_fusion) | copy-start | bytes 1540
  87.3 13.8 %copy-start.24 = (pred[128]{0:T(512)(128)(4,1)}, pred[128]{0:T(512)(128)(4,1)S(1)}, u32[]{:S(2)}) copy-start(pred[128]{0:T(512)(128)(4,1)S(1)} %compare_and_fusion.1) | copy-start | bytes 388
  87.3 13.8 %copy-start.26 = (pred[128]{0:T(512)(128)(4,1)}, pred[128]{0:T(512)(128)(4,1)S(1)}, u32[]{:S(2)}) copy-start(pred[128]{0:T(512)(128)(4,1)S(1)} %compare_and_fusion) | copy-start | bytes 388
  87.3 10.9 %collective-permute-start.8 = (bf16[256,768]{1,0:T(8,128)(2,1)S(1)}, bf16[256,768]{1,0:T(8,128)(2,1)S(1)}, u32[]{:S(2)}, u32[]{:S(2)}) collective-permute-start(bf16[256,768]{1,0:T(8,128)(2,1)S(1)} %add_convert_fusion.3), channel_id=1, source_target_pairs={{0,2},{2,4},{4,6},{6,8},{8,10},{10,12},{12,14},{14,16},{16,18},{18... | collective-permute-start | bytes 1179656 | tf_op jit(solution)/shard_map/ppermute | solution.py:19
  96.9 2.1 %copy-start.5 = (bf16[768,2048]{0,1:T(8,128)(2,1)S(1)}, bf16[768,2048]{0,1:T(8,128)(2,1)}, u32[]{:S(2)}) copy-start(bf16[768,2048]{0,1:T(8,128)(2,1)} %copy.35) | copy-start | bytes 9437188
  96.9 2.1 %copy-start.18 = (s32[128]{0:T(128)S(1)}, s32[128]{0:T(128)}, u32[]{:S(2)}) copy-start(s32[128]{0:T(128)} %broadcast_add_fusion.1) | copy-start | bytes 1540
  96.9 2.1 %copy-start.19 = (s32[128]{0:T(128)S(1)}, s32[128]{0:T(128)}, u32[]{:S(2)}) copy-start(s32[128]{0:T(128)} %broadcast_add_fusion) | copy-start | bytes 1540
  97.5 3.6 %copy-start.8 = (bf16[256,768]{1,0:T(8,128)(2,1)}, bf16[256,768]{1,0:T(8,128)(2,1)S(1)}, u32[]{:S(2)}) copy-start(bf16[256,768]{1,0:T(8,128)(2,1)S(1)} %add_convert_fusion.1) | copy-start | bytes 1179652
  98.2 0.7 copy-start.9
  103.3 4.3 %slice-start.1 = ((bf16[256,768]{1,0:T(8,128)(2,1)}), bf16[128,768]{1,0:T(8,128)(2,1)S(1)}, s32[]{:S(2)}) async-start(bf16[256,768]{1,0:T(8,128)(2,1)} %copy-done.9), calls=%async_computation.1 | async-start | bytes 393216 | tf_op jit(solution)/shard_map/slice | solution.py:160
  103.3 4.3 %copy-start.21 = (s32[128]{0:T(128)S(1)}, s32[128]{0:T(128)}, u32[]{:S(2)}) copy-start(s32[128]{0:T(128)} %copy-done.20) | copy-start | bytes 1540
  103.3 4.2 %copy-start.23 = (s32[128]{0:T(128)S(1)}, s32[128]{0:T(128)}, u32[]{:S(2)}) copy-start(s32[128]{0:T(128)} %copy-done.22) | copy-start | bytes 1540
  103.3 4.2 %copy-start.25 = (pred[128]{0:T(512)(128)(4,1)S(1)}, pred[128]{0:T(512)(128)(4,1)}, u32[]{:S(2)}) copy-start(pred[128]{0:T(512)(128)(4,1)} %copy-done.24) | copy-start | bytes 388
  103.3 4.2 %copy-start.27 = (pred[128]{0:T(512)(128)(4,1)S(1)}, pred[128]{0:T(512)(128)(4,1)}, u32[]{:S(2)}) copy-start(pred[128]{0:T(512)(128)(4,1)} %copy-done.26) | copy-start | bytes 388
  106.5 13.0 %collective-permute-start.9 = (bf16[2,8,8,16,128]{4,3,2,1,0:T(8,128)(2,1)}, bf16[2,8,8,16,128]{4,3,2,1,0:T(8,128)(2,1)}, u32[]{:S(2)}, u32[]{:S(2)}) collective-permute-start(bf16[2,8,8,16,128]{4,3,2,1,0:T(8,128)(2,1)} %bitcast.136), channel_id=1, source_target_pairs={{0,1},{1,0},{2,3},{3,2},{4,5},{5,4},{6,7},{7,6},{8,9},{9,8},{10,11... | collective-permute-start | bytes 1572872 | tf_op jit(solution)/shard_map/ppermute | solution.py:185
  107.5 4.1 %copy-start.6 = (bf16[768,2048]{0,1:T(8,128)(2,1)S(1)}, bf16[768,2048]{0,1:T(8,128)(2,1)}, u32[]{:S(2)}) copy-start(bf16[768,2048]{0,1:T(8,128)(2,1)} %copy.35) | copy-start | bytes 9437188
  107.6 4.1 %slice-start = ((bf16[256,768]{1,0:T(8,128)(2,1)}), bf16[128,768]{1,0:T(8,128)(2,1)S(1)}, s32[]{:S(2)}) async-start(bf16[256,768]{1,0:T(8,128)(2,1)} %copy-done.8), calls=%async_computation | async-start | bytes 393216 | tf_op jit(solution)/shard_map/slice | solution.py:160
  117.0 13.6 %collective-permute-start.10 = (bf16[2,8,8,16,128]{4,3,2,1,0:T(8,128)(2,1)}, bf16[2,8,8,16,128]{4,3,2,1,0:T(8,128)(2,1)S(1)}, u32[]{:S(2)}, u32[]{:S(2)}) collective-permute-start(bf16[2,8,8,16,128]{4,3,2,1,0:T(8,128)(2,1)} %bitcast.138), channel_id=1, source_target_pairs={{0,1},{1,0},{2,3},{3,2},{4,5},{5,4},{6,7},{7,6},{8,9},{9,8},{10,11... | collective-permute-start | bytes 1572872 | tf_op jit(solution)/shard_map/ppermute | solution.py:185

commit v12 on v11

--- a/solution.py
+++ b/solution.py
@@ -142,12 +142,20 @@
             sent_latent, partial_forward = lax.optimization_barrier(
                 (sent_latent, partial_forward)
             )
-        part = part + partner_sum(partial_forward)
-        latent = layer_norm(part, norm_gain[2 * LAYERS], norm_bias[2 * LAYERS]).astype(jnp.bfloat16)
         if chunk == 1:
-            sent_latent = latent
-        else:
-            own_latent = latent
+            part = part + partner_sum(partial_forward)
+            sent_latent = layer_norm(
+                part, norm_gain[2 * LAYERS], norm_bias[2 * LAYERS]
+            ).astype(jnp.bfloat16)
+            continue
+        latents = []
+        piece_rows = half_tokens // 2
+        for rows in range(0, half_tokens, piece_rows):
+            piece = part[rows:rows + piece_rows] + partner_sum(partial_forward[rows:rows + piece_rows])
+            latents.append(layer_norm(
+                piece, norm_gain[2 * LAYERS], norm_bias[2 * LAYERS]
+            ).astype(jnp.bfloat16))
+        own_latent = jnp.concatenate(latents, 0)
     arrived_latent = from_behind(sent_latent, "tile", 1)
     later = (tile_index > 0).astype(jnp.float32)
     half_side = side // 2

time: 137 us -> 139 us (1.015)
  other arithmetic: 18.9 us -> 20.6 us
  starting transfers between devices: 15.8 us -> 17.2 us
    ppermute x2 -> x3, waiting for transfers between devices: 4.55 us -> 4.26 us  [partner_sum(): other = lax.ppermute(rounded, 'head', [(0, 1), (1, 0)])]
  transfers between devices with their start and end apart: 11 -> 12, of which waited for: 7 -> 7; matrix products, arithmetic and copies ran while one was open for 55% -> 55% of each run, Pallas kernels for 0% -> 0%
where the time goes in v12:
time: 139 us; the launch traced here: 137 us
  matrix products  46.3 us (33%)
  local copies, waits for them, and re-layouts  28.3 us (20%)
  waiting for transfers between devices  24.6 us (18%)
  other arithmetic  20.6 us (15%)
  starting transfers between devices  17.2 us (12%)
    ppermute x2, waiting for transfers between devices, body(): other_rows = lax.ppermute(arranged, 'head', [(0, 1), (1, 0)])  13.6 us
    dot_general x4, matrix products, body(): lax.dot_general(latent, decode_by_depth, (((1,), (2,)), ((), ())), prefer...  10.6 us
    dot_general x2, matrix products, body(): jnp.dot(hidden, w_down[0], preferred_element_type=jnp.float32)  9.28 us
    ppermute x2, starting transfers between devices, from_behind(): return lax.ppermute(block, axis, route)  9.26 us
    sub x2, matrix products, body(): weights = jax.nn.softmax(scores, axis=-1).astype(jnp.bfloat16)  8.89 us
    unnamed x57, local copies, waits for them, and re-layouts  7.92 us
    dot_general x2, matrix products, body(): jnp.einsum('hts,shd->thd', weights, values, preferred_element_type=jnp.fl...  5.97 us
    reshape x1, local copies, waits for them, and re-layouts, embed_planes(): voxels = jnp.swapaxes(grouped, 1, 2).reshape(rows, PATCH, PATCH * PATCH)  4.86 us
  transfers between devices with their start and end apart: 12, of which 7 were waited for; matrix products, arithmetic and copies ran while one was open for 55% of the time, Pallas kernels for 0%

profile of v12, /device:TPU:31, one launch (start us, length us, event | category | flops | bytes accessed | tf_op | source)
XLA Modules:
  0.0 137.5 jit_solution(10332311818961107304)
XLA Ops:
  0.0 1.6 %collective-permute-start.4 = (bf16[384,768]{1,0:T(8,128)(2,1)}, bf16[384,768]{1,0:T(8,128)(2,1)}, u32[]{:S(2)}, u32[]{:S(2)}) collective-permute-start(bf16[384,768]{1,0:T(8,128)(2,1)} %bitcast.135), channel_id=1, source_target_pairs={{0,1},{1,0},{2,3},{3,2},{4,5},{5,4},{6,7},{7,6},{8,9},{9,8},{10,11... | collective-permute-start | bytes 1769480 | tf_op jit(solution)/shard_map/ppermute | solution.py:83
  2.7 1.9 %convert_element_type.156 = f32[512,384]{1,0:T(8,128)} convert(bf16[512,384]{1,0:T(8,128)(2,1)} %param.16) | non-fusion elementwise | flops 196608 | bytes 1179648 | tf_op jit(solution)/shard_map/convert_element_type | solution.py:86
  4.7 2.5 %broadcast_multiply_fusion = bf16[64,128,128]{2,1,0:T(8,128)(2,1)S(1)} fusion(bf16[64,128,128]{2,1,0:T(8,128)(2,1)} %param.12, bf16[64,128]{1,0:T(8,128)(2,1)S(1)} %convert_element_type.155), kind=kLoop, calls=%fused_computation.122 | loop fusion | flops 1048576 | bytes 4210688 | tf_op jit(solution)/shard_map/mul | solution.py:43
  7.1 1.9 %copy.30 = bf16[4,8,16,16,128]{4,3,2,1,0:T(8,128)(2,1)} copy(bf16[4,8,16,16,128]{4,3,1,2,0:T(8,128)(2,1)S(1)} %bitcast.126) | data formatting | bytes 4194304 | tf_op jit(solution)/shard_map/transpose | solution.py:44
  9.0 4.1 %copy.31 = bf16[32,128,256]{2,1,0:T(8,128)(2,1)} copy(bf16[32,128,256]{1,2,0:T(8,128)(2,1)} %bitcast.127) | data formatting | bytes 4194304 | tf_op jit(solution)/shard_map/transpose | solution.py:46
  13.1 4.9 %copy.32 = bf16[256,16,256]{0,1,2:T(8,128)(2,1)} copy(bf16[256,16,256]{2,1,0:T(8,128)(2,1)} %bitcast.128) | data formatting | bytes 4194304 | tf_op jit(solution)/shard_map/reshape | solution.py:46
  18.1 3.8 %fusion.166 = (bf16[256,384]{1,0:T(8,128)(2,1)}, bf16[256,384]{1,0:T(8,128)(2,1)}) fusion(f32[512,384]{1,0:T(8,128)} %convert_element_type.156, f32[32,384]{1,0:T(8,128)S(1)} %fusion.221, bf16[256,16,256]{0,1,2:T(8,128)(2,1)} %copy.32, bf16[16,256,384]{2,0,1:T(8,128)(2,1)S(1)} %bitcast.125), kind=kOutput, calls=%fused_computation.147 | convolution fusion | flops 805797888 | bytes 6471680 | tf_op jit(solution)/shard_map/dot_general | solution.py:47
  22.0 2.9 %collective-permute-start.1 = (bf16[256,384]{1,0:T(8,128)(2,1)}, bf16[256,384]{1,0:T(8,128)(2,1)S(1)}, u32[]{:S(2)}, u32[]{:S(2)}) collective-permute-start(bf16[256,384]{1,0:T(8,128)(2,1)} %get-tuple-element.28), channel_id=1, source_target_pairs={{2,0},{4,2},{6,4},{8,6},{10,8},{12,10},{14,12},{16,14},{18,16},{20... | collective-permute-start | bytes 589832 | tf_op jit(solution)/shard_map/ppermute | solution.py:19
  26.6 4.7 %copy.35 = bf16[768,2048]{0,1:T(8,128)(2,1)} copy(bf16[768,2048]{1,0:T(8,128)(2,1)} %param.23) | data formatting | bytes 6291456 | tf_op args[11]
  31.9 3.1 %collective-permute-done.1 = bf16[256,384]{1,0:T(8,128)(2,1)S(1)} collective-permute-done((bf16[256,384]{1,0:T(8,128)(2,1)}, bf16[256,384]{1,0:T(8,128)(2,1)S(1)}, u32[]{:S(2)}, u32[]{:S(2)}) %collective-permute-start.1) | collective-permute-done | bytes 196640 | tf_op jit(solution)/shard_map/ppermute | solution.py:19
  35.0 1.0 fusion.189
  36.8 1.3 fusion.167
  38.1 2.5 %collective-permute-done.2 = bf16[256,384]{1,0:T(8,128)(2,1)S(1)} collective-permute-done((bf16[256,384]{1,0:T(8,128)(2,1)S(1)}, bf16[256,384]{1,0:T(8,128)(2,1)S(1)}, u32[]{:S(2)}, u32[]{:S(2)}) %collective-permute-start.2) | collective-permute-done | bytes 196640 | tf_op jit(solution)/shard_map/ppermute | solution.py:97
  41.9 1.3 fusion.57
  43.9 0.9 fusion.215
  44.8 4.5 %fusion.217 = (f32[6,256]{1,0:T(8,128)}, f32[6,256,512]{2,1,0:T(8,128)}) fusion(bf16[256,6,64]{0,2,1:T(8,128)(2,1)} %bitcast.150, bf16[512,6,64]{0,2,1:T(8,128)(2,1)} %bitcast.145), kind=kOutput, calls=%fused_computation.224 | convolution fusion | flops 103023104 | bytes 3741696 | tf_op jit(solution)/shard_map/sub | solution.py:124
  49.3 3.3 %fusion.114 = bf16[6,64,256]{2,1,0:T(8,128)(2,1)} fusion(bf16[512,6,64]{0,2,1:T(8,128)(2,1)} %bitcast.143, f32[6,256,512]{2,1,0:T(8,128)} %get-tuple-element.32, f32[6,256]{1,0:T(8,128)} %get-tuple-element.31), kind=kOutput, calls=%fused_computation.89 | convolution fusion | flops 102334464 | bytes 3741696 | tf_op jit(solution)/shard_map/hts,shd->thd/dot_general | solution.py:125
  52.6 1.2 collective-permute-start.5
  53.8 4.4 %fusion.219 = (f32[6,256]{1,0:T(8,128)}, f32[6,256,512]{2,1,0:T(8,128)}) fusion(bf16[256,6,64]{0,2,1:T(8,128)(2,1)S(1)} %bitcast.149, bf16[512,6,64]{0,2,1:T(8,128)(2,1)} %bitcast.146), kind=kOutput, calls=%fused_computation.226 | convolution fusion | flops 103023104 | bytes 3741696 | tf_op jit(solution)/shard_map/sub | solution.py:124
  58.2 2.7 %fusion.115 = bf16[6,64,256]{2,1,0:T(8,128)(2,1)S(1)} fusion(bf16[512,6,64]{0,2,1:T(8,128)(2,1)} %bitcast.144, f32[6,256,512]{2,1,0:T(8,128)} %get-tuple-element.36, f32[6,256]{1,0:T(8,128)} %get-tuple-element.35), kind=kOutput, calls=%fused_computation.90 | convolution fusion | flops 102334464 | bytes 3741696 | tf_op jit(solution)/shard_map/hts,shd->thd/dot_general | solution.py:125
  61.4 1.3 fusion.108
  62.8 1.3 fusion.112
  64.0 1.7 %fusion.218 = (f32[256]{0:T(256)S(1)}, f32[256,768]{1,0:T(8,128)S(1)}) fusion(f32[256,768]{1,0:T(8,128)S(1)} %fusion.108, bf16[256,384]{0,1:T(8,128)(2,1)} %collective-permute-done.5, bf16[384,768]{1,0:T(8,128)(2,1)} %collective-permute-done.4, bf16[256,384]{1,0:T(8,128)(2,1)S(1)} %fusion.189, bf16[256,384]{1,0:T(8,128)(2,1)S(1)} %copy-done.12, pred[]{:T(512)S(6)} %eq.4), kind=kOutput, calls=%fused_computation.225 | convolution fusion | flops 153943808 | bytes 2753537 | tf_op jit(solution)/shard_map/dot_general | solution.py:131
  66.8 5.0 %fusion.102 = bf16[256,768]{1,0:T(8,128)(2,1)} fusion(bf16[1,1536,768]{2,1,0:T(8,128)(2,1)} %param.22, bf16[1,768,1536]{2,1,0:T(8,128)(2,1)} %param.21, f32[256,768]{1,0:T(8,128)} %copy-done.1, f32[768]{0:T(1024)S(1)} %get-tuple-element.20, f32[768]{0:T(1024)S(1)} %get-tuple-element.17, f32[256]{0:T(256)S(1)} %add_rsqrt_fusion.3, ...), kind=kOutput, calls=%fused_computation.74 | convolution fusion | flops 1212678144 | bytes 5906432 | tf_op jit(solution)/shard_map/dot_general | solution.py:140
  71.8 1.2 collective-permute-start.6
  73.1 2.1 %fusion.220 = (f32[256]{0:T(256)S(1)}, f32[256,768]{1,0:T(8,128)S(1)}) fusion(f32[256,768]{1,0:T(8,128)} %fusion.112, bf16[256,384]{0,1:T(8,128)(2,1)} %collective-permute-done.3, bf16[384,768]{1,0:T(8,128)(2,1)} %collective-permute-done.4, bf16[256,384]{1,0:T(8,128)(2,1)} %get-tuple-element.27, bf16[256,384]{1,0:T(8,128)(2,1)} %collective-permute-done, ...), kind=kOutput, calls=%fused_computation.227 | convolution fusion | flops 153943808 | bytes 2753537 | tf_op jit(solution)/shard_map/dot_general | solution.py:131
  75.1 0.9 copy-done.3
  76.8 4.3 %fusion.8 = bf16[256,768]{1,0:T(8,128)(2,1)S(1)} fusion(bf16[1,1536,768]{2,1,0:T(8,128)(2,1)} %param.22, bf16[1,768,1536]{2,1,0:T(8,128)(2,1)} %param.21, f32[256,768]{1,0:T(8,128)} %copy-done.3, f32[256]{0:T(256)} %add_rsqrt_fusion.1, f32[256]{0:T(256)S(1)} %broadcast_multiply_fusion.2, f32[768]{0:T(1024)} %copy-done.15, f32[768]{0:T(1024)S(1)} %get-tuple-element.17), kind=kOutput, calls=%fused_computation.12 | convolution fusion | flops 1212481536 | bytes 5906432 | tf_op jit(solution)/shard_map/dot_general | solution.py:140
  81.1 2.0 %collective-permute-done.6 = bf16[256,768]{1,0:T(8,128)(2,1)} collective-permute-done((bf16[256,768]{1,0:T(8,128)(2,1)}, bf16[256,768]{1,0:T(8,128)(2,1)}, u32[]{:S(2)}, u32[]{:S(2)}) %collective-permute-start.6) | collective-permute-done | bytes 393248 | tf_op jit(solution)/shard_map/ppermute | solution.py:24
  83.1 1.6 %fusion.213 = f32[256]{0:T(256)S(1)} fusion(f32[256,768]{1,0:T(8,128)} %copy-done.1, bf16[256,768]{1,0:T(8,128)(2,1)} %collective-permute-done.6, bf16[256,768]{1,0:T(8,128)(2,1)} %fusion.102), kind=kLoop, calls=%fused_computation.220 | loop fusion | flops 982784 | bytes 1573888 | tf_op jit(solution)/shard_map/reduce_sum | solution.py:29
  84.7 1.4 %multiply_reduce_fusion.4 = f32[256]{0:T(256)S(1)} fusion(f32[256]{0:T(256)S(1)} %broadcast_multiply_fusion.3, f32[256,768]{1,0:T(8,128)S(1)} %copy-done.2, bf16[256,768]{1,0:T(8,128)(2,1)} %collective-permute-done.6, bf16[256,768]{1,0:T(8,128)(2,1)} %fusion.102), kind=kLoop, calls=%fused_computation.128 | loop fusion | flops 1376000 | bytes 1574912 | tf_op jit(solution)/shard_map/reduce_sum | solution.py:31
  86.2 1.4 add_convert_fusion.2
  89.2 6.4 %collective-permute-start.8 = (bf16[256,768]{1,0:T(8,128)(2,1)S(1)}, bf16[256,768]{1,0:T(8,128)(2,1)S(1)}, u32[]{:S(2)}, u32[]{:S(2)}) collective-permute-start(bf16[256,768]{1,0:T(8,128)(2,1)S(1)} %add_convert_fusion.2), channel_id=1, source_target_pairs={{0,2},{2,4},{4,6},{6,8},{8,10},{10,12},{12,14},{14,16},{16,18},{18... | collective-permute-start | bytes 1179656 | tf_op jit(solution)/shard_map/ppermute | solution.py:19
  95.6 2.2 %collective-permute-done.10 = bf16[128,768]{1,0:T(8,128)(2,1)S(1)} collective-permute-done((bf16[128,768]{1,0:T(8,128)(2,1)S(1)}, bf16[128,768]{1,0:T(8,128)(2,1)S(1)}, u32[]{:S(2)}, u32[]{:S(2)}) %collective-permute-start.10) | collective-permute-done | bytes 196640 | tf_op jit(solution)/shard_map/ppermute | solution.py:24
  99.2 1.1 collective-permute-done.8
  101.1 2.1 %fusion.78 = f32[128,16,128]{2,0,1:T(8,128)S(1)} fusion(bf16[16,128,768]{2,0,1:T(8,128)(2,1)S(1)} %bitcast.132, s32[128]{0:T(128)S(1)} %copy-done.20, s32[128]{0:T(128)S(1)} %copy-done.19, s32[]{:T(128)S(6)} %mul.238, s32[128]{0:T(128)S(1)} %copy-done.22, s32[128]{0:T(128)S(1)} %copy-done.18, pred[128]{0:T(512)(128)(4,1)S(1)} %compare_and_fusion.1, ...), kind=kOutput, calls=%fused_computation.66 | convolution fusion | flops 406061056 | bytes 4393988 | tf_op jit(solution)/shard_map/dot_general | solution.py:172
  103.2 2.3 %divide_convert_fusion.9 = bf16[128,16,128]{2,0,1:T(8,128)(2,1)S(1)} fusion(f32[128,16,128]{2,0,1:T(8,128)S(1)} %fusion.78, bf16[16,128,768]{2,0,1:T(8,128)(2,1)S(1)} %bitcast.133, f32[]{:T(128)S(6)} %convert_element_type.195, s32[128]{0:T(128)S(1)} %copy-done.20, s32[128]{0:T(128)S(1)} %copy-done.19, s32[]{:T(128)S(6)} %mul.238, s32[128]{0:T(128)S(1)} %copy-done.22, ...), kind=kOutput, calls=%fused_computation.121 | convolution fusion | flops 409305088 | bytes 5517320 | tf_op jit(solution)/shard_map/dot_general | solution.py:172
  105.5 1.1 copy.38
  106.7 2.0 %copy.39 = bf16[16,128,128]{2,1,0:T(8,128)(2,1)} copy(bf16[16,128,128]{1,2,0:T(8,128)(2,1)} %bitcast.140) | data formatting | bytes 1048576 | tf_op jit(solution)/shard_map/transpose | solution.py:191
  108.9 4.1 %fusion.99 = f32[128,16,128]{2,0,1:T(8,128)S(1)} fusion(bf16[16,128,768]{2,0,1:T(8,128)(2,1)} %bitcast.131, s32[128]{0:T(128)S(1)} %copy-done.21, s32[128]{0:T(128)S(1)} %copy-done.19, s32[]{:T(128)S(6)} %mul.238, s32[128]{0:T(128)S(1)} %copy-done.23, s32[128]{0:T(128)S(1)} %copy-done.18, pred[128]{0:T(512)(128)(4,1)S(1)} %copy-done.25, ...), kind=kOutput, calls=%fused_computation.73 | convolution fusion | flops 406323200 | bytes 4393220 | tf_op jit(solution)/shard_map/dot_general | solution.py:172
  113.0 2.2 %divide_convert_fusion.8 = bf16[128,16,128]{2,0,1:T(8,128)(2,1)S(1)} fusion(f32[128,16,128]{2,0,1:T(8,128)S(1)} %fusion.99, bf16[16,128,768]{2,0,1:T(8,128)(2,1)S(1)} %bitcast.134, f32[]{:T(128)S(6)} %convert_element_type.195, s32[128]{0:T(128)S(1)} %copy-done.21, s32[128]{0:T(128)S(1)} %copy-done.19, s32[]{:T(128)S(6)} %mul.238, s32[128]{0:T(128)S(1)} %copy-done.23, ...), kind=kOutput, calls=%fused_computation.120 | convolution fusion | flops 408682496 | bytes 4917512 | tf_op jit(solution)/shard_map/dot_general | solution.py:172
  115.2 1.1 copy.43
  116.3 2.0 %copy.44 = bf16[16,128,128]{2,1,0:T(8,128)(2,1)} copy(bf16[16,128,128]{1,2,0:T(8,128)(2,1)} %bitcast.141) | data formatting | bytes 1048576 | tf_op jit(solution)/shard_map/transpose | solution.py:191
  118.4 1.3 collective-permute-start.11
  119.7 2.5 %collective-permute-done.9 = bf16[2,8,8,16,128]{4,3,2,1,0:T(8,128)(2,1)} collective-permute-done((bf16[2,8,8,16,128]{4,3,2,1,0:T(8,128)(2,1)}, bf16[2,8,8,16,128]{4,3,2,1,0:T(8,128)(2,1)}, u32[]{:S(2)}, u32[]{:S(2)}) %collective-permute-start.9) | collective-permute-done | bytes 524320 | tf_op jit(solution)/shard_map/ppermute | solution.py:193
  122.2 11.1 %collective-permute-done.11 = bf16[2,8,8,16,128]{4,3,2,1,0:T(8,128)(2,1)S(1)} collective-permute-done((bf16[2,8,8,16,128]{4,3,2,1,0:T(8,128)(2,1)}, bf16[2,8,8,16,128]{4,3,2,1,0:T(8,128)(2,1)S(1)}, u32[]{:S(2)}, u32[]{:S(2)}) %collective-permute-start.11) | collective-permute-done | bytes 524320 | tf_op jit(solution)/shard_map/ppermute | solution.py:193
  133.3 2.1 %fusion.141 = (bf16[2,16,8,16,128]{4,3,1,2,0:T(8,128)(2,1)S(1)}, bf16[2,16,8,16,128]{4,3,1,2,0:T(8,128)(2,1)S(1)}) fusion(bf16[2,8,8,16,128]{4,3,2,1,0:T(8,128)(2,1)} %collective-permute-done.9, bf16[2,8,8,16,128]{4,3,2,1,0:T(8,128)(2,1)} %bitcast.137, pred[]{:T(512)S(6)} %eq.4, bf16[2,8,8,16,128]{4,3,2,1,0:T(8,128)(2,1)} %bitcast.139, ...), kind=kLoop, calls=%fused_computation.117 | loop fusion | flops 3145728 | bytes 4194305 | tf_op jit(solution)/shard_map/transpose | solution.py:199
  136.0 1.5 %pad_maximum_fusion = bf16[64,128,128]{2,1,0:T(8,128)(2,1)} fusion(bf16[32,128,128]{2,1,0:T(8,128)(2,1)S(1)} %bitcast.130, bf16[32,128,128]{2,1,0:T(8,128)(2,1)S(1)} %bitcast.129), kind=kLoop, calls=%fused_computation.20 | loop fusion | flops 1048576 | bytes 4194304 | tf_op jit(solution)/shard_map/concatenate | solution.py:200
  (105 shorter events, 13.2 us)
Async XLA Ops:
  0.0 18.1 %copy-start = (bf16[4096,384]{1,0:T(8,128)(2,1)S(1)}, bf16[4096,384]{1,0:T(8,128)(2,1)}, u32[]{:S(2)}) copy-start(bf16[4096,384]{1,0:T(8,128)(2,1)} %param.14) | copy-start | bytes 9437188
  0.0 64.0 %collective-permute-start.4 = (bf16[384,768]{1,0:T(8,128)(2,1)}, bf16[384,768]{1,0:T(8,128)(2,1)}, u32[]{:S(2)}, u32[]{:S(2)}) collective-permute-start(bf16[384,768]{1,0:T(8,128)(2,1)} %bitcast.135), channel_id=1, source_target_pairs={{0,1},{1,0},{2,3},{3,2},{4,5},{5,4},{6,7},{7,6},{8,9},{9,8},{10,11... | collective-permute-start | bytes 1769480 | tf_op jit(solution)/shard_map/ppermute | solution.py:83
  13.1 4.9 %copy-start.9 = (bf16[256,384]{1,0:T(8,128)(2,1)S(1)}, bf16[256,384]{1,0:T(8,128)(2,1)}, u32[]{:S(2)}) copy-start(bf16[256,384]{1,0:T(8,128)(2,1)} %param.15) | copy-start | bytes 589828
  18.1 7.9 %copy-start.13 = (f32[3,768]{1,0:T(4,128)S(1)}, f32[3,768]{1,0:T(4,128)}, u32[]{:S(2)}) copy-start(f32[3,768]{1,0:T(4,128)} %param.17) | copy-start | bytes 27652
  22.0 13.0 %collective-permute-start.1 = (bf16[256,384]{1,0:T(8,128)(2,1)}, bf16[256,384]{1,0:T(8,128)(2,1)S(1)}, u32[]{:S(2)}, u32[]{:S(2)}) collective-permute-start(bf16[256,384]{1,0:T(8,128)(2,1)} %get-tuple-element.28), channel_id=1, source_target_pairs={{2,0},{4,2},{6,4},{8,6},{10,8},{12,10},{14,12},{16,14},{18,16},{20... | collective-permute-start | bytes 589832 | tf_op jit(solution)/shard_map/ppermute | solution.py:19
  24.8 12.0 %collective-permute-start = (bf16[256,384]{1,0:T(8,128)(2,1)}, bf16[256,384]{1,0:T(8,128)(2,1)}, u32[]{:S(2)}, u32[]{:S(2)}) collective-permute-start(bf16[256,384]{1,0:T(8,128)(2,1)} %get-tuple-element.27), channel_id=1, source_target_pairs={{0,1},{1,0},{2,3},{3,2},{4,5},{5,4},{6,7},{7,6},{8,9},{9,8},{10,11... | collective-permute-start | bytes 589832 | tf_op jit(solution)/shard_map/ppermute | solution.py:97
  26.6 5.2 %copy-start.14 = (f32[3,768]{1,0:T(4,128)S(1)}, f32[3,768]{1,0:T(4,128)}, u32[]{:S(2)}) copy-start(f32[3,768]{1,0:T(4,128)} %param.18) | copy-start | bytes 27652
  31.9 34.9 %copy-start.15 = (f32[768]{0:T(1024)}, f32[768]{0:T(1024)S(1)}, u32[]{:S(2)}) copy-start(f32[768]{0:T(1024)S(1)} %get-tuple-element.20) | copy-start | bytes 9220
  36.0 4.6 %collective-permute-start.2 = (bf16[256,384]{1,0:T(8,128)(2,1)S(1)}, bf16[256,384]{1,0:T(8,128)(2,1)S(1)}, u32[]{:S(2)}, u32[]{:S(2)}) collective-permute-start(bf16[256,384]{1,0:T(8,128)(2,1)S(1)} %fusion.189), channel_id=1, source_target_pairs={{0,1},{1,0},{2,3},{3,2},{4,5},{5,4},{6,7},{7,6},{8,9},{9,8},{10,11... | collective-permute-start | bytes 589832 | tf_op jit(solution)/shard_map/ppermute | solution.py:97
  38.1 3.8 %copy-start.16 = (f32[768]{0:T(1024)S(1)}, f32[768]{0:T(1024)}, u32[]{:S(2)}) copy-start(f32[768]{0:T(1024)} %get-tuple-element.18) | copy-start | bytes 9220
  38.1 3.8 %copy-start.17 = (bf16[1,3,768,384]{3,2,1,0:T(8,128)(2,1)S(1)}, bf16[1,3,768,384]{3,2,1,0:T(8,128)(2,1)}, u32[]{:S(2)}) copy-start(bf16[1,3,768,384]{3,2,1,0:T(8,128)(2,1)} %param.19) | copy-start | bytes 5308420
  40.6 0.7 copy-start.11
  52.6 11.4 %collective-permute-start.5 = (bf16[256,384]{0,1:T(8,128)(2,1)}, bf16[256,384]{0,1:T(8,128)(2,1)}, u32[]{:S(2)}, u32[]{:S(2)}) collective-permute-start(bf16[256,384]{0,1:T(8,128)(2,1)} %bitcast.22), channel_id=1, source_target_pairs={{0,1},{1,0},{2,3},{3,2},{4,5},{5,4},{6,7},{7,6},{8,9},{9,8},{10,11... | collective-permute-start | bytes 589832 | tf_op jit(solution)/shard_map/ppermute | solution.py:129
  58.2 3.2 %copy-start.7 = (bf16[1,384,768]{2,1,0:T(8,128)(2,1)S(1)}, bf16[1,384,768]{2,1,0:T(8,128)(2,1)}, u32[]{:S(2)}) copy-start(bf16[1,384,768]{2,1,0:T(8,128)(2,1)} %param.20) | copy-start | bytes 1769476
  60.9 3.1 %copy-start.12 = (bf16[256,384]{1,0:T(8,128)(2,1)S(1)}, bf16[256,384]{1,0:T(8,128)(2,1)}, u32[]{:S(2)}) copy-start(bf16[256,384]{1,0:T(8,128)(2,1)} %copy-done.11) | copy-start | bytes 589828
  60.9 12.1 %collective-permute-start.3 = (bf16[256,384]{0,1:T(8,128)(2,1)S(1)}, bf16[256,384]{0,1:T(8,128)(2,1)}, u32[]{:S(2)}, u32[]{:S(2)}) collective-permute-start(bf16[256,384]{0,1:T(8,128)(2,1)S(1)} %bitcast.147), channel_id=1, source_target_pairs={{0,1},{1,0},{2,3},{3,2},{4,5},{5,4},{6,7},{7,6},{8,9},{9,8},{10,11... | collective-permute-start | bytes 589832 | tf_op jit(solution)/shard_map/ppermute | solution.py:129
  65.7 0.9 copy-start.1
  71.8 11.3 %collective-permute-start.6 = (bf16[256,768]{1,0:T(8,128)(2,1)}, bf16[256,768]{1,0:T(8,128)(2,1)}, u32[]{:S(2)}, u32[]{:S(2)}) collective-permute-start(bf16[256,768]{1,0:T(8,128)(2,1)} %fusion.102), channel_id=1, source_target_pairs={{0,1},{1,0},{2,3},{3,2},{4,5},{5,4},{6,7},{7,6},{8,9},{9,8},{10,11... | collective-permute-start | bytes 1179656 | tf_op jit(solution)/shard_map/ppermute | solution.py:24
  75.1 0.9 copy-start.3
  81.1 3.6 %copy-start.2 = (f32[256,768]{1,0:T(8,128)S(1)}, f32[256,768]{1,0:T(8,128)}, u32[]{:S(2)}) copy-start(f32[256,768]{1,0:T(8,128)} %copy-done.1) | copy-start | bytes 2359300
  84.7 13.1 %copy-start.4 = (f32[256,768]{1,0:T(8,128)S(1)}, f32[256,768]{1,0:T(8,128)}, u32[]{:S(2)}) copy-start(f32[256,768]{1,0:T(8,128)} %copy-done.3) | copy-start | bytes 2359300
  87.6 13.5 %copy-start.5 = (bf16[768,2048]{0,1:T(8,128)(2,1)S(1)}, bf16[768,2048]{0,1:T(8,128)(2,1)}, u32[]{:S(2)}) copy-start(bf16[768,2048]{0,1:T(8,128)(2,1)} %copy.35) | copy-start | bytes 9437188
  87.6 13.5 %copy-start.18 = (s32[128]{0:T(128)S(1)}, s32[128]{0:T(128)}, u32[]{:S(2)}) copy-start(s32[128]{0:T(128)} %broadcast_add_fusion.1) | copy-start | bytes 1540
  87.6 13.5 %copy-start.19 = (s32[128]{0:T(128)S(1)}, s32[128]{0:T(128)}, u32[]{:S(2)}) copy-start(s32[128]{0:T(128)} %broadcast_add_fusion) | copy-start | bytes 1540
  87.6 13.5 %copy-start.20 = (s32[128]{0:T(128)S(1)}, s32[128]{0:T(128)}, u32[]{:S(2)}) copy-start(s32[128]{0:T(128)} %iota_shift-right-logical_fusion.1) | copy-start | bytes 1540
  87.6 13.5 %copy-start.22 = (s32[128]{0:T(128)S(1)}, s32[128]{0:T(128)}, u32[]{:S(2)}) copy-start(s32[128]{0:T(128)} %iota_shift-right-logical_fusion) | copy-start | bytes 1540
  87.6 8.0 %collective-permute-start.7 = (bf16[128,768]{1,0:T(8,128)(2,1)S(1)}, bf16[128,768]{1,0:T(8,128)(2,1)S(1)}, u32[]{:S(2)}, u32[]{:S(2)}) collective-permute-start(bf16[128,768]{1,0:T(8,128)(2,1)S(1)} %get-tuple-element.29), channel_id=1, source_target_pairs={{0,1},{1,0},{2,3},{3,2},{4,5},{5,4},{6,7},{7,6},{8,9},{9,8},{10,11... | collective-permute-start | bytes 589832 | tf_op jit(solution)/shard_map/ppermute | solution.py:24
  88.4 9.4 %collective-permute-start.10 = (bf16[128,768]{1,0:T(8,128)(2,1)S(1)}, bf16[128,768]{1,0:T(8,128)(2,1)S(1)}, u32[]{:S(2)}, u32[]{:S(2)}) collective-permute-start(bf16[128,768]{1,0:T(8,128)(2,1)S(1)} %get-tuple-element.30), channel_id=1, source_target_pairs={{0,1},{1,0},{2,3},{3,2},{4,5},{5,4},{6,7},{7,6},{8,9},{9,8},{10,11... | collective-permute-start | bytes 589832 | tf_op jit(solution)/shard_map/ppermute | solution.py:24
  89.2 14.0 %copy-start.24 = (pred[128]{0:T(512)(128)(4,1)}, pred[128]{0:T(512)(128)(4,1)S(1)}, u32[]{:S(2)}) copy-start(pred[128]{0:T(512)(128)(4,1)S(1)} %compare_and_fusion.1) | copy-start | bytes 388
  89.2 14.0 %copy-start.26 = (pred[128]{0:T(512)(128)(4,1)}, pred[128]{0:T(512)(128)(4,1)S(1)}, u32[]{:S(2)}) copy-start(pred[128]{0:T(512)(128)(4,1)S(1)} %compare_and_fusion) | copy-start | bytes 388
  89.2 11.1 %collective-permute-start.8 = (bf16[256,768]{1,0:T(8,128)(2,1)S(1)}, bf16[256,768]{1,0:T(8,128)(2,1)S(1)}, u32[]{:S(2)}, u32[]{:S(2)}) collective-permute-start(bf16[256,768]{1,0:T(8,128)(2,1)S(1)} %add_convert_fusion.2), channel_id=1, source_target_pairs={{0,2},{2,4},{4,6},{6,8},{8,10},{10,12},{12,14},{14,16},{16,18},{18... | collective-permute-start | bytes 1179656 | tf_op jit(solution)/shard_map/ppermute | solution.py:19
  100.3 0.8 copy-start.8
  105.5 3.4 %slice-start = ((bf16[256,768]{1,0:T(8,128)(2,1)}), bf16[128,768]{1,0:T(8,128)(2,1)S(1)}, s32[]{:S(2)}) async-start(bf16[256,768]{1,0:T(8,128)(2,1)} %copy-done.8), calls=%async_computation | async-start | bytes 393216 | tf_op jit(solution)/shard_map/slice | solution.py:168
  105.5 3.4 %copy-start.21 = (s32[128]{0:T(128)S(1)}, s32[128]{0:T(128)}, u32[]{:S(2)}) copy-start(s32[128]{0:T(128)} %iota_shift-right-logical_fusion.1) | copy-start | bytes 1540
  105.5 3.4 %copy-start.23 = (s32[128]{0:T(128)S(1)}, s32[128]{0:T(128)}, u32[]{:S(2)}) copy-start(s32[128]{0:T(128)} %iota_shift-right-logical_fusion) | copy-start | bytes 1540
  105.5 3.4 %copy-start.25 = (pred[128]{0:T(512)(128)(4,1)S(1)}, pred[128]{0:T(512)(128)(4,1)}, u32[]{:S(2)}) copy-start(pred[128]{0:T(512)(128)(4,1)} %copy-done.24) | copy-start | bytes 388
  105.5 3.4 %copy-start.27 = (pred[128]{0:T(512)(128)(4,1)S(1)}, pred[128]{0:T(512)(128)(4,1)}, u32[]{:S(2)}) copy-start(pred[128]{0:T(512)(128)(4,1)} %copy-done.26) | copy-start | bytes 388
  108.7 13.5 %collective-permute-start.9 = (bf16[2,8,8,16,128]{4,3,2,1,0:T(8,128)(2,1)}, bf16[2,8,8,16,128]{4,3,2,1,0:T(8,128)(2,1)}, u32[]{:S(2)}, u32[]{:S(2)}) collective-permute-start(bf16[2,8,8,16,128]{4,3,2,1,0:T(8,128)(2,1)} %bitcast.136), channel_id=1, source_target_pairs={{0,1},{1,0},{2,3},{3,2},{4,5},{5,4},{6,7},{7,6},{8,9},{9,8},{10,11... | collective-permute-start | bytes 1572872 | tf_op jit(solution)/shard_map/ppermute | solution.py:193
  108.9 4.1 %copy-start.6 = (bf16[768,2048]{0,1:T(8,128)(2,1)S(1)}, bf16[768,2048]{0,1:T(8,128)(2,1)}, u32[]{:S(2)}) copy-start(bf16[768,2048]{0,1:T(8,128)(2,1)} %copy.35) | copy-start | bytes 9437188
  108.9 4.1 %copy-start.10 = (bf16[128,768]{1,0:T(8,128)(2,1)S(1)}, bf16[128,768]{1,0:T(8,128)(2,1)}, u32[]{:S(2)}) copy-start(bf16[128,768]{1,0:T(8,128)(2,1)} %add_convert_fusion.8) | copy-start | bytes 589828
  118.4 14.9 %collective-permute-start.11 = (bf16[2,8,8,16,128]{4,3,2,1,0:T(8,128)(2,1)}, bf16[2,8,8,16,128]{4,3,2,1,0:T(8,128)(2,1)S(1)}, u32[]{:S(2)}, u32[]{:S(2)}) collective-permute-start(bf16[2,8,8,16,128]{4,3,2,1,0:T(8,128)(2,1)} %bitcast.138), channel_id=1, source_target_pairs={{0,1},{1,0},{2,3},{3,2},{4,5},{5,4},{6,7},{7,6},{8,9},{9,8},{10,11... | collective-permute-start | bytes 1572872 | tf_op jit(solution)/shard_map/ppermute | solution.py:193

commit v13 on v7

--- a/solution.py
+++ b/solution.py
@@ -80,16 +80,24 @@
     tile_index = lax.axis_index("tile")
     head_index = lax.axis_index("head")
     own_live = trace_mask.astype(jnp.bfloat16)
+    tile_count = lax.axis_size("tile")
+    devices = 2 * tile_count
+    across = [(index, index ^ (tile_count + 1)) for index in range(devices)]
+    other_w_decode = lax.ppermute(w_decode, ("tile", "head"), across)
     other_w_out = lax.ppermute(w_out[0], "head", [(0, 1), (1, 0)])
     local_width = embed_voxel.shape[1]
     embed_by_depth = embed_voxel.reshape(PATCH * PATCH, PATCH, local_width).transpose(1, 0, 2)
     position = position.astype(jnp.float32)
     own_embedded = embed_planes(traces, own_live, embed_by_depth, embed_mask)
-    next_embedded = from_behind(own_embedded, "tile", -1)
+    own_half = (own_embedded + position[:half_tokens]).astype(jnp.bfloat16)
+    for_previous = (own_embedded + position[half_tokens:]).astype(jnp.bfloat16)
+    next_half = jnp.where(
+        tile_index == lax.axis_size("tile") - 1,
+        position[half_tokens:].astype(jnp.bfloat16),
+        from_behind(for_previous, "tile", -1),
+    )
     halves = []
-    for rows, embedded in enumerate((own_embedded, next_embedded)):
-        embedded = embedded + position[rows * half_tokens:(rows + 1) * half_tokens]
-        embedded = embedded.astype(jnp.bfloat16)
+    for embedded in (own_half, next_half):
         other_columns = lax.ppermute(embedded, "head", [(0, 1), (1, 0)])
         halves.append(jnp.where(
             head_index == 0,
@@ -104,14 +112,18 @@
     ).astype(jnp.bfloat16)
     keys = projected[1].reshape(tokens, local_heads, HEAD_DIM)
     values = projected[2].reshape(tokens, local_heads, HEAD_DIM)
-    inner_rows = w_decode.shape[1] // (PATCH * PATCH)
+    whole_w_decode = jnp.where(
+        head_index == 0,
+        jnp.concatenate([w_decode, other_w_decode], 1),
+        jnp.concatenate([other_w_decode, w_decode], 1),
+    )
+    inner_rows = PATCH
     cell_cols = inner_rows * PATCH
     decode_by_depth = (
-        w_decode.T.reshape(inner_rows, PATCH, PATCH, -1)
+        whole_w_decode.T.reshape(inner_rows, PATCH, PATCH, -1)
         .transpose(2, 0, 1, 3)
         .reshape(PATCH, cell_cols, -1)
     )
-    decoded_chunks = {}
     for chunk in (1, 0):
         span = slice(chunk * half_tokens, (chunk + 1) * half_tokens)
         query = projected[0][span].reshape(half_tokens, local_heads, HEAD_DIM)
@@ -143,41 +155,33 @@
         latent = layer_norm(part, norm_gain[2 * LAYERS], norm_bias[2 * LAYERS]).astype(jnp.bfloat16)
         if chunk == 1:
             sent_latent = latent
-            continue
-        decoded_chunks[chunk] = lax.dot_general(
+        else:
+            own_latent = latent
+    arrived_latent = from_behind(sent_latent, "tile", 1)
+    later = (tile_index > 0).astype(jnp.float32)
+    half_side = side // 2
+    lower_piece, upper_piece = [
+        lax.dot_general(
             latent, decode_by_depth, (((1,), (2,)), ((), ())),
             preferred_element_type=jnp.float32,
         ).astype(jnp.bfloat16)
-    arrived_latent = from_behind(sent_latent, "tile", 1)
-    upper_part = lax.dot_general(
-        arrived_latent, decode_by_depth, (((1,), (2,)), ((), ())),
-        preferred_element_type=jnp.float32,
-    ).astype(jnp.bfloat16)
-    lower_part = decoded_chunks[0]
-    shape = lower_part.shape
+        for latent in (own_latent, arrived_latent)
+    ]
+    shape = lower_piece.shape
     token_a = lax.broadcasted_iota(jnp.int32, shape, 0) // (side * side)
     inner = lax.broadcasted_iota(jnp.int32, shape, 2) // PATCH
-    places = (token_a * PATCH + head_index * inner_rows + inner).astype(jnp.float32)
+    places = (token_a * PATCH + inner).astype(jnp.float32)
     lower_profile = profile_of(places)
     upper_profile = profile_of(places + HALF)
-    later = (tile_index > 0).astype(jnp.float32)
     numerator = (
-        lower_part.astype(jnp.float32) * lower_profile
-        + upper_part.astype(jnp.float32) * upper_profile
+        lower_piece.astype(jnp.float32) * lower_profile
+        + upper_piece.astype(jnp.float32) * upper_profile
     )
     denominator = lower_profile + later * upper_profile
     blended = (numerator / denominator).astype(jnp.bfloat16)
-    half_side = side // 2
     arranged = blended.reshape(half_side * side, WIN, cell_cols)
-    arranged = jnp.swapaxes(arranged, 1, 2).reshape(half_side, side, inner_rows, PATCH, WIN)
-    arranged = arranged.transpose(0, 2, 1, 3, 4)
-    other_rows = lax.ppermute(arranged, "head", [(0, 1), (1, 0)])
-    whole = jnp.where(
-        head_index == 0,
-        jnp.concatenate([arranged, other_rows], 1),
-        jnp.concatenate([other_rows, arranged], 1),
-    )
-    return whole.reshape(HALF, WIN, WIN)
+    arranged = jnp.swapaxes(arranged, 1, 2).reshape(half_side, side, PATCH, PATCH, WIN)
+    return arranged.transpose(0, 2, 1, 3, 4).reshape(HALF, WIN, WIN)
 
 
 def solution(mesh):

time: 148 us -> 124 us (0.84)
  the two profiles are of different devices: /device:TPU:22 before, /device:TPU:31 now
where the time goes in v13:
time: 124 us; the launch traced here: 123 us
  matrix products  33.8 us (27%)
  waiting for transfers between devices  30.2 us (24%)
  local copies, waits for them, and re-layouts  26.3 us (21%)
  starting transfers between devices  18 us (15%)
  other arithmetic  14.5 us (12%)
    ppermute x2, waiting for transfers between devices, body(): other_columns = lax.ppermute(embedded, 'head', [(0, 1), (1, 0)])  17.9 us
    dot_general x2, matrix products, body(): jnp.dot(hidden, w_down[0], preferred_element_type=jnp.float32)  8.06 us
    ppermute x2, starting transfers between devices, from_behind(): return lax.ppermute(block, axis, route)  7.5 us
    dot_general x2, matrix products, body(): lax.dot_general(latent, decode_by_depth, (((1,), (2,)), ((), ())), prefer...  5.78 us
    select_n x1, other arithmetic, body(): jnp.where(head_index == 0, jnp.concatenate([w_decode, other_w_decode], 1)...  5.77 us
    sub x2, matrix products, body(): weights = jax.nn.softmax(scores, axis=-1).astype(jnp.bfloat16)  5.6 us
    dot_general x2, matrix products, body(): jnp.einsum('hts,shd->thd', weights, values, preferred_element_type=jnp.fl...  5.11 us
    reshape x1, local copies, waits for them, and re-layouts, embed_planes(): voxels = jnp.swapaxes(grouped, 1, 2).reshape(rows, PATCH, PATCH * PATCH)  4.86 us
  transfers between devices with their start and end apart: 10, of which 7 were waited for; matrix products, arithmetic and copies ran while one was open for 33% of the time, Pallas kernels for 0%

profile of v13, /device:TPU:31, one launch (start us, length us, event | category | flops | bytes accessed | tf_op | source)
XLA Modules:
  0.0 123.0 jit_solution(16566162942507232894)
XLA Ops:
  0.0 2.1 %convert_element_type.136 = f32[512,384]{1,0:T(8,128)} convert(bf16[512,384]{1,0:T(8,128)(2,1)} %param.16) | non-fusion elementwise | flops 196608 | bytes 1179648 | tf_op jit(solution)/shard_map/convert_element_type | solution.py:90
  2.1 0.8 convert_element_type.135
  3.2 2.5 %broadcast_multiply_fusion = bf16[64,128,128]{2,1,0:T(8,128)(2,1)S(1)} fusion(bf16[64,128,128]{2,1,0:T(8,128)(2,1)} %param.12, bf16[64,128]{1,0:T(8,128)(2,1)S(1)} %convert_element_type.135), kind=kLoop, calls=%fused_computation.70 | loop fusion | flops 1048576 | bytes 4210688 | tf_op jit(solution)/shard_map/mul | solution.py:43
  5.7 1.9 %copy.28 = bf16[4,8,16,16,128]{4,3,2,1,0:T(8,128)(2,1)} copy(bf16[4,8,16,16,128]{4,3,1,2,0:T(8,128)(2,1)S(1)} %bitcast.113) | data formatting | bytes 4194304 | tf_op jit(solution)/shard_map/transpose | solution.py:44
  7.5 4.1 %copy.29 = bf16[32,128,256]{2,1,0:T(8,128)(2,1)} copy(bf16[32,128,256]{1,2,0:T(8,128)(2,1)} %bitcast.114) | data formatting | bytes 4194304 | tf_op jit(solution)/shard_map/transpose | solution.py:46
  11.6 4.9 %copy.30 = bf16[256,16,256]{0,1,2:T(8,128)(2,1)} copy(bf16[256,16,256]{2,1,0:T(8,128)(2,1)} %bitcast.115) | data formatting | bytes 4194304 | tf_op jit(solution)/shard_map/reshape | solution.py:46
  16.7 3.7 %fusion.93 = (bf16[256,384]{1,0:T(8,128)(2,1)S(1)}, bf16[256,384]{1,0:T(8,128)(2,1)}) fusion(f32[512,384]{1,0:T(8,128)} %convert_element_type.136, f32[32,384]{1,0:T(8,128)S(1)} %fusion.144, bf16[256,16,256]{0,1,2:T(8,128)(2,1)} %copy.30, bf16[16,256,384]{2,0,1:T(8,128)(2,1)S(1)} %bitcast.112), kind=kOutput, calls=%fused_computation.97 | convolution fusion | flops 805797888 | bytes 6471680 | tf_op jit(solution)/shard_map/dot_general | solution.py:47
  20.4 2.7 %collective-permute-start.1 = (bf16[256,384]{1,0:T(8,128)(2,1)}, bf16[256,384]{1,0:T(8,128)(2,1)S(1)}, u32[]{:S(2)}, u32[]{:S(2)}) collective-permute-start(bf16[256,384]{1,0:T(8,128)(2,1)} %get-tuple-element.20), channel_id=1, source_target_pairs={{2,0},{4,2},{6,4},{8,6},{10,8},{12,10},{14,12},{16,14},{18,16},{20... | collective-permute-start | bytes 589832 | tf_op jit(solution)/shard_map/ppermute | solution.py:19
  23.1 4.6 %copy.34 = bf16[768,2048]{0,1:T(8,128)(2,1)} copy(bf16[768,2048]{1,0:T(8,128)(2,1)} %param.23) | data formatting | bytes 6291456 | tf_op args[11]
  27.8 3.8 %collective-permute-start.8 = (bf16[768,2048]{0,1:T(8,128)(2,1)}, bf16[768,2048]{0,1:T(8,128)(2,1)}, u32[]{:S(2)}, u32[]{:S(2)}) collective-permute-start(bf16[768,2048]{0,1:T(8,128)(2,1)} %copy.34), channel_id=1, source_target_pairs={{0,65},{1,64},{2,67},{3,66},{4,69},{5,68},{6,71},{7,70},{8,73},{9,... | collective-permute-start | bytes 9437192 | tf_op jit(solution)/shard_map/ppermute | solution.py:86
  31.5 1.5 %collective-permute-start.4 = (bf16[384,768]{1,0:T(8,128)(2,1)S(1)}, bf16[384,768]{1,0:T(8,128)(2,1)}, u32[]{:S(2)}, u32[]{:S(2)}) collective-permute-start(bf16[384,768]{1,0:T(8,128)(2,1)S(1)} %bitcast.120), channel_id=1, source_target_pairs={{0,1},{1,0},{2,3},{3,2},{4,5},{5,4},{6,7},{7,6},{8,9},{9,8},{10,11... | collective-permute-start | bytes 1769480 | tf_op jit(solution)/shard_map/ppermute | solution.py:87
  33.0 0.5 collective-permute-done.1
  33.5 1.0 fusion.121
  34.6 1.7 %collective-permute-start.2 = (bf16[256,384]{1,0:T(8,128)(2,1)S(1)}, bf16[256,384]{1,0:T(8,128)(2,1)S(1)}, u32[]{:S(2)}, u32[]{:S(2)}) collective-permute-start(bf16[256,384]{1,0:T(8,128)(2,1)S(1)} %fusion.121), channel_id=1, source_target_pairs={{0,1},{1,0},{2,3},{3,2},{4,5},{5,4},{6,7},{7,6},{8,9},{9,8},{10,11... | collective-permute-start | bytes 589832 | tf_op jit(solution)/shard_map/ppermute | solution.py:101
  36.4 1.2 collective-permute-done
  37.6 16.8 %collective-permute-done.2 = bf16[256,384]{1,0:T(8,128)(2,1)S(1)} collective-permute-done((bf16[256,384]{1,0:T(8,128)(2,1)S(1)}, bf16[256,384]{1,0:T(8,128)(2,1)S(1)}, u32[]{:S(2)}, u32[]{:S(2)}) %collective-permute-start.2) | collective-permute-done | bytes 196640 | tf_op jit(solution)/shard_map/ppermute | solution.py:101
  54.7 0.3 multiply_reduce_fusion.2
  55.1 1.3 %fusion.55 = bf16[3,512,384]{1,2,0:T(8,128)(2,1)S(1)} fusion(bf16[1,3,768,384]{3,2,1,0:T(8,128)(2,1)S(1)} %copy-done.9, f32[256,768]{1,0:T(8,128)S(1)} %fusion.95, f32[256,768]{1,0:T(8,128)S(1)} %fusion.94, f32[768]{0:T(1024)S(1)} %get-tuple-element.13, f32[768]{0:T(1024)S(1)} %get-tuple-element.30, f32[512]{0:T(512)S(1)} %add_rsqrt_fusion, ...), kind=kOutput, calls=%fused_computation.52 | convolution fusion | flops 908918784 | bytes 4532224 | tf_op jit(solution)/shard_map/td,sde->ste/dot_general | solution.py:110
  56.5 2.8 %fusion.140 = (f32[6,256]{1,0:T(8,128)S(1)}, f32[6,256,512]{2,1,0:T(8,128)}) fusion(bf16[256,6,64]{0,2,1:T(8,128)(2,1)S(1)} %bitcast.131, bf16[512,6,64]{0,2,1:T(8,128)(2,1)S(1)} %bitcast.124), kind=kOutput, calls=%fused_computation.164 | convolution fusion | flops 103023104 | bytes 3741696 | tf_op jit(solution)/shard_map/sub | solution.py:133
  59.3 2.6 %fusion.71 = bf16[6,64,256]{2,1,0:T(8,128)(2,1)S(1)} fusion(bf16[512,6,64]{0,2,1:T(8,128)(2,1)S(1)} %bitcast.122, f32[6,256,512]{2,1,0:T(8,128)} %get-tuple-element.22, f32[6,256]{1,0:T(8,128)S(1)} %get-tuple-element.21), kind=kOutput, calls=%fused_computation.69 | convolution fusion | flops 102334464 | bytes 3741696 | tf_op jit(solution)/shard_map/hts,shd->thd/dot_general | solution.py:134
  61.9 0.4 collective-permute-start.3
  62.2 2.8 %fusion.141 = (f32[6,256]{1,0:T(8,128)S(1)}, f32[6,256,512]{2,1,0:T(8,128)}) fusion(bf16[256,6,64]{0,2,1:T(8,128)(2,1)S(1)} %bitcast.130, bf16[512,6,64]{0,2,1:T(8,128)(2,1)S(1)} %bitcast.125), kind=kOutput, calls=%fused_computation.165 | convolution fusion | flops 103023104 | bytes 3741696 | tf_op jit(solution)/shard_map/sub | solution.py:133
  65.0 2.6 %fusion.70 = bf16[6,64,256]{2,1,0:T(8,128)(2,1)S(1)} fusion(bf16[512,6,64]{0,2,1:T(8,128)(2,1)S(1)} %bitcast.123, f32[6,256,512]{2,1,0:T(8,128)} %get-tuple-element.24, f32[6,256]{1,0:T(8,128)S(1)} %get-tuple-element.23), kind=kOutput, calls=%fused_computation.68 | convolution fusion | flops 102334464 | bytes 3741696 | tf_op jit(solution)/shard_map/hts,shd->thd/dot_general | solution.py:134
  67.6 1.4 %collective-permute-start.5 = (bf16[256,384]{0,1:T(8,128)(2,1)S(1)}, bf16[256,384]{0,1:T(8,128)(2,1)S(1)}, u32[]{:S(2)}, u32[]{:S(2)}) collective-permute-start(bf16[256,384]{0,1:T(8,128)(2,1)S(1)} %bitcast.128), channel_id=1, source_target_pairs={{0,1},{1,0},{2,3},{3,2},{4,5},{5,4},{6,7},{7,6},{8,9},{9,8},{10,11... | collective-permute-start | bytes 589832 | tf_op jit(solution)/shard_map/ppermute | solution.py:138
  69.0 0.4 fusion.68
  69.4 0.4 fusion.64
  69.8 3.3 %collective-permute-done.5 = bf16[256,384]{0,1:T(8,128)(2,1)S(1)} collective-permute-done((bf16[256,384]{0,1:T(8,128)(2,1)S(1)}, bf16[256,384]{0,1:T(8,128)(2,1)S(1)}, u32[]{:S(2)}, u32[]{:S(2)}) %collective-permute-start.5) | collective-permute-done | bytes 196640 | tf_op jit(solution)/shard_map/ppermute | solution.py:138
  73.1 1.5 %fusion.142 = (f32[256]{0:T(256)S(1)}, f32[256,768]{1,0:T(8,128)S(1)}) fusion(f32[256,768]{1,0:T(8,128)S(1)} %fusion.64, bf16[256,384]{0,1:T(8,128)(2,1)S(1)} %collective-permute-done.5, bf16[384,768]{1,0:T(8,128)(2,1)} %collective-permute-done.4, bf16[256,384]{1,0:T(8,128)(2,1)S(1)} %fusion.121, bf16[256,384]{1,0:T(8,128)(2,1)S(1)} %copy-done.6, pred[]{:T(512)S(6)} %eq.8), kind=kOutput, calls=%fused_computation.166 | convolution fusion | flops 153943808 | bytes 2753537 | tf_op jit(solution)/shard_map/dot_general | solution.py:140
  74.7 0.2 multiply_reduce_fusion.6
  74.9 4.0 %fusion.58 = bf16[256,768]{1,0:T(8,128)(2,1)S(1)} fusion(bf16[1,1536,768]{2,1,0:T(8,128)(2,1)} %param.22, bf16[1,768,1536]{2,1,0:T(8,128)(2,1)} %param.21, f32[256,768]{1,0:T(8,128)S(1)} %get-tuple-element.26, f32[768]{0:T(1024)S(1)} %get-tuple-element.12, f32[768]{0:T(1024)S(1)} %get-tuple-element.31, f32[256]{0:T(256)S(1)} %add_rsqrt_fusion.4, ...), kind=kOutput, calls=%fused_computation.53 | convolution fusion | flops 1212678144 | bytes 5906432 | tf_op jit(solution)/shard_map/dot_general | solution.py:149
  79.0 1.0 collective-permute-start.6
  80.0 1.7 %fusion.143 = (f32[256]{0:T(256)S(1)}, f32[256,768]{1,0:T(8,128)S(1)}) fusion(f32[256,768]{1,0:T(8,128)S(1)} %fusion.68, bf16[256,384]{0,1:T(8,128)(2,1)} %collective-permute-done.3, bf16[384,768]{1,0:T(8,128)(2,1)} %collective-permute-done.4, bf16[256,384]{1,0:T(8,128)(2,1)S(1)} %get-tuple-element.19, bf16[256,384]{1,0:T(8,128)(2,1)} %copy-done.4, pred[]{:T(512)S(6)} %eq.8), kind=kOutput, calls=%fused_computation.167 | convolution fusion | flops 153943808 | bytes 2753537 | tf_op jit(solution)/shard_map/dot_general | solution.py:140
  81.7 0.2 multiply_reduce_fusion.4
  81.9 4.0 %fusion.12 = bf16[256,768]{1,0:T(8,128)(2,1)S(1)} fusion(bf16[1,1536,768]{2,1,0:T(8,128)(2,1)} %param.22, bf16[1,768,1536]{2,1,0:T(8,128)(2,1)} %param.21, f32[256,768]{1,0:T(8,128)S(1)} %get-tuple-element.28, f32[256]{0:T(256)S(1)} %add_rsqrt_fusion.2, f32[256]{0:T(256)S(1)} %broadcast_multiply_fusion.3, f32[768]{0:T(1024)S(1)} %get-tuple-element.12, ...), kind=kOutput, calls=%fused_computation.18 | convolution fusion | flops 1212481536 | bytes 5906432 | tf_op jit(solution)/shard_map/dot_general | solution.py:149
  86.0 1.8 %collective-permute-done.6 = bf16[256,768]{1,0:T(8,128)(2,1)S(1)} collective-permute-done((bf16[256,768]{1,0:T(8,128)(2,1)S(1)}, bf16[256,768]{1,0:T(8,128)(2,1)S(1)}, u32[]{:S(2)}, u32[]{:S(2)}) %collective-permute-start.6) | collective-permute-done | bytes 393248 | tf_op jit(solution)/shard_map/ppermute | solution.py:24
  88.0 0.3 multiply_reduce_fusion.5
  88.3 0.2 add_convert_fusion.3
  88.5 0.7 collective-permute-start.7
  89.3 4.8 %collective-permute-start.9 = (bf16[256,768]{1,0:T(8,128)(2,1)S(1)}, bf16[256,768]{1,0:T(8,128)(2,1)S(1)}, u32[]{:S(2)}, u32[]{:S(2)}) collective-permute-start(bf16[256,768]{1,0:T(8,128)(2,1)S(1)} %add_convert_fusion.3), channel_id=1, source_target_pairs={{0,2},{2,4},{4,6},{6,8},{8,10},{10,12},{12,14},{14,16},{16,18},{18... | collective-permute-start | bytes 1179656 | tf_op jit(solution)/shard_map/ppermute | solution.py:19
  94.1 2.5 %collective-permute-done.7 = bf16[256,768]{1,0:T(8,128)(2,1)S(1)} collective-permute-done((bf16[256,768]{1,0:T(8,128)(2,1)S(1)}, bf16[256,768]{1,0:T(8,128)(2,1)S(1)}, u32[]{:S(2)}, u32[]{:S(2)}) %collective-permute-start.7) | collective-permute-done | bytes 393248 | tf_op jit(solution)/shard_map/ppermute | solution.py:24
  96.8 0.3 multiply_reduce_fusion.3
  97.1 4.1 %collective-permute-done.8 = bf16[768,2048]{0,1:T(8,128)(2,1)} collective-permute-done((bf16[768,2048]{0,1:T(8,128)(2,1)}, bf16[768,2048]{0,1:T(8,128)(2,1)}, u32[]{:S(2)}, u32[]{:S(2)}) %collective-permute-start.8) | collective-permute-done | bytes 3145760 | tf_op jit(solution)/shard_map/ppermute | solution.py:86
  101.2 5.8 %maximum_select_fusion = bf16[768,4096]{0,1:T(8,128)(2,1)S(1)} fusion(bf16[768,2048]{0,1:T(8,128)(2,1)} %collective-permute-done.8, bf16[768,2048]{0,1:T(8,128)(2,1)} %copy.34, pred[]{:T(512)S(6)} %eq.8), kind=kLoop, calls=%fused_computation.2 | loop fusion | flops 28311552 | bytes 12582913 | tf_op jit(solution)/shard_map/jit(_where)/select_n | solution.py:115
  107.0 2.5 %fusion.4 = bf16[256,16,256]{2,0,1:T(8,128)(2,1)S(1)} fusion(bf16[16,256,768]{2,0,1:T(8,128)(2,1)S(1)} %bitcast.118, f32[256]{0:T(256)S(1)} %add_rsqrt_fusion.1, f32[256]{0:T(256)S(1)} %broadcast_multiply_fusion.2, f32[768]{0:T(1024)S(1)} %get-tuple-element.14, f32[768]{0:T(1024)S(1)} %get-tuple-element.29, f32[256,768]{1,0:T(8,128)S(1)} %get-tuple-element.28, ...), kind=kOutput, calls=%fused_computation.5 | convolution fusion | flops 1612382208 | bytes 9969664 | tf_op jit(solution)/shard_map/dot_general | solution.py:164
  109.5 3.2 %divide_convert_fusion = bf16[256,16,256]{2,0,1:T(8,128)(2,1)S(1)} fusion(f32[]{:T(128)S(6)} %convert_element_type.176, s32[256]{0:T(256)S(1)} %get-tuple-element.33, s32[256]{0:T(256)S(1)} %get-tuple-element.36, s32[256]{0:T(256)S(1)} %get-tuple-element.32, s32[256]{0:T(256)S(1)} %get-tuple-element.37, bf16[256,16,256]{2,0,1:T(8,128)(2,1)S(1)} %fusion.4, ...), kind=kOutput, calls=%fused_computation.7 | convolution fusion | flops 1634729984 | bytes 10883588 | tf_op jit(solution)/shard_map/dot_general | solution.py:164
  112.8 2.5 %copy.38 = bf16[256,16,256]{2,1,0:T(8,128)(2,1)} copy(bf16[256,16,256]{2,0,1:T(8,128)(2,1)S(1)} %divide_convert_fusion) | data formatting | bytes 4194304 | tf_op jit(solution)/shard_map/convert_element_type | solution.py:181
  115.3 4.2 %copy.39 = bf16[32,256,128]{2,1,0:T(8,128)(2,1)} copy(bf16[32,256,128]{1,2,0:T(8,128)(2,1)} %bitcast.116) | data formatting | bytes 4194304 | tf_op jit(solution)/shard_map/transpose | solution.py:183
  119.5 3.5 %copy.40 = bf16[4,16,8,16,128]{4,3,2,1,0:T(8,128)(2,1)} copy(bf16[4,16,8,16,128]{4,3,1,2,0:T(8,128)(2,1)} %bitcast.117) | data formatting | bytes 4194304 | tf_op jit(solution)/shard_map/transpose | solution.py:184
  (49 shorter events, 1.6 us)
Async XLA Ops:
  0.0 16.6 %copy-start = (bf16[4096,384]{1,0:T(8,128)(2,1)S(1)}, bf16[4096,384]{1,0:T(8,128)(2,1)}, u32[]{:S(2)}) copy-start(bf16[4096,384]{1,0:T(8,128)(2,1)} %param.14) | copy-start | bytes 9437188
  11.6 4.9 %copy-start.3 = (bf16[256,384]{1,0:T(8,128)(2,1)S(1)}, bf16[256,384]{1,0:T(8,128)(2,1)}, u32[]{:S(2)}) copy-start(bf16[256,384]{1,0:T(8,128)(2,1)} %param.15) | copy-start | bytes 589828
  20.4 11.1 %copy-start.2 = (bf16[1,384,768]{2,1,0:T(8,128)(2,1)S(1)}, bf16[1,384,768]{2,1,0:T(8,128)(2,1)}, u32[]{:S(2)}) copy-start(bf16[1,384,768]{2,1,0:T(8,128)(2,1)} %param.20) | copy-start | bytes 1769476
  20.4 15.9 %copy-start.7 = (f32[3,768]{1,0:T(4,128)S(1)}, f32[3,768]{1,0:T(4,128)}, u32[]{:S(2)}) copy-start(f32[3,768]{1,0:T(4,128)} %param.18) | copy-start | bytes 27652
  20.4 15.9 %copy-start.8 = (f32[3,768]{1,0:T(4,128)S(1)}, f32[3,768]{1,0:T(4,128)}, u32[]{:S(2)}) copy-start(f32[3,768]{1,0:T(4,128)} %param.17) | copy-start | bytes 27652
  20.4 13.1 %collective-permute-start.1 = (bf16[256,384]{1,0:T(8,128)(2,1)}, bf16[256,384]{1,0:T(8,128)(2,1)S(1)}, u32[]{:S(2)}, u32[]{:S(2)}) collective-permute-start(bf16[256,384]{1,0:T(8,128)(2,1)} %get-tuple-element.20), channel_id=1, source_target_pairs={{2,0},{4,2},{6,4},{8,6},{10,8},{12,10},{14,12},{16,14},{18,16},{20... | collective-permute-start | bytes 589832 | tf_op jit(solution)/shard_map/ppermute | solution.py:19
  27.8 73.5 %collective-permute-start.8 = (bf16[768,2048]{0,1:T(8,128)(2,1)}, bf16[768,2048]{0,1:T(8,128)(2,1)}, u32[]{:S(2)}, u32[]{:S(2)}) collective-permute-start(bf16[768,2048]{0,1:T(8,128)(2,1)} %copy.34), channel_id=1, source_target_pairs={{0,65},{1,64},{2,67},{3,66},{4,69},{5,68},{6,71},{7,70},{8,73},{9,... | collective-permute-start | bytes 9437192 | tf_op jit(solution)/shard_map/ppermute | solution.py:86
  31.5 6.0 %collective-permute-start = (bf16[256,384]{1,0:T(8,128)(2,1)S(1)}, bf16[256,384]{1,0:T(8,128)(2,1)S(1)}, u32[]{:S(2)}, u32[]{:S(2)}) collective-permute-start(bf16[256,384]{1,0:T(8,128)(2,1)S(1)} %get-tuple-element.19), channel_id=1, source_target_pairs={{0,1},{1,0},{2,3},{3,2},{4,5},{5,4},{6,7},{7,6},{8,9},{9,8},{10,11... | collective-permute-start | bytes 589832 | tf_op jit(solution)/shard_map/ppermute | solution.py:101
  31.5 38.3 %collective-permute-start.4 = (bf16[384,768]{1,0:T(8,128)(2,1)S(1)}, bf16[384,768]{1,0:T(8,128)(2,1)}, u32[]{:S(2)}, u32[]{:S(2)}) collective-permute-start(bf16[384,768]{1,0:T(8,128)(2,1)S(1)} %bitcast.120), channel_id=1, source_target_pairs={{0,1},{1,0},{2,3},{3,2},{4,5},{5,4},{6,7},{7,6},{8,9},{9,8},{10,11... | collective-permute-start | bytes 1769480 | tf_op jit(solution)/shard_map/ppermute | solution.py:87
  34.6 19.8 %collective-permute-start.2 = (bf16[256,384]{1,0:T(8,128)(2,1)S(1)}, bf16[256,384]{1,0:T(8,128)(2,1)S(1)}, u32[]{:S(2)}, u32[]{:S(2)}) collective-permute-start(bf16[256,384]{1,0:T(8,128)(2,1)S(1)} %fusion.121), channel_id=1, source_target_pairs={{0,1},{1,0},{2,3},{3,2},{4,5},{5,4},{6,7},{7,6},{8,9},{9,8},{10,11... | collective-permute-start | bytes 589832 | tf_op jit(solution)/shard_map/ppermute | solution.py:101
  37.6 17.4 %copy-start.4 = (bf16[256,384]{1,0:T(8,128)(2,1)}, bf16[256,384]{1,0:T(8,128)(2,1)S(1)}, u32[]{:S(2)}) copy-start(bf16[256,384]{1,0:T(8,128)(2,1)S(1)} %collective-permute-done) | copy-start | bytes 589828
  37.6 17.5 %copy-start.9 = (bf16[1,3,768,384]{3,2,1,0:T(8,128)(2,1)S(1)}, bf16[1,3,768,384]{3,2,1,0:T(8,128)(2,1)}, u32[]{:S(2)}) copy-start(bf16[1,3,768,384]{3,2,1,0:T(8,128)(2,1)} %param.19) | copy-start | bytes 5308420
  54.4 0.7 copy-start.5
  61.9 18.1 %collective-permute-start.3 = (bf16[256,384]{0,1:T(8,128)(2,1)S(1)}, bf16[256,384]{0,1:T(8,128)(2,1)}, u32[]{:S(2)}, u32[]{:S(2)}) collective-permute-start(bf16[256,384]{0,1:T(8,128)(2,1)S(1)} %bitcast.126), channel_id=1, source_target_pairs={{0,1},{1,0},{2,3},{3,2},{4,5},{5,4},{6,7},{7,6},{8,9},{9,8},{10,11... | collective-permute-start | bytes 589832 | tf_op jit(solution)/shard_map/ppermute | solution.py:138
  67.6 5.5 %copy-start.6 = (bf16[256,384]{1,0:T(8,128)(2,1)S(1)}, bf16[256,384]{1,0:T(8,128)(2,1)}, u32[]{:S(2)}) copy-start(bf16[256,384]{1,0:T(8,128)(2,1)} %copy-done.5) | copy-start | bytes 589828
  67.6 5.5 %collective-permute-start.5 = (bf16[256,384]{0,1:T(8,128)(2,1)S(1)}, bf16[256,384]{0,1:T(8,128)(2,1)S(1)}, u32[]{:S(2)}, u32[]{:S(2)}) collective-permute-start(bf16[256,384]{0,1:T(8,128)(2,1)S(1)} %bitcast.128), channel_id=1, source_target_pairs={{0,1},{1,0},{2,3},{3,2},{4,5},{5,4},{6,7},{7,6},{8,9},{9,8},{10,11... | collective-permute-start | bytes 589832 | tf_op jit(solution)/shard_map/ppermute | solution.py:138
  79.0 8.8 %collective-permute-start.6 = (bf16[256,768]{1,0:T(8,128)(2,1)S(1)}, bf16[256,768]{1,0:T(8,128)(2,1)S(1)}, u32[]{:S(2)}, u32[]{:S(2)}) collective-permute-start(bf16[256,768]{1,0:T(8,128)(2,1)S(1)} %fusion.58), channel_id=1, source_target_pairs={{0,1},{1,0},{2,3},{3,2},{4,5},{5,4},{6,7},{7,6},{8,9},{9,8},{10,11... | collective-permute-start | bytes 1179656 | tf_op jit(solution)/shard_map/ppermute | solution.py:24
  88.5 8.1 %collective-permute-start.7 = (bf16[256,768]{1,0:T(8,128)(2,1)S(1)}, bf16[256,768]{1,0:T(8,128)(2,1)S(1)}, u32[]{:S(2)}, u32[]{:S(2)}) collective-permute-start(bf16[256,768]{1,0:T(8,128)(2,1)S(1)} %fusion.12), channel_id=1, source_target_pairs={{0,1},{1,0},{2,3},{3,2},{4,5},{5,4},{6,7},{7,6},{8,9},{9,8},{10,11... | collective-permute-start | bytes 1179656 | tf_op jit(solution)/shard_map/ppermute | solution.py:24
  89.3 20.3 %collective-permute-start.9 = (bf16[256,768]{1,0:T(8,128)(2,1)S(1)}, bf16[256,768]{1,0:T(8,128)(2,1)S(1)}, u32[]{:S(2)}, u32[]{:S(2)}) collective-permute-start(bf16[256,768]{1,0:T(8,128)(2,1)S(1)} %add_convert_fusion.3), channel_id=1, source_target_pairs={{0,2},{2,4},{4,6},{6,8},{8,10},{10,12},{12,14},{14,16},{16,18},{18... | collective-permute-start | bytes 1179656 | tf_op jit(solution)/shard_map/ppermute | solution.py:19
  115.3 7.8 %copy-start.1 = (bf16[4096,384]{1,0:T(8,128)(2,1)S(1)}, bf16[4096,384]{1,0:T(8,128)(2,1)}, u32[]{:S(2)}) copy-start(bf16[4096,384]{1,0:T(8,128)(2,1)} %param.14) | copy-start | bytes 9437188

commit v14 on v11

--- a/solution.py
+++ b/solution.py
@@ -80,6 +80,10 @@
     tile_index = lax.axis_index("tile")
     head_index = lax.axis_index("head")
     own_live = trace_mask.astype(jnp.bfloat16)
+    tile_count = lax.axis_size("tile")
+    devices = 2 * tile_count
+    across = [(index, index ^ (tile_count + 1)) for index in range(devices)]
+    other_w_decode = lax.ppermute(w_decode, ("tile", "head"), across)
     other_w_out = lax.ppermute(w_out[0], "head", [(0, 1), (1, 0)])
     local_width = embed_voxel.shape[1]
     embed_by_depth = embed_voxel.reshape(PATCH * PATCH, PATCH, local_width).transpose(1, 0, 2)
@@ -110,11 +114,12 @@
     values = projected[2].reshape(tokens, local_heads, HEAD_DIM)
     inner_rows = w_decode.shape[1] // (PATCH * PATCH)
     cell_cols = inner_rows * PATCH
-    decode_by_depth = (
-        w_decode.T.reshape(inner_rows, PATCH, PATCH, -1)
+    decode_by_depth = [
+        columns.T.reshape(inner_rows, PATCH, PATCH, -1)
         .transpose(2, 0, 1, 3)
         .reshape(PATCH, cell_cols, -1)
-    )
+        for columns in (w_decode, other_w_decode)
+    ]
     for chunk in (1, 0):
         span = slice(chunk * half_tokens, (chunk + 1) * half_tokens)
         query = projected[0][span].reshape(half_tokens, local_heads, HEAD_DIM)
@@ -151,26 +156,19 @@
     arrived_latent = from_behind(sent_latent, "tile", 1)
     later = (tile_index > 0).astype(jnp.float32)
     half_side = side // 2
-    piece_planes = half_side // 2
-    piece_tokens = piece_planes * side * side
-    pieces = []
-    gate = None
-    for piece in range(half_side // piece_planes):
-        span = slice(piece * piece_tokens, (piece + 1) * piece_tokens)
-        latents = (own_latent[span], arrived_latent[span])
-        if gate is not None:
-            gate, latents = lax.optimization_barrier((gate, latents))
+    arranged_halves = []
+    for cells, first_row in zip(decode_by_depth, (head_index, 1 - head_index)):
         lower_piece, upper_piece = [
             lax.dot_general(
-                latent, decode_by_depth, (((1,), (2,)), ((), ())),
+                latent, cells, (((1,), (2,)), ((), ())),
                 preferred_element_type=jnp.float32,
             ).astype(jnp.bfloat16)
-            for latent in latents
+            for latent in (own_latent, arrived_latent)
         ]
         shape = lower_piece.shape
-        token_a = lax.broadcasted_iota(jnp.int32, shape, 0) // (side * side) + piece * piece_planes
+        token_a = lax.broadcasted_iota(jnp.int32, shape, 0) // (side * side)
         inner = lax.broadcasted_iota(jnp.int32, shape, 2) // PATCH
-        places = (token_a * PATCH + head_index * inner_rows + inner).astype(jnp.float32)
+        places = (token_a * PATCH + first_row * inner_rows + inner).astype(jnp.float32)
         lower_profile = profile_of(places)
         upper_profile = profile_of(places + HALF)
         numerator = (
@@ -179,17 +177,17 @@
         )
         denominator = lower_profile + later * upper_profile
         blended = (numerator / denominator).astype(jnp.bfloat16)
-        arranged = blended.reshape(piece_planes * side, WIN, cell_cols)
-        arranged = jnp.swapaxes(arranged, 1, 2).reshape(piece_planes, side, inner_rows, PATCH, WIN)
-        gate = arranged
-        other_rows = lax.ppermute(arranged, "head", [(0, 1), (1, 0)])
-        whole = jnp.where(
-            head_index == 0,
-            jnp.concatenate([arranged, other_rows], 2),
-            jnp.concatenate([other_rows, arranged], 2),
+        arranged = blended.reshape(half_side * side, WIN, cell_cols)
+        arranged_halves.append(
+            jnp.swapaxes(arranged, 1, 2).reshape(half_side, side, inner_rows, PATCH, WIN)
         )
-        pieces.append(whole.transpose(0, 2, 1, 3, 4).reshape(piece_planes * PATCH, WIN, WIN))
-    return jnp.concatenate(pieces, 0)
+    own_rows, other_rows = arranged_halves
+    whole = jnp.where(
+        head_index == 0,
+        jnp.concatenate([own_rows, other_rows], 2),
+        jnp.concatenate([other_rows, own_rows], 2),
+    )
+    return whole.transpose(0, 2, 1, 3, 4).reshape(HALF, WIN, WIN)
 
 
 def solution(mesh):

time: 137 us -> 134 us (0.978)
  the two profiles are of different devices: /device:TPU:31 before, /device:TPU:0 now
where the time goes in v14:
time: 134 us
  matrix products  42.2 us (31%)
  local copies, waits for them, and re-layouts  33.3 us (25%)
  waiting for transfers between devices  21.6 us (16%)
  starting transfers between devices  18.8 us (14%)
  other arithmetic  17.1 us (13%)
    ppermute x2, waiting for transfers between devices, partner_sum(): other = lax.ppermute(rounded, 'head', [(0, 1), (1, 0)])  15.7 us
    dot_general x2, matrix products, body(): jnp.dot(hidden, w_down[0], preferred_element_type=jnp.float32)  9.33 us
    ppermute x1, starting transfers between devices, body(): other_w_decode = lax.ppermute(w_decode, ('tile', 'head'), across)  9.3 us
    dot_general x4, matrix products, body(): lax.dot_general(latent, cells, (((1,), (2,)), ((), ())), preferred_elemen...  8.33 us
    sub x2, matrix products, body(): weights = jax.nn.softmax(scores, axis=-1).astype(jnp.bfloat16)  7.7 us
    unnamed x31, local copies, waits for them, and re-layouts  6.34 us
    dot_general x2, matrix products, body(): jnp.einsum('hts,shd->thd', weights, values, preferred_element_type=jnp.fl...  5.4 us
    ppermute x2, waiting for transfers between devices, body(): other_columns = lax.ppermute(embedded, 'head', [(0, 1), (1, 0)])  4.86 us
  transfers between devices with their start and end apart: 10, of which 5 were waited for; matrix products, arithmetic and copies ran while one was open for 42% of the time, Pallas kernels for 0%

profile of v14, /device:TPU:0, one launch (start us, length us, event | category | flops | bytes accessed | tf_op | source)
XLA Modules:
  0.0 133.5 jit_solution(5570493570267350383)
XLA Ops:
  0.0 0.9 convert_element_type.147
  1.2 1.9 %convert_element_type.148 = f32[512,384]{1,0:T(8,128)} convert(bf16[512,384]{1,0:T(8,128)(2,1)} %param.16) | non-fusion elementwise | flops 196608 | bytes 1179648 | tf_op jit(solution)/shard_map/convert_element_type | solution.py:90
  3.2 2.5 %broadcast_multiply_fusion = bf16[64,128,128]{2,1,0:T(8,128)(2,1)S(1)} fusion(bf16[64,128,128]{2,1,0:T(8,128)(2,1)} %param.12, bf16[64,128]{1,0:T(8,128)(2,1)S(1)} %convert_element_type.147), kind=kLoop, calls=%fused_computation.81 | loop fusion | flops 1048576 | bytes 4210688 | tf_op jit(solution)/shard_map/mul | solution.py:43
  5.7 1.9 %copy.31 = bf16[4,8,16,16,128]{4,3,2,1,0:T(8,128)(2,1)} copy(bf16[4,8,16,16,128]{4,3,1,2,0:T(8,128)(2,1)S(1)} %bitcast.128) | data formatting | bytes 4194304 | tf_op jit(solution)/shard_map/transpose | solution.py:44
  7.5 4.1 %copy.32 = bf16[32,128,256]{2,1,0:T(8,128)(2,1)} copy(bf16[32,128,256]{1,2,0:T(8,128)(2,1)} %bitcast.129) | data formatting | bytes 4194304 | tf_op jit(solution)/shard_map/transpose | solution.py:46
  11.6 4.9 %copy.33 = bf16[256,16,256]{0,1,2:T(8,128)(2,1)} copy(bf16[256,16,256]{2,1,0:T(8,128)(2,1)} %bitcast.130) | data formatting | bytes 4194304 | tf_op jit(solution)/shard_map/reshape | solution.py:46
  16.7 3.7 %fusion.101 = (bf16[256,384]{1,0:T(8,128)(2,1)}, bf16[256,384]{1,0:T(8,128)(2,1)S(1)}) fusion(f32[512,384]{1,0:T(8,128)} %convert_element_type.148, f32[32,384]{1,0:T(8,128)S(1)} %fusion.150, bf16[256,16,256]{0,1,2:T(8,128)(2,1)} %copy.33, bf16[16,256,384]{2,0,1:T(8,128)(2,1)S(1)} %bitcast.127), kind=kOutput, calls=%fused_computation.108 | convolution fusion | flops 805797888 | bytes 6471680 | tf_op jit(solution)/shard_map/dot_general | solution.py:47
  20.4 1.3 collective-permute-start.1
  21.7 2.1 %collective-permute-start.4 = (bf16[384,768]{1,0:T(8,128)(2,1)}, bf16[384,768]{1,0:T(8,128)(2,1)}, u32[]{:S(2)}, u32[]{:S(2)}) collective-permute-start(bf16[384,768]{1,0:T(8,128)(2,1)} %bitcast.18), channel_id=1, source_target_pairs={{0,1},{1,0},{2,3},{3,2},{4,5},{5,4},{6,7},{7,6},{8,9},{9,8},{10,11... | collective-permute-start | bytes 1769480 | tf_op jit(solution)/shard_map/ppermute | solution.py:87
  23.9 4.6 %copy.36 = bf16[768,2048]{0,1:T(8,128)(2,1)} copy(bf16[768,2048]{1,0:T(8,128)(2,1)} %param.23) | data formatting | bytes 6291456 | tf_op args[11]
  28.5 9.3 %collective-permute-start.9 = (bf16[768,2048]{0,1:T(8,128)(2,1)}, bf16[768,2048]{0,1:T(8,128)(2,1)}, u32[]{:S(2)}, u32[]{:S(2)}) collective-permute-start(bf16[768,2048]{0,1:T(8,128)(2,1)} %copy.36), channel_id=1, source_target_pairs={{0,65},{1,64},{2,67},{3,66},{4,69},{5,68},{6,71},{7,70},{8,73},{9,... | collective-permute-start | bytes 9437192 | tf_op jit(solution)/shard_map/ppermute | solution.py:86
  37.8 1.0 fusion.126
  39.0 1.5 %slice_reduce_fusion.2 = (f32[768]{0:T(1024)}, f32[768]{0:T(1024)S(1)}, f32[768]{0:T(1024)S(1)}, f32[768]{0:T(1024)S(1)}, f32[768]{0:T(1024)S(1)}, /*index=5*/f32[768]{0:T(1024)}) fusion(f32[3,768]{1,0:T(4,128)} %param.18, f32[3,768]{1,0:T(4,128)} %param.17), kind=kLoop, calls=%fused_computation.131 | loop fusion | bytes 36864 | tf_op jit(solution)/shard_map/slice | solution.py:141
  40.4 1.6 %collective-permute-done = bf16[256,384]{1,0:T(8,128)(2,1)} collective-permute-done((bf16[256,384]{1,0:T(8,128)(2,1)}, bf16[256,384]{1,0:T(8,128)(2,1)}, u32[]{:S(2)}, u32[]{:S(2)}) %collective-permute-start) | collective-permute-done | bytes 196640 | tf_op jit(solution)/shard_map/ppermute | solution.py:101
  42.1 1.3 fusion.102
  43.4 3.2 %collective-permute-done.2 = bf16[256,384]{1,0:T(8,128)(2,1)S(1)} collective-permute-done((bf16[256,384]{1,0:T(8,128)(2,1)S(1)}, bf16[256,384]{1,0:T(8,128)(2,1)S(1)}, u32[]{:S(2)}, u32[]{:S(2)}) %collective-permute-start.2) | collective-permute-done | bytes 196640 | tf_op jit(solution)/shard_map/ppermute | solution.py:101
  47.9 1.3 fusion.62
  49.9 0.9 fusion.145
  50.8 3.8 %fusion.146 = (f32[6,256]{1,0:T(8,128)S(1)}, f32[6,256,512]{2,1,0:T(8,128)}) fusion(bf16[256,6,64]{0,2,1:T(8,128)(2,1)S(1)} %bitcast.149, bf16[512,6,64]{0,2,1:T(8,128)(2,1)} %bitcast.142), kind=kOutput, calls=%fused_computation.172 | convolution fusion | flops 103023104 | bytes 3741696 | tf_op jit(solution)/shard_map/sub | solution.py:129
  54.6 2.7 %fusion.78 = bf16[6,64,256]{2,1,0:T(8,128)(2,1)S(1)} fusion(bf16[512,6,64]{0,2,1:T(8,128)(2,1)} %bitcast.140, f32[6,256,512]{2,1,0:T(8,128)} %get-tuple-element.24, f32[6,256]{1,0:T(8,128)S(1)} %get-tuple-element.23), kind=kOutput, calls=%fused_computation.80 | convolution fusion | flops 102334464 | bytes 3741696 | tf_op jit(solution)/shard_map/hts,shd->thd/dot_general | solution.py:130
  57.3 1.9 %collective-permute-start.3 = (bf16[256,384]{0,1:T(8,128)(2,1)S(1)}, bf16[256,384]{0,1:T(8,128)(2,1)}, u32[]{:S(2)}, u32[]{:S(2)}) collective-permute-start(bf16[256,384]{0,1:T(8,128)(2,1)S(1)} %bitcast.146), channel_id=1, source_target_pairs={{0,1},{1,0},{2,3},{3,2},{4,5},{5,4},{6,7},{7,6},{8,9},{9,8},{10,11... | collective-permute-start | bytes 589832 | tf_op jit(solution)/shard_map/ppermute | solution.py:134
  59.2 3.9 %fusion.147 = (f32[6,256]{1,0:T(8,128)S(1)}, f32[6,256,512]{2,1,0:T(8,128)}) fusion(bf16[256,6,64]{0,2,1:T(8,128)(2,1)} %bitcast.148, bf16[512,6,64]{0,2,1:T(8,128)(2,1)} %bitcast.143), kind=kOutput, calls=%fused_computation.173 | convolution fusion | flops 103023104 | bytes 3741696 | tf_op jit(solution)/shard_map/sub | solution.py:129
  63.1 2.7 %fusion.77 = bf16[6,64,256]{2,1,0:T(8,128)(2,1)S(1)} fusion(bf16[512,6,64]{0,2,1:T(8,128)(2,1)} %bitcast.141, f32[6,256,512]{2,1,0:T(8,128)} %get-tuple-element.26, f32[6,256]{1,0:T(8,128)S(1)} %get-tuple-element.25), kind=kOutput, calls=%fused_computation.79 | convolution fusion | flops 102334464 | bytes 3741696 | tf_op jit(solution)/shard_map/hts,shd->thd/dot_general | solution.py:130
  66.2 1.4 %fusion.75 = f32[256,768]{1,0:T(8,128)S(1)} fusion(bf16[256,384]{0,1:T(8,128)(2,1)S(1)} %bitcast.147, bf16[1,384,768]{2,1,0:T(8,128)(2,1)} %param.20), kind=kOutput, calls=%fused_computation.76 | convolution fusion | flops 151388160 | bytes 1572864 | tf_op jit(solution)/shard_map/dot_general | solution.py:135
  67.7 1.5 %fusion.71 = f32[256,768]{1,0:T(8,128)S(1)} fusion(bf16[256,384]{0,1:T(8,128)(2,1)S(1)} %bitcast.145, bf16[1,384,768]{2,1,0:T(8,128)(2,1)} %param.20), kind=kOutput, calls=%fused_computation.70 | convolution fusion | flops 151388160 | bytes 1572864 | tf_op jit(solution)/shard_map/dot_general | solution.py:135
  69.2 1.9 %fusion.149 = (f32[256]{0:T(256)S(1)}, f32[256,768]{1,0:T(8,128)S(1)}) fusion(f32[256,768]{1,0:T(8,128)S(1)} %fusion.75, bf16[256,384]{0,1:T(8,128)(2,1)} %collective-permute-done.3, bf16[384,768]{1,0:T(8,128)(2,1)} %collective-permute-done.4, bf16[256,384]{1,0:T(8,128)(2,1)} %get-tuple-element.21, bf16[256,384]{1,0:T(8,128)(2,1)} %collective-permute-done, ...), kind=kOutput, calls=%fused_computation.175 | convolution fusion | flops 153943808 | bytes 2753537 | tf_op jit(solution)/shard_map/dot_general | solution.py:136
  71.9 1.1 collective-permute-done.5
  73.0 1.5 %fusion.148 = (f32[256]{0:T(256)S(1)}, f32[256,768]{1,0:T(8,128)S(1)}) fusion(f32[256,768]{1,0:T(8,128)S(1)} %fusion.71, bf16[256,384]{0,1:T(8,128)(2,1)S(1)} %collective-permute-done.5, bf16[384,768]{1,0:T(8,128)(2,1)} %collective-permute-done.4, bf16[256,384]{1,0:T(8,128)(2,1)S(1)} %fusion.126, bf16[256,384]{1,0:T(8,128)(2,1)S(1)} %copy-done.11, pred[]{:T(512)S(6)} %eq.8), kind=kOutput, calls=%fused_computation.174 | convolution fusion | flops 153943808 | bytes 2753537 | tf_op jit(solution)/shard_map/dot_general | solution.py:136
  76.2 4.3 %fusion.65 = bf16[256,768]{1,0:T(8,128)(2,1)S(1)} fusion(bf16[1,1536,768]{2,1,0:T(8,128)(2,1)} %param.22, bf16[1,768,1536]{2,1,0:T(8,128)(2,1)} %param.21, f32[256,768]{1,0:T(8,128)} %copy-done.1, f32[768]{0:T(1024)} %get-tuple-element.12, f32[768]{0:T(1024)} %get-tuple-element.33, f32[256]{0:T(256)} %add_rsqrt_fusion.4, f32[256]{0:T(256)S(1)} %broadcast_multiply_fusion.5), kind=kOutput, calls=%fused_computation.64 | convolution fusion | flops 1212678144 | bytes 5906432 | tf_op jit(solution)/shard_map/dot_general | solution.py:145
  81.4 5.0 %fusion.12 = bf16[256,768]{1,0:T(8,128)(2,1)} fusion(bf16[1,1536,768]{2,1,0:T(8,128)(2,1)} %param.22, bf16[1,768,1536]{2,1,0:T(8,128)(2,1)} %param.21, f32[256,768]{1,0:T(8,128)} %copy-done.4, f32[256]{0:T(256)} %add_rsqrt_fusion.2, f32[256]{0:T(256)S(1)} %broadcast_multiply_fusion.3, f32[768]{0:T(1024)} %get-tuple-element.12, f32[768]{0:T(1024)} %get-tuple-element.33), kind=kOutput, calls=%fused_computation.18 | convolution fusion | flops 1212481536 | bytes 5906432 | tf_op jit(solution)/shard_map/dot_general | solution.py:145
  86.4 4.6 %collective-permute-done.6 = bf16[256,768]{1,0:T(8,128)(2,1)} collective-permute-done((bf16[256,768]{1,0:T(8,128)(2,1)S(1)}, bf16[256,768]{1,0:T(8,128)(2,1)}, u32[]{:S(2)}, u32[]{:S(2)}) %collective-permute-start.6) | collective-permute-done | bytes 393248 | tf_op jit(solution)/shard_map/ppermute | solution.py:24
  91.0 1.4 %fusion.142 = f32[256]{0:T(256)S(1)} fusion(f32[256,768]{1,0:T(8,128)} %copy-done.1, bf16[256,768]{1,0:T(8,128)(2,1)} %collective-permute-done.6, bf16[256,768]{1,0:T(8,128)(2,1)S(1)} %fusion.65), kind=kLoop, calls=%fused_computation.168 | loop fusion | flops 982784 | bytes 1573888 | tf_op jit(solution)/shard_map/reduce_sum | solution.py:29
  92.5 1.3 %multiply_reduce_fusion.5 = f32[256]{0:T(256)S(1)} fusion(f32[256]{0:T(256)S(1)} %broadcast_multiply_fusion.4, f32[256,768]{1,0:T(8,128)S(1)} %copy-done.2, bf16[256,768]{1,0:T(8,128)(2,1)} %collective-permute-done.6, bf16[256,768]{1,0:T(8,128)(2,1)S(1)} %fusion.65), kind=kLoop, calls=%fused_computation.90 | loop fusion | flops 1376000 | bytes 1574912 | tf_op jit(solution)/shard_map/reduce_sum | solution.py:31
  93.9 1.4 %add_convert_fusion.3 = bf16[256,768]{1,0:T(8,128)(2,1)S(1)} fusion(f32[768]{0:T(1024)S(1)} %get-tuple-element.14, f32[768]{0:T(1024)S(1)} %get-tuple-element.31, f32[256]{0:T(256)S(1)} %add_rsqrt_fusion.3, f32[256]{0:T(256)S(1)} %broadcast_multiply_fusion.4, f32[256,768]{1,0:T(8,128)S(1)} %copy-done.2, bf16[256,768]{1,0:T(8,128)(2,1)} %collective-permute-done.6, ...), kind=kLoop, calls=%fused_computation.89 | loop fusion | flops 1769472 | bytes 1974272 | tf_op jit(solution)/shard_map/convert_element_type | solution.py:151
  95.3 1.4 %collective-permute-start.7 = (bf16[256,768]{1,0:T(8,128)(2,1)S(1)}, bf16[256,768]{1,0:T(8,128)(2,1)S(1)}, u32[]{:S(2)}, u32[]{:S(2)}) collective-permute-start(bf16[256,768]{1,0:T(8,128)(2,1)S(1)} %copy-done.8), channel_id=1, source_target_pairs={{0,1},{1,0},{2,3},{3,2},{4,5},{5,4},{6,7},{7,6},{8,9},{9,8},{10,11... | collective-permute-start | bytes 1179656 | tf_op jit(solution)/shard_map/ppermute | solution.py:24
  96.7 1.3 collective-permute-start.8
  98.0 11.1 %collective-permute-done.7 = bf16[256,768]{1,0:T(8,128)(2,1)S(1)} collective-permute-done((bf16[256,768]{1,0:T(8,128)(2,1)S(1)}, bf16[256,768]{1,0:T(8,128)(2,1)S(1)}, u32[]{:S(2)}, u32[]{:S(2)}) %collective-permute-start.7) | collective-permute-done | bytes 393248 | tf_op jit(solution)/shard_map/ppermute | solution.py:24
  109.6 2.4 %fusion.56 = bf16[256,16,128]{2,0,1:T(8,128)(2,1)S(1)} fusion(bf16[16,128,768]{2,0,1:T(8,128)(2,1)S(1)} %bitcast.135, f32[256,768]{1,0:T(8,128)S(1)} %get-tuple-element.16, f32[256]{0:T(256)S(1)} %add_rsqrt_fusion.1, f32[256]{0:T(256)S(1)} %broadcast_multiply_fusion.2, f32[768]{0:T(1024)S(1)} %get-tuple-element.14, f32[768]{0:T(1024)S(1)} %get-tuple-element.31), kind=kOutput, calls=%fused_computation.59 | convolution fusion | flops 806813696 | bytes 4988928 | tf_op jit(solution)/shard_map/dot_general | solution.py:162
  112.0 2.5 %divide_convert_fusion.3 = bf16[256,16,128]{2,0,1:T(8,128)(2,1)S(1)} fusion(bf16[256,16,128]{2,0,1:T(8,128)(2,1)S(1)} %fusion.56, f32[]{:T(128)S(6)} %convert_element_type.188, s32[128]{0:T(128)S(1)} %get-tuple-element.36, s32[128]{0:T(128)S(1)} %get-tuple-element.37, s32[]{:T(128)S(6)} %mul.220, s32[256]{0:T(256)S(1)} %get-tuple-element.34, ...), kind=kOutput, calls=%fused_computation.31 | convolution fusion | flops 817889280 | bytes 5639560 | tf_op jit(solution)/shard_map/dot_general | solution.py:162
  114.5 1.6 %copy.39 = bf16[256,16,128]{2,1,0:T(8,128)(2,1)} copy(bf16[256,16,128]{2,0,1:T(8,128)(2,1)S(1)} %divide_convert_fusion.3) | data formatting | bytes 2097152 | tf_op jit(solution)/shard_map/convert_element_type | solution.py:179
  116.2 2.3 %copy.40 = bf16[32,128,128]{2,1,0:T(8,128)(2,1)} copy(bf16[32,128,128]{1,2,0:T(8,128)(2,1)} %bitcast.133) | data formatting | bytes 2097152 | tf_op jit(solution)/shard_map/transpose | solution.py:182
  118.5 3.0 %copy.42 = bf16[16,8,16,768]{3,2,1,0:T(8,128)(2,1)S(1)} copy(bf16[16,8,16,768]{3,0,2,1:T(8,128)(2,1)} %bitcast.40) | data formatting | bytes 6291456 | tf_op jit(solution)/shard_map/transpose | solution.py:119
  121.5 1.1 convolution_convert_fusion.1
  122.5 2.4 %divide_convert_fusion.2 = bf16[256,16,128]{2,0,1:T(8,128)(2,1)S(1)} fusion(bf16[256,16,128]{2,0,1:T(8,128)(2,1)S(1)} %convolution_convert_fusion.1, bf16[16,128,768]{2,1,0:T(8,128)(2,1)S(1)} %bitcast.138, s32[]{:T(128)S(6)} %mul.227, f32[]{:T(128)S(6)} %convert_element_type.188, s32[128]{0:T(128)S(1)} %get-tuple-element.36, s32[128]{0:T(128)S(1)} %get-tuple-element.37, ...), kind=kOutput, calls=%fused_computation.30 | convolution fusion | flops 817889280 | bytes 5639560 | tf_op jit(solution)/shard_map/dot_general | solution.py:162
  125.0 1.6 %copy.43 = bf16[256,16,128]{2,1,0:T(8,128)(2,1)} copy(bf16[256,16,128]{2,0,1:T(8,128)(2,1)S(1)} %divide_convert_fusion.2) | data formatting | bytes 2097152 | tf_op jit(solution)/shard_map/convert_element_type | solution.py:179
  126.6 2.3 %copy.44 = bf16[32,128,128]{2,1,0:T(8,128)(2,1)} copy(bf16[32,128,128]{1,2,0:T(8,128)(2,1)} %bitcast.134) | data formatting | bytes 2097152 | tf_op jit(solution)/shard_map/transpose | solution.py:182
  128.9 2.7 %fusion.22 = bf16[4,16,8,16,128]{4,3,1,2,0:T(8,128)(2,1)S(1)} fusion(bf16[4,8,8,16,128]{4,3,2,1,0:T(8,128)(2,1)} %bitcast.132, bf16[4,8,8,16,128]{4,3,2,1,0:T(8,128)(2,1)} %bitcast.131, pred[]{:T(512)S(6)} %eq.8), kind=kLoop, calls=%fused_computation.29 | loop fusion | flops 3145728 | bytes 4194305 | tf_op jit(solution)/shard_map/transpose | solution.py:190
  131.6 1.9 %copy.45 = bf16[4,16,8,16,128]{4,3,2,1,0:T(8,128)(2,1)} copy(bf16[4,16,8,16,128]{4,3,1,2,0:T(8,128)(2,1)S(1)} %fusion.22) | data formatting | bytes 4194304 | tf_op jit(solution)/shard_map/transpose | solution.py:190
  (65 shorter events, 6.9 us)
Async XLA Ops:
  0.0 16.6 %copy-start = (bf16[4096,384]{1,0:T(8,128)(2,1)S(1)}, bf16[4096,384]{1,0:T(8,128)(2,1)}, u32[]{:S(2)}) copy-start(bf16[4096,384]{1,0:T(8,128)(2,1)} %param.14) | copy-start | bytes 9437188
  11.6 4.9 %copy-start.9 = (bf16[256,384]{1,0:T(8,128)(2,1)S(1)}, bf16[256,384]{1,0:T(8,128)(2,1)}, u32[]{:S(2)}) copy-start(bf16[256,384]{1,0:T(8,128)(2,1)} %param.15) | copy-start | bytes 589828
  20.4 17.4 %collective-permute-start.1 = (bf16[256,384]{1,0:T(8,128)(2,1)S(1)}, bf16[256,384]{1,0:T(8,128)(2,1)S(1)}, u32[]{:S(2)}, u32[]{:S(2)}) collective-permute-start(bf16[256,384]{1,0:T(8,128)(2,1)S(1)} %get-tuple-element.22), channel_id=1, source_target_pairs={{2,0},{4,2},{6,4},{8,6},{10,8},{12,10},{14,12},{16,14},{18,16},{20... | collective-permute-start | bytes 589832 | tf_op jit(solution)/shard_map/ppermute | solution.py:19
  21.7 47.5 %collective-permute-start.4 = (bf16[384,768]{1,0:T(8,128)(2,1)}, bf16[384,768]{1,0:T(8,128)(2,1)}, u32[]{:S(2)}, u32[]{:S(2)}) collective-permute-start(bf16[384,768]{1,0:T(8,128)(2,1)} %bitcast.18), channel_id=1, source_target_pairs={{0,1},{1,0},{2,3},{3,2},{4,5},{5,4},{6,7},{7,6},{8,9},{9,8},{10,11... | collective-permute-start | bytes 1769480 | tf_op jit(solution)/shard_map/ppermute | solution.py:87
  23.8 18.3 %collective-permute-start = (bf16[256,384]{1,0:T(8,128)(2,1)}, bf16[256,384]{1,0:T(8,128)(2,1)}, u32[]{:S(2)}, u32[]{:S(2)}) collective-permute-start(bf16[256,384]{1,0:T(8,128)(2,1)} %get-tuple-element.21), channel_id=1, source_target_pairs={{0,1},{1,0},{2,3},{3,2},{4,5},{5,4},{6,7},{7,6},{8,9},{9,8},{10,11... | collective-permute-start | bytes 589832 | tf_op jit(solution)/shard_map/ppermute | solution.py:101
  28.5 90.0 %collective-permute-start.9 = (bf16[768,2048]{0,1:T(8,128)(2,1)}, bf16[768,2048]{0,1:T(8,128)(2,1)}, u32[]{:S(2)}, u32[]{:S(2)}) collective-permute-start(bf16[768,2048]{0,1:T(8,128)(2,1)} %copy.36), channel_id=1, source_target_pairs={{0,65},{1,64},{2,67},{3,66},{4,69},{5,68},{6,71},{7,70},{8,73},{9,... | collective-permute-start | bytes 9437192 | tf_op jit(solution)/shard_map/ppermute | solution.py:86
  38.9 7.7 %collective-permute-start.2 = (bf16[256,384]{1,0:T(8,128)(2,1)S(1)}, bf16[256,384]{1,0:T(8,128)(2,1)S(1)}, u32[]{:S(2)}, u32[]{:S(2)}) collective-permute-start(bf16[256,384]{1,0:T(8,128)(2,1)S(1)} %fusion.126), channel_id=1, source_target_pairs={{0,1},{1,0},{2,3},{3,2},{4,5},{5,4},{6,7},{7,6},{8,9},{9,8},{10,11... | collective-permute-start | bytes 589832 | tf_op jit(solution)/shard_map/ppermute | solution.py:101
  43.4 4.5 %copy-start.12 = (bf16[1,3,768,384]{3,2,1,0:T(8,128)(2,1)S(1)}, bf16[1,3,768,384]{3,2,1,0:T(8,128)(2,1)}, u32[]{:S(2)}) copy-start(bf16[1,3,768,384]{3,2,1,0:T(8,128)(2,1)} %param.19) | copy-start | bytes 5308420
  46.6 0.7 copy-start.10
  57.3 11.9 %collective-permute-start.3 = (bf16[256,384]{0,1:T(8,128)(2,1)S(1)}, bf16[256,384]{0,1:T(8,128)(2,1)}, u32[]{:S(2)}, u32[]{:S(2)}) collective-permute-start(bf16[256,384]{0,1:T(8,128)(2,1)S(1)} %bitcast.146), channel_id=1, source_target_pairs={{0,1},{1,0},{2,3},{3,2},{4,5},{5,4},{6,7},{7,6},{8,9},{9,8},{10,11... | collective-permute-start | bytes 589832 | tf_op jit(solution)/shard_map/ppermute | solution.py:134
  65.8 7.2 %collective-permute-start.5 = (bf16[256,384]{0,1:T(8,128)(2,1)S(1)}, bf16[256,384]{0,1:T(8,128)(2,1)S(1)}, u32[]{:S(2)}, u32[]{:S(2)}) collective-permute-start(bf16[256,384]{0,1:T(8,128)(2,1)S(1)} %bitcast.144), channel_id=1, source_target_pairs={{0,1},{1,0},{2,3},{3,2},{4,5},{5,4},{6,7},{7,6},{8,9},{9,8},{10,11... | collective-permute-start | bytes 589832 | tf_op jit(solution)/shard_map/ppermute | solution.py:134
  69.2 3.8 %copy-start.11 = (bf16[256,384]{1,0:T(8,128)(2,1)S(1)}, bf16[256,384]{1,0:T(8,128)(2,1)}, u32[]{:S(2)}) copy-start(bf16[256,384]{1,0:T(8,128)(2,1)} %copy-done.10) | copy-start | bytes 589828
  71.1 0.9 copy-start.4
  74.5 0.9 copy-start.1
  80.5 10.6 %collective-permute-start.6 = (bf16[256,768]{1,0:T(8,128)(2,1)S(1)}, bf16[256,768]{1,0:T(8,128)(2,1)}, u32[]{:S(2)}, u32[]{:S(2)}) collective-permute-start(bf16[256,768]{1,0:T(8,128)(2,1)S(1)} %fusion.65), channel_id=1, source_target_pairs={{0,1},{1,0},{2,3},{3,2},{4,5},{5,4},{6,7},{7,6},{8,9},{9,8},{10,11... | collective-permute-start | bytes 1179656 | tf_op jit(solution)/shard_map/ppermute | solution.py:24
  86.4 6.1 %copy-start.2 = (f32[256,768]{1,0:T(8,128)S(1)}, f32[256,768]{1,0:T(8,128)}, u32[]{:S(2)}) copy-start(f32[256,768]{1,0:T(8,128)} %copy-done.1) | copy-start | bytes 2359300
  92.5 2.8 %copy-start.8 = (bf16[256,768]{1,0:T(8,128)(2,1)S(1)}, bf16[256,768]{1,0:T(8,128)(2,1)}, u32[]{:S(2)}) copy-start(bf16[256,768]{1,0:T(8,128)(2,1)} %fusion.12) | copy-start | bytes 1179652
  92.5 16.6 %copy-start.5 = (f32[256,768]{1,0:T(8,128)S(1)}, f32[256,768]{1,0:T(8,128)}, u32[]{:S(2)}) copy-start(f32[256,768]{1,0:T(8,128)} %copy-done.4) | copy-start | bytes 2359300
  93.9 15.7 %copy-start.3 = (bf16[768,2048]{0,1:T(8,128)(2,1)S(1)}, bf16[768,2048]{0,1:T(8,128)(2,1)}, u32[]{:S(2)}) copy-start(bf16[768,2048]{0,1:T(8,128)(2,1)} %copy.36) | copy-start | bytes 9437188
  95.3 13.8 %collective-permute-start.7 = (bf16[256,768]{1,0:T(8,128)(2,1)S(1)}, bf16[256,768]{1,0:T(8,128)(2,1)S(1)}, u32[]{:S(2)}, u32[]{:S(2)}) collective-permute-start(bf16[256,768]{1,0:T(8,128)(2,1)S(1)} %copy-done.8), channel_id=1, source_target_pairs={{0,1},{1,0},{2,3},{3,2},{4,5},{5,4},{6,7},{7,6},{8,9},{9,8},{10,11... | collective-permute-start | bytes 1179656 | tf_op jit(solution)/shard_map/ppermute | solution.py:24
  96.7 15.3 %collective-permute-start.8 = (bf16[256,768]{1,0:T(8,128)(2,1)S(1)}, bf16[256,768]{1,0:T(8,128)(2,1)S(1)}, u32[]{:S(2)}, u32[]{:S(2)}) collective-permute-start(bf16[256,768]{1,0:T(8,128)(2,1)S(1)} %add_convert_fusion.3), channel_id=1, source_target_pairs={{0,2},{2,4},{4,6},{6,8},{8,10},{10,12},{12,14},{14,16},{16,18},{18... | collective-permute-start | bytes 1179656 | tf_op jit(solution)/shard_map/ppermute | solution.py:19
  109.3 2.7 %copy-start.6 = (f32[256,768]{1,0:T(8,128)}, f32[256,768]{1,0:T(8,128)S(1)}, u32[]{:S(2)}) copy-start(f32[256,768]{1,0:T(8,128)S(1)} %get-tuple-element.16) | copy-start | bytes 2359300
  112.0 2.5 %copy-start.13 = (bf16[256,768]{1,0:T(8,128)(2,1)}, bf16[256,768]{1,0:T(8,128)(2,1)S(1)}, u32[]{:S(2)}) copy-start(bf16[256,768]{1,0:T(8,128)(2,1)S(1)} %collective-permute-done.8) | copy-start | bytes 1179652
  118.5 3.0 %copy-start.7 = (f32[256,768]{1,0:T(8,128)S(1)}, f32[256,768]{1,0:T(8,128)}, u32[]{:S(2)}) copy-start(f32[256,768]{1,0:T(8,128)} %copy-done.6) | copy-start | bytes 2359300
  121.5 1.1 copy-start.14

commit v15 on v13

--- a/solution.py
+++ b/solution.py
@@ -83,7 +83,13 @@
     tile_count = lax.axis_size("tile")
     devices = 2 * tile_count
     across = [(index, index ^ (tile_count + 1)) for index in range(devices)]
-    other_w_decode = lax.ppermute(w_decode, ("tile", "head"), across)
+    own_cells = w_decode.shape[1] // (PATCH * PATCH)
+    own_by_depth = (
+        w_decode.T.reshape(own_cells, PATCH, PATCH, -1)
+        .transpose(2, 0, 1, 3)
+        .reshape(PATCH, own_cells * PATCH, -1)
+    )
+    other_by_depth = lax.ppermute(own_by_depth, ("tile", "head"), across)
     other_w_out = lax.ppermute(w_out[0], "head", [(0, 1), (1, 0)])
     local_width = embed_voxel.shape[1]
     embed_by_depth = embed_voxel.reshape(PATCH * PATCH, PATCH, local_width).transpose(1, 0, 2)
@@ -112,17 +118,12 @@
     ).astype(jnp.bfloat16)
     keys = projected[1].reshape(tokens, local_heads, HEAD_DIM)
     values = projected[2].reshape(tokens, local_heads, HEAD_DIM)
-    whole_w_decode = jnp.where(
-        head_index == 0,
-        jnp.concatenate([w_decode, other_w_decode], 1),
-        jnp.concatenate([other_w_decode, w_decode], 1),
-    )
     inner_rows = PATCH
     cell_cols = inner_rows * PATCH
-    decode_by_depth = (
-        whole_w_decode.T.reshape(inner_rows, PATCH, PATCH, -1)
-        .transpose(2, 0, 1, 3)
-        .reshape(PATCH, cell_cols, -1)
+    decode_by_depth = jnp.where(
+        head_index == 0,
+        jnp.concatenate([own_by_depth, other_by_depth], 1),
+        jnp.concatenate([other_by_depth, own_by_depth], 1),
     )
     for chunk in (1, 0):
         span = slice(chunk * half_tokens, (chunk + 1) * half_tokens)

time: 124 us -> 138 us (1.11)
  the two profiles are of different devices: /device:TPU:31 before, /device:TPU:0 now
where the time goes in v15:
time: 138 us; the launch traced here: 136 us
  matrix products  51.2 us (37%)
  local copies, waits for them, and re-layouts  35.1 us (25%)
  other arithmetic  18.4 us (13%)
  starting transfers between devices  17.5 us (13%)
  waiting for transfers between devices  14 us (10%)
    dot_general x2, matrix products, body(): lax.dot_general(latent, decode_by_depth, (((1,), (2,)), ((), ())), prefer...  15.6 us
    dot_general x2, matrix products, body(): jnp.dot(hidden, w_down[0], preferred_element_type=jnp.float32)  9.32 us
    ppermute x1, starting transfers between devices, body(): other_by_depth = lax.ppermute(own_by_depth, ('tile', 'head'), across)  9.3 us
    sub x2, matrix products, body(): weights = jax.nn.softmax(scores, axis=-1).astype(jnp.bfloat16)  7.69 us
    ppermute x2, waiting for transfers between devices, partner_sum(): other = lax.ppermute(rounded, 'head', [(0, 1), (1, 0)])  7.27 us
    unnamed x15, local copies, waits for them, and re-layouts  6.27 us
    dot_general x2, matrix products, body(): jnp.einsum('hts,shd->thd', weights, values, preferred_element_type=jnp.fl...  5.41 us
    reduce_sum x5, other arithmetic, layer_norm(): variance = jnp.mean(centered * centered, axis=-1, keepdims=True)  4.85 us
  transfers between devices with their start and end apart: 10, of which 4 were waited for; matrix products, arithmetic and copies ran while one was open for 47% of the time, Pallas kernels for 0%

profile of v15, /device:TPU:0, one launch (start us, length us, event | category | flops | bytes accessed | tf_op | source)
XLA Modules:
  0.0 136.5 jit_solution(4550956598781673348)
XLA Ops:
  0.0 0.9 convert_element_type.135
  1.1 2.5 %broadcast_multiply_fusion = bf16[64,128,128]{2,1,0:T(8,128)(2,1)S(1)} fusion(bf16[64,128,128]{2,1,0:T(8,128)(2,1)} %param.12, bf16[64,128]{1,0:T(8,128)(2,1)S(1)} %convert_element_type.135), kind=kLoop, calls=%fused_computation.67 | loop fusion | flops 1048576 | bytes 4210688 | tf_op jit(solution)/shard_map/mul | solution.py:43
  3.5 1.9 %copy.27 = bf16[4,8,16,16,128]{4,3,2,1,0:T(8,128)(2,1)} copy(bf16[4,8,16,16,128]{4,3,1,2,0:T(8,128)(2,1)S(1)} %bitcast.114) | data formatting | bytes 4194304 | tf_op jit(solution)/shard_map/transpose | solution.py:44
  5.4 4.1 %copy.28 = bf16[32,128,256]{2,1,0:T(8,128)(2,1)} copy(bf16[32,128,256]{1,2,0:T(8,128)(2,1)} %bitcast.115) | data formatting | bytes 4194304 | tf_op jit(solution)/shard_map/transpose | solution.py:46
  9.5 4.8 %copy.29 = bf16[256,16,256]{0,1,2:T(8,128)(2,1)} copy(bf16[256,16,256]{2,1,0:T(8,128)(2,1)} %bitcast.116) | data formatting | bytes 4194304 | tf_op jit(solution)/shard_map/reshape | solution.py:46
  14.3 1.9 %convert_element_type.136 = f32[512,384]{1,0:T(8,128)} convert(bf16[512,384]{1,0:T(8,128)(2,1)} %param.16) | non-fusion elementwise | flops 196608 | bytes 1179648 | tf_op jit(solution)/shard_map/convert_element_type | solution.py:96
  16.5 1.1 fusion.141
  17.5 3.7 %fusion.88 = (bf16[256,384]{1,0:T(8,128)(2,1)}, bf16[256,384]{1,0:T(8,128)(2,1)S(1)}) fusion(f32[512,384]{1,0:T(8,128)} %convert_element_type.136, f32[32,384]{1,0:T(8,128)S(1)} %fusion.141, bf16[256,16,256]{0,1,2:T(8,128)(2,1)} %copy.29, bf16[16,256,384]{2,0,1:T(8,128)(2,1)S(1)} %bitcast.112), kind=kOutput, calls=%fused_computation.94 | convolution fusion | flops 805797888 | bytes 6471680 | tf_op jit(solution)/shard_map/dot_general | solution.py:47
  21.3 1.3 collective-permute-start.1
  22.6 2.1 %collective-permute-start = (bf16[256,384]{1,0:T(8,128)(2,1)}, bf16[256,384]{1,0:T(8,128)(2,1)}, u32[]{:S(2)}, u32[]{:S(2)}) collective-permute-start(bf16[256,384]{1,0:T(8,128)(2,1)} %get-tuple-element.19), channel_id=1, source_target_pairs={{0,1},{1,0},{2,3},{3,2},{4,5},{5,4},{6,7},{7,6},{8,9},{9,8},{10,11... | collective-permute-start | bytes 589832 | tf_op jit(solution)/shard_map/ppermute | solution.py:107
  24.8 4.7 %copy.32 = bf16[768,2048]{0,1:T(8,128)(2,1)} copy(bf16[768,2048]{1,0:T(8,128)(2,1)} %param.23) | data formatting | bytes 6291456 | tf_op args[11]
  29.4 4.6 %copy.34 = bf16[16,128,768]{2,1,0:T(8,128)(2,1)} copy(bf16[16,128,768]{2,0,1:T(8,128)(2,1)} %bitcast.113) | data formatting | bytes 6291456 | tf_op jit(solution)/shard_map/reshape | solution.py:90
  34.0 9.3 %collective-permute-start.8 = (bf16[16,128,768]{2,1,0:T(8,128)(2,1)}, bf16[16,128,768]{2,1,0:T(8,128)(2,1)}, u32[]{:S(2)}, u32[]{:S(2)}) collective-permute-start(bf16[16,128,768]{2,1,0:T(8,128)(2,1)} %copy.34), channel_id=1, source_target_pairs={{0,65},{1,64},{2,67},{3,66},{4,69},{5,68},{6,71},{7,70},{8,73},{9,... | collective-permute-start | bytes 9437192 | tf_op jit(solution)/shard_map/ppermute | solution.py:92
  43.3 1.2 fusion.116
  44.6 1.5 %slice_reduce_fusion.2 = (f32[768]{0:T(1024)}, f32[768]{0:T(1024)S(1)}, f32[768]{0:T(1024)S(1)}, f32[768]{0:T(1024)S(1)}, f32[768]{0:T(1024)S(1)}, /*index=5*/f32[768]{0:T(1024)}) fusion(f32[3,768]{1,0:T(4,128)} %param.18, f32[3,768]{1,0:T(4,128)} %param.17), kind=kLoop, calls=%fused_computation.120 | loop fusion | bytes 36864 | tf_op jit(solution)/shard_map/slice | solution.py:146
  46.0 1.3 fusion.89
  47.4 2.9 %collective-permute-done.2 = bf16[256,384]{1,0:T(8,128)(2,1)S(1)} collective-permute-done((bf16[256,384]{1,0:T(8,128)(2,1)S(1)}, bf16[256,384]{1,0:T(8,128)(2,1)S(1)}, u32[]{:S(2)}, u32[]{:S(2)}) %collective-permute-start.2) | collective-permute-done | bytes 196640 | tf_op jit(solution)/shard_map/ppermute | solution.py:107
  50.2 0.7 copy-done.4
  51.5 1.3 fusion.49
  52.8 0.9 fusion.136
  53.7 0.7 fusion.135
  54.4 3.8 %fusion.137 = (f32[6,256]{1,0:T(8,128)S(1)}, f32[6,256,512]{2,1,0:T(8,128)}) fusion(bf16[256,6,64]{0,2,1:T(8,128)(2,1)S(1)} %bitcast.129, bf16[512,6,64]{0,2,1:T(8,128)(2,1)} %bitcast.122), kind=kOutput, calls=%fused_computation.163 | convolution fusion | flops 103023104 | bytes 3741696 | tf_op jit(solution)/shard_map/sub | solution.py:134
  58.2 2.7 %fusion.65 = bf16[6,64,256]{2,1,0:T(8,128)(2,1)S(1)} fusion(bf16[512,6,64]{0,2,1:T(8,128)(2,1)} %bitcast.120, f32[6,256,512]{2,1,0:T(8,128)} %get-tuple-element.22, f32[6,256]{1,0:T(8,128)S(1)} %get-tuple-element.21), kind=kOutput, calls=%fused_computation.65 | convolution fusion | flops 102334464 | bytes 3741696 | tf_op jit(solution)/shard_map/hts,shd->thd/dot_general | solution.py:135
  61.0 3.9 %fusion.138 = (f32[6,256]{1,0:T(8,128)S(1)}, f32[6,256,512]{2,1,0:T(8,128)}) fusion(bf16[256,6,64]{0,2,1:T(8,128)(2,1)} %bitcast.128, bf16[512,6,64]{0,2,1:T(8,128)(2,1)} %bitcast.123), kind=kOutput, calls=%fused_computation.164 | convolution fusion | flops 103023104 | bytes 3741696 | tf_op jit(solution)/shard_map/sub | solution.py:134
  64.9 2.7 %fusion.64 = bf16[6,64,256]{2,1,0:T(8,128)(2,1)S(1)} fusion(bf16[512,6,64]{0,2,1:T(8,128)(2,1)} %bitcast.121, f32[6,256,512]{2,1,0:T(8,128)} %get-tuple-element.24, f32[6,256]{1,0:T(8,128)S(1)} %get-tuple-element.23), kind=kOutput, calls=%fused_computation.64 | convolution fusion | flops 102334464 | bytes 3741696 | tf_op jit(solution)/shard_map/hts,shd->thd/dot_general | solution.py:135
  67.6 2.3 %collective-permute-start.5 = (bf16[256,384]{0,1:T(8,128)(2,1)S(1)}, bf16[256,384]{0,1:T(8,128)(2,1)S(1)}, u32[]{:S(2)}, u32[]{:S(2)}) collective-permute-start(bf16[256,384]{0,1:T(8,128)(2,1)S(1)} %bitcast.124), channel_id=1, source_target_pairs={{0,1},{1,0},{2,3},{3,2},{4,5},{5,4},{6,7},{7,6},{8,9},{9,8},{10,11... | collective-permute-start | bytes 589832 | tf_op jit(solution)/shard_map/ppermute | solution.py:139
  69.9 1.4 %fusion.62 = f32[256,768]{1,0:T(8,128)S(1)} fusion(bf16[256,384]{0,1:T(8,128)(2,1)S(1)} %bitcast.127, bf16[1,384,768]{2,1,0:T(8,128)(2,1)} %param.20), kind=kOutput, calls=%fused_computation.61 | convolution fusion | flops 151388160 | bytes 1572864 | tf_op jit(solution)/shard_map/dot_general | solution.py:140
  71.4 1.5 %fusion.58 = f32[256,768]{1,0:T(8,128)S(1)} fusion(bf16[256,384]{0,1:T(8,128)(2,1)S(1)} %bitcast.125, bf16[1,384,768]{2,1,0:T(8,128)(2,1)} %param.20), kind=kOutput, calls=%fused_computation.55 | convolution fusion | flops 151388160 | bytes 1572864 | tf_op jit(solution)/shard_map/dot_general | solution.py:140
  72.8 2.6 %fusion.140 = (f32[256]{0:T(256)S(1)}, f32[256,768]{1,0:T(8,128)}) fusion(f32[256,768]{1,0:T(8,128)S(1)} %fusion.62, bf16[256,384]{0,1:T(8,128)(2,1)} %collective-permute-done.3, bf16[384,768]{1,0:T(8,128)(2,1)} %collective-permute-done.4, bf16[256,384]{1,0:T(8,128)(2,1)} %get-tuple-element.19, bf16[256,384]{1,0:T(8,128)(2,1)} %collective-permute-done, ...), kind=kOutput, calls=%fused_computation.166 | convolution fusion | flops 153943808 | bytes 2753537 | tf_op jit(solution)/shard_map/dot_general | solution.py:141
  75.5 1.5 %fusion.139 = (f32[256]{0:T(256)S(1)}, f32[256,768]{1,0:T(8,128)S(1)}) fusion(f32[256,768]{1,0:T(8,128)S(1)} %fusion.58, bf16[256,384]{0,1:T(8,128)(2,1)S(1)} %collective-permute-done.5, bf16[384,768]{1,0:T(8,128)(2,1)} %collective-permute-done.4, bf16[256,384]{1,0:T(8,128)(2,1)S(1)} %fusion.116, bf16[256,384]{1,0:T(8,128)(2,1)S(1)} %copy-done.5, pred[]{:T(512)S(6)} %eq.8), kind=kOutput, calls=%fused_computation.165 | convolution fusion | flops 153943808 | bytes 2753537 | tf_op jit(solution)/shard_map/dot_general | solution.py:141
  77.0 0.9 copy-done.1
  78.7 4.3 %fusion.52 = bf16[256,768]{1,0:T(8,128)(2,1)S(1)} fusion(bf16[1,1536,768]{2,1,0:T(8,128)(2,1)} %param.22, bf16[1,768,1536]{2,1,0:T(8,128)(2,1)} %param.21, f32[256,768]{1,0:T(8,128)} %copy-done.1, f32[768]{0:T(1024)} %get-tuple-element.12, f32[768]{0:T(1024)} %get-tuple-element.31, f32[256]{0:T(256)} %add_rsqrt_fusion.4, f32[256]{0:T(256)S(1)} %broadcast_multiply_fusion.5), kind=kOutput, calls=%fused_computation.49 | convolution fusion | flops 1212678144 | bytes 5906432 | tf_op jit(solution)/shard_map/dot_general | solution.py:150
  83.2 1.4 multiply_reduce_fusion.4
  84.6 5.0 %fusion.8 = bf16[256,768]{1,0:T(8,128)(2,1)} fusion(bf16[1,1536,768]{2,1,0:T(8,128)(2,1)} %param.22, bf16[1,768,1536]{2,1,0:T(8,128)(2,1)} %param.21, f32[256,768]{1,0:T(8,128)} %get-tuple-element.28, f32[256]{0:T(256)S(1)} %add_rsqrt_fusion.2, f32[256]{0:T(256)S(1)} %broadcast_multiply_fusion.3, f32[768]{0:T(1024)} %get-tuple-element.12, ...), kind=kOutput, calls=%fused_computation.14 | convolution fusion | flops 1212481536 | bytes 5906432 | tf_op jit(solution)/shard_map/dot_general | solution.py:150
  89.6 1.4 %collective-permute-done.6 = bf16[256,768]{1,0:T(8,128)(2,1)} collective-permute-done((bf16[256,768]{1,0:T(8,128)(2,1)S(1)}, bf16[256,768]{1,0:T(8,128)(2,1)}, u32[]{:S(2)}, u32[]{:S(2)}) %collective-permute-start.6) | collective-permute-done | bytes 393248 | tf_op jit(solution)/shard_map/ppermute | solution.py:24
  91.0 1.4 %fusion.133 = f32[256]{0:T(256)S(1)} fusion(f32[256,768]{1,0:T(8,128)} %copy-done.1, bf16[256,768]{1,0:T(8,128)(2,1)} %collective-permute-done.6, bf16[256,768]{1,0:T(8,128)(2,1)S(1)} %fusion.52), kind=kLoop, calls=%fused_computation.159 | loop fusion | flops 982784 | bytes 1573888 | tf_op jit(solution)/shard_map/reduce_sum | solution.py:29
  92.4 1.5 %multiply_reduce_fusion.5 = f32[256]{0:T(256)S(1)} fusion(f32[256]{0:T(256)S(1)} %broadcast_multiply_fusion.4, f32[256,768]{1,0:T(8,128)} %copy-done.1, bf16[256,768]{1,0:T(8,128)(2,1)} %collective-permute-done.6, bf16[256,768]{1,0:T(8,128)(2,1)S(1)} %fusion.52), kind=kLoop, calls=%fused_computation.76 | loop fusion | flops 1376000 | bytes 1574912 | tf_op jit(solution)/shard_map/reduce_sum | solution.py:31
  93.9 2.0 %add_convert_fusion.3 = bf16[256,768]{1,0:T(8,128)(2,1)} fusion(f32[768]{0:T(1024)S(1)} %get-tuple-element.14, f32[768]{0:T(1024)S(1)} %get-tuple-element.29, f32[256]{0:T(256)S(1)} %add_rsqrt_fusion.3, f32[256]{0:T(256)S(1)} %broadcast_multiply_fusion.4, f32[256,768]{1,0:T(8,128)S(1)} %copy-done.2, bf16[256,768]{1,0:T(8,128)(2,1)} %collective-permute-done.6, ...), kind=kLoop, calls=%fused_computation.75 | loop fusion | flops 1769472 | bytes 1974272 | tf_op jit(solution)/shard_map/convert_element_type | solution.py:156
  96.6 1.4 %collective-permute-start.9 = (bf16[256,768]{1,0:T(8,128)(2,1)}, bf16[256,768]{1,0:T(8,128)(2,1)S(1)}, u32[]{:S(2)}, u32[]{:S(2)}) collective-permute-start(bf16[256,768]{1,0:T(8,128)(2,1)} %add_convert_fusion.3), channel_id=1, source_target_pairs={{0,2},{2,4},{4,6},{6,8},{8,10},{10,12},{12,14},{14,16},{16,18},{18... | collective-permute-start | bytes 1179656 | tf_op jit(solution)/shard_map/ppermute | solution.py:19
  98.0 5.9 %collective-permute-done.7 = bf16[256,768]{1,0:T(8,128)(2,1)S(1)} collective-permute-done((bf16[256,768]{1,0:T(8,128)(2,1)}, bf16[256,768]{1,0:T(8,128)(2,1)S(1)}, u32[]{:S(2)}, u32[]{:S(2)}) %collective-permute-start.7) | collective-permute-done | bytes 393248 | tf_op jit(solution)/shard_map/ppermute | solution.py:24
  103.9 1.4 %fusion.134 = f32[256]{0:T(256)S(1)} fusion(f32[256,768]{1,0:T(8,128)} %get-tuple-element.28, bf16[256,768]{1,0:T(8,128)(2,1)S(1)} %collective-permute-done.7, bf16[256,768]{1,0:T(8,128)(2,1)} %fusion.8), kind=kLoop, calls=%fused_computation.160 | loop fusion | flops 982784 | bytes 1573888 | tf_op jit(solution)/shard_map/reduce_sum | solution.py:29
  105.4 1.5 %multiply_reduce_fusion.3 = f32[256]{0:T(256)S(1)} fusion(f32[256]{0:T(256)S(1)} %broadcast_multiply_fusion.2, f32[256,768]{1,0:T(8,128)} %get-tuple-element.28, bf16[256,768]{1,0:T(8,128)(2,1)S(1)} %collective-permute-done.7, bf16[256,768]{1,0:T(8,128)(2,1)} %fusion.8), kind=kLoop, calls=%fused_computation.71 | loop fusion | flops 1376000 | bytes 1574912 | tf_op jit(solution)/shard_map/reduce_sum | solution.py:31
  106.9 3.8 %collective-permute-done.8 = bf16[16,128,768]{2,1,0:T(8,128)(2,1)} collective-permute-done((bf16[16,128,768]{2,1,0:T(8,128)(2,1)}, bf16[16,128,768]{2,1,0:T(8,128)(2,1)}, u32[]{:S(2)}, u32[]{:S(2)}) %collective-permute-start.8) | collective-permute-done | bytes 3145760 | tf_op jit(solution)/shard_map/ppermute | solution.py:92
  110.7 7.5 %fusion.66 = bf16[256,16,256]{2,0,1:T(8,128)(2,1)S(1)} fusion(bf16[16,128,768]{2,1,0:T(8,128)(2,1)} %collective-permute-done.8, bf16[16,128,768]{2,1,0:T(8,128)(2,1)} %copy.34, pred[]{:T(512)S(6)} %eq.8, f32[256]{0:T(256)S(1)} %add_rsqrt_fusion.1, f32[256]{0:T(256)S(1)} %broadcast_multiply_fusion.2, f32[768]{0:T(1024)S(1)} %get-tuple-element.14, ...), kind=kOutput, calls=%fused_computation.66 | convolution fusion | flops 1640693760 | bytes 9969665 | tf_op jit(solution)/shard_map/dot_general | solution.py:165
  118.2 8.1 %divide_convert_fusion = bf16[256,16,256]{2,0,1:T(8,128)(2,1)S(1)} fusion(f32[]{:T(128)S(6)} %convert_element_type.176, s32[256]{0:T(256)S(1)} %get-tuple-element.33, s32[256]{0:T(256)S(1)} %get-tuple-element.36, s32[256]{0:T(256)S(1)} %get-tuple-element.32, s32[256]{0:T(256)S(1)} %get-tuple-element.37, bf16[256,16,256]{2,0,1:T(8,128)(2,1)S(1)} %fusion.66, ...), kind=kOutput, calls=%fused_computation.3 | convolution fusion | flops 1663041536 | bytes 10883589 | tf_op jit(solution)/shard_map/dot_general | solution.py:165
  126.3 2.5 %copy.36 = bf16[256,16,256]{2,1,0:T(8,128)(2,1)} copy(bf16[256,16,256]{2,0,1:T(8,128)(2,1)S(1)} %divide_convert_fusion) | data formatting | bytes 4194304 | tf_op jit(solution)/shard_map/convert_element_type | solution.py:182
  128.9 4.1 %copy.37 = bf16[32,256,128]{2,1,0:T(8,128)(2,1)} copy(bf16[32,256,128]{1,2,0:T(8,128)(2,1)} %bitcast.117) | data formatting | bytes 4194304 | tf_op jit(solution)/shard_map/transpose | solution.py:184
  133.0 3.5 %copy.38 = bf16[4,16,8,16,128]{4,3,2,1,0:T(8,128)(2,1)} copy(bf16[4,16,8,16,128]{4,3,1,2,0:T(8,128)(2,1)} %bitcast.118) | data formatting | bytes 4194304 | tf_op jit(solution)/shard_map/transpose | solution.py:185
  (43 shorter events, 2.8 us)
Async XLA Ops:
  0.0 17.5 %copy-start = (bf16[4096,384]{1,0:T(8,128)(2,1)S(1)}, bf16[4096,384]{1,0:T(8,128)(2,1)}, u32[]{:S(2)}) copy-start(bf16[4096,384]{1,0:T(8,128)(2,1)} %param.14) | copy-start | bytes 9437188
  21.3 22.1 %collective-permute-start.1 = (bf16[256,384]{1,0:T(8,128)(2,1)S(1)}, bf16[256,384]{1,0:T(8,128)(2,1)S(1)}, u32[]{:S(2)}, u32[]{:S(2)}) collective-permute-start(bf16[256,384]{1,0:T(8,128)(2,1)S(1)} %get-tuple-element.20), channel_id=1, source_target_pairs={{2,0},{4,2},{6,4},{8,6},{10,8},{12,10},{14,12},{16,14},{18,16},{20... | collective-permute-start | bytes 589832 | tf_op jit(solution)/shard_map/ppermute | solution.py:19
  22.6 23.5 %collective-permute-start = (bf16[256,384]{1,0:T(8,128)(2,1)}, bf16[256,384]{1,0:T(8,128)(2,1)}, u32[]{:S(2)}, u32[]{:S(2)}) collective-permute-start(bf16[256,384]{1,0:T(8,128)(2,1)} %get-tuple-element.19), channel_id=1, source_target_pairs={{0,1},{1,0},{2,3},{3,2},{4,5},{5,4},{6,7},{7,6},{8,9},{9,8},{10,11... | collective-permute-start | bytes 589832 | tf_op jit(solution)/shard_map/ppermute | solution.py:107
  24.7 48.2 %collective-permute-start.4 = (bf16[384,768]{1,0:T(8,128)(2,1)}, bf16[384,768]{1,0:T(8,128)(2,1)}, u32[]{:S(2)}, u32[]{:S(2)}) collective-permute-start(bf16[384,768]{1,0:T(8,128)(2,1)} %bitcast.18), channel_id=1, source_target_pairs={{0,1},{1,0},{2,3},{3,2},{4,5},{5,4},{6,7},{7,6},{8,9},{9,8},{10,11... | collective-permute-start | bytes 1769480 | tf_op jit(solution)/shard_map/ppermute | solution.py:93
  34.0 76.7 %collective-permute-start.8 = (bf16[16,128,768]{2,1,0:T(8,128)(2,1)}, bf16[16,128,768]{2,1,0:T(8,128)(2,1)}, u32[]{:S(2)}, u32[]{:S(2)}) collective-permute-start(bf16[16,128,768]{2,1,0:T(8,128)(2,1)} %copy.34), channel_id=1, source_target_pairs={{0,65},{1,64},{2,67},{3,66},{4,69},{5,68},{6,71},{7,70},{8,73},{9,... | collective-permute-start | bytes 9437192 | tf_op jit(solution)/shard_map/ppermute | solution.py:92
  43.3 8.2 %copy-start.6 = (bf16[1,3,768,384]{3,2,1,0:T(8,128)(2,1)S(1)}, bf16[1,3,768,384]{3,2,1,0:T(8,128)(2,1)}, u32[]{:S(2)}) copy-start(bf16[1,3,768,384]{3,2,1,0:T(8,128)(2,1)} %param.19) | copy-start | bytes 5308420
  44.5 5.8 %collective-permute-start.2 = (bf16[256,384]{1,0:T(8,128)(2,1)S(1)}, bf16[256,384]{1,0:T(8,128)(2,1)S(1)}, u32[]{:S(2)}, u32[]{:S(2)}) collective-permute-start(bf16[256,384]{1,0:T(8,128)(2,1)S(1)} %fusion.116), channel_id=1, source_target_pairs={{0,1},{1,0},{2,3},{3,2},{4,5},{5,4},{6,7},{7,6},{8,9},{9,8},{10,11... | collective-permute-start | bytes 589832 | tf_op jit(solution)/shard_map/ppermute | solution.py:107
  50.2 0.7 copy-start.4
  60.9 11.9 %collective-permute-start.3 = (bf16[256,384]{0,1:T(8,128)(2,1)S(1)}, bf16[256,384]{0,1:T(8,128)(2,1)}, u32[]{:S(2)}, u32[]{:S(2)}) collective-permute-start(bf16[256,384]{0,1:T(8,128)(2,1)S(1)} %bitcast.126), channel_id=1, source_target_pairs={{0,1},{1,0},{2,3},{3,2},{4,5},{5,4},{6,7},{7,6},{8,9},{9,8},{10,11... | collective-permute-start | bytes 589832 | tf_op jit(solution)/shard_map/ppermute | solution.py:139
  67.6 7.8 %copy-start.5 = (bf16[256,384]{1,0:T(8,128)(2,1)S(1)}, bf16[256,384]{1,0:T(8,128)(2,1)}, u32[]{:S(2)}) copy-start(bf16[256,384]{1,0:T(8,128)(2,1)} %copy-done.4) | copy-start | bytes 589828
  67.6 7.8 %collective-permute-start.5 = (bf16[256,384]{0,1:T(8,128)(2,1)S(1)}, bf16[256,384]{0,1:T(8,128)(2,1)S(1)}, u32[]{:S(2)}, u32[]{:S(2)}) collective-permute-start(bf16[256,384]{0,1:T(8,128)(2,1)S(1)} %bitcast.124), channel_id=1, source_target_pairs={{0,1},{1,0},{2,3},{3,2},{4,5},{5,4},{6,7},{7,6},{8,9},{9,8},{10,11... | collective-permute-start | bytes 589832 | tf_op jit(solution)/shard_map/ppermute | solution.py:139
  77.0 0.9 copy-start.1
  83.0 8.0 %collective-permute-start.6 = (bf16[256,768]{1,0:T(8,128)(2,1)S(1)}, bf16[256,768]{1,0:T(8,128)(2,1)}, u32[]{:S(2)}, u32[]{:S(2)}) collective-permute-start(bf16[256,768]{1,0:T(8,128)(2,1)S(1)} %fusion.52), channel_id=1, source_target_pairs={{0,1},{1,0},{2,3},{3,2},{4,5},{5,4},{6,7},{7,6},{8,9},{9,8},{10,11... | collective-permute-start | bytes 1179656 | tf_op jit(solution)/shard_map/ppermute | solution.py:24
  89.6 4.3 %copy-start.2 = (f32[256,768]{1,0:T(8,128)S(1)}, f32[256,768]{1,0:T(8,128)}, u32[]{:S(2)}) copy-start(f32[256,768]{1,0:T(8,128)} %copy-done.1) | copy-start | bytes 2359300
  95.9 8.0 %collective-permute-start.7 = (bf16[256,768]{1,0:T(8,128)(2,1)}, bf16[256,768]{1,0:T(8,128)(2,1)S(1)}, u32[]{:S(2)}, u32[]{:S(2)}) collective-permute-start(bf16[256,768]{1,0:T(8,128)(2,1)} %fusion.8), channel_id=1, source_target_pairs={{0,1},{1,0},{2,3},{3,2},{4,5},{5,4},{6,7},{7,6},{8,9},{9,8},{10,11... | collective-permute-start | bytes 1179656 | tf_op jit(solution)/shard_map/ppermute | solution.py:24
  96.6 14.2 %copy-start.3 = (f32[256,768]{1,0:T(8,128)S(1)}, f32[256,768]{1,0:T(8,128)}, u32[]{:S(2)}) copy-start(f32[256,768]{1,0:T(8,128)} %get-tuple-element.28) | copy-start | bytes 2359300
  96.6 21.7 %collective-permute-start.9 = (bf16[256,768]{1,0:T(8,128)(2,1)}, bf16[256,768]{1,0:T(8,128)(2,1)S(1)}, u32[]{:S(2)}, u32[]{:S(2)}) collective-permute-start(bf16[256,768]{1,0:T(8,128)(2,1)} %add_convert_fusion.3), channel_id=1, source_target_pairs={{0,2},{2,4},{4,6},{6,8},{8,10},{10,12},{12,14},{14,16},{16,18},{18... | collective-permute-start | bytes 1179656 | tf_op jit(solution)/shard_map/ppermute | solution.py:19

commit v16 on v13

--- a/solution.py
+++ b/solution.py
@@ -84,7 +84,7 @@
     devices = 2 * tile_count
     across = [(index, index ^ (tile_count + 1)) for index in range(devices)]
     other_w_decode = lax.ppermute(w_decode, ("tile", "head"), across)
-    other_w_out = lax.ppermute(w_out[0], "head", [(0, 1), (1, 0)])
+    other_w_out = lax.ppermute(w_out[0], ("tile", "head"), across)
     local_width = embed_voxel.shape[1]
     embed_by_depth = embed_voxel.reshape(PATCH * PATCH, PATCH, local_width).transpose(1, 0, 2)
     position = position.astype(jnp.float32)

time: 124 us -> 165 us (1.33)
  waiting for transfers between devices: 30.2 us -> 71.4 us
  starting transfers between devices: 18 us -> 16.3 us
    ppermute x1, waiting for transfers between devices: 0.01 us -> 56.6 us  [body(): other_w_out = lax.ppermute(w_out[0], ('tile', 'head'), across)]
    ppermute x2, waiting for transfers between devices: 17.9 us -> 5.41 us  [body(): other_columns = lax.ppermute(embedded, 'head', [(0, 1), (1, 0)])]
    ppermute x1, waiting for transfers between devices: 4.14 us -> 0.01 us  [body(): other_w_decode = lax.ppermute(w_decode, ('tile', 'head'), across)]
    ppermute x2, waiting for transfers between devices: 3.29 us -> 0.01 us  [body(): other_attended = lax.ppermute(attended, 'head', [(0, 1), (1, 0)])]
    ppermute x2, waiting for transfers between devices: 4.29 us -> 7.56 us  [partner_sum(): other = lax.ppermute(rounded, 'head', [(0, 1), (1, 0)])]
  transfers between devices with their start and end apart: 10 -> 10, of which waited for: 7 -> 6; matrix products, arithmetic and copies ran while one was open for 33% -> 25% of each run, Pallas kernels for 0% -> 0%
where the time goes in v16:
time: 165 us; the launch traced here: 163 us
  waiting for transfers between devices  71.4 us (43%)
  matrix products  33.8 us (20%)
  local copies, waits for them, and re-layouts  26.3 us (16%)
  starting transfers between devices  16.3 us (10%)
  other arithmetic  14.5 us (9%)
    ppermute x1, waiting for transfers between devices, body(): other_w_out = lax.ppermute(w_out[0], ('tile', 'head'), across)  56.6 us
    ppermute x2, starting transfers between devices, from_behind(): return lax.ppermute(block, axis, route)  8.31 us
    dot_general x2, matrix products, body(): jnp.dot(hidden, w_down[0], preferred_element_type=jnp.float32)  8.06 us
    ppermute x2, waiting for transfers between devices, partner_sum(): other = lax.ppermute(rounded, 'head', [(0, 1), (1, 0)])  7.56 us
    dot_general x2, matrix products, body(): lax.dot_general(latent, decode_by_depth, (((1,), (2,)), ((), ())), prefer...  5.81 us
    select_n x1, other arithmetic, body(): jnp.where(head_index == 0, jnp.concatenate([w_decode, other_w_decode], 1)...  5.78 us
    sub x2, matrix products, body(): weights = jax.nn.softmax(scores, axis=-1).astype(jnp.bfloat16)  5.59 us
    ppermute x2, waiting for transfers between devices, body(): other_columns = lax.ppermute(embedded, 'head', [(0, 1), (1, 0)])  5.41 us
  transfers between devices with their start and end apart: 10, of which 6 were waited for; matrix products, arithmetic and copies ran while one was open for 25% of the time, Pallas kernels for 0%

profile of v16, /device:TPU:31, one launch (start us, length us, event | category | flops | bytes accessed | tf_op | source)
XLA Modules:
  0.0 162.6 jit_solution(14981339461951542526)
XLA Ops:
  0.0 2.1 %convert_element_type.136 = f32[512,384]{1,0:T(8,128)} convert(bf16[512,384]{1,0:T(8,128)(2,1)} %param.16) | non-fusion elementwise | flops 196608 | bytes 1179648 | tf_op jit(solution)/shard_map/convert_element_type | solution.py:90
  2.1 0.8 convert_element_type.135
  3.0 0.2 reshape.123
  3.2 2.5 %broadcast_multiply_fusion = bf16[64,128,128]{2,1,0:T(8,128)(2,1)S(1)} fusion(bf16[64,128,128]{2,1,0:T(8,128)(2,1)} %param.12, bf16[64,128]{1,0:T(8,128)(2,1)S(1)} %convert_element_type.135), kind=kLoop, calls=%fused_computation.70 | loop fusion | flops 1048576 | bytes 4210688 | tf_op jit(solution)/shard_map/mul | solution.py:43
  5.7 1.9 %copy.28 = bf16[4,8,16,16,128]{4,3,2,1,0:T(8,128)(2,1)} copy(bf16[4,8,16,16,128]{4,3,1,2,0:T(8,128)(2,1)S(1)} %bitcast.113) | data formatting | bytes 4194304 | tf_op jit(solution)/shard_map/transpose | solution.py:44
  7.5 4.1 %copy.29 = bf16[32,128,256]{2,1,0:T(8,128)(2,1)} copy(bf16[32,128,256]{1,2,0:T(8,128)(2,1)} %bitcast.114) | data formatting | bytes 4194304 | tf_op jit(solution)/shard_map/transpose | solution.py:46
  11.6 4.9 %copy.30 = bf16[256,16,256]{0,1,2:T(8,128)(2,1)} copy(bf16[256,16,256]{2,1,0:T(8,128)(2,1)} %bitcast.115) | data formatting | bytes 4194304 | tf_op jit(solution)/shard_map/reshape | solution.py:46
  16.7 3.7 %fusion.93 = (bf16[256,384]{1,0:T(8,128)(2,1)S(1)}, bf16[256,384]{1,0:T(8,128)(2,1)}) fusion(f32[512,384]{1,0:T(8,128)} %convert_element_type.136, f32[32,384]{1,0:T(8,128)S(1)} %fusion.144, bf16[256,16,256]{0,1,2:T(8,128)(2,1)} %copy.30, bf16[16,256,384]{2,0,1:T(8,128)(2,1)S(1)} %bitcast.112), kind=kOutput, calls=%fused_computation.97 | convolution fusion | flops 805797888 | bytes 6471680 | tf_op jit(solution)/shard_map/dot_general | solution.py:47
  20.4 2.7 %collective-permute-start.1 = (bf16[256,384]{1,0:T(8,128)(2,1)}, bf16[256,384]{1,0:T(8,128)(2,1)S(1)}, u32[]{:S(2)}, u32[]{:S(2)}) collective-permute-start(bf16[256,384]{1,0:T(8,128)(2,1)} %get-tuple-element.20), channel_id=1, source_target_pairs={{2,0},{4,2},{6,4},{8,6},{10,8},{12,10},{14,12},{16,14},{18,16},{20... | collective-permute-start | bytes 589832 | tf_op jit(solution)/shard_map/ppermute | solution.py:19
  23.1 4.6 %copy.34 = bf16[768,2048]{0,1:T(8,128)(2,1)} copy(bf16[768,2048]{1,0:T(8,128)(2,1)} %param.23) | data formatting | bytes 6291456 | tf_op args[11]
  27.8 3.8 %collective-permute-start.8 = (bf16[768,2048]{0,1:T(8,128)(2,1)}, bf16[768,2048]{0,1:T(8,128)(2,1)}, u32[]{:S(2)}, u32[]{:S(2)}) collective-permute-start(bf16[768,2048]{0,1:T(8,128)(2,1)} %copy.34), channel_id=1, source_target_pairs={{0,65},{1,64},{2,67},{3,66},{4,69},{5,68},{6,71},{7,70},{8,73},{9,... | collective-permute-start | bytes 9437192 | tf_op jit(solution)/shard_map/ppermute | solution.py:86
  31.7 1.9 %collective-permute-done.1 = bf16[256,384]{1,0:T(8,128)(2,1)S(1)} collective-permute-done((bf16[256,384]{1,0:T(8,128)(2,1)}, bf16[256,384]{1,0:T(8,128)(2,1)S(1)}, u32[]{:S(2)}, u32[]{:S(2)}) %collective-permute-start.1) | collective-permute-done | bytes 196640 | tf_op jit(solution)/shard_map/ppermute | solution.py:19
  33.5 1.0 fusion.121
  34.6 1.7 %collective-permute-start.2 = (bf16[256,384]{1,0:T(8,128)(2,1)S(1)}, bf16[256,384]{1,0:T(8,128)(2,1)S(1)}, u32[]{:S(2)}, u32[]{:S(2)}) collective-permute-start(bf16[256,384]{1,0:T(8,128)(2,1)S(1)} %fusion.121), channel_id=1, source_target_pairs={{0,1},{1,0},{2,3},{3,2},{4,5},{5,4},{6,7},{7,6},{8,9},{9,8},{10,11... | collective-permute-start | bytes 589832 | tf_op jit(solution)/shard_map/ppermute | solution.py:101
  36.4 1.2 collective-permute-done
  37.6 4.2 %collective-permute-done.2 = bf16[256,384]{1,0:T(8,128)(2,1)S(1)} collective-permute-done((bf16[256,384]{1,0:T(8,128)(2,1)S(1)}, bf16[256,384]{1,0:T(8,128)(2,1)S(1)}, u32[]{:S(2)}, u32[]{:S(2)}) %collective-permute-start.2) | collective-permute-done | bytes 196640 | tf_op jit(solution)/shard_map/ppermute | solution.py:101
  42.1 0.3 multiply_reduce_fusion.2
  42.6 1.3 fusion.55
  44.0 2.8 %fusion.140 = (f32[6,256]{1,0:T(8,128)S(1)}, f32[6,256,512]{2,1,0:T(8,128)}) fusion(bf16[256,6,64]{0,2,1:T(8,128)(2,1)S(1)} %bitcast.131, bf16[512,6,64]{0,2,1:T(8,128)(2,1)S(1)} %bitcast.124), kind=kOutput, calls=%fused_computation.164 | convolution fusion | flops 103023104 | bytes 3741696 | tf_op jit(solution)/shard_map/sub | solution.py:133
  46.8 2.6 %fusion.71 = bf16[6,64,256]{2,1,0:T(8,128)(2,1)S(1)} fusion(bf16[512,6,64]{0,2,1:T(8,128)(2,1)S(1)} %bitcast.122, f32[6,256,512]{2,1,0:T(8,128)} %get-tuple-element.22, f32[6,256]{1,0:T(8,128)S(1)} %get-tuple-element.21), kind=kOutput, calls=%fused_computation.69 | convolution fusion | flops 102334464 | bytes 3741696 | tf_op jit(solution)/shard_map/hts,shd->thd/dot_general | solution.py:134
  49.3 1.0 collective-permute-start.3
  50.3 2.8 %fusion.141 = (f32[6,256]{1,0:T(8,128)S(1)}, f32[6,256,512]{2,1,0:T(8,128)}) fusion(bf16[256,6,64]{0,2,1:T(8,128)(2,1)S(1)} %bitcast.130, bf16[512,6,64]{0,2,1:T(8,128)(2,1)S(1)} %bitcast.125), kind=kOutput, calls=%fused_computation.165 | convolution fusion | flops 103023104 | bytes 3741696 | tf_op jit(solution)/shard_map/sub | solution.py:133
  53.1 2.6 %fusion.70 = bf16[6,64,256]{2,1,0:T(8,128)(2,1)S(1)} fusion(bf16[512,6,64]{0,2,1:T(8,128)(2,1)S(1)} %bitcast.123, f32[6,256,512]{2,1,0:T(8,128)} %get-tuple-element.24, f32[6,256]{1,0:T(8,128)S(1)} %get-tuple-element.23), kind=kOutput, calls=%fused_computation.68 | convolution fusion | flops 102334464 | bytes 3741696 | tf_op jit(solution)/shard_map/hts,shd->thd/dot_general | solution.py:134
  55.7 0.8 collective-permute-start.5
  56.5 0.4 fusion.68
  56.9 0.4 fusion.64
  57.3 56.6 %collective-permute-done.4 = bf16[384,768]{1,0:T(8,128)(2,1)} collective-permute-done((bf16[384,768]{1,0:T(8,128)(2,1)S(1)}, bf16[384,768]{1,0:T(8,128)(2,1)}, u32[]{:S(2)}, u32[]{:S(2)}) %collective-permute-start.4) | collective-permute-done | bytes 589856 | tf_op jit(solution)/shard_map/ppermute | solution.py:87
  113.9 1.5 fusion.142
  115.4 0.2 multiply_reduce_fusion.6
  115.7 4.0 %fusion.58 = bf16[256,768]{1,0:T(8,128)(2,1)S(1)} fusion(bf16[1,1536,768]{2,1,0:T(8,128)(2,1)} %param.22, bf16[1,768,1536]{2,1,0:T(8,128)(2,1)} %param.21, f32[256,768]{1,0:T(8,128)S(1)} %get-tuple-element.26, f32[768]{0:T(1024)S(1)} %get-tuple-element.12, f32[768]{0:T(1024)S(1)} %get-tuple-element.31, f32[256]{0:T(256)S(1)} %add_rsqrt_fusion.4, ...), kind=kOutput, calls=%fused_computation.53 | convolution fusion | flops 1212678144 | bytes 5906432 | tf_op jit(solution)/shard_map/dot_general | solution.py:149
  119.7 0.4 collective-permute-start.6
  120.1 1.7 %fusion.143 = (f32[256]{0:T(256)S(1)}, f32[256,768]{1,0:T(8,128)S(1)}) fusion(f32[256,768]{1,0:T(8,128)S(1)} %fusion.68, bf16[256,384]{0,1:T(8,128)(2,1)} %collective-permute-done.3, bf16[384,768]{1,0:T(8,128)(2,1)} %collective-permute-done.4, bf16[256,384]{1,0:T(8,128)(2,1)S(1)} %get-tuple-element.19, bf16[256,384]{1,0:T(8,128)(2,1)} %copy-done.4, pred[]{:T(512)S(6)} %eq.8), kind=kOutput, calls=%fused_computation.167 | convolution fusion | flops 153943808 | bytes 2753537 | tf_op jit(solution)/shard_map/dot_general | solution.py:140
  121.9 0.2 multiply_reduce_fusion.4
  122.1 4.0 %fusion.12 = bf16[256,768]{1,0:T(8,128)(2,1)S(1)} fusion(bf16[1,1536,768]{2,1,0:T(8,128)(2,1)} %param.22, bf16[1,768,1536]{2,1,0:T(8,128)(2,1)} %param.21, f32[256,768]{1,0:T(8,128)S(1)} %get-tuple-element.28, f32[256]{0:T(256)S(1)} %add_rsqrt_fusion.2, f32[256]{0:T(256)S(1)} %broadcast_multiply_fusion.3, f32[768]{0:T(1024)S(1)} %get-tuple-element.12, ...), kind=kOutput, calls=%fused_computation.18 | convolution fusion | flops 1212481536 | bytes 5906432 | tf_op jit(solution)/shard_map/dot_general | solution.py:149
  126.2 3.8 %collective-permute-done.6 = bf16[256,768]{1,0:T(8,128)(2,1)S(1)} collective-permute-done((bf16[256,768]{1,0:T(8,128)(2,1)S(1)}, bf16[256,768]{1,0:T(8,128)(2,1)S(1)}, u32[]{:S(2)}, u32[]{:S(2)}) %collective-permute-start.6) | collective-permute-done | bytes 393248 | tf_op jit(solution)/shard_map/ppermute | solution.py:24
  130.0 0.2 fusion.136
  130.2 0.3 multiply_reduce_fusion.5
  130.5 0.2 add_convert_fusion.3
  130.9 5.6 %collective-permute-start.9 = (bf16[256,768]{1,0:T(8,128)(2,1)S(1)}, bf16[256,768]{1,0:T(8,128)(2,1)S(1)}, u32[]{:S(2)}, u32[]{:S(2)}) collective-permute-start(bf16[256,768]{1,0:T(8,128)(2,1)S(1)} %add_convert_fusion.3), channel_id=1, source_target_pairs={{0,2},{2,4},{4,6},{6,8},{8,10},{10,12},{12,14},{14,16},{16,18},{18... | collective-permute-start | bytes 1179656 | tf_op jit(solution)/shard_map/ppermute | solution.py:19
  136.5 3.7 %collective-permute-done.7 = bf16[256,768]{1,0:T(8,128)(2,1)S(1)} collective-permute-done((bf16[256,768]{1,0:T(8,128)(2,1)S(1)}, bf16[256,768]{1,0:T(8,128)(2,1)S(1)}, u32[]{:S(2)}, u32[]{:S(2)}) %collective-permute-start.7) | collective-permute-done | bytes 393248 | tf_op jit(solution)/shard_map/ppermute | solution.py:24
  140.2 0.2 fusion.137
  140.4 0.3 multiply_reduce_fusion.3
  140.7 5.8 %maximum_select_fusion = bf16[768,4096]{0,1:T(8,128)(2,1)S(1)} fusion(bf16[768,2048]{0,1:T(8,128)(2,1)} %collective-permute-done.8, bf16[768,2048]{0,1:T(8,128)(2,1)} %copy.34, pred[]{:T(512)S(6)} %eq.8), kind=kLoop, calls=%fused_computation.2 | loop fusion | flops 28311552 | bytes 12582913 | tf_op jit(solution)/shard_map/jit(_where)/select_n | solution.py:115
  146.5 2.6 %fusion.4 = bf16[256,16,256]{2,0,1:T(8,128)(2,1)S(1)} fusion(bf16[16,256,768]{2,0,1:T(8,128)(2,1)S(1)} %bitcast.118, f32[256]{0:T(256)S(1)} %add_rsqrt_fusion.1, f32[256]{0:T(256)S(1)} %broadcast_multiply_fusion.2, f32[768]{0:T(1024)S(1)} %get-tuple-element.14, f32[768]{0:T(1024)S(1)} %get-tuple-element.29, f32[256,768]{1,0:T(8,128)S(1)} %get-tuple-element.28, ...), kind=kOutput, calls=%fused_computation.5 | convolution fusion | flops 1612382208 | bytes 9969664 | tf_op jit(solution)/shard_map/dot_general | solution.py:164
  149.1 3.2 %divide_convert_fusion = bf16[256,16,256]{2,0,1:T(8,128)(2,1)S(1)} fusion(f32[]{:T(128)S(6)} %convert_element_type.176, s32[256]{0:T(256)S(1)} %get-tuple-element.33, s32[256]{0:T(256)S(1)} %get-tuple-element.36, s32[256]{0:T(256)S(1)} %get-tuple-element.32, s32[256]{0:T(256)S(1)} %get-tuple-element.37, bf16[256,16,256]{2,0,1:T(8,128)(2,1)S(1)} %fusion.4, ...), kind=kOutput, calls=%fused_computation.7 | convolution fusion | flops 1634729984 | bytes 10883588 | tf_op jit(solution)/shard_map/dot_general | solution.py:164
  152.4 2.5 %copy.38 = bf16[256,16,256]{2,1,0:T(8,128)(2,1)} copy(bf16[256,16,256]{2,0,1:T(8,128)(2,1)S(1)} %divide_convert_fusion) | data formatting | bytes 4194304 | tf_op jit(solution)/shard_map/convert_element_type | solution.py:181
  154.9 4.2 %copy.39 = bf16[32,256,128]{2,1,0:T(8,128)(2,1)} copy(bf16[32,256,128]{1,2,0:T(8,128)(2,1)} %bitcast.116) | data formatting | bytes 4194304 | tf_op jit(solution)/shard_map/transpose | solution.py:183
  159.1 3.5 %copy.40 = bf16[4,16,8,16,128]{4,3,2,1,0:T(8,128)(2,1)} copy(bf16[4,16,8,16,128]{4,3,1,2,0:T(8,128)(2,1)} %bitcast.117) | data formatting | bytes 4194304 | tf_op jit(solution)/shard_map/transpose | solution.py:184
  (49 shorter events, 1.2 us)
Async XLA Ops:
  0.0 16.6 %copy-start = (bf16[4096,384]{1,0:T(8,128)(2,1)S(1)}, bf16[4096,384]{1,0:T(8,128)(2,1)}, u32[]{:S(2)}) copy-start(bf16[4096,384]{1,0:T(8,128)(2,1)} %param.14) | copy-start | bytes 9437188
  11.6 4.9 %copy-start.3 = (bf16[256,384]{1,0:T(8,128)(2,1)S(1)}, bf16[256,384]{1,0:T(8,128)(2,1)}, u32[]{:S(2)}) copy-start(bf16[256,384]{1,0:T(8,128)(2,1)} %param.15) | copy-start | bytes 589828
  20.4 11.1 %copy-start.2 = (bf16[1,384,768]{2,1,0:T(8,128)(2,1)S(1)}, bf16[1,384,768]{2,1,0:T(8,128)(2,1)}, u32[]{:S(2)}) copy-start(bf16[1,384,768]{2,1,0:T(8,128)(2,1)} %param.20) | copy-start | bytes 1769476
  20.4 15.9 %copy-start.7 = (f32[3,768]{1,0:T(4,128)S(1)}, f32[3,768]{1,0:T(4,128)}, u32[]{:S(2)}) copy-start(f32[3,768]{1,0:T(4,128)} %param.18) | copy-start | bytes 27652
  20.4 15.9 %copy-start.8 = (f32[3,768]{1,0:T(4,128)S(1)}, f32[3,768]{1,0:T(4,128)}, u32[]{:S(2)}) copy-start(f32[3,768]{1,0:T(4,128)} %param.17) | copy-start | bytes 27652
  20.4 13.1 %collective-permute-start.1 = (bf16[256,384]{1,0:T(8,128)(2,1)}, bf16[256,384]{1,0:T(8,128)(2,1)S(1)}, u32[]{:S(2)}, u32[]{:S(2)}) collective-permute-start(bf16[256,384]{1,0:T(8,128)(2,1)} %get-tuple-element.20), channel_id=1, source_target_pairs={{2,0},{4,2},{6,4},{8,6},{10,8},{12,10},{14,12},{16,14},{18,16},{20... | collective-permute-start | bytes 589832 | tf_op jit(solution)/shard_map/ppermute | solution.py:19
  27.8 113.0 %collective-permute-start.8 = (bf16[768,2048]{0,1:T(8,128)(2,1)}, bf16[768,2048]{0,1:T(8,128)(2,1)}, u32[]{:S(2)}, u32[]{:S(2)}) collective-permute-start(bf16[768,2048]{0,1:T(8,128)(2,1)} %copy.34), channel_id=1, source_target_pairs={{0,65},{1,64},{2,67},{3,66},{4,69},{5,68},{6,71},{7,70},{8,73},{9,... | collective-permute-start | bytes 9437192 | tf_op jit(solution)/shard_map/ppermute | solution.py:86
  31.5 6.0 %collective-permute-start = (bf16[256,384]{1,0:T(8,128)(2,1)S(1)}, bf16[256,384]{1,0:T(8,128)(2,1)S(1)}, u32[]{:S(2)}, u32[]{:S(2)}) collective-permute-start(bf16[256,384]{1,0:T(8,128)(2,1)S(1)} %get-tuple-element.19), channel_id=1, source_target_pairs={{0,1},{1,0},{2,3},{3,2},{4,5},{5,4},{6,7},{7,6},{8,9},{9,8},{10,11... | collective-permute-start | bytes 589832 | tf_op jit(solution)/shard_map/ppermute | solution.py:101
  31.5 82.3 %collective-permute-start.4 = (bf16[384,768]{1,0:T(8,128)(2,1)S(1)}, bf16[384,768]{1,0:T(8,128)(2,1)}, u32[]{:S(2)}, u32[]{:S(2)}) collective-permute-start(bf16[384,768]{1,0:T(8,128)(2,1)S(1)} %bitcast.120), channel_id=1, source_target_pairs={{0,65},{1,64},{2,67},{3,66},{4,69},{5,68},{6,71},{7,70},{8,73},{9,... | collective-permute-start | bytes 1769480 | tf_op jit(solution)/shard_map/ppermute | solution.py:87
  34.6 7.3 %collective-permute-start.2 = (bf16[256,384]{1,0:T(8,128)(2,1)S(1)}, bf16[256,384]{1,0:T(8,128)(2,1)S(1)}, u32[]{:S(2)}, u32[]{:S(2)}) collective-permute-start(bf16[256,384]{1,0:T(8,128)(2,1)S(1)} %fusion.121), channel_id=1, source_target_pairs={{0,1},{1,0},{2,3},{3,2},{4,5},{5,4},{6,7},{7,6},{8,9},{9,8},{10,11... | collective-permute-start | bytes 589832 | tf_op jit(solution)/shard_map/ppermute | solution.py:101
  37.6 4.9 %copy-start.4 = (bf16[256,384]{1,0:T(8,128)(2,1)}, bf16[256,384]{1,0:T(8,128)(2,1)S(1)}, u32[]{:S(2)}) copy-start(bf16[256,384]{1,0:T(8,128)(2,1)S(1)} %collective-permute-done) | copy-start | bytes 589828
  37.6 4.9 %copy-start.9 = (bf16[1,3,768,384]{3,2,1,0:T(8,128)(2,1)S(1)}, bf16[1,3,768,384]{3,2,1,0:T(8,128)(2,1)}, u32[]{:S(2)}) copy-start(bf16[1,3,768,384]{3,2,1,0:T(8,128)(2,1)} %param.19) | copy-start | bytes 5308420
  41.9 0.7 copy-start.5
  49.3 70.8 %collective-permute-start.3 = (bf16[256,384]{0,1:T(8,128)(2,1)S(1)}, bf16[256,384]{0,1:T(8,128)(2,1)}, u32[]{:S(2)}, u32[]{:S(2)}) collective-permute-start(bf16[256,384]{0,1:T(8,128)(2,1)S(1)} %bitcast.126), channel_id=1, source_target_pairs={{0,1},{1,0},{2,3},{3,2},{4,5},{5,4},{6,7},{7,6},{8,9},{9,8},{10,11... | collective-permute-start | bytes 589832 | tf_op jit(solution)/shard_map/ppermute | solution.py:138
  55.7 58.2 %copy-start.6 = (bf16[256,384]{1,0:T(8,128)(2,1)S(1)}, bf16[256,384]{1,0:T(8,128)(2,1)}, u32[]{:S(2)}) copy-start(bf16[256,384]{1,0:T(8,128)(2,1)} %copy-done.5) | copy-start | bytes 589828
  55.7 58.2 %collective-permute-start.5 = (bf16[256,384]{0,1:T(8,128)(2,1)S(1)}, bf16[256,384]{0,1:T(8,128)(2,1)S(1)}, u32[]{:S(2)}, u32[]{:S(2)}) collective-permute-start(bf16[256,384]{0,1:T(8,128)(2,1)S(1)} %bitcast.128), channel_id=1, source_target_pairs={{0,1},{1,0},{2,3},{3,2},{4,5},{5,4},{6,7},{7,6},{8,9},{9,8},{10,11... | collective-permute-start | bytes 589832 | tf_op jit(solution)/shard_map/ppermute | solution.py:138
  119.7 10.3 %collective-permute-start.6 = (bf16[256,768]{1,0:T(8,128)(2,1)S(1)}, bf16[256,768]{1,0:T(8,128)(2,1)S(1)}, u32[]{:S(2)}, u32[]{:S(2)}) collective-permute-start(bf16[256,768]{1,0:T(8,128)(2,1)S(1)} %fusion.58), channel_id=1, source_target_pairs={{0,1},{1,0},{2,3},{3,2},{4,5},{5,4},{6,7},{7,6},{8,9},{9,8},{10,11... | collective-permute-start | bytes 1179656 | tf_op jit(solution)/shard_map/ppermute | solution.py:24
  130.8 9.5 %collective-permute-start.7 = (bf16[256,768]{1,0:T(8,128)(2,1)S(1)}, bf16[256,768]{1,0:T(8,128)(2,1)S(1)}, u32[]{:S(2)}, u32[]{:S(2)}) collective-permute-start(bf16[256,768]{1,0:T(8,128)(2,1)S(1)} %fusion.12), channel_id=1, source_target_pairs={{0,1},{1,0},{2,3},{3,2},{4,5},{5,4},{6,7},{7,6},{8,9},{9,8},{10,11... | collective-permute-start | bytes 1179656 | tf_op jit(solution)/shard_map/ppermute | solution.py:24
  130.9 18.2 %collective-permute-start.9 = (bf16[256,768]{1,0:T(8,128)(2,1)S(1)}, bf16[256,768]{1,0:T(8,128)(2,1)S(1)}, u32[]{:S(2)}, u32[]{:S(2)}) collective-permute-start(bf16[256,768]{1,0:T(8,128)(2,1)S(1)} %add_convert_fusion.3), channel_id=1, source_target_pairs={{0,2},{2,4},{4,6},{6,8},{8,10},{10,12},{12,14},{14,16},{16,18},{18... | collective-permute-start | bytes 1179656 | tf_op jit(solution)/shard_map/ppermute | solution.py:19
  154.9 7.8 %copy-start.1 = (bf16[4096,384]{1,0:T(8,128)(2,1)S(1)}, bf16[4096,384]{1,0:T(8,128)(2,1)}, u32[]{:S(2)}) copy-start(bf16[4096,384]{1,0:T(8,128)(2,1)} %param.14) | copy-start | bytes 9437188

commit v17 on v13

--- a/solution.py
+++ b/solution.py
@@ -112,10 +112,10 @@
     ).astype(jnp.bfloat16)
     keys = projected[1].reshape(tokens, local_heads, HEAD_DIM)
     values = projected[2].reshape(tokens, local_heads, HEAD_DIM)
-    whole_w_decode = jnp.where(
-        head_index == 0,
-        jnp.concatenate([w_decode, other_w_decode], 1),
-        jnp.concatenate([other_w_decode, w_decode], 1),
+    local_columns = w_decode.shape[1]
+    whole_w_decode = lax.dynamic_slice_in_dim(
+        jnp.concatenate([w_decode, other_w_decode, w_decode], 1),
+        head_index * local_columns, 2 * local_columns, 1,
     )
     inner_rows = PATCH
     cell_cols = inner_rows * PATCH

time: 124 us -> 128 us (1.032)
  local copies, waits for them, and re-layouts: 26.3 us -> 28.5 us
    concatenate x0 -> x1, other arithmetic: none -> 6.74 us  [body(): jnp.concatenate([w_decode, other_w_decode, w_decode], 1)]
    select_n x1 -> x0, other arithmetic: 5.77 us -> none  [body(): jnp.where(head_index == 0, jnp.concatenate([w_decode, other_w_decode], 1)...]
    transpose x0 -> x1, local copies, waits for them, and re-layouts: none -> 2.12 us  [body(): decode_by_depth = whole_w_decode.T.reshape(inner_rows, PATCH, PATCH, -1)....]
  transfers between devices with their start and end apart: 10 -> 10, of which waited for: 7 -> 7; matrix products, arithmetic and copies ran while one was open for 33% -> 34% of each run, Pallas kernels for 0% -> 0%
where the time goes in v17:
time: 128 us; the launch traced here: 127 us
  matrix products  34.6 us (27%)
  waiting for transfers between devices  30.4 us (24%)
  local copies, waits for them, and re-layouts  28.5 us (22%)
  starting transfers between devices  17.8 us (14%)
  other arithmetic  15.4 us (12%)
    ppermute x2, waiting for transfers between devices, body(): other_columns = lax.ppermute(embedded, 'head', [(0, 1), (1, 0)])  17.9 us
    dot_general x2, matrix products, body(): jnp.dot(hidden, w_down[0], preferred_element_type=jnp.float32)  8.06 us
    ppermute x2, starting transfers between devices, from_behind(): return lax.ppermute(block, axis, route)  7.28 us
    concatenate x1, other arithmetic, body(): jnp.concatenate([w_decode, other_w_decode, w_decode], 1)  6.74 us
    dot_general x2, matrix products, body(): lax.dot_general(latent, decode_by_depth, (((1,), (2,)), ((), ())), prefer...  6.57 us
    sub x2, matrix products, body(): weights = jax.nn.softmax(scores, axis=-1).astype(jnp.bfloat16)  5.6 us
    dot_general x2, matrix products, body(): jnp.einsum('hts,shd->thd', weights, values, preferred_element_type=jnp.fl...  5.11 us
    reshape x1, local copies, waits for them, and re-layouts, embed_planes(): voxels = jnp.swapaxes(grouped, 1, 2).reshape(rows, PATCH, PATCH * PATCH)  4.86 us
  transfers between devices with their start and end apart: 10, of which 7 were waited for; matrix products, arithmetic and copies ran while one was open for 34% of the time, Pallas kernels for 0%

profile of v17, /device:TPU:31, one launch (start us, length us, event | category | flops | bytes accessed | tf_op | source)
XLA Modules:
  0.0 126.9 jit_solution(1393253336477493191)
XLA Ops:
  0.0 2.1 %convert_element_type.136 = f32[512,384]{1,0:T(8,128)} convert(bf16[512,384]{1,0:T(8,128)(2,1)} %param.16) | non-fusion elementwise | flops 196608 | bytes 1179648 | tf_op jit(solution)/shard_map/convert_element_type | solution.py:90
  2.1 0.8 convert_element_type.135
  3.2 2.5 %broadcast_multiply_fusion = bf16[64,128,128]{2,1,0:T(8,128)(2,1)S(1)} fusion(bf16[64,128,128]{2,1,0:T(8,128)(2,1)} %param.12, bf16[64,128]{1,0:T(8,128)(2,1)S(1)} %convert_element_type.135), kind=kLoop, calls=%fused_computation.70 | loop fusion | flops 1048576 | bytes 4210688 | tf_op jit(solution)/shard_map/mul | solution.py:43
  5.7 1.9 %copy.27 = bf16[4,8,16,16,128]{4,3,2,1,0:T(8,128)(2,1)} copy(bf16[4,8,16,16,128]{4,3,1,2,0:T(8,128)(2,1)S(1)} %bitcast.115) | data formatting | bytes 4194304 | tf_op jit(solution)/shard_map/transpose | solution.py:44
  7.5 4.1 %copy.28 = bf16[32,128,256]{2,1,0:T(8,128)(2,1)} copy(bf16[32,128,256]{1,2,0:T(8,128)(2,1)} %bitcast.116) | data formatting | bytes 4194304 | tf_op jit(solution)/shard_map/transpose | solution.py:46
  11.6 4.9 %copy.29 = bf16[256,16,256]{0,1,2:T(8,128)(2,1)} copy(bf16[256,16,256]{2,1,0:T(8,128)(2,1)} %bitcast.117) | data formatting | bytes 4194304 | tf_op jit(solution)/shard_map/reshape | solution.py:46
  16.7 3.7 %fusion.90 = (bf16[256,384]{1,0:T(8,128)(2,1)S(1)}, bf16[256,384]{1,0:T(8,128)(2,1)}) fusion(f32[512,384]{1,0:T(8,128)} %convert_element_type.136, f32[32,384]{1,0:T(8,128)S(1)} %fusion.141, bf16[256,16,256]{0,1,2:T(8,128)(2,1)} %copy.29, bf16[16,256,384]{2,0,1:T(8,128)(2,1)S(1)} %bitcast.113), kind=kOutput, calls=%fused_computation.98 | convolution fusion | flops 805797888 | bytes 6471680 | tf_op jit(solution)/shard_map/dot_general | solution.py:47
  20.4 2.7 %collective-permute-start.1 = (bf16[256,384]{1,0:T(8,128)(2,1)}, bf16[256,384]{1,0:T(8,128)(2,1)S(1)}, u32[]{:S(2)}, u32[]{:S(2)}) collective-permute-start(bf16[256,384]{1,0:T(8,128)(2,1)} %get-tuple-element.20), channel_id=1, source_target_pairs={{2,0},{4,2},{6,4},{8,6},{10,8},{12,10},{14,12},{16,14},{18,16},{20... | collective-permute-start | bytes 589832 | tf_op jit(solution)/shard_map/ppermute | solution.py:19
  23.1 4.6 %copy.33 = bf16[768,2048]{0,1:T(8,128)(2,1)} copy(bf16[768,2048]{1,0:T(8,128)(2,1)} %param.23) | data formatting | bytes 6291456 | tf_op args[11]
  27.8 3.8 %collective-permute-start.8 = (bf16[768,2048]{0,1:T(8,128)(2,1)}, bf16[768,2048]{0,1:T(8,128)(2,1)}, u32[]{:S(2)}, u32[]{:S(2)}) collective-permute-start(bf16[768,2048]{0,1:T(8,128)(2,1)} %copy.33), channel_id=1, source_target_pairs={{0,65},{1,64},{2,67},{3,66},{4,69},{5,68},{6,71},{7,70},{8,73},{9,... | collective-permute-start | bytes 9437192 | tf_op jit(solution)/shard_map/ppermute | solution.py:86
  31.5 1.5 %collective-permute-start.4 = (bf16[384,768]{1,0:T(8,128)(2,1)S(1)}, bf16[384,768]{1,0:T(8,128)(2,1)}, u32[]{:S(2)}, u32[]{:S(2)}) collective-permute-start(bf16[384,768]{1,0:T(8,128)(2,1)S(1)} %bitcast.122), channel_id=1, source_target_pairs={{0,1},{1,0},{2,3},{3,2},{4,5},{5,4},{6,7},{7,6},{8,9},{9,8},{10,11... | collective-permute-start | bytes 1769480 | tf_op jit(solution)/shard_map/ppermute | solution.py:87
  33.0 0.5 collective-permute-done.1
  33.5 1.0 fusion.118
  34.6 1.7 %collective-permute-start.2 = (bf16[256,384]{1,0:T(8,128)(2,1)S(1)}, bf16[256,384]{1,0:T(8,128)(2,1)S(1)}, u32[]{:S(2)}, u32[]{:S(2)}) collective-permute-start(bf16[256,384]{1,0:T(8,128)(2,1)S(1)} %fusion.118), channel_id=1, source_target_pairs={{0,1},{1,0},{2,3},{3,2},{4,5},{5,4},{6,7},{7,6},{8,9},{9,8},{10,11... | collective-permute-start | bytes 589832 | tf_op jit(solution)/shard_map/ppermute | solution.py:101
  36.4 1.2 collective-permute-done
  37.6 16.8 %collective-permute-done.2 = bf16[256,384]{1,0:T(8,128)(2,1)S(1)} collective-permute-done((bf16[256,384]{1,0:T(8,128)(2,1)S(1)}, bf16[256,384]{1,0:T(8,128)(2,1)S(1)}, u32[]{:S(2)}, u32[]{:S(2)}) %collective-permute-start.2) | collective-permute-done | bytes 196640 | tf_op jit(solution)/shard_map/ppermute | solution.py:101
  54.7 0.3 multiply_reduce_fusion.2
  55.1 1.3 %fusion.51 = bf16[3,512,384]{1,2,0:T(8,128)(2,1)S(1)} fusion(bf16[1,3,768,384]{3,2,1,0:T(8,128)(2,1)S(1)} %copy-done.9, f32[256,768]{1,0:T(8,128)S(1)} %fusion.92, f32[256,768]{1,0:T(8,128)S(1)} %fusion.91, f32[768]{0:T(1024)S(1)} %get-tuple-element.13, f32[768]{0:T(1024)S(1)} %get-tuple-element.32, f32[512]{0:T(512)S(1)} %add_rsqrt_fusion, ...), kind=kOutput, calls=%fused_computation.52 | convolution fusion | flops 908918784 | bytes 4532224 | tf_op jit(solution)/shard_map/td,sde->ste/dot_general | solution.py:110
  56.5 2.8 %fusion.137 = (f32[6,256]{1,0:T(8,128)S(1)}, f32[6,256,512]{2,1,0:T(8,128)}) fusion(bf16[256,6,64]{0,2,1:T(8,128)(2,1)S(1)} %bitcast.133, bf16[512,6,64]{0,2,1:T(8,128)(2,1)S(1)} %bitcast.126), kind=kOutput, calls=%fused_computation.165 | convolution fusion | flops 103023104 | bytes 3741696 | tf_op jit(solution)/shard_map/sub | solution.py:133
  59.3 2.6 %fusion.67 = bf16[6,64,256]{2,1,0:T(8,128)(2,1)S(1)} fusion(bf16[512,6,64]{0,2,1:T(8,128)(2,1)S(1)} %bitcast.124, f32[6,256,512]{2,1,0:T(8,128)} %get-tuple-element.22, f32[6,256]{1,0:T(8,128)S(1)} %get-tuple-element.21), kind=kOutput, calls=%fused_computation.69 | convolution fusion | flops 102334464 | bytes 3741696 | tf_op jit(solution)/shard_map/hts,shd->thd/dot_general | solution.py:134
  61.9 0.4 collective-permute-start.3
  62.2 2.8 %fusion.138 = (f32[6,256]{1,0:T(8,128)S(1)}, f32[6,256,512]{2,1,0:T(8,128)}) fusion(bf16[256,6,64]{0,2,1:T(8,128)(2,1)S(1)} %bitcast.132, bf16[512,6,64]{0,2,1:T(8,128)(2,1)S(1)} %bitcast.127), kind=kOutput, calls=%fused_computation.166 | convolution fusion | flops 103023104 | bytes 3741696 | tf_op jit(solution)/shard_map/sub | solution.py:133
  65.0 2.6 %fusion.66 = bf16[6,64,256]{2,1,0:T(8,128)(2,1)S(1)} fusion(bf16[512,6,64]{0,2,1:T(8,128)(2,1)S(1)} %bitcast.125, f32[6,256,512]{2,1,0:T(8,128)} %get-tuple-element.24, f32[6,256]{1,0:T(8,128)S(1)} %get-tuple-element.23), kind=kOutput, calls=%fused_computation.68 | convolution fusion | flops 102334464 | bytes 3741696 | tf_op jit(solution)/shard_map/hts,shd->thd/dot_general | solution.py:134
  67.6 1.4 %collective-permute-start.5 = (bf16[256,384]{0,1:T(8,128)(2,1)S(1)}, bf16[256,384]{0,1:T(8,128)(2,1)S(1)}, u32[]{:S(2)}, u32[]{:S(2)}) collective-permute-start(bf16[256,384]{0,1:T(8,128)(2,1)S(1)} %bitcast.130), channel_id=1, source_target_pairs={{0,1},{1,0},{2,3},{3,2},{4,5},{5,4},{6,7},{7,6},{8,9},{9,8},{10,11... | collective-permute-start | bytes 589832 | tf_op jit(solution)/shard_map/ppermute | solution.py:138
  69.0 0.4 fusion.64
  69.4 0.4 fusion.60
  69.8 3.3 %collective-permute-done.5 = bf16[256,384]{0,1:T(8,128)(2,1)S(1)} collective-permute-done((bf16[256,384]{0,1:T(8,128)(2,1)S(1)}, bf16[256,384]{0,1:T(8,128)(2,1)S(1)}, u32[]{:S(2)}, u32[]{:S(2)}) %collective-permute-start.5) | collective-permute-done | bytes 196640 | tf_op jit(solution)/shard_map/ppermute | solution.py:138
  73.1 1.5 %fusion.139 = (f32[256]{0:T(256)S(1)}, f32[256,768]{1,0:T(8,128)S(1)}) fusion(f32[256,768]{1,0:T(8,128)S(1)} %fusion.60, bf16[256,384]{0,1:T(8,128)(2,1)S(1)} %collective-permute-done.5, bf16[384,768]{1,0:T(8,128)(2,1)} %collective-permute-done.4, bf16[256,384]{1,0:T(8,128)(2,1)S(1)} %fusion.118, bf16[256,384]{1,0:T(8,128)(2,1)S(1)} %copy-done.6, pred[]{:T(512)S(6)} %eq.7), kind=kOutput, calls=%fused_computation.167 | convolution fusion | flops 153943808 | bytes 2753537 | tf_op jit(solution)/shard_map/dot_general | solution.py:140
  74.7 0.2 multiply_reduce_fusion.6
  74.9 4.0 %fusion.54 = bf16[256,768]{1,0:T(8,128)(2,1)S(1)} fusion(bf16[1,1536,768]{2,1,0:T(8,128)(2,1)} %param.22, bf16[1,768,1536]{2,1,0:T(8,128)(2,1)} %param.21, f32[256,768]{1,0:T(8,128)S(1)} %get-tuple-element.26, f32[768]{0:T(1024)S(1)} %get-tuple-element.12, f32[768]{0:T(1024)S(1)} %get-tuple-element.33, f32[256]{0:T(256)S(1)} %add_rsqrt_fusion.4, ...), kind=kOutput, calls=%fused_computation.53 | convolution fusion | flops 1212678144 | bytes 5906432 | tf_op jit(solution)/shard_map/dot_general | solution.py:149
  79.0 1.0 collective-permute-start.6
  80.0 1.7 %fusion.140 = (f32[256]{0:T(256)S(1)}, f32[256,768]{1,0:T(8,128)S(1)}) fusion(f32[256,768]{1,0:T(8,128)S(1)} %fusion.64, bf16[256,384]{0,1:T(8,128)(2,1)} %collective-permute-done.3, bf16[384,768]{1,0:T(8,128)(2,1)} %collective-permute-done.4, bf16[256,384]{1,0:T(8,128)(2,1)S(1)} %get-tuple-element.19, bf16[256,384]{1,0:T(8,128)(2,1)} %copy-done.4, pred[]{:T(512)S(6)} %eq.7), kind=kOutput, calls=%fused_computation.168 | convolution fusion | flops 153943808 | bytes 2753537 | tf_op jit(solution)/shard_map/dot_general | solution.py:140
  81.9 4.0 %fusion.10 = bf16[256,768]{1,0:T(8,128)(2,1)S(1)} fusion(bf16[1,1536,768]{2,1,0:T(8,128)(2,1)} %param.22, bf16[1,768,1536]{2,1,0:T(8,128)(2,1)} %param.21, f32[256,768]{1,0:T(8,128)S(1)} %get-tuple-element.28, f32[256]{0:T(256)S(1)} %add_rsqrt_fusion.2, f32[256]{0:T(256)S(1)} %broadcast_multiply_fusion.3, f32[768]{0:T(1024)S(1)} %get-tuple-element.12, ...), kind=kOutput, calls=%fused_computation.18 | convolution fusion | flops 1212481536 | bytes 5906432 | tf_op jit(solution)/shard_map/dot_general | solution.py:149
  86.0 1.8 %collective-permute-done.6 = bf16[256,768]{1,0:T(8,128)(2,1)S(1)} collective-permute-done((bf16[256,768]{1,0:T(8,128)(2,1)S(1)}, bf16[256,768]{1,0:T(8,128)(2,1)S(1)}, u32[]{:S(2)}, u32[]{:S(2)}) %collective-permute-start.6) | collective-permute-done | bytes 393248 | tf_op jit(solution)/shard_map/ppermute | solution.py:24
  88.0 0.3 multiply_reduce_fusion.5
  88.3 0.2 add_convert_fusion.3
  88.5 0.7 collective-permute-start.7
  89.3 4.6 %collective-permute-start.9 = (bf16[256,768]{1,0:T(8,128)(2,1)S(1)}, bf16[256,768]{1,0:T(8,128)(2,1)S(1)}, u32[]{:S(2)}, u32[]{:S(2)}) collective-permute-start(bf16[256,768]{1,0:T(8,128)(2,1)S(1)} %add_convert_fusion.3), channel_id=1, source_target_pairs={{0,2},{2,4},{4,6},{6,8},{8,10},{10,12},{12,14},{14,16},{16,18},{18... | collective-permute-start | bytes 1179656 | tf_op jit(solution)/shard_map/ppermute | solution.py:19
  93.8 2.7 %collective-permute-done.7 = bf16[256,768]{1,0:T(8,128)(2,1)S(1)} collective-permute-done((bf16[256,768]{1,0:T(8,128)(2,1)S(1)}, bf16[256,768]{1,0:T(8,128)(2,1)S(1)}, u32[]{:S(2)}, u32[]{:S(2)}) %collective-permute-start.7) | collective-permute-done | bytes 393248 | tf_op jit(solution)/shard_map/ppermute | solution.py:24
  96.8 0.3 multiply_reduce_fusion.3
  97.1 4.1 %collective-permute-done.8 = bf16[768,2048]{0,1:T(8,128)(2,1)} collective-permute-done((bf16[768,2048]{0,1:T(8,128)(2,1)}, bf16[768,2048]{0,1:T(8,128)(2,1)}, u32[]{:S(2)}, u32[]{:S(2)}) %collective-permute-start.8) | collective-permute-done | bytes 3145760 | tf_op jit(solution)/shard_map/ppermute | solution.py:86
  101.2 6.7 %fusion.3 = bf16[768,4096]{0,1:T(8,128)(2,1)S(1)} fusion(s32[]{:T(128)S(6)} %select_n.48, bf16[768,2048]{0,1:T(8,128)(2,1)} %copy.33, bf16[768,2048]{0,1:T(8,128)(2,1)} %collective-permute-done.8), kind=kLoop, calls=%fused_computation.6 | loop fusion | flops 18874368 | bytes 12582916 | tf_op jit(solution)/shard_map/concatenate | solution.py:117
  108.0 2.1 %copy.35 = bf16[16,16,16,768]{3,2,1,0:T(8,128)(2,1)S(1)} copy(bf16[16,16,16,768]{3,0,2,1:T(8,128)(2,1)S(1)} %bitcast.114) | data formatting | bytes 12582912 | tf_op jit(solution)/shard_map/transpose | solution.py:124
  110.1 2.0 %fusion.88 = bf16[256,16,256]{2,0,1:T(8,128)(2,1)S(1)} fusion(bf16[16,256,768]{2,1,0:T(8,128)(2,1)S(1)} %bitcast.120, f32[256]{0:T(256)S(1)} %add_rsqrt_fusion.1, f32[256]{0:T(256)S(1)} %broadcast_multiply_fusion.2, f32[768]{0:T(1024)S(1)} %get-tuple-element.14, f32[768]{0:T(1024)S(1)} %get-tuple-element.31, f32[256,768]{1,0:T(8,128)S(1)} %get-tuple-element.28, ...), kind=kOutput, calls=%fused_computation.96 | convolution fusion | flops 1612382208 | bytes 9969664 | tf_op jit(solution)/shard_map/dot_general | solution.py:164
  112.1 4.6 %divide_convert_fusion = bf16[256,16,256]{2,0,1:T(8,128)(2,1)S(1)} fusion(f32[]{:T(128)S(6)} %convert_element_type.176, s32[256]{0:T(256)S(1)} %get-tuple-element.35, s32[256]{0:T(256)S(1)} %get-tuple-element.36, s32[256]{0:T(256)S(1)} %get-tuple-element.34, s32[256]{0:T(256)S(1)} %get-tuple-element.37, bf16[256,16,256]{2,0,1:T(8,128)(2,1)S(1)} %fusion.88, ...), kind=kOutput, calls=%fused_computation.7 | convolution fusion | flops 1634729984 | bytes 10883588 | tf_op jit(solution)/shard_map/dot_general | solution.py:164
  116.7 2.5 %copy.36 = bf16[256,16,256]{2,1,0:T(8,128)(2,1)} copy(bf16[256,16,256]{2,0,1:T(8,128)(2,1)S(1)} %divide_convert_fusion) | data formatting | bytes 4194304 | tf_op jit(solution)/shard_map/convert_element_type | solution.py:181
  119.2 4.2 %copy.37 = bf16[32,256,128]{2,1,0:T(8,128)(2,1)} copy(bf16[32,256,128]{1,2,0:T(8,128)(2,1)} %bitcast.118) | data formatting | bytes 4194304 | tf_op jit(solution)/shard_map/transpose | solution.py:183
  123.4 3.5 %copy.38 = bf16[4,16,8,16,128]{4,3,2,1,0:T(8,128)(2,1)} copy(bf16[4,16,8,16,128]{4,3,1,2,0:T(8,128)(2,1)} %bitcast.119) | data formatting | bytes 4194304 | tf_op jit(solution)/shard_map/transpose | solution.py:184
  (50 shorter events, 1.8 us)
Async XLA Ops:
  0.0 16.6 %copy-start = (bf16[4096,384]{1,0:T(8,128)(2,1)S(1)}, bf16[4096,384]{1,0:T(8,128)(2,1)}, u32[]{:S(2)}) copy-start(bf16[4096,384]{1,0:T(8,128)(2,1)} %param.14) | copy-start | bytes 9437188
  11.6 4.9 %copy-start.3 = (bf16[256,384]{1,0:T(8,128)(2,1)S(1)}, bf16[256,384]{1,0:T(8,128)(2,1)}, u32[]{:S(2)}) copy-start(bf16[256,384]{1,0:T(8,128)(2,1)} %param.15) | copy-start | bytes 589828
  20.4 11.1 %copy-start.2 = (bf16[1,384,768]{2,1,0:T(8,128)(2,1)S(1)}, bf16[1,384,768]{2,1,0:T(8,128)(2,1)}, u32[]{:S(2)}) copy-start(bf16[1,384,768]{2,1,0:T(8,128)(2,1)} %param.20) | copy-start | bytes 1769476
  20.4 15.9 %copy-start.7 = (f32[3,768]{1,0:T(4,128)S(1)}, f32[3,768]{1,0:T(4,128)}, u32[]{:S(2)}) copy-start(f32[3,768]{1,0:T(4,128)} %param.18) | copy-start | bytes 27652
  20.4 15.9 %copy-start.8 = (f32[3,768]{1,0:T(4,128)S(1)}, f32[3,768]{1,0:T(4,128)}, u32[]{:S(2)}) copy-start(f32[3,768]{1,0:T(4,128)} %param.17) | copy-start | bytes 27652
  20.4 13.1 %collective-permute-start.1 = (bf16[256,384]{1,0:T(8,128)(2,1)}, bf16[256,384]{1,0:T(8,128)(2,1)S(1)}, u32[]{:S(2)}, u32[]{:S(2)}) collective-permute-start(bf16[256,384]{1,0:T(8,128)(2,1)} %get-tuple-element.20), channel_id=1, source_target_pairs={{2,0},{4,2},{6,4},{8,6},{10,8},{12,10},{14,12},{16,14},{18,16},{20... | collective-permute-start | bytes 589832 | tf_op jit(solution)/shard_map/ppermute | solution.py:19
  27.8 73.5 %collective-permute-start.8 = (bf16[768,2048]{0,1:T(8,128)(2,1)}, bf16[768,2048]{0,1:T(8,128)(2,1)}, u32[]{:S(2)}, u32[]{:S(2)}) collective-permute-start(bf16[768,2048]{0,1:T(8,128)(2,1)} %copy.33), channel_id=1, source_target_pairs={{0,65},{1,64},{2,67},{3,66},{4,69},{5,68},{6,71},{7,70},{8,73},{9,... | collective-permute-start | bytes 9437192 | tf_op jit(solution)/shard_map/ppermute | solution.py:86
  31.5 6.0 %collective-permute-start = (bf16[256,384]{1,0:T(8,128)(2,1)S(1)}, bf16[256,384]{1,0:T(8,128)(2,1)S(1)}, u32[]{:S(2)}, u32[]{:S(2)}) collective-permute-start(bf16[256,384]{1,0:T(8,128)(2,1)S(1)} %get-tuple-element.19), channel_id=1, source_target_pairs={{0,1},{1,0},{2,3},{3,2},{4,5},{5,4},{6,7},{7,6},{8,9},{9,8},{10,11... | collective-permute-start | bytes 589832 | tf_op jit(solution)/shard_map/ppermute | solution.py:101
  31.5 38.3 %collective-permute-start.4 = (bf16[384,768]{1,0:T(8,128)(2,1)S(1)}, bf16[384,768]{1,0:T(8,128)(2,1)}, u32[]{:S(2)}, u32[]{:S(2)}) collective-permute-start(bf16[384,768]{1,0:T(8,128)(2,1)S(1)} %bitcast.122), channel_id=1, source_target_pairs={{0,1},{1,0},{2,3},{3,2},{4,5},{5,4},{6,7},{7,6},{8,9},{9,8},{10,11... | collective-permute-start | bytes 1769480 | tf_op jit(solution)/shard_map/ppermute | solution.py:87
  34.6 19.8 %collective-permute-start.2 = (bf16[256,384]{1,0:T(8,128)(2,1)S(1)}, bf16[256,384]{1,0:T(8,128)(2,1)S(1)}, u32[]{:S(2)}, u32[]{:S(2)}) collective-permute-start(bf16[256,384]{1,0:T(8,128)(2,1)S(1)} %fusion.118), channel_id=1, source_target_pairs={{0,1},{1,0},{2,3},{3,2},{4,5},{5,4},{6,7},{7,6},{8,9},{9,8},{10,11... | collective-permute-start | bytes 589832 | tf_op jit(solution)/shard_map/ppermute | solution.py:101
  37.6 17.4 %copy-start.4 = (bf16[256,384]{1,0:T(8,128)(2,1)}, bf16[256,384]{1,0:T(8,128)(2,1)S(1)}, u32[]{:S(2)}) copy-start(bf16[256,384]{1,0:T(8,128)(2,1)S(1)} %collective-permute-done) | copy-start | bytes 589828
  37.6 17.5 %copy-start.9 = (bf16[1,3,768,384]{3,2,1,0:T(8,128)(2,1)S(1)}, bf16[1,3,768,384]{3,2,1,0:T(8,128)(2,1)}, u32[]{:S(2)}) copy-start(bf16[1,3,768,384]{3,2,1,0:T(8,128)(2,1)} %param.19) | copy-start | bytes 5308420
  54.4 0.7 copy-start.5
  61.9 18.1 %collective-permute-start.3 = (bf16[256,384]{0,1:T(8,128)(2,1)S(1)}, bf16[256,384]{0,1:T(8,128)(2,1)}, u32[]{:S(2)}, u32[]{:S(2)}) collective-permute-start(bf16[256,384]{0,1:T(8,128)(2,1)S(1)} %bitcast.128), channel_id=1, source_target_pairs={{0,1},{1,0},{2,3},{3,2},{4,5},{5,4},{6,7},{7,6},{8,9},{9,8},{10,11... | collective-permute-start | bytes 589832 | tf_op jit(solution)/shard_map/ppermute | solution.py:138
  67.6 5.5 %copy-start.6 = (bf16[256,384]{1,0:T(8,128)(2,1)S(1)}, bf16[256,384]{1,0:T(8,128)(2,1)}, u32[]{:S(2)}) copy-start(bf16[256,384]{1,0:T(8,128)(2,1)} %copy-done.5) | copy-start | bytes 589828
  67.6 5.5 %collective-permute-start.5 = (bf16[256,384]{0,1:T(8,128)(2,1)S(1)}, bf16[256,384]{0,1:T(8,128)(2,1)S(1)}, u32[]{:S(2)}, u32[]{:S(2)}) collective-permute-start(bf16[256,384]{0,1:T(8,128)(2,1)S(1)} %bitcast.130), channel_id=1, source_target_pairs={{0,1},{1,0},{2,3},{3,2},{4,5},{5,4},{6,7},{7,6},{8,9},{9,8},{10,11... | collective-permute-start | bytes 589832 | tf_op jit(solution)/shard_map/ppermute | solution.py:138
  79.0 8.8 %collective-permute-start.6 = (bf16[256,768]{1,0:T(8,128)(2,1)S(1)}, bf16[256,768]{1,0:T(8,128)(2,1)S(1)}, u32[]{:S(2)}, u32[]{:S(2)}) collective-permute-start(bf16[256,768]{1,0:T(8,128)(2,1)S(1)} %fusion.54), channel_id=1, source_target_pairs={{0,1},{1,0},{2,3},{3,2},{4,5},{5,4},{6,7},{7,6},{8,9},{9,8},{10,11... | collective-permute-start | bytes 1179656 | tf_op jit(solution)/shard_map/ppermute | solution.py:24
  88.5 8.1 %collective-permute-start.7 = (bf16[256,768]{1,0:T(8,128)(2,1)S(1)}, bf16[256,768]{1,0:T(8,128)(2,1)S(1)}, u32[]{:S(2)}, u32[]{:S(2)}) collective-permute-start(bf16[256,768]{1,0:T(8,128)(2,1)S(1)} %fusion.10), channel_id=1, source_target_pairs={{0,1},{1,0},{2,3},{3,2},{4,5},{5,4},{6,7},{7,6},{8,9},{9,8},{10,11... | collective-permute-start | bytes 1179656 | tf_op jit(solution)/shard_map/ppermute | solution.py:24
  89.3 22.8 %collective-permute-start.9 = (bf16[256,768]{1,0:T(8,128)(2,1)S(1)}, bf16[256,768]{1,0:T(8,128)(2,1)S(1)}, u32[]{:S(2)}, u32[]{:S(2)}) collective-permute-start(bf16[256,768]{1,0:T(8,128)(2,1)S(1)} %add_convert_fusion.3), channel_id=1, source_target_pairs={{0,2},{2,4},{4,6},{6,8},{8,10},{10,12},{12,14},{14,16},{16,18},{18... | collective-permute-start | bytes 1179656 | tf_op jit(solution)/shard_map/ppermute | solution.py:19
  119.2 7.8 %copy-start.1 = (bf16[4096,384]{1,0:T(8,128)(2,1)S(1)}, bf16[4096,384]{1,0:T(8,128)(2,1)}, u32[]{:S(2)}) copy-start(bf16[4096,384]{1,0:T(8,128)(2,1)} %param.14) | copy-start | bytes 9437188

commit v18 on v13

--- a/solution.py
+++ b/solution.py
@@ -83,7 +83,8 @@
     tile_count = lax.axis_size("tile")
     devices = 2 * tile_count
     across = [(index, index ^ (tile_count + 1)) for index in range(devices)]
-    other_w_decode = lax.ppermute(w_decode, ("tile", "head"), across)
+    own_cells_first = w_decode.T
+    other_cells_first = lax.ppermute(own_cells_first, ("tile", "head"), across)
     other_w_out = lax.ppermute(w_out[0], "head", [(0, 1), (1, 0)])
     local_width = embed_voxel.shape[1]
     embed_by_depth = embed_voxel.reshape(PATCH * PATCH, PATCH, local_width).transpose(1, 0, 2)
@@ -112,15 +113,15 @@
     ).astype(jnp.bfloat16)
     keys = projected[1].reshape(tokens, local_heads, HEAD_DIM)
     values = projected[2].reshape(tokens, local_heads, HEAD_DIM)
-    whole_w_decode = jnp.where(
+    cells_first = jnp.where(
         head_index == 0,
-        jnp.concatenate([w_decode, other_w_decode], 1),
-        jnp.concatenate([other_w_decode, w_decode], 1),
+        jnp.concatenate([own_cells_first, other_cells_first], 0),
+        jnp.concatenate([other_cells_first, own_cells_first], 0),
     )
     inner_rows = PATCH
     cell_cols = inner_rows * PATCH
     decode_by_depth = (
-        whole_w_decode.T.reshape(inner_rows, PATCH, PATCH, -1)
+        cells_first.reshape(inner_rows, PATCH, PATCH, -1)
         .transpose(2, 0, 1, 3)
         .reshape(PATCH, cell_cols, -1)
     )

time: 124 us -> 124 us (level)
  no operation moved by 1% of the time
where the time goes in v18:
time: 124 us; the launch traced here: 123 us
  matrix products  33.8 us (27%)
  waiting for transfers between devices  30.2 us (24%)
  local copies, waits for them, and re-layouts  26.3 us (21%)
  starting transfers between devices  18 us (15%)
  other arithmetic  14.5 us (12%)
    ppermute x2, waiting for transfers between devices, body(): other_columns = lax.ppermute(embedded, 'head', [(0, 1), (1, 0)])  17.9 us
    dot_general x2, matrix products, body(): jnp.dot(hidden, w_down[0], preferred_element_type=jnp.float32)  8.06 us
    ppermute x2, starting transfers between devices, from_behind(): return lax.ppermute(block, axis, route)  7.5 us
    dot_general x2, matrix products, body(): lax.dot_general(latent, decode_by_depth, (((1,), (2,)), ((), ())), prefer...  5.78 us
    select_n x1, other arithmetic, body(): jnp.where(head_index == 0, jnp.concatenate([own_cells_first, other_cells_...  5.77 us
    sub x2, matrix products, body(): weights = jax.nn.softmax(scores, axis=-1).astype(jnp.bfloat16)  5.6 us
    dot_general x2, matrix products, body(): jnp.einsum('hts,shd->thd', weights, values, preferred_element_type=jnp.fl...  5.11 us
    reshape x1, local copies, waits for them, and re-layouts, embed_planes(): voxels = jnp.swapaxes(grouped, 1, 2).reshape(rows, PATCH, PATCH * PATCH)  4.86 us
  transfers between devices with their start and end apart: 10, of which 7 were waited for; matrix products, arithmetic and copies ran while one was open for 33% of the time, Pallas kernels for 0%

profile of v18, /device:TPU:31, one launch (start us, length us, event | category | flops | bytes accessed | tf_op | source)
XLA Modules:
  0.0 123.0 jit_solution(9133045898663709457)
XLA Ops:
  0.0 2.1 %convert_element_type.136 = f32[512,384]{1,0:T(8,128)} convert(bf16[512,384]{1,0:T(8,128)(2,1)} %param.16) | non-fusion elementwise | flops 196608 | bytes 1179648 | tf_op jit(solution)/shard_map/convert_element_type | solution.py:91
  2.1 0.8 convert_element_type.135
  3.2 2.5 %broadcast_multiply_fusion = bf16[64,128,128]{2,1,0:T(8,128)(2,1)S(1)} fusion(bf16[64,128,128]{2,1,0:T(8,128)(2,1)} %param.12, bf16[64,128]{1,0:T(8,128)(2,1)S(1)} %convert_element_type.135), kind=kLoop, calls=%fused_computation.70 | loop fusion | flops 1048576 | bytes 4210688 | tf_op jit(solution)/shard_map/mul | solution.py:43
  5.7 1.9 %copy.26 = bf16[4,8,16,16,128]{4,3,2,1,0:T(8,128)(2,1)} copy(bf16[4,8,16,16,128]{4,3,1,2,0:T(8,128)(2,1)S(1)} %bitcast.112) | data formatting | bytes 4194304 | tf_op jit(solution)/shard_map/transpose | solution.py:44
  7.5 4.1 %copy.27 = bf16[32,128,256]{2,1,0:T(8,128)(2,1)} copy(bf16[32,128,256]{1,2,0:T(8,128)(2,1)} %bitcast.113) | data formatting | bytes 4194304 | tf_op jit(solution)/shard_map/transpose | solution.py:46
  11.6 4.9 %copy.28 = bf16[256,16,256]{0,1,2:T(8,128)(2,1)} copy(bf16[256,16,256]{2,1,0:T(8,128)(2,1)} %bitcast.114) | data formatting | bytes 4194304 | tf_op jit(solution)/shard_map/reshape | solution.py:46
  16.7 3.7 %fusion.93 = (bf16[256,384]{1,0:T(8,128)(2,1)S(1)}, bf16[256,384]{1,0:T(8,128)(2,1)}) fusion(f32[512,384]{1,0:T(8,128)} %convert_element_type.136, f32[32,384]{1,0:T(8,128)S(1)} %fusion.144, bf16[256,16,256]{0,1,2:T(8,128)(2,1)} %copy.28, bf16[16,256,384]{2,0,1:T(8,128)(2,1)S(1)} %bitcast.111), kind=kOutput, calls=%fused_computation.97 | convolution fusion | flops 805797888 | bytes 6471680 | tf_op jit(solution)/shard_map/dot_general | solution.py:47
  20.4 2.7 %collective-permute-start.1 = (bf16[256,384]{1,0:T(8,128)(2,1)}, bf16[256,384]{1,0:T(8,128)(2,1)S(1)}, u32[]{:S(2)}, u32[]{:S(2)}) collective-permute-start(bf16[256,384]{1,0:T(8,128)(2,1)} %get-tuple-element.20), channel_id=1, source_target_pairs={{2,0},{4,2},{6,4},{8,6},{10,8},{12,10},{14,12},{16,14},{18,16},{20... | collective-permute-start | bytes 589832 | tf_op jit(solution)/shard_map/ppermute | solution.py:19
  23.1 4.6 %copy.31 = bf16[768,2048]{0,1:T(8,128)(2,1)} copy(bf16[768,2048]{1,0:T(8,128)(2,1)} %param.23) | data formatting | bytes 6291456 | tf_op args[11]
  27.8 3.8 %collective-permute-start.8 = (bf16[2048,768]{1,0:T(8,128)(2,1)}, bf16[2048,768]{1,0:T(8,128)(2,1)}, u32[]{:S(2)}, u32[]{:S(2)}) collective-permute-start(bf16[2048,768]{1,0:T(8,128)(2,1)} %bitcast.27), channel_id=1, source_target_pairs={{0,65},{1,64},{2,67},{3,66},{4,69},{5,68},{6,71},{7,70},{8,73},{9,... | collective-permute-start | bytes 9437192 | tf_op jit(solution)/shard_map/ppermute | solution.py:87
  31.5 1.5 %collective-permute-start.4 = (bf16[384,768]{1,0:T(8,128)(2,1)S(1)}, bf16[384,768]{1,0:T(8,128)(2,1)}, u32[]{:S(2)}, u32[]{:S(2)}) collective-permute-start(bf16[384,768]{1,0:T(8,128)(2,1)S(1)} %bitcast.119), channel_id=1, source_target_pairs={{0,1},{1,0},{2,3},{3,2},{4,5},{5,4},{6,7},{7,6},{8,9},{9,8},{10,11... | collective-permute-start | bytes 1769480 | tf_op jit(solution)/shard_map/ppermute | solution.py:88
  33.0 0.5 collective-permute-done.1
  33.5 1.0 fusion.121
  34.6 1.7 %collective-permute-start.2 = (bf16[256,384]{1,0:T(8,128)(2,1)S(1)}, bf16[256,384]{1,0:T(8,128)(2,1)S(1)}, u32[]{:S(2)}, u32[]{:S(2)}) collective-permute-start(bf16[256,384]{1,0:T(8,128)(2,1)S(1)} %fusion.121), channel_id=1, source_target_pairs={{0,1},{1,0},{2,3},{3,2},{4,5},{5,4},{6,7},{7,6},{8,9},{9,8},{10,11... | collective-permute-start | bytes 589832 | tf_op jit(solution)/shard_map/ppermute | solution.py:102
  36.4 1.2 collective-permute-done
  37.6 16.8 %collective-permute-done.2 = bf16[256,384]{1,0:T(8,128)(2,1)S(1)} collective-permute-done((bf16[256,384]{1,0:T(8,128)(2,1)S(1)}, bf16[256,384]{1,0:T(8,128)(2,1)S(1)}, u32[]{:S(2)}, u32[]{:S(2)}) %collective-permute-start.2) | collective-permute-done | bytes 196640 | tf_op jit(solution)/shard_map/ppermute | solution.py:102
  54.7 0.3 multiply_reduce_fusion.2
  55.1 1.3 %fusion.55 = bf16[3,512,384]{1,2,0:T(8,128)(2,1)S(1)} fusion(bf16[1,3,768,384]{3,2,1,0:T(8,128)(2,1)S(1)} %copy-done.9, f32[256,768]{1,0:T(8,128)S(1)} %fusion.95, f32[256,768]{1,0:T(8,128)S(1)} %fusion.94, f32[768]{0:T(1024)S(1)} %get-tuple-element.13, f32[768]{0:T(1024)S(1)} %get-tuple-element.30, f32[512]{0:T(512)S(1)} %add_rsqrt_fusion, ...), kind=kOutput, calls=%fused_computation.52 | convolution fusion | flops 908918784 | bytes 4532224 | tf_op jit(solution)/shard_map/td,sde->ste/dot_general | solution.py:111
  56.5 2.8 %fusion.140 = (f32[6,256]{1,0:T(8,128)S(1)}, f32[6,256,512]{2,1,0:T(8,128)}) fusion(bf16[256,6,64]{0,2,1:T(8,128)(2,1)S(1)} %bitcast.130, bf16[512,6,64]{0,2,1:T(8,128)(2,1)S(1)} %bitcast.123), kind=kOutput, calls=%fused_computation.164 | convolution fusion | flops 103023104 | bytes 3741696 | tf_op jit(solution)/shard_map/sub | solution.py:134
  59.3 2.6 %fusion.71 = bf16[6,64,256]{2,1,0:T(8,128)(2,1)S(1)} fusion(bf16[512,6,64]{0,2,1:T(8,128)(2,1)S(1)} %bitcast.121, f32[6,256,512]{2,1,0:T(8,128)} %get-tuple-element.22, f32[6,256]{1,0:T(8,128)S(1)} %get-tuple-element.21), kind=kOutput, calls=%fused_computation.69 | convolution fusion | flops 102334464 | bytes 3741696 | tf_op jit(solution)/shard_map/hts,shd->thd/dot_general | solution.py:135
  61.9 0.4 collective-permute-start.3
  62.2 2.8 %fusion.141 = (f32[6,256]{1,0:T(8,128)S(1)}, f32[6,256,512]{2,1,0:T(8,128)}) fusion(bf16[256,6,64]{0,2,1:T(8,128)(2,1)S(1)} %bitcast.129, bf16[512,6,64]{0,2,1:T(8,128)(2,1)S(1)} %bitcast.124), kind=kOutput, calls=%fused_computation.165 | convolution fusion | flops 103023104 | bytes 3741696 | tf_op jit(solution)/shard_map/sub | solution.py:134
  65.0 2.6 %fusion.70 = bf16[6,64,256]{2,1,0:T(8,128)(2,1)S(1)} fusion(bf16[512,6,64]{0,2,1:T(8,128)(2,1)S(1)} %bitcast.122, f32[6,256,512]{2,1,0:T(8,128)} %get-tuple-element.24, f32[6,256]{1,0:T(8,128)S(1)} %get-tuple-element.23), kind=kOutput, calls=%fused_computation.68 | convolution fusion | flops 102334464 | bytes 3741696 | tf_op jit(solution)/shard_map/hts,shd->thd/dot_general | solution.py:135
  67.6 1.4 %collective-permute-start.5 = (bf16[256,384]{0,1:T(8,128)(2,1)S(1)}, bf16[256,384]{0,1:T(8,128)(2,1)S(1)}, u32[]{:S(2)}, u32[]{:S(2)}) collective-permute-start(bf16[256,384]{0,1:T(8,128)(2,1)S(1)} %bitcast.127), channel_id=1, source_target_pairs={{0,1},{1,0},{2,3},{3,2},{4,5},{5,4},{6,7},{7,6},{8,9},{9,8},{10,11... | collective-permute-start | bytes 589832 | tf_op jit(solution)/shard_map/ppermute | solution.py:139
  69.0 0.4 fusion.68
  69.4 0.4 fusion.64
  69.8 3.3 %collective-permute-done.5 = bf16[256,384]{0,1:T(8,128)(2,1)S(1)} collective-permute-done((bf16[256,384]{0,1:T(8,128)(2,1)S(1)}, bf16[256,384]{0,1:T(8,128)(2,1)S(1)}, u32[]{:S(2)}, u32[]{:S(2)}) %collective-permute-start.5) | collective-permute-done | bytes 196640 | tf_op jit(solution)/shard_map/ppermute | solution.py:139
  73.1 1.5 %fusion.142 = (f32[256]{0:T(256)S(1)}, f32[256,768]{1,0:T(8,128)S(1)}) fusion(f32[256,768]{1,0:T(8,128)S(1)} %fusion.64, bf16[256,384]{0,1:T(8,128)(2,1)S(1)} %collective-permute-done.5, bf16[384,768]{1,0:T(8,128)(2,1)} %collective-permute-done.4, bf16[256,384]{1,0:T(8,128)(2,1)S(1)} %fusion.121, bf16[256,384]{1,0:T(8,128)(2,1)S(1)} %copy-done.6, pred[]{:T(512)S(6)} %eq.8), kind=kOutput, calls=%fused_computation.166 | convolution fusion | flops 153943808 | bytes 2753537 | tf_op jit(solution)/shard_map/dot_general | solution.py:141
  74.7 0.2 multiply_reduce_fusion.6
  74.9 4.0 %fusion.58 = bf16[256,768]{1,0:T(8,128)(2,1)S(1)} fusion(bf16[1,1536,768]{2,1,0:T(8,128)(2,1)} %param.22, bf16[1,768,1536]{2,1,0:T(8,128)(2,1)} %param.21, f32[256,768]{1,0:T(8,128)S(1)} %get-tuple-element.26, f32[768]{0:T(1024)S(1)} %get-tuple-element.12, f32[768]{0:T(1024)S(1)} %get-tuple-element.31, f32[256]{0:T(256)S(1)} %add_rsqrt_fusion.4, ...), kind=kOutput, calls=%fused_computation.53 | convolution fusion | flops 1212678144 | bytes 5906432 | tf_op jit(solution)/shard_map/dot_general | solution.py:150
  79.0 1.0 collective-permute-start.6
  80.0 1.7 %fusion.143 = (f32[256]{0:T(256)S(1)}, f32[256,768]{1,0:T(8,128)S(1)}) fusion(f32[256,768]{1,0:T(8,128)S(1)} %fusion.68, bf16[256,384]{0,1:T(8,128)(2,1)} %collective-permute-done.3, bf16[384,768]{1,0:T(8,128)(2,1)} %collective-permute-done.4, bf16[256,384]{1,0:T(8,128)(2,1)S(1)} %get-tuple-element.19, bf16[256,384]{1,0:T(8,128)(2,1)} %copy-done.4, pred[]{:T(512)S(6)} %eq.8), kind=kOutput, calls=%fused_computation.167 | convolution fusion | flops 153943808 | bytes 2753537 | tf_op jit(solution)/shard_map/dot_general | solution.py:141
  81.7 0.2 multiply_reduce_fusion.4
  81.9 4.0 %fusion.12 = bf16[256,768]{1,0:T(8,128)(2,1)S(1)} fusion(bf16[1,1536,768]{2,1,0:T(8,128)(2,1)} %param.22, bf16[1,768,1536]{2,1,0:T(8,128)(2,1)} %param.21, f32[256,768]{1,0:T(8,128)S(1)} %get-tuple-element.28, f32[256]{0:T(256)S(1)} %add_rsqrt_fusion.2, f32[256]{0:T(256)S(1)} %broadcast_multiply_fusion.3, f32[768]{0:T(1024)S(1)} %get-tuple-element.12, ...), kind=kOutput, calls=%fused_computation.18 | convolution fusion | flops 1212481536 | bytes 5906432 | tf_op jit(solution)/shard_map/dot_general | solution.py:150
  86.0 1.8 %collective-permute-done.6 = bf16[256,768]{1,0:T(8,128)(2,1)S(1)} collective-permute-done((bf16[256,768]{1,0:T(8,128)(2,1)S(1)}, bf16[256,768]{1,0:T(8,128)(2,1)S(1)}, u32[]{:S(2)}, u32[]{:S(2)}) %collective-permute-start.6) | collective-permute-done | bytes 393248 | tf_op jit(solution)/shard_map/ppermute | solution.py:24
  88.0 0.3 multiply_reduce_fusion.5
  88.3 0.2 add_convert_fusion.3
  88.5 0.7 collective-permute-start.7
  89.3 4.8 %collective-permute-start.9 = (bf16[256,768]{1,0:T(8,128)(2,1)S(1)}, bf16[256,768]{1,0:T(8,128)(2,1)S(1)}, u32[]{:S(2)}, u32[]{:S(2)}) collective-permute-start(bf16[256,768]{1,0:T(8,128)(2,1)S(1)} %add_convert_fusion.3), channel_id=1, source_target_pairs={{0,2},{2,4},{4,6},{6,8},{8,10},{10,12},{12,14},{14,16},{16,18},{18... | collective-permute-start | bytes 1179656 | tf_op jit(solution)/shard_map/ppermute | solution.py:19
  94.1 2.5 %collective-permute-done.7 = bf16[256,768]{1,0:T(8,128)(2,1)S(1)} collective-permute-done((bf16[256,768]{1,0:T(8,128)(2,1)S(1)}, bf16[256,768]{1,0:T(8,128)(2,1)S(1)}, u32[]{:S(2)}, u32[]{:S(2)}) %collective-permute-start.7) | collective-permute-done | bytes 393248 | tf_op jit(solution)/shard_map/ppermute | solution.py:24
  96.8 0.3 multiply_reduce_fusion.3
  97.1 4.1 %collective-permute-done.8 = bf16[2048,768]{1,0:T(8,128)(2,1)} collective-permute-done((bf16[2048,768]{1,0:T(8,128)(2,1)}, bf16[2048,768]{1,0:T(8,128)(2,1)}, u32[]{:S(2)}, u32[]{:S(2)}) %collective-permute-start.8) | collective-permute-done | bytes 3145760 | tf_op jit(solution)/shard_map/ppermute | solution.py:87
  101.2 5.8 %maximum_select_fusion = bf16[4096,768]{1,0:T(8,128)(2,1)S(1)} fusion(bf16[2048,768]{1,0:T(8,128)(2,1)} %collective-permute-done.8, bf16[2048,768]{1,0:T(8,128)(2,1)} %bitcast.27, pred[]{:T(512)S(6)} %eq.8), kind=kLoop, calls=%fused_computation.2 | loop fusion | flops 28311552 | bytes 12582913 | tf_op jit(solution)/shard_map/jit(_where)/select_n | solution.py:116
  107.0 2.5 %fusion.4 = bf16[256,16,256]{2,0,1:T(8,128)(2,1)S(1)} fusion(bf16[16,256,768]{2,0,1:T(8,128)(2,1)S(1)} %bitcast.117, f32[256]{0:T(256)S(1)} %add_rsqrt_fusion.1, f32[256]{0:T(256)S(1)} %broadcast_multiply_fusion.2, f32[768]{0:T(1024)S(1)} %get-tuple-element.14, f32[768]{0:T(1024)S(1)} %get-tuple-element.29, f32[256,768]{1,0:T(8,128)S(1)} %get-tuple-element.28, ...), kind=kOutput, calls=%fused_computation.5 | convolution fusion | flops 1612382208 | bytes 9969664 | tf_op jit(solution)/shard_map/dot_general | solution.py:165
  109.5 3.2 %divide_convert_fusion = bf16[256,16,256]{2,0,1:T(8,128)(2,1)S(1)} fusion(f32[]{:T(128)S(6)} %convert_element_type.176, s32[256]{0:T(256)S(1)} %get-tuple-element.33, s32[256]{0:T(256)S(1)} %get-tuple-element.36, s32[256]{0:T(256)S(1)} %get-tuple-element.32, s32[256]{0:T(256)S(1)} %get-tuple-element.37, bf16[256,16,256]{2,0,1:T(8,128)(2,1)S(1)} %fusion.4, ...), kind=kOutput, calls=%fused_computation.7 | convolution fusion | flops 1634729984 | bytes 10883588 | tf_op jit(solution)/shard_map/dot_general | solution.py:165
  112.8 2.5 %copy.34 = bf16[256,16,256]{2,1,0:T(8,128)(2,1)} copy(bf16[256,16,256]{2,0,1:T(8,128)(2,1)S(1)} %divide_convert_fusion) | data formatting | bytes 4194304 | tf_op jit(solution)/shard_map/convert_element_type | solution.py:182
  115.3 4.2 %copy.35 = bf16[32,256,128]{2,1,0:T(8,128)(2,1)} copy(bf16[32,256,128]{1,2,0:T(8,128)(2,1)} %bitcast.115) | data formatting | bytes 4194304 | tf_op jit(solution)/shard_map/transpose | solution.py:184
  119.5 3.5 %copy.36 = bf16[4,16,8,16,128]{4,3,2,1,0:T(8,128)(2,1)} copy(bf16[4,16,8,16,128]{4,3,1,2,0:T(8,128)(2,1)} %bitcast.116) | data formatting | bytes 4194304 | tf_op jit(solution)/shard_map/transpose | solution.py:185
  (49 shorter events, 1.6 us)
Async XLA Ops:
  0.0 16.6 %copy-start = (bf16[4096,384]{1,0:T(8,128)(2,1)S(1)}, bf16[4096,384]{1,0:T(8,128)(2,1)}, u32[]{:S(2)}) copy-start(bf16[4096,384]{1,0:T(8,128)(2,1)} %param.14) | copy-start | bytes 9437188
  11.6 4.9 %copy-start.3 = (bf16[256,384]{1,0:T(8,128)(2,1)S(1)}, bf16[256,384]{1,0:T(8,128)(2,1)}, u32[]{:S(2)}) copy-start(bf16[256,384]{1,0:T(8,128)(2,1)} %param.15) | copy-start | bytes 589828
  20.4 11.1 %copy-start.2 = (bf16[1,384,768]{2,1,0:T(8,128)(2,1)S(1)}, bf16[1,384,768]{2,1,0:T(8,128)(2,1)}, u32[]{:S(2)}) copy-start(bf16[1,384,768]{2,1,0:T(8,128)(2,1)} %param.20) | copy-start | bytes 1769476
  20.4 15.9 %copy-start.7 = (f32[3,768]{1,0:T(4,128)S(1)}, f32[3,768]{1,0:T(4,128)}, u32[]{:S(2)}) copy-start(f32[3,768]{1,0:T(4,128)} %param.18) | copy-start | bytes 27652
  20.4 15.9 %copy-start.8 = (f32[3,768]{1,0:T(4,128)S(1)}, f32[3,768]{1,0:T(4,128)}, u32[]{:S(2)}) copy-start(f32[3,768]{1,0:T(4,128)} %param.17) | copy-start | bytes 27652
  20.4 13.1 %collective-permute-start.1 = (bf16[256,384]{1,0:T(8,128)(2,1)}, bf16[256,384]{1,0:T(8,128)(2,1)S(1)}, u32[]{:S(2)}, u32[]{:S(2)}) collective-permute-start(bf16[256,384]{1,0:T(8,128)(2,1)} %get-tuple-element.20), channel_id=1, source_target_pairs={{2,0},{4,2},{6,4},{8,6},{10,8},{12,10},{14,12},{16,14},{18,16},{20... | collective-permute-start | bytes 589832 | tf_op jit(solution)/shard_map/ppermute | solution.py:19
  27.8 73.5 %collective-permute-start.8 = (bf16[2048,768]{1,0:T(8,128)(2,1)}, bf16[2048,768]{1,0:T(8,128)(2,1)}, u32[]{:S(2)}, u32[]{:S(2)}) collective-permute-start(bf16[2048,768]{1,0:T(8,128)(2,1)} %bitcast.27), channel_id=1, source_target_pairs={{0,65},{1,64},{2,67},{3,66},{4,69},{5,68},{6,71},{7,70},{8,73},{9,... | collective-permute-start | bytes 9437192 | tf_op jit(solution)/shard_map/ppermute | solution.py:87
  31.5 6.0 %collective-permute-start = (bf16[256,384]{1,0:T(8,128)(2,1)S(1)}, bf16[256,384]{1,0:T(8,128)(2,1)S(1)}, u32[]{:S(2)}, u32[]{:S(2)}) collective-permute-start(bf16[256,384]{1,0:T(8,128)(2,1)S(1)} %get-tuple-element.19), channel_id=1, source_target_pairs={{0,1},{1,0},{2,3},{3,2},{4,5},{5,4},{6,7},{7,6},{8,9},{9,8},{10,11... | collective-permute-start | bytes 589832 | tf_op jit(solution)/shard_map/ppermute | solution.py:102
  31.5 38.3 %collective-permute-start.4 = (bf16[384,768]{1,0:T(8,128)(2,1)S(1)}, bf16[384,768]{1,0:T(8,128)(2,1)}, u32[]{:S(2)}, u32[]{:S(2)}) collective-permute-start(bf16[384,768]{1,0:T(8,128)(2,1)S(1)} %bitcast.119), channel_id=1, source_target_pairs={{0,1},{1,0},{2,3},{3,2},{4,5},{5,4},{6,7},{7,6},{8,9},{9,8},{10,11... | collective-permute-start | bytes 1769480 | tf_op jit(solution)/shard_map/ppermute | solution.py:88
  34.6 19.8 %collective-permute-start.2 = (bf16[256,384]{1,0:T(8,128)(2,1)S(1)}, bf16[256,384]{1,0:T(8,128)(2,1)S(1)}, u32[]{:S(2)}, u32[]{:S(2)}) collective-permute-start(bf16[256,384]{1,0:T(8,128)(2,1)S(1)} %fusion.121), channel_id=1, source_target_pairs={{0,1},{1,0},{2,3},{3,2},{4,5},{5,4},{6,7},{7,6},{8,9},{9,8},{10,11... | collective-permute-start | bytes 589832 | tf_op jit(solution)/shard_map/ppermute | solution.py:102
  37.6 17.4 %copy-start.4 = (bf16[256,384]{1,0:T(8,128)(2,1)}, bf16[256,384]{1,0:T(8,128)(2,1)S(1)}, u32[]{:S(2)}) copy-start(bf16[256,384]{1,0:T(8,128)(2,1)S(1)} %collective-permute-done) | copy-start | bytes 589828
  37.6 17.5 %copy-start.9 = (bf16[1,3,768,384]{3,2,1,0:T(8,128)(2,1)S(1)}, bf16[1,3,768,384]{3,2,1,0:T(8,128)(2,1)}, u32[]{:S(2)}) copy-start(bf16[1,3,768,384]{3,2,1,0:T(8,128)(2,1)} %param.19) | copy-start | bytes 5308420
  54.4 0.7 copy-start.5
  61.9 18.1 %collective-permute-start.3 = (bf16[256,384]{0,1:T(8,128)(2,1)S(1)}, bf16[256,384]{0,1:T(8,128)(2,1)}, u32[]{:S(2)}, u32[]{:S(2)}) collective-permute-start(bf16[256,384]{0,1:T(8,128)(2,1)S(1)} %bitcast.125), channel_id=1, source_target_pairs={{0,1},{1,0},{2,3},{3,2},{4,5},{5,4},{6,7},{7,6},{8,9},{9,8},{10,11... | collective-permute-start | bytes 589832 | tf_op jit(solution)/shard_map/ppermute | solution.py:139
  67.6 5.5 %copy-start.6 = (bf16[256,384]{1,0:T(8,128)(2,1)S(1)}, bf16[256,384]{1,0:T(8,128)(2,1)}, u32[]{:S(2)}) copy-start(bf16[256,384]{1,0:T(8,128)(2,1)} %copy-done.5) | copy-start | bytes 589828
  67.6 5.5 %collective-permute-start.5 = (bf16[256,384]{0,1:T(8,128)(2,1)S(1)}, bf16[256,384]{0,1:T(8,128)(2,1)S(1)}, u32[]{:S(2)}, u32[]{:S(2)}) collective-permute-start(bf16[256,384]{0,1:T(8,128)(2,1)S(1)} %bitcast.127), channel_id=1, source_target_pairs={{0,1},{1,0},{2,3},{3,2},{4,5},{5,4},{6,7},{7,6},{8,9},{9,8},{10,11... | collective-permute-start | bytes 589832 | tf_op jit(solution)/shard_map/ppermute | solution.py:139
  79.0 8.8 %collective-permute-start.6 = (bf16[256,768]{1,0:T(8,128)(2,1)S(1)}, bf16[256,768]{1,0:T(8,128)(2,1)S(1)}, u32[]{:S(2)}, u32[]{:S(2)}) collective-permute-start(bf16[256,768]{1,0:T(8,128)(2,1)S(1)} %fusion.58), channel_id=1, source_target_pairs={{0,1},{1,0},{2,3},{3,2},{4,5},{5,4},{6,7},{7,6},{8,9},{9,8},{10,11... | collective-permute-start | bytes 1179656 | tf_op jit(solution)/shard_map/ppermute | solution.py:24
  88.5 8.1 %collective-permute-start.7 = (bf16[256,768]{1,0:T(8,128)(2,1)S(1)}, bf16[256,768]{1,0:T(8,128)(2,1)S(1)}, u32[]{:S(2)}, u32[]{:S(2)}) collective-permute-start(bf16[256,768]{1,0:T(8,128)(2,1)S(1)} %fusion.12), channel_id=1, source_target_pairs={{0,1},{1,0},{2,3},{3,2},{4,5},{5,4},{6,7},{7,6},{8,9},{9,8},{10,11... | collective-permute-start | bytes 1179656 | tf_op jit(solution)/shard_map/ppermute | solution.py:24
  89.3 20.3 %collective-permute-start.9 = (bf16[256,768]{1,0:T(8,128)(2,1)S(1)}, bf16[256,768]{1,0:T(8,128)(2,1)S(1)}, u32[]{:S(2)}, u32[]{:S(2)}) collective-permute-start(bf16[256,768]{1,0:T(8,128)(2,1)S(1)} %add_convert_fusion.3), channel_id=1, source_target_pairs={{0,2},{2,4},{4,6},{6,8},{8,10},{10,12},{12,14},{14,16},{16,18},{18... | collective-permute-start | bytes 1179656 | tf_op jit(solution)/shard_map/ppermute | solution.py:19
  115.3 7.8 %copy-start.1 = (bf16[4096,384]{1,0:T(8,128)(2,1)S(1)}, bf16[4096,384]{1,0:T(8,128)(2,1)}, u32[]{:S(2)}) copy-start(bf16[4096,384]{1,0:T(8,128)(2,1)} %param.14) | copy-start | bytes 9437188

commit v19 on v18

--- a/solution.py
+++ b/solution.py
@@ -113,11 +113,7 @@
     ).astype(jnp.bfloat16)
     keys = projected[1].reshape(tokens, local_heads, HEAD_DIM)
     values = projected[2].reshape(tokens, local_heads, HEAD_DIM)
-    cells_first = jnp.where(
-        head_index == 0,
-        jnp.concatenate([own_cells_first, other_cells_first], 0),
-        jnp.concatenate([other_cells_first, own_cells_first], 0),
-    )
+    cells_first = jnp.concatenate([own_cells_first, other_cells_first], 0)
     inner_rows = PATCH
     cell_cols = inner_rows * PATCH
     decode_by_depth = (
@@ -170,7 +166,11 @@
     ]
     shape = lower_piece.shape
     token_a = lax.broadcasted_iota(jnp.int32, shape, 0) // (side * side)
-    inner = lax.broadcasted_iota(jnp.int32, shape, 2) // PATCH
+    columns = lax.broadcasted_iota(jnp.int32, shape, 2)
+    half_rows = PATCH // 2
+    block = columns // (half_rows * PATCH)
+    true_block = block + head_index - 2 * block * head_index
+    inner = true_block * half_rows + (columns // PATCH) % half_rows
     places = (token_a * PATCH + inner).astype(jnp.float32)
     lower_profile = profile_of(places)
     upper_profile = profile_of(places + HALF)
@@ -181,7 +181,9 @@
     denominator = lower_profile + later * upper_profile
     blended = (numerator / denominator).astype(jnp.bfloat16)
     arranged = blended.reshape(half_side * side, WIN, cell_cols)
-    arranged = jnp.swapaxes(arranged, 1, 2).reshape(half_side, side, PATCH, PATCH, WIN)
+    arranged = jnp.swapaxes(arranged, 1, 2).reshape(half_side, side, 2, PATCH // 2, PATCH, WIN)
+    arranged = jnp.where(head_index == 0, arranged, arranged[:, :, ::-1])
+    arranged = arranged.reshape(half_side, side, PATCH, PATCH, WIN)
     return arranged.transpose(0, 2, 1, 3, 4).reshape(HALF, WIN, WIN)
 
 

time: 124 us -> 124 us (level)
  matrix products: 33.8 us -> 36 us
  local copies, waits for them, and re-layouts: 26.3 us -> 24.2 us
  waiting for transfers between devices: 30.2 us -> 28.2 us
    concatenate x0 -> x1, other arithmetic: none -> 3.25 us  [body(): cells_first = jnp.concatenate([own_cells_first, other_cells_first], 0)]
    select_n x1, other arithmetic: 5.77 us -> 3.14 us  [body(): arranged = jnp.where(head_index == 0, arranged, arranged[:, :, ::-1])]
    transpose x1, local copies, waits for them, and re-layouts: 3.5 us -> 1.91 us  [body(): return arranged.transpose(0, 2, 1, 3, 4).reshape(HALF, WIN, WIN)]
    ppermute x1, waiting for transfers between devices: 4.14 us -> 2.69 us  [body(): other_cells_first = lax.ppermute(own_cells_first, ('tile', 'head'), across)]
    dot_general x1, matrix products: 1.31 us -> 2.75 us  [body(): jnp.einsum('td,sde->ste', normed, w_qkv[0], preferred_element_type=jnp.fl...]
    convert_element_type x1, local copies, waits for them, and re-layouts: 2.5 us -> 1.2 us  [body(): blended = (numerator / denominator).astype(jnp.bfloat16)]
    transpose x1 -> x2, local copies, waits for them, and re-layouts: 4.25 us -> 4.98 us  [the longest x1 2.86 us: body(): jnp.swapaxes(arranged, 1, 2)]
    unnamed x21 -> x23, local copies, waits for them, and re-layouts: 4.81 us -> 4.82 us
  transfers between devices with their start and end apart: 10 -> 10, of which waited for: 7 -> 7; matrix products, arithmetic and copies ran while one was open for 33% -> 34% of each run, Pallas kernels for 0% -> 0%
where the time goes in v19:
time: 124 us; the launch traced here: 122 us
  matrix products  36 us (29%)
  waiting for transfers between devices  28.2 us (23%)
  local copies, waits for them, and re-layouts  24.2 us (20%)
  starting transfers between devices  18 us (15%)
  other arithmetic  15.6 us (13%)
    ppermute x2, waiting for transfers between devices, body(): other_columns = lax.ppermute(embedded, 'head', [(0, 1), (1, 0)])  17.5 us
    dot_general x2, matrix products, body(): jnp.dot(hidden, w_down[0], preferred_element_type=jnp.float32)  8.06 us
    ppermute x2, starting transfers between devices, from_behind(): return lax.ppermute(block, axis, route)  7.48 us
    dot_general x2, matrix products, body(): lax.dot_general(latent, decode_by_depth, (((1,), (2,)), ((), ())), prefer...  6.53 us
    sub x2, matrix products, body(): weights = jax.nn.softmax(scores, axis=-1).astype(jnp.bfloat16)  5.6 us
    dot_general x2, matrix products, body(): jnp.einsum('hts,shd->thd', weights, values, preferred_element_type=jnp.fl...  5.11 us
    reshape x1, local copies, waits for them, and re-layouts, embed_planes(): voxels = jnp.swapaxes(grouped, 1, 2).reshape(rows, PATCH, PATCH * PATCH)  4.86 us
    unnamed x23, local copies, waits for them, and re-layouts  4.82 us
  transfers between devices with their start and end apart: 10, of which 7 were waited for; matrix products, arithmetic and copies ran while one was open for 34% of the time, Pallas kernels for 0%

profile of v19, /device:TPU:31, one launch (start us, length us, event | category | flops | bytes accessed | tf_op | source)
XLA Modules:
  0.0 122.3 jit_solution(61588652423688964)
XLA Ops:
  0.0 2.1 %convert_element_type.130 = f32[512,384]{1,0:T(8,128)} convert(bf16[512,384]{1,0:T(8,128)(2,1)} %param.16) | non-fusion elementwise | flops 196608 | bytes 1179648 | tf_op jit(solution)/shard_map/convert_element_type | solution.py:91
  2.1 0.8 convert_element_type.129
  3.2 2.5 %broadcast_multiply_fusion = bf16[64,128,128]{2,1,0:T(8,128)(2,1)S(1)} fusion(bf16[64,128,128]{2,1,0:T(8,128)(2,1)} %param.12, bf16[64,128]{1,0:T(8,128)(2,1)S(1)} %convert_element_type.129), kind=kLoop, calls=%fused_computation.80 | loop fusion | flops 1048576 | bytes 4210688 | tf_op jit(solution)/shard_map/mul | solution.py:43
  5.7 1.9 %copy.26 = bf16[4,8,16,16,128]{4,3,2,1,0:T(8,128)(2,1)} copy(bf16[4,8,16,16,128]{4,3,1,2,0:T(8,128)(2,1)S(1)} %bitcast.117) | data formatting | bytes 4194304 | tf_op jit(solution)/shard_map/transpose | solution.py:44
  7.5 4.1 %copy.27 = bf16[32,128,256]{2,1,0:T(8,128)(2,1)} copy(bf16[32,128,256]{1,2,0:T(8,128)(2,1)} %bitcast.118) | data formatting | bytes 4194304 | tf_op jit(solution)/shard_map/transpose | solution.py:46
  11.6 4.9 %copy.28 = bf16[256,16,256]{0,1,2:T(8,128)(2,1)} copy(bf16[256,16,256]{2,1,0:T(8,128)(2,1)} %bitcast.119) | data formatting | bytes 4194304 | tf_op jit(solution)/shard_map/reshape | solution.py:46
  16.7 3.7 %fusion.94 = (bf16[256,384]{1,0:T(8,128)(2,1)S(1)}, bf16[256,384]{1,0:T(8,128)(2,1)}) fusion(f32[512,384]{1,0:T(8,128)} %convert_element_type.130, f32[32,384]{1,0:T(8,128)S(1)} %fusion.145, bf16[256,16,256]{0,1,2:T(8,128)(2,1)} %copy.28, bf16[16,256,384]{2,0,1:T(8,128)(2,1)S(1)} %bitcast.113), kind=kOutput, calls=%fused_computation.108 | convolution fusion | flops 805797888 | bytes 6471680 | tf_op jit(solution)/shard_map/dot_general | solution.py:47
  20.4 2.7 %collective-permute-start.1 = (bf16[256,384]{1,0:T(8,128)(2,1)}, bf16[256,384]{1,0:T(8,128)(2,1)S(1)}, u32[]{:S(2)}, u32[]{:S(2)}) collective-permute-start(bf16[256,384]{1,0:T(8,128)(2,1)} %get-tuple-element.20), channel_id=1, source_target_pairs={{2,0},{4,2},{6,4},{8,6},{10,8},{12,10},{14,12},{16,14},{18,16},{20... | collective-permute-start | bytes 589832 | tf_op jit(solution)/shard_map/ppermute | solution.py:19
  23.1 4.6 %copy.31 = bf16[768,2048]{0,1:T(8,128)(2,1)} copy(bf16[768,2048]{1,0:T(8,128)(2,1)} %param.23) | data formatting | bytes 6291456 | tf_op args[11]
  27.8 3.8 %collective-permute-start.8 = (bf16[2048,768]{1,0:T(8,128)(2,1)}, bf16[2048,768]{1,0:T(8,128)(2,1)}, u32[]{:S(2)}, u32[]{:S(2)}) collective-permute-start(bf16[2048,768]{1,0:T(8,128)(2,1)} %bitcast.27), channel_id=1, source_target_pairs={{0,65},{1,64},{2,67},{3,66},{4,69},{5,68},{6,71},{7,70},{8,73},{9,... | collective-permute-start | bytes 9437192 | tf_op jit(solution)/shard_map/ppermute | solution.py:87
  31.5 1.5 %collective-permute-start.4 = (bf16[384,768]{1,0:T(8,128)(2,1)S(1)}, bf16[384,768]{1,0:T(8,128)(2,1)}, u32[]{:S(2)}, u32[]{:S(2)}) collective-permute-start(bf16[384,768]{1,0:T(8,128)(2,1)S(1)} %bitcast.123), channel_id=1, source_target_pairs={{0,1},{1,0},{2,3},{3,2},{4,5},{5,4},{6,7},{7,6},{8,9},{9,8},{10,11... | collective-permute-start | bytes 1769480 | tf_op jit(solution)/shard_map/ppermute | solution.py:88
  33.1 0.5 collective-permute-done.1
  33.5 1.0 fusion.122
  34.6 1.7 %collective-permute-start.2 = (bf16[256,384]{1,0:T(8,128)(2,1)S(1)}, bf16[256,384]{1,0:T(8,128)(2,1)S(1)}, u32[]{:S(2)}, u32[]{:S(2)}) collective-permute-start(bf16[256,384]{1,0:T(8,128)(2,1)S(1)} %fusion.122), channel_id=1, source_target_pairs={{0,1},{1,0},{2,3},{3,2},{4,5},{5,4},{6,7},{7,6},{8,9},{9,8},{10,11... | collective-permute-start | bytes 589832 | tf_op jit(solution)/shard_map/ppermute | solution.py:102
  36.3 0.5 compare_and_fusion
  36.8 0.7 collective-permute-done
  37.6 16.8 %collective-permute-done.2 = bf16[256,384]{1,0:T(8,128)(2,1)S(1)} collective-permute-done((bf16[256,384]{1,0:T(8,128)(2,1)S(1)}, bf16[256,384]{1,0:T(8,128)(2,1)S(1)}, u32[]{:S(2)}, u32[]{:S(2)}) %collective-permute-start.2) | collective-permute-done | bytes 196640 | tf_op jit(solution)/shard_map/ppermute | solution.py:102
  54.7 0.3 multiply_reduce_fusion.2
  55.1 2.8 %fusion.55 = bf16[3,512,384]{1,2,0:T(8,128)(2,1)S(1)} fusion(bf16[1,3,768,384]{3,2,1,0:T(8,128)(2,1)} %param.19, f32[256,768]{1,0:T(8,128)S(1)} %fusion.96, f32[256,768]{1,0:T(8,128)S(1)} %fusion.95, f32[768]{0:T(1024)S(1)} %get-tuple-element.13, f32[768]{0:T(1024)S(1)} %get-tuple-element.30, f32[512]{0:T(512)S(1)} %add_rsqrt_fusion, ...), kind=kOutput, calls=%fused_computation.62 | convolution fusion | flops 908918784 | bytes 4532224 | tf_op jit(solution)/shard_map/td,sde->ste/dot_general | solution.py:111
  58.0 2.8 %fusion.141 = (f32[6,256]{1,0:T(8,128)S(1)}, f32[6,256,512]{2,1,0:T(8,128)}) fusion(bf16[256,6,64]{0,2,1:T(8,128)(2,1)S(1)} %bitcast.134, bf16[512,6,64]{0,2,1:T(8,128)(2,1)S(1)} %bitcast.127), kind=kOutput, calls=%fused_computation.179 | convolution fusion | flops 103023104 | bytes 3741696 | tf_op jit(solution)/shard_map/sub | solution.py:130
  60.8 2.6 %fusion.71 = bf16[6,64,256]{2,1,0:T(8,128)(2,1)S(1)} fusion(bf16[512,6,64]{0,2,1:T(8,128)(2,1)S(1)} %bitcast.125, f32[6,256,512]{2,1,0:T(8,128)} %get-tuple-element.22, f32[6,256]{1,0:T(8,128)S(1)} %get-tuple-element.21), kind=kOutput, calls=%fused_computation.79 | convolution fusion | flops 102334464 | bytes 3741696 | tf_op jit(solution)/shard_map/hts,shd->thd/dot_general | solution.py:131
  63.3 0.4 collective-permute-start.3
  63.7 2.8 %fusion.142 = (f32[6,256]{1,0:T(8,128)S(1)}, f32[6,256,512]{2,1,0:T(8,128)}) fusion(bf16[256,6,64]{0,2,1:T(8,128)(2,1)S(1)} %bitcast.133, bf16[512,6,64]{0,2,1:T(8,128)(2,1)S(1)} %bitcast.128), kind=kOutput, calls=%fused_computation.180 | convolution fusion | flops 103023104 | bytes 3741696 | tf_op jit(solution)/shard_map/sub | solution.py:130
  66.5 2.6 %fusion.70 = bf16[6,64,256]{2,1,0:T(8,128)(2,1)S(1)} fusion(bf16[512,6,64]{0,2,1:T(8,128)(2,1)S(1)} %bitcast.126, f32[6,256,512]{2,1,0:T(8,128)} %get-tuple-element.24, f32[6,256]{1,0:T(8,128)S(1)} %get-tuple-element.23), kind=kOutput, calls=%fused_computation.78 | convolution fusion | flops 102334464 | bytes 3741696 | tf_op jit(solution)/shard_map/hts,shd->thd/dot_general | solution.py:131
  69.0 1.4 %collective-permute-start.5 = (bf16[256,384]{0,1:T(8,128)(2,1)S(1)}, bf16[256,384]{0,1:T(8,128)(2,1)S(1)}, u32[]{:S(2)}, u32[]{:S(2)}) collective-permute-start(bf16[256,384]{0,1:T(8,128)(2,1)S(1)} %bitcast.131), channel_id=1, source_target_pairs={{0,1},{1,0},{2,3},{3,2},{4,5},{5,4},{6,7},{7,6},{8,9},{9,8},{10,11... | collective-permute-start | bytes 589832 | tf_op jit(solution)/shard_map/ppermute | solution.py:135
  70.5 0.4 fusion.68
  70.9 0.4 fusion.64
  71.3 3.3 %collective-permute-done.5 = bf16[256,384]{0,1:T(8,128)(2,1)S(1)} collective-permute-done((bf16[256,384]{0,1:T(8,128)(2,1)S(1)}, bf16[256,384]{0,1:T(8,128)(2,1)S(1)}, u32[]{:S(2)}, u32[]{:S(2)}) %collective-permute-start.5) | collective-permute-done | bytes 196640 | tf_op jit(solution)/shard_map/ppermute | solution.py:135
  74.6 1.5 %fusion.143 = (f32[256]{0:T(256)S(1)}, f32[256,768]{1,0:T(8,128)S(1)}) fusion(f32[256,768]{1,0:T(8,128)S(1)} %fusion.64, bf16[256,384]{0,1:T(8,128)(2,1)S(1)} %collective-permute-done.5, bf16[384,768]{1,0:T(8,128)(2,1)} %collective-permute-done.4, bf16[256,384]{1,0:T(8,128)(2,1)S(1)} %fusion.122, bf16[256,384]{1,0:T(8,128)(2,1)S(1)} %copy-done.6, pred[]{:T(512)S(6)} %eq.10), kind=kOutput, calls=%fused_computation.181 | convolution fusion | flops 153943808 | bytes 2753537 | tf_op jit(solution)/shard_map/dot_general | solution.py:137
  76.4 4.0 %fusion.58 = bf16[256,768]{1,0:T(8,128)(2,1)S(1)} fusion(bf16[1,1536,768]{2,1,0:T(8,128)(2,1)} %param.22, bf16[1,768,1536]{2,1,0:T(8,128)(2,1)} %param.21, f32[256,768]{1,0:T(8,128)S(1)} %get-tuple-element.26, f32[768]{0:T(1024)S(1)} %get-tuple-element.12, f32[768]{0:T(1024)S(1)} %get-tuple-element.31, f32[256]{0:T(256)S(1)} %add_rsqrt_fusion.4, ...), kind=kOutput, calls=%fused_computation.63 | convolution fusion | flops 1212678144 | bytes 5906432 | tf_op jit(solution)/shard_map/dot_general | solution.py:146
  80.4 1.0 collective-permute-start.6
  81.4 1.7 %fusion.144 = (f32[256]{0:T(256)S(1)}, f32[256,768]{1,0:T(8,128)S(1)}) fusion(f32[256,768]{1,0:T(8,128)S(1)} %fusion.68, bf16[256,384]{0,1:T(8,128)(2,1)} %collective-permute-done.3, bf16[384,768]{1,0:T(8,128)(2,1)} %collective-permute-done.4, bf16[256,384]{1,0:T(8,128)(2,1)S(1)} %get-tuple-element.19, bf16[256,384]{1,0:T(8,128)(2,1)} %copy-done.4, ...), kind=kOutput, calls=%fused_computation.182 | convolution fusion | flops 153943808 | bytes 2753537 | tf_op jit(solution)/shard_map/dot_general | solution.py:137
  83.4 4.0 %fusion.14 = bf16[256,768]{1,0:T(8,128)(2,1)S(1)} fusion(bf16[1,1536,768]{2,1,0:T(8,128)(2,1)} %param.22, bf16[1,768,1536]{2,1,0:T(8,128)(2,1)} %param.21, f32[256,768]{1,0:T(8,128)S(1)} %get-tuple-element.28, f32[256]{0:T(256)S(1)} %add_rsqrt_fusion.2, f32[256]{0:T(256)S(1)} %broadcast_multiply_fusion.3, f32[768]{0:T(1024)S(1)} %get-tuple-element.12, ...), kind=kOutput, calls=%fused_computation.28 | convolution fusion | flops 1212481536 | bytes 5906432 | tf_op jit(solution)/shard_map/dot_general | solution.py:146
  87.4 1.8 %collective-permute-done.6 = bf16[256,768]{1,0:T(8,128)(2,1)S(1)} collective-permute-done((bf16[256,768]{1,0:T(8,128)(2,1)S(1)}, bf16[256,768]{1,0:T(8,128)(2,1)S(1)}, u32[]{:S(2)}, u32[]{:S(2)}) %collective-permute-start.6) | collective-permute-done | bytes 393248 | tf_op jit(solution)/shard_map/ppermute | solution.py:24
  89.4 0.3 multiply_reduce_fusion.5
  90.0 0.7 collective-permute-start.7
  90.7 4.8 %collective-permute-start.9 = (bf16[256,768]{1,0:T(8,128)(2,1)S(1)}, bf16[256,768]{1,0:T(8,128)(2,1)S(1)}, u32[]{:S(2)}, u32[]{:S(2)}) collective-permute-start(bf16[256,768]{1,0:T(8,128)(2,1)S(1)} %add_convert_fusion.3), channel_id=1, source_target_pairs={{0,2},{2,4},{4,6},{6,8},{8,10},{10,12},{12,14},{14,16},{16,18},{18... | collective-permute-start | bytes 1179656 | tf_op jit(solution)/shard_map/ppermute | solution.py:19
  95.5 2.5 %collective-permute-done.7 = bf16[256,768]{1,0:T(8,128)(2,1)S(1)} collective-permute-done((bf16[256,768]{1,0:T(8,128)(2,1)S(1)}, bf16[256,768]{1,0:T(8,128)(2,1)S(1)}, u32[]{:S(2)}, u32[]{:S(2)}) %collective-permute-start.7) | collective-permute-done | bytes 393248 | tf_op jit(solution)/shard_map/ppermute | solution.py:24
  98.2 0.3 multiply_reduce_fusion.3
  98.5 2.7 %collective-permute-done.8 = bf16[2048,768]{1,0:T(8,128)(2,1)} collective-permute-done((bf16[2048,768]{1,0:T(8,128)(2,1)}, bf16[2048,768]{1,0:T(8,128)(2,1)}, u32[]{:S(2)}, u32[]{:S(2)}) %collective-permute-start.8) | collective-permute-done | bytes 3145760 | tf_op jit(solution)/shard_map/ppermute | solution.py:87
  101.2 3.3 %pad_maximum_fusion = bf16[4096,768]{1,0:T(8,128)(2,1)S(1)} fusion(bf16[2048,768]{1,0:T(8,128)(2,1)} %collective-permute-done.8, bf16[2048,768]{1,0:T(8,128)(2,1)} %bitcast.27), kind=kLoop, calls=%fused_computation.5 | loop fusion | flops 12582912 | bytes 12582912 | tf_op jit(solution)/shard_map/concatenate | solution.py:116
  104.5 2.1 %copy.32 = bf16[16,16,16,768]{3,2,1,0:T(8,128)(2,1)S(1)} copy(bf16[16,16,16,768]{3,0,2,1:T(8,128)(2,1)S(1)} %bitcast.114) | data formatting | bytes 12582912 | tf_op jit(solution)/shard_map/transpose | solution.py:121
  106.6 2.0 %fusion.92 = bf16[256,16,256]{2,0,1:T(8,128)(2,1)S(1)} fusion(bf16[16,256,768]{2,1,0:T(8,128)(2,1)S(1)} %bitcast.121, f32[256]{0:T(256)S(1)} %add_rsqrt_fusion.1, f32[256]{0:T(256)S(1)} %broadcast_multiply_fusion.2, f32[768]{0:T(1024)S(1)} %get-tuple-element.14, f32[768]{0:T(1024)S(1)} %get-tuple-element.29, f32[256,768]{1,0:T(8,128)S(1)} %get-tuple-element.28, ...), kind=kOutput, calls=%fused_computation.106 | convolution fusion | flops 1612382208 | bytes 9969664 | tf_op jit(solution)/shard_map/dot_general | solution.py:161
  108.6 4.6 %divide_convert_fusion = bf16[256,16,256]{2,0,1:T(8,128)(2,1)S(1)} fusion(f32[]{:T(128)S(6)} %convert_element_type.170, s32[256]{0:T(256)S(1)} %get-tuple-element.33, s32[256]{0:T(256)S(1)} %get-tuple-element.37, s32[]{:T(128)S(6)} %mul.215, s32[]{:T(128)S(6)} %axis_index.22, s32[256]{0:T(256)S(1)} %get-tuple-element.36, s32[256]{0:T(256)S(1)} %get-tuple-element.38, ...), kind=kOutput, calls=%fused_computation.16 | convolution fusion | flops 1652555776 | bytes 10885900 | tf_op jit(solution)/shard_map/dot_general | solution.py:161
  113.2 1.2 copy.33
  114.4 2.9 %copy.34 = bf16[32,256,128]{2,1,0:T(8,128)(2,1)} copy(bf16[32,256,128]{1,2,0:T(8,128)(2,1)S(1)} %bitcast.120) | data formatting | bytes 4194304 | tf_op jit(solution)/shard_map/transpose | solution.py:184
  117.3 3.1 %reverse_select_fusion = bf16[4,8,2,8,16,128]{5,4,3,2,1,0:T(8,128)(2,1)S(1)} fusion(bf16[4,8,2,8,16,128]{5,4,3,2,1,0:T(8,128)(2,1)} %bitcast.115, pred[]{:T(512)S(6)} %eq.10), kind=kLoop, calls=%fused_computation.17 | loop fusion | flops 1048576 | bytes 4194305 | tf_op jit(solution)/shard_map/jit(_where)/select_n | solution.py:185
  120.4 1.9 %copy.35 = bf16[4,16,8,16,128]{4,3,2,1,0:T(8,128)(2,1)} copy(bf16[4,16,8,16,128]{4,3,1,2,0:T(8,128)(2,1)S(1)} %bitcast.116) | data formatting | bytes 4194304 | tf_op jit(solution)/shard_map/transpose | solution.py:187
  (55 shorter events, 2.3 us)
Async XLA Ops:
  0.0 16.6 %copy-start = (bf16[4096,384]{1,0:T(8,128)(2,1)S(1)}, bf16[4096,384]{1,0:T(8,128)(2,1)}, u32[]{:S(2)}) copy-start(bf16[4096,384]{1,0:T(8,128)(2,1)} %param.14) | copy-start | bytes 9437188
  11.6 4.9 %copy-start.3 = (bf16[256,384]{1,0:T(8,128)(2,1)S(1)}, bf16[256,384]{1,0:T(8,128)(2,1)}, u32[]{:S(2)}) copy-start(bf16[256,384]{1,0:T(8,128)(2,1)} %param.15) | copy-start | bytes 589828
  20.4 11.1 %copy-start.2 = (bf16[1,384,768]{2,1,0:T(8,128)(2,1)S(1)}, bf16[1,384,768]{2,1,0:T(8,128)(2,1)}, u32[]{:S(2)}) copy-start(bf16[1,384,768]{2,1,0:T(8,128)(2,1)} %param.20) | copy-start | bytes 1769476
  20.4 12.6 %copy-start.7 = (f32[3,768]{1,0:T(4,128)S(1)}, f32[3,768]{1,0:T(4,128)}, u32[]{:S(2)}) copy-start(f32[3,768]{1,0:T(4,128)} %param.18) | copy-start | bytes 27652
  20.4 12.6 %copy-start.8 = (f32[3,768]{1,0:T(4,128)S(1)}, f32[3,768]{1,0:T(4,128)}, u32[]{:S(2)}) copy-start(f32[3,768]{1,0:T(4,128)} %param.17) | copy-start | bytes 27652
  20.4 13.1 %collective-permute-start.1 = (bf16[256,384]{1,0:T(8,128)(2,1)}, bf16[256,384]{1,0:T(8,128)(2,1)S(1)}, u32[]{:S(2)}, u32[]{:S(2)}) collective-permute-start(bf16[256,384]{1,0:T(8,128)(2,1)} %get-tuple-element.20), channel_id=1, source_target_pairs={{2,0},{4,2},{6,4},{8,6},{10,8},{12,10},{14,12},{16,14},{18,16},{20... | collective-permute-start | bytes 589832 | tf_op jit(solution)/shard_map/ppermute | solution.py:19
  27.8 73.5 %collective-permute-start.8 = (bf16[2048,768]{1,0:T(8,128)(2,1)}, bf16[2048,768]{1,0:T(8,128)(2,1)}, u32[]{:S(2)}, u32[]{:S(2)}) collective-permute-start(bf16[2048,768]{1,0:T(8,128)(2,1)} %bitcast.27), channel_id=1, source_target_pairs={{0,65},{1,64},{2,67},{3,66},{4,69},{5,68},{6,71},{7,70},{8,73},{9,... | collective-permute-start | bytes 9437192 | tf_op jit(solution)/shard_map/ppermute | solution.py:87
  31.5 6.0 %collective-permute-start = (bf16[256,384]{1,0:T(8,128)(2,1)S(1)}, bf16[256,384]{1,0:T(8,128)(2,1)S(1)}, u32[]{:S(2)}, u32[]{:S(2)}) collective-permute-start(bf16[256,384]{1,0:T(8,128)(2,1)S(1)} %get-tuple-element.19), channel_id=1, source_target_pairs={{0,1},{1,0},{2,3},{3,2},{4,5},{5,4},{6,7},{7,6},{8,9},{9,8},{10,11... | collective-permute-start | bytes 589832 | tf_op jit(solution)/shard_map/ppermute | solution.py:102
  31.5 39.7 %collective-permute-start.4 = (bf16[384,768]{1,0:T(8,128)(2,1)S(1)}, bf16[384,768]{1,0:T(8,128)(2,1)}, u32[]{:S(2)}, u32[]{:S(2)}) collective-permute-start(bf16[384,768]{1,0:T(8,128)(2,1)S(1)} %bitcast.123), channel_id=1, source_target_pairs={{0,1},{1,0},{2,3},{3,2},{4,5},{5,4},{6,7},{7,6},{8,9},{9,8},{10,11... | collective-permute-start | bytes 1769480 | tf_op jit(solution)/shard_map/ppermute | solution.py:88
  34.6 19.8 %collective-permute-start.2 = (bf16[256,384]{1,0:T(8,128)(2,1)S(1)}, bf16[256,384]{1,0:T(8,128)(2,1)S(1)}, u32[]{:S(2)}, u32[]{:S(2)}) collective-permute-start(bf16[256,384]{1,0:T(8,128)(2,1)S(1)} %fusion.122), channel_id=1, source_target_pairs={{0,1},{1,0},{2,3},{3,2},{4,5},{5,4},{6,7},{7,6},{8,9},{9,8},{10,11... | collective-permute-start | bytes 589832 | tf_op jit(solution)/shard_map/ppermute | solution.py:102
  37.6 20.3 %copy-start.4 = (bf16[256,384]{1,0:T(8,128)(2,1)}, bf16[256,384]{1,0:T(8,128)(2,1)S(1)}, u32[]{:S(2)}) copy-start(bf16[256,384]{1,0:T(8,128)(2,1)S(1)} %collective-permute-done) | copy-start | bytes 589828
  54.4 0.7 copy-start.5
  63.3 18.1 %collective-permute-start.3 = (bf16[256,384]{0,1:T(8,128)(2,1)S(1)}, bf16[256,384]{0,1:T(8,128)(2,1)}, u32[]{:S(2)}, u32[]{:S(2)}) collective-permute-start(bf16[256,384]{0,1:T(8,128)(2,1)S(1)} %bitcast.129), channel_id=1, source_target_pairs={{0,1},{1,0},{2,3},{3,2},{4,5},{5,4},{6,7},{7,6},{8,9},{9,8},{10,11... | collective-permute-start | bytes 589832 | tf_op jit(solution)/shard_map/ppermute | solution.py:135
  69.0 5.5 %copy-start.6 = (bf16[256,384]{1,0:T(8,128)(2,1)S(1)}, bf16[256,384]{1,0:T(8,128)(2,1)}, u32[]{:S(2)}) copy-start(bf16[256,384]{1,0:T(8,128)(2,1)} %copy-done.5) | copy-start | bytes 589828
  69.0 5.5 %collective-permute-start.5 = (bf16[256,384]{0,1:T(8,128)(2,1)S(1)}, bf16[256,384]{0,1:T(8,128)(2,1)S(1)}, u32[]{:S(2)}, u32[]{:S(2)}) collective-permute-start(bf16[256,384]{0,1:T(8,128)(2,1)S(1)} %bitcast.131), channel_id=1, source_target_pairs={{0,1},{1,0},{2,3},{3,2},{4,5},{5,4},{6,7},{7,6},{8,9},{9,8},{10,11... | collective-permute-start | bytes 589832 | tf_op jit(solution)/shard_map/ppermute | solution.py:135
  80.4 8.8 %collective-permute-start.6 = (bf16[256,768]{1,0:T(8,128)(2,1)S(1)}, bf16[256,768]{1,0:T(8,128)(2,1)S(1)}, u32[]{:S(2)}, u32[]{:S(2)}) collective-permute-start(bf16[256,768]{1,0:T(8,128)(2,1)S(1)} %fusion.58), channel_id=1, source_target_pairs={{0,1},{1,0},{2,3},{3,2},{4,5},{5,4},{6,7},{7,6},{8,9},{9,8},{10,11... | collective-permute-start | bytes 1179656 | tf_op jit(solution)/shard_map/ppermute | solution.py:24
  90.0 8.1 %collective-permute-start.7 = (bf16[256,768]{1,0:T(8,128)(2,1)S(1)}, bf16[256,768]{1,0:T(8,128)(2,1)S(1)}, u32[]{:S(2)}, u32[]{:S(2)}) collective-permute-start(bf16[256,768]{1,0:T(8,128)(2,1)S(1)} %fusion.14), channel_id=1, source_target_pairs={{0,1},{1,0},{2,3},{3,2},{4,5},{5,4},{6,7},{7,6},{8,9},{9,8},{10,11... | collective-permute-start | bytes 1179656 | tf_op jit(solution)/shard_map/ppermute | solution.py:24
  90.7 17.9 %collective-permute-start.9 = (bf16[256,768]{1,0:T(8,128)(2,1)S(1)}, bf16[256,768]{1,0:T(8,128)(2,1)S(1)}, u32[]{:S(2)}, u32[]{:S(2)}) collective-permute-start(bf16[256,768]{1,0:T(8,128)(2,1)S(1)} %add_convert_fusion.3), channel_id=1, source_target_pairs={{0,2},{2,4},{4,6},{6,8},{8,10},{10,12},{12,14},{14,16},{16,18},{18... | collective-permute-start | bytes 1179656 | tf_op jit(solution)/shard_map/ppermute | solution.py:19
  106.6 2.0 %copy-start.9 = (pred[256]{0:T(512)(128)(4,1)S(1)}, pred[256]{0:T(512)(128)(4,1)}, u32[]{:S(2)}) copy-start(pred[256]{0:T(512)(128)(4,1)} %get-tuple-element.34) | copy-start | bytes 772
  106.6 2.0 %copy-start.10 = (pred[256]{0:T(512)(128)(4,1)S(1)}, pred[256]{0:T(512)(128)(4,1)}, u32[]{:S(2)}) copy-start(pred[256]{0:T(512)(128)(4,1)} %get-tuple-element.35) | copy-start | bytes 772
  117.3 5.1 %copy-start.1 = (bf16[4096,384]{1,0:T(8,128)(2,1)S(1)}, bf16[4096,384]{1,0:T(8,128)(2,1)}, u32[]{:S(2)}) copy-start(bf16[4096,384]{1,0:T(8,128)(2,1)} %param.14) | copy-start | bytes 9437188

commit v20 on v18

--- a/solution.py
+++ b/solution.py
@@ -92,14 +92,25 @@
     own_embedded = embed_planes(traces, own_live, embed_by_depth, embed_mask)
     own_half = (own_embedded + position[:half_tokens]).astype(jnp.bfloat16)
     for_previous = (own_embedded + position[half_tokens:]).astype(jnp.bfloat16)
-    next_half = jnp.where(
-        tile_index == lax.axis_size("tile") - 1,
-        position[half_tokens:].astype(jnp.bfloat16),
-        from_behind(for_previous, "tile", -1),
+    last_tile = tile_index == lax.axis_size("tile") - 1
+    upper_position = position[half_tokens:].astype(jnp.bfloat16)
+    pair = [(0, 1), (1, 0)]
+    diagonal = [
+        ((tile + 1) * 2 + head, tile * 2 + 1 - head)
+        for tile in range(lax.axis_size("tile") - 1)
+        for head in range(2)
+    ]
+    next_own = jnp.where(last_tile, upper_position, from_behind(for_previous, "tile", -1))
+    next_other = jnp.where(
+        last_tile,
+        lax.ppermute(upper_position, "head", pair),
+        lax.ppermute(for_previous, ("tile", "head"), diagonal),
     )
     halves = []
-    for embedded in (own_half, next_half):
-        other_columns = lax.ppermute(embedded, "head", [(0, 1), (1, 0)])
+    for embedded, other_columns in (
+        (own_half, lax.ppermute(own_half, "head", pair)),
+        (next_own, next_other),
+    ):
         halves.append(jnp.where(
             head_index == 0,
             jnp.concatenate([embedded, other_columns], 1),

time: 124 us -> 137 us (1.10)
  the two profiles are of different devices: /device:TPU:31 before, /device:TPU:0 now
where the time goes in v20:
time: 137 us; the launch traced here: 136 us
  waiting for transfers between devices  42.5 us (31%)
  matrix products  33.8 us (25%)
  local copies, waits for them, and re-layouts  26.2 us (19%)
  starting transfers between devices  19.5 us (14%)
  other arithmetic  13.5 us (10%)
    ppermute x2, waiting for transfers between devices, partner_sum(): other = lax.ppermute(rounded, 'head', [(0, 1), (1, 0)])  16.3 us
    ppermute x1, waiting for transfers between devices, body(): lax.ppermute(upper_position, 'head', pair)  15.3 us
    ppermute x1, starting transfers between devices, body(): other_cells_first = lax.ppermute(own_cells_first, ('tile', 'head'), across)  10 us
    dot_general x2, matrix products, body(): jnp.dot(hidden, w_down[0], preferred_element_type=jnp.float32)  8.1 us
    select_n x1, other arithmetic, body(): jnp.where(head_index == 0, jnp.concatenate([own_cells_first, other_cells_...  5.78 us
    dot_general x2, matrix products, body(): lax.dot_general(latent, decode_by_depth, (((1,), (2,)), ((), ())), prefer...  5.77 us
    sub x2, matrix products, body(): weights = jax.nn.softmax(scores, axis=-1).astype(jnp.bfloat16)  5.6 us
    ppermute x1, waiting for transfers between devices, body(): lax.ppermute(own_half, 'head', pair)  5.52 us
  transfers between devices with their start and end apart: 11, of which 5 were waited for; matrix products, arithmetic and copies ran while one was open for 29% of the time, Pallas kernels for 0%

profile of v20, /device:TPU:0, one launch (start us, length us, event | category | flops | bytes accessed | tf_op | source)
XLA Modules:
  0.0 135.9 jit_solution(7012444207179853156)
XLA Ops:
  0.0 2.1 %convert_element_type.136 = f32[512,384]{1,0:T(8,128)} convert(bf16[512,384]{1,0:T(8,128)(2,1)} %param.16) | non-fusion elementwise | flops 196608 | bytes 1179648 | tf_op jit(solution)/shard_map/convert_element_type | solution.py:91
  2.1 0.8 convert_element_type.135
  3.0 0.2 reshape.125
  3.2 2.5 %broadcast_multiply_fusion = bf16[64,128,128]{2,1,0:T(8,128)(2,1)S(1)} fusion(bf16[64,128,128]{2,1,0:T(8,128)(2,1)} %param.12, bf16[64,128]{1,0:T(8,128)(2,1)S(1)} %convert_element_type.135), kind=kLoop, calls=%fused_computation.70 | loop fusion | flops 1048576 | bytes 4210688 | tf_op jit(solution)/shard_map/mul | solution.py:43
  5.7 1.9 %copy.26 = bf16[4,8,16,16,128]{4,3,2,1,0:T(8,128)(2,1)} copy(bf16[4,8,16,16,128]{4,3,1,2,0:T(8,128)(2,1)S(1)} %bitcast.112) | data formatting | bytes 4194304 | tf_op jit(solution)/shard_map/transpose | solution.py:44
  7.6 4.1 %copy.27 = bf16[32,128,256]{2,1,0:T(8,128)(2,1)} copy(bf16[32,128,256]{1,2,0:T(8,128)(2,1)} %bitcast.113) | data formatting | bytes 4194304 | tf_op jit(solution)/shard_map/transpose | solution.py:46
  11.7 4.9 %copy.28 = bf16[256,16,256]{0,1,2:T(8,128)(2,1)} copy(bf16[256,16,256]{2,1,0:T(8,128)(2,1)} %bitcast.114) | data formatting | bytes 4194304 | tf_op jit(solution)/shard_map/reshape | solution.py:46
  16.7 3.7 %fusion.93 = (bf16[256,384]{1,0:T(8,128)(2,1)S(1)}, bf16[256,384]{1,0:T(8,128)(2,1)}) fusion(f32[512,384]{1,0:T(8,128)} %convert_element_type.136, f32[32,384]{1,0:T(8,128)S(1)} %fusion.143, bf16[256,16,256]{0,1,2:T(8,128)(2,1)} %copy.28, bf16[16,256,384]{2,0,1:T(8,128)(2,1)S(1)} %bitcast.111), kind=kOutput, calls=%fused_computation.97 | convolution fusion | flops 805797888 | bytes 6471680 | tf_op jit(solution)/shard_map/dot_general | solution.py:47
  20.4 1.4 %collective-permute-start.1 = (bf16[256,384]{1,0:T(8,128)(2,1)}, bf16[256,384]{1,0:T(8,128)(2,1)S(1)}, u32[]{:S(2)}, u32[]{:S(2)}) collective-permute-start(bf16[256,384]{1,0:T(8,128)(2,1)} %get-tuple-element.22), channel_id=1, source_target_pairs={{2,0},{4,2},{6,4},{8,6},{10,8},{12,10},{14,12},{16,14},{18,16},{20... | collective-permute-start | bytes 589832 | tf_op jit(solution)/shard_map/ppermute | solution.py:19
  21.9 1.3 collective-permute-start.3
  23.2 4.6 %copy.31 = bf16[768,2048]{0,1:T(8,128)(2,1)} copy(bf16[768,2048]{1,0:T(8,128)(2,1)} %param.23) | data formatting | bytes 6291456 | tf_op args[11]
  27.8 10.0 %collective-permute-start.9 = (bf16[2048,768]{1,0:T(8,128)(2,1)}, bf16[2048,768]{1,0:T(8,128)(2,1)}, u32[]{:S(2)}, u32[]{:S(2)}) collective-permute-start(bf16[2048,768]{1,0:T(8,128)(2,1)} %bitcast.27), channel_id=1, source_target_pairs={{0,65},{1,64},{2,67},{3,66},{4,69},{5,68},{6,71},{7,70},{8,73},{9,... | collective-permute-start | bytes 9437192 | tf_op jit(solution)/shard_map/ppermute | solution.py:87
  37.9 2.0 %collective-permute-start.5 = (bf16[384,768]{1,0:T(8,128)(2,1)S(1)}, bf16[384,768]{1,0:T(8,128)(2,1)}, u32[]{:S(2)}, u32[]{:S(2)}) collective-permute-start(bf16[384,768]{1,0:T(8,128)(2,1)S(1)} %bitcast.119), channel_id=1, source_target_pairs={{0,1},{1,0},{2,3},{3,2},{4,5},{5,4},{6,7},{7,6},{8,9},{9,8},{10,11... | collective-permute-start | bytes 1769480 | tf_op jit(solution)/shard_map/ppermute | solution.py:88
  40.1 5.5 %collective-permute-done = bf16[256,384]{1,0:T(8,128)(2,1)S(1)} collective-permute-done((bf16[256,384]{1,0:T(8,128)(2,1)S(1)}, bf16[256,384]{1,0:T(8,128)(2,1)S(1)}, u32[]{:S(2)}, u32[]{:S(2)}) %collective-permute-start) | collective-permute-done | bytes 196640 | tf_op jit(solution)/shard_map/ppermute | solution.py:111
  45.7 15.3 %collective-permute-done.2 = bf16[256,384]{1,0:T(8,128)(2,1)S(1)} collective-permute-done((bf16[256,384]{1,0:T(8,128)(2,1)S(1)}, bf16[256,384]{1,0:T(8,128)(2,1)S(1)}, u32[]{:S(2)}, u32[]{:S(2)}) %collective-permute-start.2) | collective-permute-done | bytes 196640 | tf_op jit(solution)/shard_map/ppermute | solution.py:106
  61.3 0.3 multiply_reduce_fusion.2
  61.6 1.3 fusion.55
  63.0 2.8 %fusion.139 = (f32[6,256]{1,0:T(8,128)S(1)}, f32[6,256,512]{2,1,0:T(8,128)}) fusion(bf16[256,6,64]{0,2,1:T(8,128)(2,1)S(1)} %bitcast.130, bf16[512,6,64]{0,2,1:T(8,128)(2,1)S(1)} %bitcast.123), kind=kOutput, calls=%fused_computation.165 | convolution fusion | flops 103023104 | bytes 3741696 | tf_op jit(solution)/shard_map/sub | solution.py:145
  65.8 2.6 %fusion.71 = bf16[6,64,256]{2,1,0:T(8,128)(2,1)S(1)} fusion(bf16[512,6,64]{0,2,1:T(8,128)(2,1)S(1)} %bitcast.121, f32[6,256,512]{2,1,0:T(8,128)} %get-tuple-element.24, f32[6,256]{1,0:T(8,128)S(1)} %get-tuple-element.23), kind=kOutput, calls=%fused_computation.69 | convolution fusion | flops 102334464 | bytes 3741696 | tf_op jit(solution)/shard_map/hts,shd->thd/dot_general | solution.py:146
  68.4 1.3 collective-permute-start.4
  69.7 2.8 %fusion.140 = (f32[6,256]{1,0:T(8,128)S(1)}, f32[6,256,512]{2,1,0:T(8,128)}) fusion(bf16[256,6,64]{0,2,1:T(8,128)(2,1)S(1)} %bitcast.129, bf16[512,6,64]{0,2,1:T(8,128)(2,1)S(1)} %bitcast.124), kind=kOutput, calls=%fused_computation.166 | convolution fusion | flops 103023104 | bytes 3741696 | tf_op jit(solution)/shard_map/sub | solution.py:145
  72.5 2.6 %fusion.70 = bf16[6,64,256]{2,1,0:T(8,128)(2,1)S(1)} fusion(bf16[512,6,64]{0,2,1:T(8,128)(2,1)S(1)} %bitcast.122, f32[6,256,512]{2,1,0:T(8,128)} %get-tuple-element.26, f32[6,256]{1,0:T(8,128)S(1)} %get-tuple-element.25), kind=kOutput, calls=%fused_computation.68 | convolution fusion | flops 102334464 | bytes 3741696 | tf_op jit(solution)/shard_map/hts,shd->thd/dot_general | solution.py:146
  75.0 1.1 collective-permute-start.6
  76.1 0.4 fusion.68
  76.5 0.4 fusion.64
  76.9 5.4 %collective-permute-done.6 = bf16[256,384]{0,1:T(8,128)(2,1)S(1)} collective-permute-done((bf16[256,384]{0,1:T(8,128)(2,1)S(1)}, bf16[256,384]{0,1:T(8,128)(2,1)S(1)}, u32[]{:S(2)}, u32[]{:S(2)}) %collective-permute-start.6) | collective-permute-done | bytes 196640 | tf_op jit(solution)/shard_map/ppermute | solution.py:150
  82.3 1.5 %fusion.141 = (f32[256]{0:T(256)S(1)}, f32[256,768]{1,0:T(8,128)S(1)}) fusion(f32[256,768]{1,0:T(8,128)S(1)} %fusion.64, bf16[256,384]{0,1:T(8,128)(2,1)S(1)} %collective-permute-done.6, bf16[384,768]{1,0:T(8,128)(2,1)} %collective-permute-done.5, bf16[256,384]{1,0:T(8,128)(2,1)S(1)} %get-tuple-element.15, bf16[256,384]{1,0:T(8,128)(2,1)S(1)} %broadcast_select_fusion, ...), kind=kOutput, calls=%fused_computation.167 | convolution fusion | flops 153943808 | bytes 2753537 | tf_op jit(solution)/shard_map/dot_general | solution.py:152
  83.9 0.2 multiply_reduce_fusion.6
  84.1 4.1 %fusion.58 = bf16[256,768]{1,0:T(8,128)(2,1)S(1)} fusion(bf16[1,1536,768]{2,1,0:T(8,128)(2,1)} %param.22, bf16[1,768,1536]{2,1,0:T(8,128)(2,1)} %param.21, f32[256,768]{1,0:T(8,128)S(1)} %get-tuple-element.28, f32[768]{0:T(1024)S(1)} %get-tuple-element.12, f32[768]{0:T(1024)S(1)} %get-tuple-element.33, f32[256]{0:T(256)S(1)} %add_rsqrt_fusion.4, ...), kind=kOutput, calls=%fused_computation.53 | convolution fusion | flops 1212678144 | bytes 5906432 | tf_op jit(solution)/shard_map/dot_general | solution.py:161
  88.2 0.4 collective-permute-start.7
  88.6 1.7 %fusion.142 = (f32[256]{0:T(256)S(1)}, f32[256,768]{1,0:T(8,128)S(1)}) fusion(f32[256,768]{1,0:T(8,128)S(1)} %fusion.68, bf16[256,384]{0,1:T(8,128)(2,1)} %collective-permute-done.4, bf16[384,768]{1,0:T(8,128)(2,1)} %collective-permute-done.5, bf16[256,384]{1,0:T(8,128)(2,1)S(1)} %copy-done.6, bf16[256,384]{1,0:T(8,128)(2,1)} %copy-done.7, pred[]{:T(512)S(6)} %eq.8), kind=kOutput, calls=%fused_computation.168 | convolution fusion | flops 153943808 | bytes 2753537 | tf_op jit(solution)/shard_map/dot_general | solution.py:152
  90.4 0.2 multiply_reduce_fusion.4
  90.6 4.0 %fusion.12 = bf16[256,768]{1,0:T(8,128)(2,1)S(1)} fusion(bf16[1,1536,768]{2,1,0:T(8,128)(2,1)} %param.22, bf16[1,768,1536]{2,1,0:T(8,128)(2,1)} %param.21, f32[256,768]{1,0:T(8,128)S(1)} %get-tuple-element.30, f32[256]{0:T(256)S(1)} %add_rsqrt_fusion.2, f32[256]{0:T(256)S(1)} %broadcast_multiply_fusion.3, f32[768]{0:T(1024)S(1)} %get-tuple-element.12, ...), kind=kOutput, calls=%fused_computation.18 | convolution fusion | flops 1212481536 | bytes 5906432 | tf_op jit(solution)/shard_map/dot_general | solution.py:161
  94.6 4.2 %collective-permute-done.7 = bf16[256,768]{1,0:T(8,128)(2,1)S(1)} collective-permute-done((bf16[256,768]{1,0:T(8,128)(2,1)S(1)}, bf16[256,768]{1,0:T(8,128)(2,1)S(1)}, u32[]{:S(2)}, u32[]{:S(2)}) %collective-permute-start.7) | collective-permute-done | bytes 393248 | tf_op jit(solution)/shard_map/ppermute | solution.py:24
  98.8 0.2 fusion.135
  99.0 0.3 multiply_reduce_fusion.5
  99.3 0.2 add_convert_fusion.3
  99.5 0.4 collective-permute-start.8
  99.9 1.5 %collective-permute-start.10 = (bf16[256,768]{1,0:T(8,128)(2,1)S(1)}, bf16[256,768]{1,0:T(8,128)(2,1)S(1)}, u32[]{:S(2)}, u32[]{:S(2)}) collective-permute-start(bf16[256,768]{1,0:T(8,128)(2,1)S(1)} %add_convert_fusion.3), channel_id=1, source_target_pairs={{0,2},{2,4},{4,6},{6,8},{8,10},{10,12},{12,14},{14,16},{16,18},{18... | collective-permute-start | bytes 1179656 | tf_op jit(solution)/shard_map/ppermute | solution.py:19
  101.5 12.1 %collective-permute-done.8 = bf16[256,768]{1,0:T(8,128)(2,1)S(1)} collective-permute-done((bf16[256,768]{1,0:T(8,128)(2,1)S(1)}, bf16[256,768]{1,0:T(8,128)(2,1)S(1)}, u32[]{:S(2)}, u32[]{:S(2)}) %collective-permute-start.8) | collective-permute-done | bytes 393248 | tf_op jit(solution)/shard_map/ppermute | solution.py:24
  113.6 0.2 fusion.136
  113.8 0.3 multiply_reduce_fusion.3
  114.1 5.8 %maximum_select_fusion = bf16[4096,768]{1,0:T(8,128)(2,1)S(1)} fusion(bf16[2048,768]{1,0:T(8,128)(2,1)} %collective-permute-done.9, bf16[2048,768]{1,0:T(8,128)(2,1)} %bitcast.27, pred[]{:T(512)S(6)} %eq.8), kind=kLoop, calls=%fused_computation.2 | loop fusion | flops 28311552 | bytes 12582913 | tf_op jit(solution)/shard_map/jit(_where)/select_n | solution.py:127
  119.9 2.5 %fusion.4 = bf16[256,16,256]{2,0,1:T(8,128)(2,1)S(1)} fusion(bf16[16,256,768]{2,0,1:T(8,128)(2,1)S(1)} %bitcast.117, f32[256]{0:T(256)S(1)} %add_rsqrt_fusion.1, f32[256]{0:T(256)S(1)} %broadcast_multiply_fusion.2, f32[768]{0:T(1024)S(1)} %get-tuple-element.14, f32[768]{0:T(1024)S(1)} %get-tuple-element.31, f32[256,768]{1,0:T(8,128)S(1)} %get-tuple-element.30, ...), kind=kOutput, calls=%fused_computation.5 | convolution fusion | flops 1612382208 | bytes 9969664 | tf_op jit(solution)/shard_map/dot_general | solution.py:176
  122.4 3.2 %divide_convert_fusion = bf16[256,16,256]{2,0,1:T(8,128)(2,1)S(1)} fusion(f32[]{:T(128)S(6)} %convert_element_type.176, s32[256]{0:T(256)S(1)} %get-tuple-element.35, s32[256]{0:T(256)S(1)} %get-tuple-element.38, s32[256]{0:T(256)S(1)} %get-tuple-element.34, s32[256]{0:T(256)S(1)} %get-tuple-element.39, bf16[256,16,256]{2,0,1:T(8,128)(2,1)S(1)} %fusion.4, ...), kind=kOutput, calls=%fused_computation.7 | convolution fusion | flops 1634729984 | bytes 10883588 | tf_op jit(solution)/shard_map/dot_general | solution.py:176
  125.7 2.5 %copy.34 = bf16[256,16,256]{2,1,0:T(8,128)(2,1)} copy(bf16[256,16,256]{2,0,1:T(8,128)(2,1)S(1)} %divide_convert_fusion) | data formatting | bytes 4194304 | tf_op jit(solution)/shard_map/convert_element_type | solution.py:193
  128.2 4.2 %copy.35 = bf16[32,256,128]{2,1,0:T(8,128)(2,1)} copy(bf16[32,256,128]{1,2,0:T(8,128)(2,1)} %bitcast.115) | data formatting | bytes 4194304 | tf_op jit(solution)/shard_map/transpose | solution.py:195
  132.4 3.5 %copy.36 = bf16[4,16,8,16,128]{4,3,2,1,0:T(8,128)(2,1)} copy(bf16[4,16,8,16,128]{4,3,1,2,0:T(8,128)(2,1)} %bitcast.116) | data formatting | bytes 4194304 | tf_op jit(solution)/shard_map/transpose | solution.py:196
  (54 shorter events, 1.1 us)
Async XLA Ops:
  0.0 16.7 %copy-start = (bf16[4096,384]{1,0:T(8,128)(2,1)S(1)}, bf16[4096,384]{1,0:T(8,128)(2,1)}, u32[]{:S(2)}) copy-start(bf16[4096,384]{1,0:T(8,128)(2,1)} %param.14) | copy-start | bytes 9437188
  11.7 4.9 %copy-start.4 = (bf16[256,384]{1,0:T(8,128)(2,1)S(1)}, bf16[256,384]{1,0:T(8,128)(2,1)}, u32[]{:S(2)}) copy-start(bf16[256,384]{1,0:T(8,128)(2,1)} %param.15) | copy-start | bytes 589828
  20.4 25.2 %copy-start.5 = (bf16[256,384]{1,0:T(8,128)(2,1)}, bf16[256,384]{1,0:T(8,128)(2,1)S(1)}, u32[]{:S(2)}) copy-start(bf16[256,384]{1,0:T(8,128)(2,1)S(1)} %get-tuple-element.21) | copy-start | bytes 589828
  20.4 17.5 %copy-start.2 = (bf16[1,384,768]{2,1,0:T(8,128)(2,1)S(1)}, bf16[1,384,768]{2,1,0:T(8,128)(2,1)}, u32[]{:S(2)}) copy-start(bf16[1,384,768]{2,1,0:T(8,128)(2,1)} %param.20) | copy-start | bytes 1769476
  20.4 19.5 %copy-start.3 = (bf16[512,384]{1,0:T(8,128)(2,1)S(1)}, bf16[512,384]{1,0:T(8,128)(2,1)}, u32[]{:S(2)}) copy-start(bf16[512,384]{1,0:T(8,128)(2,1)} %param.16) | copy-start | bytes 1179652
  20.4 19.6 %copy-start.8 = (f32[3,768]{1,0:T(4,128)S(1)}, f32[3,768]{1,0:T(4,128)}, u32[]{:S(2)}) copy-start(f32[3,768]{1,0:T(4,128)} %param.18) | copy-start | bytes 27652
  20.4 19.6 %copy-start.9 = (f32[3,768]{1,0:T(4,128)S(1)}, f32[3,768]{1,0:T(4,128)}, u32[]{:S(2)}) copy-start(f32[3,768]{1,0:T(4,128)} %param.17) | copy-start | bytes 27652
  20.4 19.4 %collective-permute-start.1 = (bf16[256,384]{1,0:T(8,128)(2,1)}, bf16[256,384]{1,0:T(8,128)(2,1)S(1)}, u32[]{:S(2)}, u32[]{:S(2)}) collective-permute-start(bf16[256,384]{1,0:T(8,128)(2,1)} %get-tuple-element.22), channel_id=1, source_target_pairs={{2,0},{4,2},{6,4},{8,6},{10,8},{12,10},{14,12},{16,14},{18,16},{20... | collective-permute-start | bytes 589832 | tf_op jit(solution)/shard_map/ppermute | solution.py:19
  21.9 23.9 %collective-permute-start.3 = (bf16[256,384]{1,0:T(8,128)(2,1)}, bf16[256,384]{1,0:T(8,128)(2,1)S(1)}, u32[]{:S(2)}, u32[]{:S(2)}) collective-permute-start(bf16[256,384]{1,0:T(8,128)(2,1)} %get-tuple-element.22), channel_id=1, source_target_pairs={{2,1},{3,0},{4,3},{5,2},{6,5},{7,4},{8,7},{9,6},{10,9},{11,8},{12,... | collective-permute-start | bytes 589832 | tf_op jit(solution)/shard_map/ppermute | solution.py:107
  27.8 86.2 %collective-permute-start.9 = (bf16[2048,768]{1,0:T(8,128)(2,1)}, bf16[2048,768]{1,0:T(8,128)(2,1)}, u32[]{:S(2)}, u32[]{:S(2)}) collective-permute-start(bf16[2048,768]{1,0:T(8,128)(2,1)} %bitcast.27), channel_id=1, source_target_pairs={{0,65},{1,64},{2,67},{3,66},{4,69},{5,68},{6,71},{7,70},{8,73},{9,... | collective-permute-start | bytes 9437192 | tf_op jit(solution)/shard_map/ppermute | solution.py:87
  37.8 7.8 %collective-permute-start = (bf16[256,384]{1,0:T(8,128)(2,1)S(1)}, bf16[256,384]{1,0:T(8,128)(2,1)S(1)}, u32[]{:S(2)}, u32[]{:S(2)}) collective-permute-start(bf16[256,384]{1,0:T(8,128)(2,1)S(1)} %get-tuple-element.21), channel_id=1, source_target_pairs={{0,1},{1,0},{2,3},{3,2},{4,5},{5,4},{6,7},{7,6},{8,9},{9,8},{10,11... | collective-permute-start | bytes 589832 | tf_op jit(solution)/shard_map/ppermute | solution.py:111
  37.9 39.0 %collective-permute-start.5 = (bf16[384,768]{1,0:T(8,128)(2,1)S(1)}, bf16[384,768]{1,0:T(8,128)(2,1)}, u32[]{:S(2)}, u32[]{:S(2)}) collective-permute-start(bf16[384,768]{1,0:T(8,128)(2,1)S(1)} %bitcast.119), channel_id=1, source_target_pairs={{0,1},{1,0},{2,3},{3,2},{4,5},{5,4},{6,7},{7,6},{8,9},{9,8},{10,11... | collective-permute-start | bytes 1769480 | tf_op jit(solution)/shard_map/ppermute | solution.py:88
  39.9 21.1 %collective-permute-start.2 = (bf16[256,384]{1,0:T(8,128)(2,1)S(1)}, bf16[256,384]{1,0:T(8,128)(2,1)S(1)}, u32[]{:S(2)}, u32[]{:S(2)}) collective-permute-start(bf16[256,384]{1,0:T(8,128)(2,1)S(1)} %get-tuple-element.16), channel_id=1, source_target_pairs={{0,1},{1,0},{2,3},{3,2},{4,5},{5,4},{6,7},{7,6},{8,9},{9,8},{10,11... | collective-permute-start | bytes 589832 | tf_op jit(solution)/shard_map/ppermute | solution.py:106
  45.6 15.4 %copy-start.7 = (bf16[256,384]{1,0:T(8,128)(2,1)}, bf16[256,384]{1,0:T(8,128)(2,1)S(1)}, u32[]{:S(2)}) copy-start(bf16[256,384]{1,0:T(8,128)(2,1)S(1)} %collective-permute-done) | copy-start | bytes 589828
  45.7 15.9 %copy-start.10 = (bf16[1,3,768,384]{3,2,1,0:T(8,128)(2,1)S(1)}, bf16[1,3,768,384]{3,2,1,0:T(8,128)(2,1)}, u32[]{:S(2)}) copy-start(bf16[1,3,768,384]{3,2,1,0:T(8,128)(2,1)} %param.19) | copy-start | bytes 5308420
  68.4 20.2 %collective-permute-start.4 = (bf16[256,384]{0,1:T(8,128)(2,1)S(1)}, bf16[256,384]{0,1:T(8,128)(2,1)}, u32[]{:S(2)}, u32[]{:S(2)}) collective-permute-start(bf16[256,384]{0,1:T(8,128)(2,1)S(1)} %bitcast.125), channel_id=1, source_target_pairs={{0,1},{1,0},{2,3},{3,2},{4,5},{5,4},{6,7},{7,6},{8,9},{9,8},{10,11... | collective-permute-start | bytes 589832 | tf_op jit(solution)/shard_map/ppermute | solution.py:150
  75.0 7.3 %collective-permute-start.6 = (bf16[256,384]{0,1:T(8,128)(2,1)S(1)}, bf16[256,384]{0,1:T(8,128)(2,1)S(1)}, u32[]{:S(2)}, u32[]{:S(2)}) collective-permute-start(bf16[256,384]{0,1:T(8,128)(2,1)S(1)} %bitcast.127), channel_id=1, source_target_pairs={{0,1},{1,0},{2,3},{3,2},{4,5},{5,4},{6,7},{7,6},{8,9},{9,8},{10,11... | collective-permute-start | bytes 589832 | tf_op jit(solution)/shard_map/ppermute | solution.py:150
  84.1 4.5 %copy-start.6 = (bf16[256,384]{1,0:T(8,128)(2,1)S(1)}, bf16[256,384]{1,0:T(8,128)(2,1)}, u32[]{:S(2)}) copy-start(bf16[256,384]{1,0:T(8,128)(2,1)} %copy-done.5) | copy-start | bytes 589828
  88.2 10.6 %collective-permute-start.7 = (bf16[256,768]{1,0:T(8,128)(2,1)S(1)}, bf16[256,768]{1,0:T(8,128)(2,1)S(1)}, u32[]{:S(2)}, u32[]{:S(2)}) collective-permute-start(bf16[256,768]{1,0:T(8,128)(2,1)S(1)} %fusion.58), channel_id=1, source_target_pairs={{0,1},{1,0},{2,3},{3,2},{4,5},{5,4},{6,7},{7,6},{8,9},{9,8},{10,11... | collective-permute-start | bytes 1179656 | tf_op jit(solution)/shard_map/ppermute | solution.py:24
  99.5 14.0 %collective-permute-start.8 = (bf16[256,768]{1,0:T(8,128)(2,1)S(1)}, bf16[256,768]{1,0:T(8,128)(2,1)S(1)}, u32[]{:S(2)}, u32[]{:S(2)}) collective-permute-start(bf16[256,768]{1,0:T(8,128)(2,1)S(1)} %fusion.12), channel_id=1, source_target_pairs={{0,1},{1,0},{2,3},{3,2},{4,5},{5,4},{6,7},{7,6},{8,9},{9,8},{10,11... | collective-permute-start | bytes 1179656 | tf_op jit(solution)/shard_map/ppermute | solution.py:24
  99.9 22.5 %collective-permute-start.10 = (bf16[256,768]{1,0:T(8,128)(2,1)S(1)}, bf16[256,768]{1,0:T(8,128)(2,1)S(1)}, u32[]{:S(2)}, u32[]{:S(2)}) collective-permute-start(bf16[256,768]{1,0:T(8,128)(2,1)S(1)} %add_convert_fusion.3), channel_id=1, source_target_pairs={{0,2},{2,4},{4,6},{6,8},{8,10},{10,12},{12,14},{14,16},{16,18},{18... | collective-permute-start | bytes 1179656 | tf_op jit(solution)/shard_map/ppermute | solution.py:19
  128.2 7.8 %copy-start.1 = (bf16[4096,384]{1,0:T(8,128)(2,1)S(1)}, bf16[4096,384]{1,0:T(8,128)(2,1)}, u32[]{:S(2)}) copy-start(bf16[4096,384]{1,0:T(8,128)(2,1)} %param.14) | copy-start | bytes 9437188

commit v21 on v18

--- a/solution.py
+++ b/solution.py
@@ -148,10 +148,6 @@
             jnp.dot(normed, w_up[0], preferred_element_type=jnp.float32), approximate=True
         ).astype(jnp.bfloat16)
         partial_forward = jnp.dot(hidden, w_down[0], preferred_element_type=jnp.float32)
-        if chunk == 0:
-            sent_latent, partial_forward = lax.optimization_barrier(
-                (sent_latent, partial_forward)
-            )
         part = part + partner_sum(partial_forward)
         latent = layer_norm(part, norm_gain[2 * LAYERS], norm_bias[2 * LAYERS]).astype(jnp.bfloat16)
         if chunk == 1:

time: 124 us -> 122 us (0.984)
  the two profiles are of different devices: /device:TPU:31 before, /device:TPU:0 now
where the time goes in v21:
time: 122 us; the launch traced here: 121 us
  matrix products  36 us (30%)
  waiting for transfers between devices  29.6 us (24%)
  local copies, waits for them, and re-layouts  27.1 us (22%)
  starting transfers between devices  13.9 us (11%)
  other arithmetic  13.8 us (11%)
    ppermute x2, waiting for transfers between devices, body(): other_columns = lax.ppermute(embedded, 'head', [(0, 1), (1, 0)])  18.8 us
    ppermute x2, waiting for transfers between devices, partner_sum(): other = lax.ppermute(rounded, 'head', [(0, 1), (1, 0)])  8.49 us
    dot_general x2, matrix products, body(): jnp.dot(hidden, w_down[0], preferred_element_type=jnp.float32)  8.1 us
    dot_general x2, matrix products, body(): lax.dot_general(latent, decode_by_depth, (((1,), (2,)), ((), ())), prefer...  5.79 us
    sub x2, matrix products, body(): weights = jax.nn.softmax(scores, axis=-1).astype(jnp.bfloat16)  5.6 us
    unnamed x39, local copies, waits for them, and re-layouts  5.59 us
    dot_general x2, matrix products, body(): jnp.einsum('hts,shd->thd', weights, values, preferred_element_type=jnp.fl...  5.11 us
    reshape x1, local copies, waits for them, and re-layouts, embed_planes(): voxels = jnp.swapaxes(grouped, 1, 2).reshape(rows, PATCH, PATCH * PATCH)  4.86 us
  transfers between devices with their start and end apart: 10, of which 5 were waited for; matrix products, arithmetic and copies ran while one was open for 48% of the time, Pallas kernels for 0%

profile of v21, /device:TPU:0, one launch (start us, length us, event | category | flops | bytes accessed | tf_op | source)
XLA Modules:
  0.0 120.7 jit_solution(14499232065283973720)
XLA Ops:
  0.0 4.8 %copy.31 = bf16[768,2048]{0,1:T(8,128)(2,1)} copy(bf16[768,2048]{1,0:T(8,128)(2,1)} %param.23) | data formatting | bytes 6291456 | tf_op args[11]
  4.8 4.1 %collective-permute-start.6 = (bf16[2048,768]{1,0:T(8,128)(2,1)}, bf16[2048,768]{1,0:T(8,128)(2,1)}, u32[]{:S(2)}, u32[]{:S(2)}) collective-permute-start(bf16[2048,768]{1,0:T(8,128)(2,1)} %bitcast.114), channel_id=1, source_target_pairs={{0,65},{1,64},{2,67},{3,66},{4,69},{5,68},{6,71},{7,70},{8,73},{9,... | collective-permute-start | bytes 9437192 | tf_op jit(solution)/shard_map/ppermute | solution.py:87
  9.0 1.0 convert_element_type.136
  9.9 0.8 convert_element_type.135
  11.0 2.5 %broadcast_multiply_fusion = bf16[64,128,128]{2,1,0:T(8,128)(2,1)S(1)} fusion(bf16[64,128,128]{2,1,0:T(8,128)(2,1)} %param.12, bf16[64,128]{1,0:T(8,128)(2,1)S(1)} %convert_element_type.135), kind=kLoop, calls=%fused_computation.71 | loop fusion | flops 1048576 | bytes 4210688 | tf_op jit(solution)/shard_map/mul | solution.py:43
  13.5 1.9 %copy.26 = bf16[4,8,16,16,128]{4,3,2,1,0:T(8,128)(2,1)} copy(bf16[4,8,16,16,128]{4,3,1,2,0:T(8,128)(2,1)S(1)} %bitcast.116) | data formatting | bytes 4194304 | tf_op jit(solution)/shard_map/transpose | solution.py:44
  15.4 4.1 %copy.27 = bf16[32,128,256]{2,1,0:T(8,128)(2,1)} copy(bf16[32,128,256]{1,2,0:T(8,128)(2,1)} %bitcast.117) | data formatting | bytes 4194304 | tf_op jit(solution)/shard_map/transpose | solution.py:46
  19.5 4.9 %copy.28 = bf16[256,16,256]{0,1,2:T(8,128)(2,1)} copy(bf16[256,16,256]{2,1,0:T(8,128)(2,1)} %bitcast.118) | data formatting | bytes 4194304 | tf_op jit(solution)/shard_map/reshape | solution.py:46
  24.5 3.8 %fusion.96 = (bf16[256,384]{1,0:T(8,128)(2,1)S(1)}, bf16[256,384]{1,0:T(8,128)(2,1)}) fusion(f32[512,384]{1,0:T(8,128)} %convert_element_type.136, f32[32,384]{1,0:T(8,128)S(1)} %fusion.147, bf16[256,16,256]{0,1,2:T(8,128)(2,1)} %copy.28, bf16[16,256,384]{2,0,1:T(8,128)(2,1)S(1)} %bitcast.113), kind=kOutput, calls=%fused_computation.98 | convolution fusion | flops 805797888 | bytes 6471680 | tf_op jit(solution)/shard_map/dot_general | solution.py:47
  28.3 1.3 %collective-permute-start.1 = (bf16[256,384]{1,0:T(8,128)(2,1)}, bf16[256,384]{1,0:T(8,128)(2,1)S(1)}, u32[]{:S(2)}, u32[]{:S(2)}) collective-permute-start(bf16[256,384]{1,0:T(8,128)(2,1)} %get-tuple-element.16), channel_id=1, source_target_pairs={{2,0},{4,2},{6,4},{8,6},{10,8},{12,10},{14,12},{16,14},{18,16},{20... | collective-permute-start | bytes 589832 | tf_op jit(solution)/shard_map/ppermute | solution.py:19
  29.6 2.0 %collective-permute-start.4 = (bf16[384,768]{1,0:T(8,128)(2,1)}, bf16[384,768]{1,0:T(8,128)(2,1)}, u32[]{:S(2)}, u32[]{:S(2)}) collective-permute-start(bf16[384,768]{1,0:T(8,128)(2,1)} %bitcast.18), channel_id=1, source_target_pairs={{0,1},{1,0},{2,3},{3,2},{4,5},{5,4},{6,7},{7,6},{8,9},{9,8},{10,11... | collective-permute-start | bytes 1769480 | tf_op jit(solution)/shard_map/ppermute | solution.py:88
  31.7 0.6 iota_shift-right-logical_fusion
  32.3 0.5 broadcast_add_fusion
  32.9 1.0 fusion.124
  34.1 0.5 compare_and_fusion
  34.6 2.6 %collective-permute-done = bf16[256,384]{1,0:T(8,128)(2,1)S(1)} collective-permute-done((bf16[256,384]{1,0:T(8,128)(2,1)S(1)}, bf16[256,384]{1,0:T(8,128)(2,1)S(1)}, u32[]{:S(2)}, u32[]{:S(2)}) %collective-permute-start) | collective-permute-done | bytes 196640 | tf_op jit(solution)/shard_map/ppermute | solution.py:102
  37.3 0.6 copy-done.7
  37.9 16.2 %collective-permute-done.2 = bf16[256,384]{1,0:T(8,128)(2,1)S(1)} collective-permute-done((bf16[256,384]{1,0:T(8,128)(2,1)S(1)}, bf16[256,384]{1,0:T(8,128)(2,1)S(1)}, u32[]{:S(2)}, u32[]{:S(2)}) %collective-permute-start.2) | collective-permute-done | bytes 196640 | tf_op jit(solution)/shard_map/ppermute | solution.py:102
  54.4 0.3 multiply_reduce_fusion.2
  54.8 1.3 %fusion.55 = bf16[3,512,384]{1,2,0:T(8,128)(2,1)S(1)} fusion(bf16[1,3,768,384]{3,2,1,0:T(8,128)(2,1)S(1)} %copy-done.16, f32[256,768]{1,0:T(8,128)S(1)} %fusion.98, f32[256,768]{1,0:T(8,128)S(1)} %fusion.97, f32[768]{0:T(1024)S(1)} %get-tuple-element.9, f32[768]{0:T(1024)S(1)} %get-tuple-element.26, f32[512]{0:T(512)S(1)} %add_rsqrt_fusion, ...), kind=kOutput, calls=%fused_computation.52 | convolution fusion | flops 908918784 | bytes 4532224 | tf_op jit(solution)/shard_map/td,sde->ste/dot_general | solution.py:111
  56.2 2.8 %fusion.143 = (f32[6,256]{1,0:T(8,128)S(1)}, f32[6,256,512]{2,1,0:T(8,128)}) fusion(bf16[256,6,64]{0,2,1:T(8,128)(2,1)S(1)} %bitcast.133, bf16[512,6,64]{0,2,1:T(8,128)(2,1)S(1)} %bitcast.126), kind=kOutput, calls=%fused_computation.165 | convolution fusion | flops 103023104 | bytes 3741696 | tf_op jit(solution)/shard_map/sub | solution.py:134
  59.0 2.6 %fusion.74 = bf16[6,64,256]{2,1,0:T(8,128)(2,1)S(1)} fusion(bf16[512,6,64]{0,2,1:T(8,128)(2,1)S(1)} %bitcast.124, f32[6,256,512]{2,1,0:T(8,128)} %get-tuple-element.18, f32[6,256]{1,0:T(8,128)S(1)} %get-tuple-element.17), kind=kOutput, calls=%fused_computation.70 | convolution fusion | flops 102334464 | bytes 3741696 | tf_op jit(solution)/shard_map/hts,shd->thd/dot_general | solution.py:135
  61.7 2.8 %fusion.145 = (f32[6,256]{1,0:T(8,128)S(1)}, f32[6,256,512]{2,1,0:T(8,128)}) fusion(bf16[256,6,64]{0,2,1:T(8,128)(2,1)S(1)} %bitcast.132, bf16[512,6,64]{0,2,1:T(8,128)(2,1)S(1)} %bitcast.127), kind=kOutput, calls=%fused_computation.167 | convolution fusion | flops 103023104 | bytes 3741696 | tf_op jit(solution)/shard_map/sub | solution.py:134
  64.5 2.6 %fusion.73 = bf16[6,64,256]{2,1,0:T(8,128)(2,1)S(1)} fusion(bf16[512,6,64]{0,2,1:T(8,128)(2,1)S(1)} %bitcast.125, f32[6,256,512]{2,1,0:T(8,128)} %get-tuple-element.22, f32[6,256]{1,0:T(8,128)S(1)} %get-tuple-element.21), kind=kOutput, calls=%fused_computation.69 | convolution fusion | flops 102334464 | bytes 3741696 | tf_op jit(solution)/shard_map/hts,shd->thd/dot_general | solution.py:135
  67.0 2.3 %collective-permute-start.7 = (bf16[256,384]{0,1:T(8,128)(2,1)S(1)}, bf16[256,384]{0,1:T(8,128)(2,1)S(1)}, u32[]{:S(2)}, u32[]{:S(2)}) collective-permute-start(bf16[256,384]{0,1:T(8,128)(2,1)S(1)} %bitcast.130), channel_id=1, source_target_pairs={{0,1},{1,0},{2,3},{3,2},{4,5},{5,4},{6,7},{7,6},{8,9},{9,8},{10,11... | collective-permute-start | bytes 589832 | tf_op jit(solution)/shard_map/ppermute | solution.py:139
  69.3 1.4 %fusion.71 = f32[256,768]{1,0:T(8,128)S(1)} fusion(bf16[256,384]{0,1:T(8,128)(2,1)S(1)} %bitcast.129, bf16[1,384,768]{2,1,0:T(8,128)(2,1)} %param.20), kind=kOutput, calls=%fused_computation.66 | convolution fusion | flops 151388160 | bytes 1572864 | tf_op jit(solution)/shard_map/dot_general | solution.py:140
  70.7 1.5 %fusion.67 = f32[256,768]{1,0:T(8,128)S(1)} fusion(bf16[256,384]{0,1:T(8,128)(2,1)S(1)} %bitcast.131, bf16[1,384,768]{2,1,0:T(8,128)(2,1)} %param.20), kind=kOutput, calls=%fused_computation.60 | convolution fusion | flops 151388160 | bytes 1572864 | tf_op jit(solution)/shard_map/dot_general | solution.py:140
  72.2 2.3 %collective-permute-done.7 = bf16[256,384]{0,1:T(8,128)(2,1)S(1)} collective-permute-done((bf16[256,384]{0,1:T(8,128)(2,1)S(1)}, bf16[256,384]{0,1:T(8,128)(2,1)S(1)}, u32[]{:S(2)}, u32[]{:S(2)}) %collective-permute-start.7) | collective-permute-done | bytes 196640 | tf_op jit(solution)/shard_map/ppermute | solution.py:139
  74.5 1.6 %fusion.146 = (f32[256]{0:T(256)S(1)}, f32[256,768]{1,0:T(8,128)S(1)}) fusion(f32[256,768]{1,0:T(8,128)S(1)} %fusion.67, bf16[256,384]{0,1:T(8,128)(2,1)S(1)} %collective-permute-done.7, bf16[384,768]{1,0:T(8,128)(2,1)} %collective-permute-done.4, bf16[256,384]{1,0:T(8,128)(2,1)S(1)} %fusion.124, bf16[256,384]{1,0:T(8,128)(2,1)S(1)} %copy-done.9, pred[]{:T(512)S(6)} %eq.8), kind=kOutput, calls=%fused_computation.168 | convolution fusion | flops 153943808 | bytes 2753537 | tf_op jit(solution)/shard_map/dot_general | solution.py:141
  76.0 0.2 multiply_reduce_fusion.4
  76.3 4.1 %fusion.61 = bf16[256,768]{1,0:T(8,128)(2,1)S(1)} fusion(bf16[1,1536,768]{2,1,0:T(8,128)(2,1)} %param.22, bf16[1,768,1536]{2,1,0:T(8,128)(2,1)} %param.21, f32[256,768]{1,0:T(8,128)S(1)} %get-tuple-element.24, f32[256]{0:T(256)S(1)} %add_rsqrt_fusion.2, f32[256]{0:T(256)S(1)} %broadcast_multiply_fusion.3, f32[768]{0:T(1024)S(1)} %get-tuple-element.8, ...), kind=kOutput, calls=%fused_computation.54 | convolution fusion | flops 1212678144 | bytes 5906432 | tf_op jit(solution)/shard_map/dot_general | solution.py:150
  80.4 1.8 %collective-permute-start.8 = (bf16[256,768]{1,0:T(8,128)(2,1)S(1)}, bf16[256,768]{1,0:T(8,128)(2,1)S(1)}, u32[]{:S(2)}, u32[]{:S(2)}) collective-permute-start(bf16[256,768]{1,0:T(8,128)(2,1)S(1)} %fusion.61), channel_id=1, source_target_pairs={{0,1},{1,0},{2,3},{3,2},{4,5},{5,4},{6,7},{7,6},{8,9},{9,8},{10,11... | collective-permute-start | bytes 1179656 | tf_op jit(solution)/shard_map/ppermute | solution.py:24
  82.2 1.7 %fusion.144 = (f32[256]{0:T(256)S(1)}, f32[256,768]{1,0:T(8,128)S(1)}) fusion(f32[256,768]{1,0:T(8,128)S(1)} %fusion.71, bf16[256,384]{0,1:T(8,128)(2,1)} %collective-permute-done.3, bf16[384,768]{1,0:T(8,128)(2,1)} %collective-permute-done.4, bf16[256,384]{1,0:T(8,128)(2,1)S(1)} %copy-done.6, bf16[256,384]{1,0:T(8,128)(2,1)} %copy-done.7, pred[]{:T(512)S(6)} %eq.8), kind=kOutput, calls=%fused_computation.166 | convolution fusion | flops 153943808 | bytes 2753537 | tf_op jit(solution)/shard_map/dot_general | solution.py:141
  83.9 0.2 multiply_reduce_fusion.6
  84.2 4.0 %fusion.58 = bf16[256,768]{1,0:T(8,128)(2,1)S(1)} fusion(bf16[1,1536,768]{2,1,0:T(8,128)(2,1)} %param.22, bf16[1,768,1536]{2,1,0:T(8,128)(2,1)} %param.21, f32[256,768]{1,0:T(8,128)S(1)} %get-tuple-element.20, f32[768]{0:T(1024)S(1)} %get-tuple-element.8, f32[768]{0:T(1024)S(1)} %get-tuple-element.27, f32[256]{0:T(256)S(1)} %add_rsqrt_fusion.4, ...), kind=kOutput, calls=%fused_computation.53 | convolution fusion | flops 1212678144 | bytes 5906432 | tf_op jit(solution)/shard_map/dot_general | solution.py:150
  88.2 0.4 collective-permute-start.5
  88.6 3.6 %collective-permute-done.8 = bf16[256,768]{1,0:T(8,128)(2,1)S(1)} collective-permute-done((bf16[256,768]{1,0:T(8,128)(2,1)S(1)}, bf16[256,768]{1,0:T(8,128)(2,1)S(1)}, u32[]{:S(2)}, u32[]{:S(2)}) %collective-permute-start.8) | collective-permute-done | bytes 393248 | tf_op jit(solution)/shard_map/ppermute | solution.py:24
  92.4 0.3 multiply_reduce_fusion.3
  92.7 0.2 add_convert_fusion.1
  93.0 1.7 %collective-permute-start.9 = (bf16[256,768]{1,0:T(8,128)(2,1)S(1)}, bf16[256,768]{1,0:T(8,128)(2,1)S(1)}, u32[]{:S(2)}, u32[]{:S(2)}) collective-permute-start(bf16[256,768]{1,0:T(8,128)(2,1)S(1)} %add_convert_fusion.1), channel_id=1, source_target_pairs={{0,2},{2,4},{4,6},{6,8},{8,10},{10,12},{12,14},{14,16},{16,18},{18... | collective-permute-start | bytes 1179656 | tf_op jit(solution)/shard_map/ppermute | solution.py:19
  94.6 4.9 %collective-permute-done.5 = bf16[256,768]{1,0:T(8,128)(2,1)S(1)} collective-permute-done((bf16[256,768]{1,0:T(8,128)(2,1)S(1)}, bf16[256,768]{1,0:T(8,128)(2,1)S(1)}, u32[]{:S(2)}, u32[]{:S(2)}) %collective-permute-start.5) | collective-permute-done | bytes 393248 | tf_op jit(solution)/shard_map/ppermute | solution.py:24
  99.7 0.3 multiply_reduce_fusion.5
  100.0 4.5 %maximum_select_fusion = bf16[4096,768]{1,0:T(8,128)(2,1)S(1)} fusion(bf16[2048,768]{1,0:T(8,128)(2,1)} %collective-permute-done.6, bf16[2048,768]{1,0:T(8,128)(2,1)S(1)} %bitcast.115, pred[]{:T(512)S(6)} %eq.8), kind=kLoop, calls=%fused_computation.2 | loop fusion | flops 28311552 | bytes 12582913 | tf_op jit(solution)/shard_map/jit(_where)/select_n | solution.py:116
  104.6 2.6 %fusion.4 = bf16[256,16,256]{2,0,1:T(8,128)(2,1)S(1)} fusion(bf16[16,256,768]{2,0,1:T(8,128)(2,1)S(1)} %bitcast.121, f32[768]{0:T(1024)S(1)} %get-tuple-element.10, f32[768]{0:T(1024)S(1)} %get-tuple-element.25, f32[256]{0:T(256)S(1)} %add_rsqrt_fusion.3, f32[256]{0:T(256)S(1)} %broadcast_multiply_fusion.4, f32[256,768]{1,0:T(8,128)S(1)} %get-tuple-element.20, ...), kind=kOutput, calls=%fused_computation.5 | convolution fusion | flops 1612382208 | bytes 9969664 | tf_op jit(solution)/shard_map/dot_general | solution.py:161
  107.2 3.2 %divide_convert_fusion = bf16[256,16,256]{2,0,1:T(8,128)(2,1)S(1)} fusion(f32[]{:T(128)S(6)} %convert_element_type.176, s32[256]{0:T(256)S(1)} %copy-done.13, s32[256]{0:T(256)S(1)} %copy-done.14, s32[256]{0:T(256)S(1)} %copy-done.12, s32[256]{0:T(256)S(1)} %copy-done.15, bf16[256,16,256]{2,0,1:T(8,128)(2,1)S(1)} %fusion.4, ...), kind=kOutput, calls=%fused_computation.7 | convolution fusion | flops 1634729984 | bytes 10883588 | tf_op jit(solution)/shard_map/dot_general | solution.py:161
  110.5 2.5 %copy.34 = bf16[256,16,256]{2,1,0:T(8,128)(2,1)} copy(bf16[256,16,256]{2,0,1:T(8,128)(2,1)S(1)} %divide_convert_fusion) | data formatting | bytes 4194304 | tf_op jit(solution)/shard_map/convert_element_type | solution.py:178
  113.0 4.2 %copy.35 = bf16[32,256,128]{2,1,0:T(8,128)(2,1)} copy(bf16[32,256,128]{1,2,0:T(8,128)(2,1)} %bitcast.119) | data formatting | bytes 4194304 | tf_op jit(solution)/shard_map/transpose | solution.py:180
  117.2 3.5 %copy.36 = bf16[4,16,8,16,128]{4,3,2,1,0:T(8,128)(2,1)} copy(bf16[4,16,8,16,128]{4,3,1,2,0:T(8,128)(2,1)} %bitcast.120) | data formatting | bytes 4194304 | tf_op jit(solution)/shard_map/transpose | solution.py:181
  (67 shorter events, 1.9 us)
Async XLA Ops:
  0.0 24.5 %copy-start = (bf16[4096,384]{1,0:T(8,128)(2,1)S(1)}, bf16[4096,384]{1,0:T(8,128)(2,1)}, u32[]{:S(2)}) copy-start(bf16[4096,384]{1,0:T(8,128)(2,1)} %param.14) | copy-start | bytes 9437188
  0.0 9.0 %copy-start.3 = (bf16[512,384]{1,0:T(8,128)(2,1)S(1)}, bf16[512,384]{1,0:T(8,128)(2,1)}, u32[]{:S(2)}) copy-start(bf16[512,384]{1,0:T(8,128)(2,1)} %param.16) | copy-start | bytes 1179652
  4.8 95.2 %collective-permute-start.6 = (bf16[2048,768]{1,0:T(8,128)(2,1)}, bf16[2048,768]{1,0:T(8,128)(2,1)}, u32[]{:S(2)}, u32[]{:S(2)}) collective-permute-start(bf16[2048,768]{1,0:T(8,128)(2,1)} %bitcast.114), channel_id=1, source_target_pairs={{0,65},{1,64},{2,67},{3,66},{4,69},{5,68},{6,71},{7,70},{8,73},{9,... | collective-permute-start | bytes 9437192 | tf_op jit(solution)/shard_map/ppermute | solution.py:87
  19.5 4.9 %copy-start.4 = (bf16[256,384]{1,0:T(8,128)(2,1)S(1)}, bf16[256,384]{1,0:T(8,128)(2,1)}, u32[]{:S(2)}) copy-start(bf16[256,384]{1,0:T(8,128)(2,1)} %param.15) | copy-start | bytes 589828
  24.5 8.3 %copy-start.10 = (f32[3,768]{1,0:T(4,128)S(1)}, f32[3,768]{1,0:T(4,128)}, u32[]{:S(2)}) copy-start(f32[3,768]{1,0:T(4,128)} %param.18) | copy-start | bytes 27652
  24.5 8.3 %copy-start.11 = (f32[3,768]{1,0:T(4,128)S(1)}, f32[3,768]{1,0:T(4,128)}, u32[]{:S(2)}) copy-start(f32[3,768]{1,0:T(4,128)} %param.17) | copy-start | bytes 27652
  28.3 26.4 %copy-start.5 = (bf16[256,384]{1,0:T(8,128)(2,1)}, bf16[256,384]{1,0:T(8,128)(2,1)S(1)}, u32[]{:S(2)}) copy-start(bf16[256,384]{1,0:T(8,128)(2,1)S(1)} %get-tuple-element.15) | copy-start | bytes 589828
  28.3 4.6 %collective-permute-start.1 = (bf16[256,384]{1,0:T(8,128)(2,1)}, bf16[256,384]{1,0:T(8,128)(2,1)S(1)}, u32[]{:S(2)}, u32[]{:S(2)}) collective-permute-start(bf16[256,384]{1,0:T(8,128)(2,1)} %get-tuple-element.16), channel_id=1, source_target_pairs={{2,0},{4,2},{6,4},{8,6},{10,8},{12,10},{14,12},{16,14},{18,16},{20... | collective-permute-start | bytes 589832 | tf_op jit(solution)/shard_map/ppermute | solution.py:19
  29.6 7.7 %collective-permute-start = (bf16[256,384]{1,0:T(8,128)(2,1)S(1)}, bf16[256,384]{1,0:T(8,128)(2,1)S(1)}, u32[]{:S(2)}, u32[]{:S(2)}) collective-permute-start(bf16[256,384]{1,0:T(8,128)(2,1)S(1)} %get-tuple-element.15), channel_id=1, source_target_pairs={{0,1},{1,0},{2,3},{3,2},{4,5},{5,4},{6,7},{7,6},{8,9},{9,8},{10,11... | collective-permute-start | bytes 589832 | tf_op jit(solution)/shard_map/ppermute | solution.py:102
  29.6 42.6 %collective-permute-start.4 = (bf16[384,768]{1,0:T(8,128)(2,1)}, bf16[384,768]{1,0:T(8,128)(2,1)}, u32[]{:S(2)}, u32[]{:S(2)}) collective-permute-start(bf16[384,768]{1,0:T(8,128)(2,1)} %bitcast.18), channel_id=1, source_target_pairs={{0,1},{1,0},{2,3},{3,2},{4,5},{5,4},{6,7},{7,6},{8,9},{9,8},{10,11... | collective-permute-start | bytes 1769480 | tf_op jit(solution)/shard_map/ppermute | solution.py:88
  33.9 20.2 %collective-permute-start.2 = (bf16[256,384]{1,0:T(8,128)(2,1)S(1)}, bf16[256,384]{1,0:T(8,128)(2,1)S(1)}, u32[]{:S(2)}, u32[]{:S(2)}) collective-permute-start(bf16[256,384]{1,0:T(8,128)(2,1)S(1)} %fusion.124), channel_id=1, source_target_pairs={{0,1},{1,0},{2,3},{3,2},{4,5},{5,4},{6,7},{7,6},{8,9},{9,8},{10,11... | collective-permute-start | bytes 589832 | tf_op jit(solution)/shard_map/ppermute | solution.py:102
  37.3 0.7 copy-start.7
  37.9 16.8 %copy-start.16 = (bf16[1,3,768,384]{3,2,1,0:T(8,128)(2,1)S(1)}, bf16[1,3,768,384]{3,2,1,0:T(8,128)(2,1)}, u32[]{:S(2)}) copy-start(bf16[1,3,768,384]{3,2,1,0:T(8,128)(2,1)} %param.19) | copy-start | bytes 5308420
  54.1 0.7 copy-start.8
  61.6 20.6 %collective-permute-start.3 = (bf16[256,384]{0,1:T(8,128)(2,1)S(1)}, bf16[256,384]{0,1:T(8,128)(2,1)}, u32[]{:S(2)}, u32[]{:S(2)}) collective-permute-start(bf16[256,384]{0,1:T(8,128)(2,1)S(1)} %bitcast.128), channel_id=1, source_target_pairs={{0,1},{1,0},{2,3},{3,2},{4,5},{5,4},{6,7},{7,6},{8,9},{9,8},{10,11... | collective-permute-start | bytes 589832 | tf_op jit(solution)/shard_map/ppermute | solution.py:139
  67.0 7.5 %copy-start.9 = (bf16[256,384]{1,0:T(8,128)(2,1)S(1)}, bf16[256,384]{1,0:T(8,128)(2,1)}, u32[]{:S(2)}) copy-start(bf16[256,384]{1,0:T(8,128)(2,1)} %copy-done.8) | copy-start | bytes 589828
  67.0 7.4 %collective-permute-start.7 = (bf16[256,384]{0,1:T(8,128)(2,1)S(1)}, bf16[256,384]{0,1:T(8,128)(2,1)S(1)}, u32[]{:S(2)}, u32[]{:S(2)}) collective-permute-start(bf16[256,384]{0,1:T(8,128)(2,1)S(1)} %bitcast.130), channel_id=1, source_target_pairs={{0,1},{1,0},{2,3},{3,2},{4,5},{5,4},{6,7},{7,6},{8,9},{9,8},{10,11... | collective-permute-start | bytes 589832 | tf_op jit(solution)/shard_map/ppermute | solution.py:139
  76.3 5.9 %copy-start.6 = (bf16[256,384]{1,0:T(8,128)(2,1)S(1)}, bf16[256,384]{1,0:T(8,128)(2,1)}, u32[]{:S(2)}) copy-start(bf16[256,384]{1,0:T(8,128)(2,1)} %copy-done.5) | copy-start | bytes 589828
  80.4 11.9 %collective-permute-start.8 = (bf16[256,768]{1,0:T(8,128)(2,1)S(1)}, bf16[256,768]{1,0:T(8,128)(2,1)S(1)}, u32[]{:S(2)}, u32[]{:S(2)}) collective-permute-start(bf16[256,768]{1,0:T(8,128)(2,1)S(1)} %fusion.61), channel_id=1, source_target_pairs={{0,1},{1,0},{2,3},{3,2},{4,5},{5,4},{6,7},{7,6},{8,9},{9,8},{10,11... | collective-permute-start | bytes 1179656 | tf_op jit(solution)/shard_map/ppermute | solution.py:24
  88.2 11.3 %collective-permute-start.5 = (bf16[256,768]{1,0:T(8,128)(2,1)S(1)}, bf16[256,768]{1,0:T(8,128)(2,1)S(1)}, u32[]{:S(2)}, u32[]{:S(2)}) collective-permute-start(bf16[256,768]{1,0:T(8,128)(2,1)S(1)} %fusion.58), channel_id=1, source_target_pairs={{0,1},{1,0},{2,3},{3,2},{4,5},{5,4},{6,7},{7,6},{8,9},{9,8},{10,11... | collective-permute-start | bytes 1179656 | tf_op jit(solution)/shard_map/ppermute | solution.py:24
  92.7 7.3 %copy-start.2 = (bf16[768,2048]{0,1:T(8,128)(2,1)S(1)}, bf16[768,2048]{0,1:T(8,128)(2,1)}, u32[]{:S(2)}) copy-start(bf16[768,2048]{0,1:T(8,128)(2,1)} %copy.31) | copy-start | bytes 9437188
  93.0 14.2 %collective-permute-start.9 = (bf16[256,768]{1,0:T(8,128)(2,1)S(1)}, bf16[256,768]{1,0:T(8,128)(2,1)S(1)}, u32[]{:S(2)}, u32[]{:S(2)}) collective-permute-start(bf16[256,768]{1,0:T(8,128)(2,1)S(1)} %add_convert_fusion.1), channel_id=1, source_target_pairs={{0,2},{2,4},{4,6},{6,8},{8,10},{10,12},{12,14},{14,16},{16,18},{18... | collective-permute-start | bytes 1179656 | tf_op jit(solution)/shard_map/ppermute | solution.py:19
  104.5 2.6 %copy-start.12 = (s32[256]{0:T(256)S(1)}, s32[256]{0:T(256)}, u32[]{:S(2)}) copy-start(s32[256]{0:T(256)} %get-tuple-element.28) | copy-start | bytes 3076
  104.6 2.6 %copy-start.13 = (s32[256]{0:T(256)S(1)}, s32[256]{0:T(256)}, u32[]{:S(2)}) copy-start(s32[256]{0:T(256)} %get-tuple-element.29) | copy-start | bytes 3076
  104.6 2.6 %copy-start.14 = (s32[256]{0:T(256)S(1)}, s32[256]{0:T(256)}, u32[]{:S(2)}) copy-start(s32[256]{0:T(256)} %get-tuple-element.32) | copy-start | bytes 3076
  104.6 2.6 %copy-start.15 = (s32[256]{0:T(256)S(1)}, s32[256]{0:T(256)}, u32[]{:S(2)}) copy-start(s32[256]{0:T(256)} %get-tuple-element.33) | copy-start | bytes 3076
  104.6 2.6 %copy-start.17 = (pred[256]{0:T(512)(128)(4,1)S(1)}, pred[256]{0:T(512)(128)(4,1)}, u32[]{:S(2)}) copy-start(pred[256]{0:T(512)(128)(4,1)} %get-tuple-element.30) | copy-start | bytes 772
  104.6 2.6 %copy-start.18 = (pred[256]{0:T(512)(128)(4,1)S(1)}, pred[256]{0:T(512)(128)(4,1)}, u32[]{:S(2)}) copy-start(pred[256]{0:T(512)(128)(4,1)} %get-tuple-element.31) | copy-start | bytes 772
  113.0 7.8 %copy-start.1 = (bf16[4096,384]{1,0:T(8,128)(2,1)S(1)}, bf16[4096,384]{1,0:T(8,128)(2,1)}, u32[]{:S(2)}) copy-start(bf16[4096,384]{1,0:T(8,128)(2,1)} %param.14) | copy-start | bytes 9437188
